TPU v7x, 32 devices: a whole 2x2x4 slice. The times are simulated.
32 devices in a mesh: shots: 2 (over y), depth: 4 (over x, core), strip: 4 (over z).
Axes of the slice: x: 2, y: 2, z: 4, core: 2. Of those that a mesh axis runs over, the one named last changes fastest.
Arguments:
- surface: float32 [2, 8, 32, 2048], P(None, 'shots', 'strip'), parts along dimension 1, may hold values from -6 to 6
- omegas: float32 [4], replicated, may hold values from 1 to 3
- region_speed: float32 [8], replicated, may hold values from 1 to 2
- fd_coeff: float32 [8], replicated, may hold values from 0.02 to 0.08
- region_index: int32 [12, 32, 2048], P('depth', 'strip'), may hold values from 0 to 7
- ref_region: int32 [12], P('depth'), may hold values from 0 to 7
Outputs:
- image: float32 [12, 32, 4096], P('depth', 'strip', 'shots'), parts along dimension 2
There are 2 independent parts, one for each index of `shots`. A program takes and returns all parts, laid end to end along the dimension named above; an argument that names none is the same for every part. Nothing has to cross between parts.
All inputs are finite; a program needn't handle non-finite values.
Results may differ from a plain program's by a relative error of at most 0.00015.
Values sent between devices are 32-bit elements; how exact they have to be, the bound alone decides.
No kernel may reach another device: no remote copies, remote signals or barrier semaphores. Data moves between devices by JAX's collectives and lax.ppermute only.
A program may use at most 64 MiB of HBM per device.

v0:
```python
import math

import ml_dtypes
import numpy as np
import jax
import jax.numpy as jnp
from jax import lax
from jax.experimental import pallas as pl
from jax.experimental.pallas import tpu as pltpu
from jax.sharding import PartitionSpec as P

DAMPING = 0.05
PRECISE = lax.Precision.HIGHEST


def padded_2(cells, sides, width):
    for axis, dim in sides:
        count = lax.axis_size(axis)
        ends = count - 1
        head = lax.slice_in_dim(cells, 0, width, axis=dim)
        tail = lax.slice_in_dim(cells, cells.shape[dim] - width, cells.shape[dim], axis=dim)
        cells = jnp.concatenate(
            [
                lax.ppermute(tail, axis, [(i, (i + 1) % count) for i in range(ends)]),
                cells,
                lax.ppermute(head, axis, [((i + 1) % count, i) for i in range(ends)]),
            ],
            axis=dim,
        )
    return cells


def from_behind(value, axis, steps):
    count = lax.axis_size(axis)
    first, last = (max(0, -steps), min(count, count - steps))
    return lax.ppermute(value, axis, [(source, source + steps) for source in range(first, last)])


def complex_scale(values, cosine, sine_part):
    return jnp.stack(
        [values[0] * cosine - values[1] * sine_part, values[0] * sine_part + values[1] * cosine]
    )


def angle_pair(numerator, period):
    angle_grid = numerator.astype(jnp.float32) * (2.0 * math.pi / period)
    return (jnp.cos(angle_grid), jnp.sin(angle_grid))


def block_matrix(cosine, sine_part, forward):
    sign_flip = 1.0 if forward else -1.0
    return jnp.stack(
        [jnp.stack([cosine, -sign_flip * sine_part]), jnp.stack([sign_flip * sine_part, cosine])]
    )


def build_tables(line_len):
    block_len = 128
    outer_len = line_len // block_len
    inner_idx = jnp.arange(block_len)
    outer_idx = jnp.arange(outer_len)
    cos_large, sin_large = angle_pair(
        inner_idx[:, None] * inner_idx[None, :] % block_len, block_len
    )
    cos_small, sin_small = angle_pair(
        outer_idx[:, None] * outer_idx[None, :] % outer_len, outer_len
    )
    cos_twist, sin_twist = angle_pair(outer_idx[:, None] * inner_idx[None, :], line_len)
    wave_index = outer_idx[:, None] + outer_len * inner_idx[None, :]
    signed = jnp.where(wave_index >= line_len // 2, wave_index - line_len, wave_index)
    kx_grid = signed.astype(jnp.float32) * (2.0 * math.pi / line_len)
    small_fwd = block_matrix(cos_small, sin_small, True)
    small_inv = block_matrix(cos_small, sin_small, False)
    large_fwd = block_matrix(cos_large, sin_large, True)
    large_inv = block_matrix(cos_large, sin_large, False)
    return (small_fwd, small_inv, large_fwd, large_inv, cos_twist, sin_twist, kx_grid)


def forward_line(wavefield, tables):
    small_fwd, small_inv, large_fwd, large_inv, cos_twist, sin_twist, kx_grid = tables
    row_count = wavefield.shape[1]
    pieces = wavefield.reshape(2, row_count, cos_twist.shape[0], cos_twist.shape[1])
    mixed_part = jnp.einsum("zrab,zwca->wrcb", pieces, small_fwd, precision=PRECISE)
    mixed_part = complex_scale(mixed_part, cos_twist, -sin_twist)
    return jnp.einsum("zrcb,zwbd->wrcd", mixed_part, large_fwd, precision=PRECISE)


def inverse_line(spectrum, tables):
    small_fwd, small_inv, large_fwd, large_inv, cos_twist, sin_twist, kx_grid = tables
    row_count = spectrum.shape[1]
    line_len = cos_twist.shape[0] * cos_twist.shape[1]
    mixed_part = jnp.einsum("zrcd,zwdb->wrcb", spectrum, large_inv, precision=PRECISE)
    mixed_part = complex_scale(mixed_part, cos_twist, sin_twist)
    pieces = jnp.einsum("zrcb,zwca->wrab", mixed_part, small_inv, precision=PRECISE)
    return pieces.reshape(2, row_count, line_len) * (1.0 / line_len)


def lookup(regions, entries):
    picked = jnp.zeros(regions.shape, jnp.float32)
    for region_no in range(entries.shape[0]):
        picked = picked + jnp.where(regions == region_no, entries[region_no], 0.0)
    return picked


def depth_step(wavefield, omega_now, slow_cells, coef_cells, ref_slow, tables, pad_rows):
    kx_grid = tables[6]
    wave_ref = omega_now * ref_slow
    excess = wave_ref * wave_ref - kx_grid * kx_grid
    decay_line = jnp.exp(-jnp.sqrt(jnp.maximum(-excess, 0.0)))
    vertical = jnp.sqrt(jnp.maximum(excess, 0.0))
    spectrum = complex_scale(
        forward_line(wavefield, tables),
        decay_line * jnp.cos(vertical),
        decay_line * jnp.sin(vertical),
    )
    wavefield = inverse_line(spectrum, tables)
    phase_cell = omega_now * (slow_cells - ref_slow)
    wavefield = complex_scale(wavefield, jnp.cos(phase_cell), jnp.sin(phase_cell))
    padded = pad_rows(wavefield)
    laplace = (
        padded[:, :-2]
        + padded[:, 2:]
        + jnp.roll(wavefield, 1, 2)
        + jnp.roll(wavefield, -1, 2)
        - 4.0 * wavefield
    )
    return wavefield + complex_scale(laplace, DAMPING, coef_cells / omega_now)


def march(wavefield, omega_now, slow_block, coef_block, ref_block, tables, pad_rows):
    traces = []
    for step_no in range(slow_block.shape[0]):
        wavefield = depth_step(
            wavefield,
            omega_now,
            slow_block[step_no],
            coef_block[step_no],
            ref_block[step_no],
            tables,
            pad_rows,
        )
        traces.append(wavefield[0])
    return (wavefield, jnp.stack(traces))


def shards_general(surface, omegas, region_speed, fd_coeff, region_index, ref_region):
    line_len = surface.shape[3]
    rows_here = surface.shape[2]
    freq_count = surface.shape[1]
    step_count = region_index.shape[0]
    tables = build_tables(line_len)
    inv_speed = 1.0 / region_speed
    segment_no = lax.axis_index("depth")
    segment_count = lax.axis_size("depth")

    def pad_near(values):
        return padded_2(values, (("strip", 1),), 1)

    slow_cells = lookup(region_index, inv_speed)
    coef_cells = lookup(region_index, fd_coeff)
    ref_cells = lookup(ref_region, inv_speed)
    freq_index = jnp.arange(freq_count)
    image_out = jnp.zeros((step_count, rows_here, line_len), jnp.float32)
    arriving = jnp.zeros((2, rows_here, line_len), jnp.float32)
    tick_count = freq_count + segment_count - 1
    for tick_no in range(tick_count):
        batch_no = tick_no - segment_no
        is_live = (batch_no >= 0) & (batch_no < freq_count)
        clipped = jnp.clip(batch_no, 0, freq_count - 1)
        picked = lax.dynamic_index_in_dim(surface, clipped, 1, keepdims=False)
        entering = jnp.where(segment_no == 0, picked, arriving)
        omega_now = jnp.sum(jnp.where(freq_index == clipped, omegas, 0.0))
        leaving, traces = march(
            entering, omega_now, slow_cells, coef_cells, ref_cells, tables, pad_near
        )
        image_out = image_out + jnp.where(is_live, traces, 0.0)
        if tick_no + 1 < tick_count:
            arriving = from_behind(leaving, "depth", 1)
    return image_out


LANE = 128
FFT_BLOCKS = 16
ROW_CHUNK = 8


def fft4(x0, x1, x2, x3, sign):
    s0 = (x0[0] + x2[0], x0[1] + x2[1])
    d0 = (x0[0] - x2[0], x0[1] - x2[1])
    s1 = (x1[0] + x3[0], x1[1] + x3[1])
    d1 = (x1[0] - x3[0], x1[1] - x3[1])
    if sign < 0:
        wd = (d1[1], -d1[0])
    else:
        wd = (-d1[1], d1[0])
    return (
        (s0[0] + s1[0], s0[1] + s1[1]),
        (d0[0] + wd[0], d0[1] + wd[1]),
        (s0[0] - s1[0], s0[1] - s1[1]),
        (d0[0] - wd[0], d0[1] - wd[1]),
    )


def turn_const(value, power, sign):
    if power == 4:
        return (-value[1], value[0]) if sign > 0 else (value[1], -value[0])
    angle = sign * 2.0 * math.pi * power / 16.0
    cr, ci = (math.cos(angle), math.sin(angle))
    return (value[0] * cr - value[1] * ci, value[0] * ci + value[1] * cr)


def fft16(parts, sign):
    mid = [[None] * 4 for _ in range(4)]
    for a0 in range(4):
        ys = fft4(parts[a0], parts[4 + a0], parts[8 + a0], parts[12 + a0], sign)
        for c0 in range(4):
            power = a0 * c0
            mid[a0][c0] = ys[c0] if power == 0 else turn_const(ys[c0], power, sign)
    out = [None] * 16
    for c0 in range(4):
        zs = fft4(mid[0][c0], mid[1][c0], mid[2][c0], mid[3][c0], sign)
        for c1 in range(4):
            out[c0 + 4 * c1] = zs[c1]
    return out


def pick(regions, values):
    level = list(values)
    bit = 1
    while len(level) > 1:
        chosen = (regions & bit) != 0
        level = [jnp.where(chosen, level[i + 1], level[i]) for i in range(0, len(level), 2)]
        bit *= 2
    return jnp.broadcast_to(level[0], regions.shape)


def split_dot(values, hi_ref, lo_ref):
    high = values.astype(jnp.bfloat16)
    low = (values - high.astype(jnp.float32)).astype(jnp.bfloat16)
    main = jnp.dot(high, hi_ref[...], preferred_element_type=jnp.float32)
    fix = jnp.dot(high, lo_ref[...], preferred_element_type=jnp.float32) + jnp.dot(
        low, hi_ref[:, :], preferred_element_type=jnp.float32
    )
    return main + fix


def section_kernel(
    tab_ref, w_ref, rid_ref, mult_ref, tw_ref, fhi_ref, flo_ref, ghi_ref, glo_ref,
    wout_ref, img_ref, a_ref, y_ref, v_ref, *, table_len
):
    rows = w_ref.shape[1]
    line_len = w_ref.shape[2]
    steps = rid_ref.shape[0]
    chunks = rows // ROW_CHUNK
    inv_len = 1.0 / line_len
    wout_ref[...] = w_ref[...]

    def blk(a):
        return slice(a * LANE, (a + 1) * LANE)

    def one_step(k, carry):
        base = k * (3 * table_len)
        cos_t = [tab_ref[base + g] for g in range(table_len)]
        sin_t = [tab_ref[base + table_len + g] for g in range(table_len)]
        gain_t = [tab_ref[base + 2 * table_len + g] for g in range(table_len)]

        def forward_chunk(i, c):
            y0 = pl.multiple_of(i * ROW_CHUNK, ROW_CHUNK)
            parts = [
                (wout_ref[0, pl.ds(y0, ROW_CHUNK), blk(a)], wout_ref[1, pl.ds(y0, ROW_CHUNK), blk(a)])
                for a in range(FFT_BLOCKS)
            ]
            spec = fft16(parts, -1)
            for cc in range(FFT_BLOCKS):
                tc = tw_ref[0, cc:cc + 1, :]
                ts = tw_ref[1, cc:cc + 1, :]
                xr, xi = spec[cc]
                a_ref[pl.ds(cc * rows + y0, ROW_CHUNK), 0:LANE] = xr * tc + xi * ts
                a_ref[pl.ds(cc * rows + y0, ROW_CHUNK), LANE:2 * LANE] = xi * tc - xr * ts
            return c

        lax.fori_loop(0, chunks, forward_chunk, 0)
        y_ref[...] = split_dot(a_ref[...], fhi_ref, flo_ref)
        for cc in range(FFT_BLOCKS):
            band = slice(cc * rows, (cc + 1) * rows)
            yr = y_ref[band, 0:LANE]
            yi = y_ref[band, LANE:2 * LANE]
            mr = mult_ref[k, 0, cc:cc + 1, :]
            mi = mult_ref[k, 1, cc:cc + 1, :]
            a_ref[band, 0:LANE] = yr * mr - yi * mi
            a_ref[band, LANE:2 * LANE] = yr * mi + yi * mr
        y_ref[...] = split_dot(a_ref[...], ghi_ref, glo_ref)

        def inverse_chunk(i, c):
            y0 = pl.multiple_of(i * ROW_CHUNK, ROW_CHUNK)
            parts = []
            for cc in range(FFT_BLOCKS):
                zr = y_ref[pl.ds(cc * rows + y0, ROW_CHUNK), 0:LANE]
                zi = y_ref[pl.ds(cc * rows + y0, ROW_CHUNK), LANE:2 * LANE]
                tc = tw_ref[0, cc:cc + 1, :]
                ts = tw_ref[1, cc:cc + 1, :]
                parts.append((zr * tc - zi * ts, zr * ts + zi * tc))
            back = fft16(parts, 1)
            for a in range(FFT_BLOCKS):
                ur = back[a][0] * inv_len
                ui = back[a][1] * inv_len
                regions = rid_ref[k, pl.ds(y0, ROW_CHUNK), blk(a)]
                cs = pick(regions, cos_t)
                sn = pick(regions, sin_t)
                v_ref[0, pl.ds(y0, ROW_CHUNK), blk(a)] = ur * cs - ui * sn
                v_ref[1, pl.ds(y0, ROW_CHUNK), blk(a)] = ur * sn + ui * cs
            return c

        lax.fori_loop(0, chunks, inverse_chunk, 0)
        row_id = lax.broadcasted_iota(jnp.int32, (rows, LANE), 0)
        lane_id = lax.broadcasted_iota(jnp.int32, (rows, LANE), 1)
        for a in range(FFT_BLOCKS):
            prev_b = blk((a - 1) % FFT_BLOCKS)
            next_b = blk((a + 1) % FFT_BLOCKS)
            lap = []
            here = []
            for part in range(2):
                v = v_ref[part, :, blk(a)]
                vp = v_ref[part, :, prev_b]
                vn = v_ref[part, :, next_b]
                above = jnp.where(row_id == 0, 0.0, pltpu.roll(v, 1, 0))
                below = jnp.where(row_id == rows - 1, 0.0, pltpu.roll(v, rows - 1, 0))
                left = jnp.where(lane_id == 0, pltpu.roll(vp, 1, 1), pltpu.roll(v, 1, 1))
                right = jnp.where(
                    lane_id == LANE - 1, pltpu.roll(vn, LANE - 1, 1), pltpu.roll(v, LANE - 1, 1)
                )
                lap.append(above + below + left + right - 4.0 * v)
                here.append(v)
            gain = pick(rid_ref[k, :, blk(a)], gain_t)
            new_re = here[0] + (lap[0] * DAMPING - lap[1] * gain)
            new_im = here[1] + (lap[0] * gain + lap[1] * DAMPING)
            wout_ref[0, :, blk(a)] = new_re
            wout_ref[1, :, blk(a)] = new_im
            img_ref[k, :, blk(a)] = new_re
        return carry

    lax.fori_loop(0, steps, one_step, 0)


def fast_constants(line_len):
    outer = line_len // LANE
    b = np.arange(LANE)
    ang = 2.0 * np.pi * (np.outer(b, b) % LANE) / LANE
    cos_m, sin_m = (np.cos(ang), np.sin(ang))
    fwd = np.block([[cos_m, -sin_m], [sin_m, cos_m]])
    inv = np.block([[cos_m, sin_m], [-sin_m, cos_m]])

    def halves(m):
        hi = m.astype(ml_dtypes.bfloat16)
        lo = (m - hi.astype(np.float64)).astype(ml_dtypes.bfloat16)
        return (hi, lo)

    c = np.arange(outer)
    tw_ang = 2.0 * np.pi * np.outer(c, b) / line_len
    twiddle = np.stack([np.cos(tw_ang), np.sin(tw_ang)]).astype(np.float32)
    q = c[:, None] + outer * b[None, :]
    signed = np.where(q >= line_len // 2, q - line_len, q).astype(np.float32)
    kx_cd = signed * np.float32(2.0 * math.pi / line_len)
    return (halves(fwd), halves(inv), twiddle, kx_cd.astype(np.float32))


def run_section(wave, regions, table, mult, consts):
    (fhi, flo), (ghi, glo), twiddle, _ = consts
    rows, line_len = wave.shape[1], wave.shape[2]
    steps = regions.shape[0]
    table_len = table.shape[0] // (3 * steps)
    vmem = pl.BlockSpec(memory_space=pltpu.VMEM)
    flops = steps * (2 * 3 * 2 * (FFT_BLOCKS * rows) * 256 * 256 + 400 * rows * line_len)
    return pl.pallas_call(
        lambda *refs: section_kernel(*refs, table_len=table_len),
        out_shape=(
            jax.ShapeDtypeStruct(wave.shape, jnp.float32),
            jax.ShapeDtypeStruct((steps, rows, line_len), jnp.float32),
        ),
        in_specs=[pl.BlockSpec(memory_space=pltpu.SMEM)] + [vmem] * 8,
        out_specs=(vmem, vmem),
        scratch_shapes=[
            pltpu.VMEM((FFT_BLOCKS * rows, 2 * LANE), jnp.float32),
            pltpu.VMEM((FFT_BLOCKS * rows, 2 * LANE), jnp.float32),
            pltpu.VMEM((2, rows, line_len), jnp.float32),
        ],
        cost_estimate=pl.CostEstimate(
            flops=flops, transcendentals=0, bytes_accessed=4 * rows * line_len * 6 * steps
        ),
    )(table, wave, regions, mult, jnp.asarray(twiddle), jnp.asarray(fhi), jnp.asarray(flo),
      jnp.asarray(ghi), jnp.asarray(glo))


def section_tables(omega, region_speed, fd_coeff, ref_region, kx_cd):
    inv_speed = 1.0 / region_speed
    ref_slow = inv_speed[ref_region]
    regions = region_speed.shape[0]
    padded = 1 << max(1, (regions - 1).bit_length())
    extra = padded - regions
    phase = omega * (inv_speed[None, :] - ref_slow[:, None])
    gain = jnp.broadcast_to(fd_coeff / omega, phase.shape)
    parts = [jnp.cos(phase), jnp.sin(phase), gain]
    if extra:
        parts = [jnp.concatenate([p, jnp.repeat(p[:, -1:], extra, axis=1)], axis=1) for p in parts]
    table = jnp.stack(parts, axis=1).reshape(-1)
    wave_ref = omega * ref_slow
    wave_ref = wave_ref[:, None, None]
    excess = wave_ref * wave_ref - kx_cd * kx_cd
    decay_line = jnp.exp(-jnp.sqrt(jnp.maximum(-excess, 0.0)))
    vertical = jnp.sqrt(jnp.maximum(excess, 0.0))
    mult = jnp.stack([decay_line * jnp.cos(vertical), decay_line * jnp.sin(vertical)], axis=1)
    return (table, mult)


def fast_fits(surface, region_index, region_speed):
    freq_count = surface.shape[1]
    rows = surface.shape[2] * lax.axis_size("strip")
    line_len = surface.shape[3]
    return (
        freq_count == lax.axis_size("strip")
        and line_len == FFT_BLOCKS * LANE
        and rows % ROW_CHUNK == 0
        and rows <= 64
        and region_speed.shape[0] <= 16
    )


def shards(surface, omegas, region_speed, fd_coeff, region_index, ref_region):
    if not fast_fits(surface, region_index, region_speed):
        return shards_general(surface, omegas, region_speed, fd_coeff, region_index, ref_region)
    line_len = surface.shape[3]
    segment_no = lax.axis_index("depth")
    segment_count = lax.axis_size("depth")
    strip_no = lax.axis_index("strip")
    consts = fast_constants(line_len)
    regions = lax.all_gather(region_index, "strip", axis=1, tiled=True)
    wave = lax.all_to_all(surface, "strip", 1, 2, tiled=True)[:, 0]
    omega = lax.dynamic_index_in_dim(omegas, strip_no, 0, keepdims=False)
    table, mult = section_tables(omega, region_speed, fd_coeff, ref_region, jnp.asarray(consts[3]))
    image = jnp.zeros(regions.shape, jnp.float32)

    def live(wave, image):
        return run_section(wave, regions, table, mult, consts)

    def idle(wave, image):
        return (wave, image)

    for tick_no in range(segment_count):
        wave, image = lax.cond(segment_no == tick_no, live, idle, wave, image)
        if tick_no + 1 < segment_count:
            wave = from_behind(wave, "depth", 1)
    return lax.psum_scatter(image, "strip", scatter_dimension=1, tiled=True)


def solution(mesh):
    in_specs = (
        P(None, "shots", "strip", None),
        P(),
        P(),
        P(),
        P("depth", "strip", None),
        P("depth"),
    )
    out_specs = P("depth", "strip", "shots")
    return jax.shard_map(shards, mesh=mesh, in_specs=in_specs, out_specs=out_specs, check_vma=False)
```

profile of v0, /device:TPU:0, one launch (start us, length us, event | category | flops | bytes accessed | tf_op | source)
XLA Modules:
  0.0 126.1 jit_solution(17725686521726236681)
XLA Ops:
  6.5 1.9 %copy.14 = f32[2,4,8,2048]{3,2,0,1:T(8,128)} copy(f32[2,4,8,2048]{3,2,1,0:T(8,128)} %param.20) | data formatting | bytes 1048576 | tf_op args[0]
  8.4 6.3 %all-to-all-start = ((f32[2,4,8,2048]{3,2,0,1:T(8,128)}), f32[2,4,8,2048]{3,2,0,1:T(8,128)S(1)}, u32[]{:S(2)}, u32[]{:S(2)}) async-start(f32[2,4,8,2048]{3,2,0,1:T(8,128)} %copy.14), calls=%async_computation | async-start | bytes 1048576 | tf_op jit(solution)/shard_map/all_to_all | solution.py:437
  14.8 0.0 reduce-scatter.2.cloned.1.call-start
  14.8 0.7 copy-done.1
  15.4 0.7 copy-done.2
  16.1 0.0 copy-start.3
  16.1 0.6 copy-done.3
  16.7 0.7 dynamic_slice.4
  17.4 0.6 gather_fusion
  18.0 0.9 fusion.10
  18.9 0.7 broadcast_divide_fusion
  19.6 0.1 reshape.129
  19.7 0.7 multiply_multiply_fusion
  20.4 0.0 copy-done.5
  20.4 0.2 fusion.5
  20.7 22.2 %all_gather.3 = s32[3,32,2048]{2,1,0:T(8,128)S(1)} all-gather(s32[3,8,2048]{2,1,0:T(8,128)S(1)} %copy-done), channel_id=1, replica_groups=mesh['shots'=2,'depth'=4,'strip'=4] {'strip'}, dimensions={1}, use_global_device_ids=true | all-gather | bytes 983040 | tf_op jit(solution)/shard_map/all_gather | solution.py:436
  42.9 0.0 copy-start.10
  42.9 0.0 all-to-all-done
  42.9 0.8 copy-done.6
  43.7 0.1 copy-done.7
  43.8 0.1 copy-done.8
  43.9 0.1 copy-done.9
  43.9 8.1 %conditional.4 = ((f32[2,32,2048]{2,1,0:T(8,128)S(1)}, f32[3,32,2048]{2,1,0:T(8,128)})) conditional(s32[]{:T(128)} %convert_element_type.15, f32[2,32,2048]{2,1,0:T(8,128)S(1)} %bitcast.4, (f32[72]{0:T(128)S(1)}, f32[2,32,2048]{2,1,0:T(8,128)S(1)}, s32[3,32,2048]{2,1,0:T(8,128)S(1)}, f32[3,2,16,128]{3,2,1,0:T(8,128)S(1)}, ...), branch_computations={%region_0.1_spmd, %region_1.2_spmd} | conditional | flops 1286602752 | bytes 4718600 | solution.py:449
  43.9 8.1 %branch_1_fun.4 = (f32[2,32,2048]{2,1,0:T(8,128)S(1)}, f32[3,32,2048]{2,1,0:T(8,128)}) custom-call(f32[72]{0:T(128)S(1)} %get-tuple-element.95.refs_0_, f32[2,32,2048]{2,1,0:T(8,128)S(1)} %get-tuple-element.96.refs_1_, s32[3,32,2048]{2,1,0:T(8,128)S(1)} %get-tuple-element.97.refs_2_, f32[3,2,16,128]{3,2,1,0:T(8,128)S(1)} %get-tuple-element.98.refs_3_, ...), custom_call_target="tpu_custom_call" | custom-call | flops 1286602752 | bytes 4718592 | tf_op jit(solution)/shard_map/cond/branch_1_fun/pallas_call | solution.py:374
  52.1 1.3 %collective-permute-start = (f32[2,32,2048]{2,1,0:T(8,128)S(1)}, f32[2,32,2048]{2,1,0:T(8,128)S(1)}, u32[]{:S(2)}, u32[]{:S(2)}) collective-permute-start(f32[2,32,2048]{2,1,0:T(8,128)S(1)} %get-tuple-element.138), channel_id=1, source_target_pairs={{0,4},{4,8},{8,12},{1,5},{5,9},{9,13},{2,6},{6,10},{10,14},{3,7},{... | collective-permute-start | bytes 1572872 | tf_op jit(solution)/shard_map/ppermute | solution.py:36
  53.4 1.5 %collective-permute-done = f32[2,32,2048]{2,1,0:T(8,128)S(1)} collective-permute-done((f32[2,32,2048]{2,1,0:T(8,128)S(1)}, f32[2,32,2048]{2,1,0:T(8,128)S(1)}, u32[]{:S(2)}, u32[]{:S(2)}) %collective-permute-start) | collective-permute-done | bytes 524320 | tf_op jit(solution)/shard_map/ppermute | solution.py:36
  54.9 11.8 %collective-permute-start.1 = (f32[2,32,2048]{2,1,0:T(8,128)S(1)}, f32[2,32,2048]{2,1,0:T(8,128)S(1)}, u32[]{:S(2)}, u32[]{:S(2)}) collective-permute-start(f32[2,32,2048]{2,1,0:T(8,128)S(1)} %get-tuple-element.140), channel_id=1, source_target_pairs={{0,4},{4,8},{8,12},{1,5},{5,9},{9,13},{2,6},{6,10},{10,14},{3,7},{... | collective-permute-start | bytes 1572872 | tf_op jit(solution)/shard_map/ppermute | solution.py:36
  66.7 1.5 %collective-permute-done.1 = f32[2,32,2048]{2,1,0:T(8,128)S(1)} collective-permute-done((f32[2,32,2048]{2,1,0:T(8,128)S(1)}, f32[2,32,2048]{2,1,0:T(8,128)S(1)}, u32[]{:S(2)}, u32[]{:S(2)}) %collective-permute-start.1) | collective-permute-done | bytes 524320 | tf_op jit(solution)/shard_map/ppermute | solution.py:36
  68.2 6.5 %collective-permute-start.2 = (f32[2,32,2048]{2,1,0:T(8,128)S(1)}, f32[2,32,2048]{2,1,0:T(8,128)S(1)}, u32[]{:S(2)}, u32[]{:S(2)}) collective-permute-start(f32[2,32,2048]{2,1,0:T(8,128)S(1)} %get-tuple-element.143), channel_id=1, source_target_pairs={{0,4},{4,8},{8,12},{1,5},{5,9},{9,13},{2,6},{6,10},{10,14},{3,7},{... | collective-permute-start | bytes 1572872 | tf_op jit(solution)/shard_map/ppermute | solution.py:36
  74.7 1.5 %collective-permute-done.2 = f32[2,32,2048]{2,1,0:T(8,128)S(1)} collective-permute-done((f32[2,32,2048]{2,1,0:T(8,128)S(1)}, f32[2,32,2048]{2,1,0:T(8,128)S(1)}, u32[]{:S(2)}, u32[]{:S(2)}) %collective-permute-start.2) | collective-permute-done | bytes 524320 | tf_op jit(solution)/shard_map/ppermute | solution.py:36
  76.2 0.0 reduce-scatter.2.cloned.1.call-update
  76.2 43.0 %reduce-scatter.2.cloned.1.call-done = f32[3,8,2048]{2,1,0:T(8,128)} async-done(((f32[3,32,2048]{2,1,0:T(8,128)}), f32[3,8,2048]{2,1,0:T(8,128)}) %reduce-scatter.2.cloned.1.call-update) | async-done | bytes 196624 | tf_op jit(solution)/shard_map/reduce_scatter | solution.py:452
  (22 shorter events, 0.1 us)
Async XLA Ops:
  8.4 34.4 %all-to-all-start = ((f32[2,4,8,2048]{3,2,0,1:T(8,128)}), f32[2,4,8,2048]{3,2,0,1:T(8,128)S(1)}, u32[]{:S(2)}, u32[]{:S(2)}) async-start(f32[2,4,8,2048]{3,2,0,1:T(8,128)} %copy.14), calls=%async_computation | async-start | bytes 1048576 | tf_op jit(solution)/shard_map/all_to_all | solution.py:437
  14.8 104.5 %reduce-scatter.2.cloned.1.call-start = ((), (), s32[]{:S(2)}) async-start(), calls=%async_computation.2 | async-start | bytes 983040 | tf_op jit(solution)/shard_map/reduce_scatter | solution.py:452
  14.8 0.7 copy-start.1
  15.4 0.7 copy-start.2
  16.1 0.7 copy-start.3
  17.4 1.5 %copy-start.4 = (f32[8]{0:T(128)S(1)}, f32[8]{0:T(128)}, u32[]{:S(2)}) copy-start(f32[8]{0:T(128)} %param.23) | copy-start | bytes 100
  17.4 3.0 %copy-start.5 = (f32[16,128]{1,0:T(8,128)S(1)}, f32[16,128]{1,0:T(8,128)}, u32[]{:S(2)}) copy-start(f32[16,128]{1,0:T(8,128)} %constant.50) | copy-start | bytes 24580
  18.0 2.6 %copy-start = (s32[3,8,2048]{2,1,0:T(8,128)S(1)}, s32[3,8,2048]{2,1,0:T(8,128)}, u32[]{:S(2)}) copy-start(s32[3,8,2048]{2,1,0:T(8,128)} %param.24) | copy-start | bytes 589828
  42.8 0.9 copy-start.6
  42.8 1.0 copy-start.7
  42.8 1.0 copy-start.8
  42.8 1.1 copy-start.9
  42.9 1.1 copy-start.10
  52.1 2.8 %collective-permute-start = (f32[2,32,2048]{2,1,0:T(8,128)S(1)}, f32[2,32,2048]{2,1,0:T(8,128)S(1)}, u32[]{:S(2)}, u32[]{:S(2)}) collective-permute-start(f32[2,32,2048]{2,1,0:T(8,128)S(1)} %get-tuple-element.138), channel_id=1, source_target_pairs={{0,4},{4,8},{8,12},{1,5},{5,9},{9,13},{2,6},{6,10},{10,14},{3,7},{... | collective-permute-start | bytes 1572872 | tf_op jit(solution)/shard_map/ppermute | solution.py:36
  54.9 13.3 %collective-permute-start.1 = (f32[2,32,2048]{2,1,0:T(8,128)S(1)}, f32[2,32,2048]{2,1,0:T(8,128)S(1)}, u32[]{:S(2)}, u32[]{:S(2)}) collective-permute-start(f32[2,32,2048]{2,1,0:T(8,128)S(1)} %get-tuple-element.140), channel_id=1, source_target_pairs={{0,4},{4,8},{8,12},{1,5},{5,9},{9,13},{2,6},{6,10},{10,14},{3,7},{... | collective-permute-start | bytes 1572872 | tf_op jit(solution)/shard_map/ppermute | solution.py:36
  68.2 8.0 %collective-permute-start.2 = (f32[2,32,2048]{2,1,0:T(8,128)S(1)}, f32[2,32,2048]{2,1,0:T(8,128)S(1)}, u32[]{:S(2)}, u32[]{:S(2)}) collective-permute-start(f32[2,32,2048]{2,1,0:T(8,128)S(1)} %get-tuple-element.143), channel_id=1, source_target_pairs={{0,4},{4,8},{8,12},{1,5},{5,9},{9,13},{2,6},{6,10},{10,14},{3,7},{... | collective-permute-start | bytes 1572872 | tf_op jit(solution)/shard_map/ppermute | solution.py:36
Sparse Core Ops, SparseCore 0:
  76.4 42.8 reduce-scatter.1
where the time goes:
time: 126 us
  waiting for transfers between devices  47.5 us (38%)
  starting transfers between devices  26 us (21%)
  blocking collectives  22.2 us (18%)
  between operations  13.6 us (11%)
  Pallas kernels  8.13 us (6%)
  local copies, waits for them, and re-layouts  6.31 us (5%)
  other arithmetic  2.46 us (2%)
    reduce_scatter x1, waiting for transfers between devices, shards(): return lax.psum_scatter(image, 'strip', scatter_dimension=1, tiled=True)  43 us
    all_gather x1, blocking collectives, shards(): regions = lax.all_gather(region_index, 'strip', axis=1, tiled=True)  22.2 us
    ppermute x3, starting transfers between devices, from_behind(): lax.ppermute(value, axis, [(source, source + steps) for source in range(f...  19.7 us
    pallas_call x1, Pallas kernels, run_section(): pl.pallas_call(lambda *refs: section_kernel(*refs, table_len=table_len),...  8.13 us
    all_to_all x1, starting transfers between devices, shards(): wave = lax.all_to_all(surface, 'strip', 1, 2, tiled=True)[:, 0]  6.32 us
    unnamed x23, local copies, waits for them, and re-layouts  4.89 us
    ppermute x3, waiting for transfers between devices, from_behind(): lax.ppermute(value, axis, [(source, source + steps) for source in range(f...  4.44 us
  transfers between devices with their start and end apart: 5, of which 4 were waited for; matrix products, arithmetic and copies ran while one was open for 3% of the time, Pallas kernels for 0%

commit v1 on v0

--- a/solution.py
+++ b/solution.py
@@ -425,16 +425,50 @@
     )
 
 
+def strip_pairs(depths, strip_count, shift):
+    return [
+        (d * strip_count + r, d * strip_count + (r + shift) % strip_count)
+        for d in depths
+        for r in range(strip_count)
+    ]
+
+
+def gather_rows(local, depths, strip_no, strip_count, row_axis):
+    rows = local.shape[row_axis]
+    shape = list(local.shape)
+    shape[row_axis] = rows * strip_count
+    full = jnp.zeros(shape, local.dtype)
+    start = [0] * len(shape)
+    start[row_axis] = strip_no * rows
+    full = lax.dynamic_update_slice(full, local, start)
+    for shift in range(1, strip_count):
+        got = lax.ppermute(local, ("depth", "strip"), strip_pairs(depths, strip_count, shift))
+        start = [0] * len(shape)
+        start[row_axis] = ((strip_no - shift) % strip_count) * rows
+        full = lax.dynamic_update_slice(full, got, start)
+    return full
+
+
 def shards(surface, omegas, region_speed, fd_coeff, region_index, ref_region):
     if not fast_fits(surface, region_index, region_speed):
         return shards_general(surface, omegas, region_speed, fd_coeff, region_index, ref_region)
     line_len = surface.shape[3]
+    rows_here = surface.shape[2]
     segment_no = lax.axis_index("depth")
     segment_count = lax.axis_size("depth")
     strip_no = lax.axis_index("strip")
+    strip_count = lax.axis_size("strip")
     consts = fast_constants(line_len)
-    regions = lax.all_gather(region_index, "strip", axis=1, tiled=True)
-    wave = lax.all_to_all(surface, "strip", 1, 2, tiled=True)[:, 0]
+    mine = lax.dynamic_index_in_dim(surface, strip_no, 1, keepdims=False)
+    wave = jnp.zeros((2, rows_here * strip_count, line_len), jnp.float32)
+    wave = lax.dynamic_update_slice(wave, mine, (0, strip_no * rows_here, 0))
+    for shift in range(1, strip_count):
+        target = (strip_no + shift) % strip_count
+        piece = lax.dynamic_index_in_dim(surface, target, 1, keepdims=False)
+        got = lax.ppermute(piece, ("depth", "strip"), strip_pairs([0], strip_count, shift))
+        source = (strip_no - shift) % strip_count
+        wave = lax.dynamic_update_slice(wave, got, (0, source * rows_here, 0))
+    regions = gather_rows(region_index, range(segment_count), strip_no, strip_count, 1)
     omega = lax.dynamic_index_in_dim(omegas, strip_no, 0, keepdims=False)
     table, mult = section_tables(omega, region_speed, fd_coeff, ref_region, jnp.asarray(consts[3]))
     image = jnp.zeros(regions.shape, jnp.float32)
@@ -445,11 +479,21 @@
     def idle(wave, image):
         return (wave, image)
 
+    arrived = []
     for tick_no in range(segment_count):
         wave, image = lax.cond(segment_no == tick_no, live, idle, wave, image)
         if tick_no + 1 < segment_count:
             wave = from_behind(wave, "depth", 1)
-    return lax.psum_scatter(image, "strip", scatter_dimension=1, tiled=True)
+        for shift in range(1, strip_count):
+            target = (strip_no + shift) % strip_count
+            piece = lax.dynamic_slice_in_dim(image, target * rows_here, rows_here, axis=1)
+            arrived.append(
+                lax.ppermute(piece, ("depth", "strip"), strip_pairs([tick_no], strip_count, shift))
+            )
+    total = lax.dynamic_slice_in_dim(image, strip_no * rows_here, rows_here, axis=1)
+    for piece in arrived:
+        total = total + piece
+    return total
 
 
 def solution(mesh):

time: 126 us -> 107 us (0.85)
  the two profiles are of different devices: /device:TPU:0 before, /device:TPU:11 now
where the time goes in v1:
time: 107 us; the launch traced here: 106 us
  waiting for transfers between devices  61.3 us (57%)
  starting transfers between devices  24.3 us (23%)
  Pallas kernels  8.75 us (8%)
  local copies, waits for them, and re-layouts  8.2 us (8%)
  other arithmetic  3.09 us (3%)
    ppermute x3, waiting for transfers between devices, from_behind(): lax.ppermute(value, axis, [(source, source + steps) for source in range(f...  45.1 us
    ppermute x12, starting transfers between devices, shards(): lax.ppermute(piece, ('depth', 'strip'), strip_pairs([tick_no], strip_coun...  14.7 us
    ppermute x12, waiting for transfers between devices, shards(): lax.ppermute(piece, ('depth', 'strip'), strip_pairs([tick_no], strip_coun...  10.5 us
    pallas_call x1, Pallas kernels, run_section(): pl.pallas_call(lambda *refs: section_kernel(*refs, table_len=table_len),...  8.75 us
    ppermute x3, waiting for transfers between devices, gather_rows(): lax.ppermute(local, ('depth', 'strip'), strip_pairs(depths, strip_count,...  5.8 us
    ppermute x3, starting transfers between devices, from_behind(): lax.ppermute(value, axis, [(source, source + steps) for source in range(f...  3.88 us
    ppermute x3, starting transfers between devices, gather_rows(): lax.ppermute(local, ('depth', 'strip'), strip_pairs(depths, strip_count,...  3.77 us
    unnamed x24, local copies, waits for them, and re-layouts  2.85 us
  transfers between devices with their start and end apart: 21, of which 8 were waited for; matrix products, arithmetic and copies ran while one was open for 7% of the time, Pallas kernels for 8%

profile of v1, /device:TPU:11, one launch (start us, length us, event | category | flops | bytes accessed | tf_op | source)
XLA Modules:
  0.0 106.4 jit_solution(6578718339905004605)
XLA Ops:
  0.0 1.3 %collective-permute-start.3 = (s32[3,8,2048]{2,1,0:T(8,128)}, s32[3,8,2048]{2,1,0:T(8,128)S(1)}, u32[]{:S(2)}, u32[]{:S(2)}) collective-permute-start(s32[3,8,2048]{2,1,0:T(8,128)} %param.24), channel_id=1, source_target_pairs={{0,1},{1,2},{2,3},{3,0},{4,5},{5,6},{6,7},{7,4},{8,9},{9,10},{10,1... | collective-permute-start | bytes 589832 | tf_op jit(solution)/shard_map/ppermute | solution.py:445
  1.3 1.0 collective-permute-start.4
  2.3 1.5 %collective-permute-start.5 = (s32[3,8,2048]{2,1,0:T(8,128)}, s32[3,8,2048]{2,1,0:T(8,128)S(1)}, u32[]{:S(2)}, u32[]{:S(2)}) collective-permute-start(s32[3,8,2048]{2,1,0:T(8,128)} %param.24), channel_id=1, source_target_pairs={{0,3},{1,0},{2,1},{3,2},{4,7},{5,4},{6,5},{7,6},{8,11},{9,8},{10,9... | collective-permute-start | bytes 589832 | tf_op jit(solution)/shard_map/ppermute | solution.py:445
  3.8 1.1 dynamic-slice_bitcast_fusion
  4.8 0.7 collective-permute-start
  9.4 0.8 fusion.10
  10.9 0.8 copy-done
  11.9 0.9 bitcast_dynamic-update-slice_fusion
  14.7 3.2 %collective-permute-done.4 = s32[3,8,2048]{2,1,0:T(8,128)S(1)} collective-permute-done((s32[3,8,2048]{2,1,0:T(8,128)}, s32[3,8,2048]{2,1,0:T(8,128)S(1)}, u32[]{:S(2)}, u32[]{:S(2)}) %collective-permute-start.4) | collective-permute-done | bytes 196640 | tf_op jit(solution)/shard_map/ppermute | solution.py:445
  17.9 2.6 %collective-permute-done.5 = s32[3,8,2048]{2,1,0:T(8,128)S(1)} collective-permute-done((s32[3,8,2048]{2,1,0:T(8,128)}, s32[3,8,2048]{2,1,0:T(8,128)S(1)}, u32[]{:S(2)}, u32[]{:S(2)}) %collective-permute-start.5) | collective-permute-done | bytes 196640 | tf_op jit(solution)/shard_map/ppermute | solution.py:445
  20.7 1.3 %collective-permute-start.6 = (f32[2,32,2048]{2,1,0:T(8,128)S(1)}, f32[2,32,2048]{2,1,0:T(8,128)S(1)}, u32[]{:S(2)}, u32[]{:S(2)}) collective-permute-start(f32[2,32,2048]{2,1,0:T(8,128)S(1)} %get-tuple-element.143), channel_id=1, source_target_pairs={{0,4},{4,8},{8,12},{1,5},{5,9},{9,13},{2,6},{6,10},{10,14},{3,7},{... | collective-permute-start | bytes 1572872 | tf_op jit(solution)/shard_map/ppermute | solution.py:36
  22.0 2.5 %collective-permute-done.6 = f32[2,32,2048]{2,1,0:T(8,128)S(1)} collective-permute-done((f32[2,32,2048]{2,1,0:T(8,128)S(1)}, f32[2,32,2048]{2,1,0:T(8,128)S(1)}, u32[]{:S(2)}, u32[]{:S(2)}) %collective-permute-start.6) | collective-permute-done | bytes 524320 | tf_op jit(solution)/shard_map/ppermute | solution.py:36
  24.6 1.3 %collective-permute-start.7 = (f32[2,32,2048]{2,1,0:T(8,128)S(1)}, f32[2,32,2048]{2,1,0:T(8,128)}, u32[]{:S(2)}, u32[]{:S(2)}) collective-permute-start(f32[2,32,2048]{2,1,0:T(8,128)S(1)} %get-tuple-element.145), channel_id=1, source_target_pairs={{0,4},{4,8},{8,12},{1,5},{5,9},{9,13},{2,6},{6,10},{10,14},{3,7},{... | collective-permute-start | bytes 1572872 | tf_op jit(solution)/shard_map/ppermute | solution.py:36
  25.9 10.6 %collective-permute-done.7 = f32[2,32,2048]{2,1,0:T(8,128)} collective-permute-done((f32[2,32,2048]{2,1,0:T(8,128)S(1)}, f32[2,32,2048]{2,1,0:T(8,128)}, u32[]{:S(2)}, u32[]{:S(2)}) %collective-permute-start.7) | collective-permute-done | bytes 524320 | tf_op jit(solution)/shard_map/ppermute | solution.py:36
  36.5 1.3 %collective-permute-start.8 = (f32[2,32,2048]{2,1,0:T(8,128)}, f32[2,32,2048]{2,1,0:T(8,128)}, u32[]{:S(2)}, u32[]{:S(2)}) collective-permute-start(f32[2,32,2048]{2,1,0:T(8,128)} %get-tuple-element.148), channel_id=1, source_target_pairs={{0,4},{4,8},{8,12},{1,5},{5,9},{9,13},{2,6},{6,10},{10,14},{3,7},{... | collective-permute-start | bytes 1572872 | tf_op jit(solution)/shard_map/ppermute | solution.py:36
  37.8 0.8 constant_dynamic-slice_fusion.10
  39.3 0.7 collective-permute-start.11
  40.0 0.7 collective-permute-start.9
  40.6 0.8 constant_dynamic-slice_fusion.7
  42.2 32.0 %collective-permute-done.8 = f32[2,32,2048]{2,1,0:T(8,128)} collective-permute-done((f32[2,32,2048]{2,1,0:T(8,128)}, f32[2,32,2048]{2,1,0:T(8,128)}, u32[]{:S(2)}, u32[]{:S(2)}) %collective-permute-start.8) | collective-permute-done | bytes 524320 | tf_op jit(solution)/shard_map/ppermute | solution.py:36
  74.8 8.8 %conditional.7 = (f32[3,32,2048]{2,1,0:T(8,128)S(1)}) conditional(s32[]{:T(128)} %convert_element_type.12, f32[3,32,2048]{2,1,0:T(8,128)S(1)} %get-tuple-element.147, (f32[72]{0:T(128)S(1)}, f32[2,32,2048]{2,1,0:T(8,128)}, s32[3,32,2048]{2,1,0:T(8,128)S(1)}, f32[3,2,16,128]{3,2,1,0:T(8,128)}, f32[2,16,128]{2,1,0:T(8,128)}, ...), branch_computations={%region_6.7_spmd, %region_7.8_spmd} | conditional | flops 1286602752 | bytes 4718600 | solution.py:484
  74.8 8.7 %branch_1_fun.6 = (f32[2,32,2048]{2,1,0:T(8,128)}, f32[3,32,2048]{2,1,0:T(8,128)S(1)}) custom-call(f32[72]{0:T(128)S(1)} %get-tuple-element.126.refs_0_, f32[2,32,2048]{2,1,0:T(8,128)} %get-tuple-element.127.refs_1_, s32[3,32,2048]{2,1,0:T(8,128)S(1)} %get-tuple-element.128.refs_2_, f32[3,2,16,128]{3,2,1,0:T(8,128)} %get-tuple-element.129.refs_3_, ...), custom_call_target="tpu_custom_call" | custom-call | flops 1286602752 | bytes 4718592 | tf_op jit(solution)/shard_map/cond/branch_1_fun/pallas_call | solution.py:374
  84.3 0.7 collective-permute-start.15
  85.0 0.7 collective-permute-start.16
  85.7 0.7 collective-permute-start.17
  86.4 3.6 %collective-permute-start.18 = (f32[3,8,2048]{2,1,0:T(8,128)S(1)}, f32[3,8,2048]{2,1,0:T(8,128)S(1)}, u32[]{:S(2)}, u32[]{:S(2)}) collective-permute-start(f32[3,8,2048]{2,1,0:T(8,128)S(1)} %get-tuple-element.176), channel_id=1, source_target_pairs={{12,13},{13,14},{14,15},{15,12},{28,29},{29,30},{30,31},{31,28}} | collective-permute-start | bytes 589832 | tf_op jit(solution)/shard_map/ppermute | solution.py:491
  90.1 1.9 %collective-permute-start.19 = (f32[3,8,2048]{2,1,0:T(8,128)S(1)}, f32[3,8,2048]{2,1,0:T(8,128)S(1)}, u32[]{:S(2)}, u32[]{:S(2)}) collective-permute-start(f32[3,8,2048]{2,1,0:T(8,128)S(1)} %get-tuple-element.178), channel_id=1, source_target_pairs={{12,14},{13,15},{14,12},{15,13},{28,30},{29,31},{30,28},{31,29}} | collective-permute-start | bytes 589832 | tf_op jit(solution)/shard_map/ppermute | solution.py:491
  92.0 3.1 %collective-permute-start.20 = (f32[3,8,2048]{2,1,0:T(8,128)S(1)}, f32[3,8,2048]{2,1,0:T(8,128)S(1)}, u32[]{:S(2)}, u32[]{:S(2)}) collective-permute-start(f32[3,8,2048]{2,1,0:T(8,128)S(1)} %get-tuple-element.177), channel_id=1, source_target_pairs={{12,15},{13,12},{14,13},{15,14},{28,31},{29,28},{30,29},{31,30}} | collective-permute-start | bytes 589832 | tf_op jit(solution)/shard_map/ppermute | solution.py:491
  95.1 6.9 %collective-permute-done.18 = f32[3,8,2048]{2,1,0:T(8,128)S(1)} collective-permute-done((f32[3,8,2048]{2,1,0:T(8,128)S(1)}, f32[3,8,2048]{2,1,0:T(8,128)S(1)}, u32[]{:S(2)}, u32[]{:S(2)}) %collective-permute-start.18) | collective-permute-done | bytes 196640 | tf_op jit(solution)/shard_map/ppermute | solution.py:491
  102.1 2.1 %collective-permute-done.19 = f32[3,8,2048]{2,1,0:T(8,128)S(1)} collective-permute-done((f32[3,8,2048]{2,1,0:T(8,128)S(1)}, f32[3,8,2048]{2,1,0:T(8,128)S(1)}, u32[]{:S(2)}, u32[]{:S(2)}) %collective-permute-start.19) | collective-permute-done | bytes 196640 | tf_op jit(solution)/shard_map/ppermute | solution.py:491
  104.2 1.4 %collective-permute-done.20 = f32[3,8,2048]{2,1,0:T(8,128)S(1)} collective-permute-done((f32[3,8,2048]{2,1,0:T(8,128)S(1)}, f32[3,8,2048]{2,1,0:T(8,128)S(1)}, u32[]{:S(2)}, u32[]{:S(2)}) %collective-permute-start.20) | collective-permute-done | bytes 196640 | tf_op jit(solution)/shard_map/ppermute | solution.py:491
  105.6 0.8 add_add_fusion
  (71 shorter events, 9.5 us)
Async XLA Ops:
  0.0 14.6 %collective-permute-start.3 = (s32[3,8,2048]{2,1,0:T(8,128)}, s32[3,8,2048]{2,1,0:T(8,128)S(1)}, u32[]{:S(2)}, u32[]{:S(2)}) collective-permute-start(s32[3,8,2048]{2,1,0:T(8,128)} %param.24), channel_id=1, source_target_pairs={{0,1},{1,2},{2,3},{3,0},{4,5},{5,6},{6,7},{7,4},{8,9},{9,10},{10,1... | collective-permute-start | bytes 589832 | tf_op jit(solution)/shard_map/ppermute | solution.py:445
  1.3 16.5 %collective-permute-start.4 = (s32[3,8,2048]{2,1,0:T(8,128)}, s32[3,8,2048]{2,1,0:T(8,128)S(1)}, u32[]{:S(2)}, u32[]{:S(2)}) collective-permute-start(s32[3,8,2048]{2,1,0:T(8,128)} %param.24), channel_id=1, source_target_pairs={{0,2},{1,3},{2,0},{3,1},{4,6},{5,7},{6,4},{7,5},{8,10},{9,11},{10,... | collective-permute-start | bytes 589832 | tf_op jit(solution)/shard_map/ppermute | solution.py:445
  2.3 18.2 %collective-permute-start.5 = (s32[3,8,2048]{2,1,0:T(8,128)}, s32[3,8,2048]{2,1,0:T(8,128)S(1)}, u32[]{:S(2)}, u32[]{:S(2)}) collective-permute-start(s32[3,8,2048]{2,1,0:T(8,128)} %param.24), channel_id=1, source_target_pairs={{0,3},{1,0},{2,1},{3,2},{4,7},{5,4},{6,5},{7,6},{8,11},{9,8},{10,9... | collective-permute-start | bytes 589832 | tf_op jit(solution)/shard_map/ppermute | solution.py:445
  4.8 9.0 %collective-permute-start = (f32[2,8,2048]{2,1,0:T(8,128)S(1)}, f32[2,8,2048]{2,1,0:T(8,128)S(1)}, u32[]{:S(2)}, u32[]{:S(2)}) collective-permute-start(f32[2,8,2048]{2,1,0:T(8,128)S(1)} %get-tuple-element.180), channel_id=1, source_target_pairs={{0,1},{1,2},{2,3},{3,0},{16,17},{17,18},{18,19},{19,16}} | collective-permute-start | bytes 393224 | tf_op jit(solution)/shard_map/ppermute | solution.py:468
  5.5 9.0 %collective-permute-start.1 = (f32[2,8,2048]{2,1,0:T(8,128)S(1)}, f32[2,8,2048]{2,1,0:T(8,128)S(1)}, u32[]{:S(2)}, u32[]{:S(2)}) collective-permute-start(f32[2,8,2048]{2,1,0:T(8,128)S(1)} %get-tuple-element.181), channel_id=1, source_target_pairs={{0,2},{1,3},{2,0},{3,1},{16,18},{17,19},{18,16},{19,17}} | collective-permute-start | bytes 393224 | tf_op jit(solution)/shard_map/ppermute | solution.py:468
  6.2 0.7 copy-start.2
  7.5 0.7 copy-start.4
  10.8 0.9 copy-start
  11.8 1.0 copy-start.5
  11.8 1.6 %copy-start.6 = (f32[16,128]{1,0:T(8,128)S(1)}, f32[16,128]{1,0:T(8,128)}, u32[]{:S(2)}) copy-start(f32[16,128]{1,0:T(8,128)} %constant.131) | copy-start | bytes 24580
  13.8 22.6 %copy-start.1 = (f32[3,2,16,128]{3,2,1,0:T(8,128)}, f32[3,2,16,128]{3,2,1,0:T(8,128)S(1)}, u32[]{:S(2)}) copy-start(f32[3,2,16,128]{3,2,1,0:T(8,128)S(1)} %pad_maximum_fusion) | copy-start | bytes 147460
  13.9 0.7 collective-permute-start.2
  17.8 2.7 %copy-start.11 = (bf16[256,256]{1,0:T(8,128)(2,1)S(1)}, bf16[256,256]{1,0:T(8,128)(2,1)}, u32[]{:S(2)}) copy-start(bf16[256,256]{1,0:T(8,128)(2,1)} %constant.127.clone) | copy-start | bytes 393220
  17.8 2.7 %copy-start.13 = (f32[2,16,128]{2,1,0:T(8,128)S(1)}, f32[2,16,128]{2,1,0:T(8,128)}, u32[]{:S(2)}) copy-start(f32[2,16,128]{2,1,0:T(8,128)} %constant.123.clone) | copy-start | bytes 49156
  17.8 2.7 %copy-start.7 = (bf16[256,256]{1,0:T(8,128)(2,1)S(1)}, bf16[256,256]{1,0:T(8,128)(2,1)}, u32[]{:S(2)}) copy-start(bf16[256,256]{1,0:T(8,128)(2,1)} %constant.124.clone) | copy-start | bytes 393220
  17.9 2.7 %copy-start.8 = (bf16[256,256]{1,0:T(8,128)(2,1)S(1)}, bf16[256,256]{1,0:T(8,128)(2,1)}, u32[]{:S(2)}) copy-start(bf16[256,256]{1,0:T(8,128)(2,1)} %constant.125.clone) | copy-start | bytes 393220
  17.9 2.7 %copy-start.9 = (bf16[256,256]{1,0:T(8,128)(2,1)S(1)}, bf16[256,256]{1,0:T(8,128)(2,1)}, u32[]{:S(2)}) copy-start(bf16[256,256]{1,0:T(8,128)(2,1)} %constant.126.clone) | copy-start | bytes 393220
  20.7 3.8 %collective-permute-start.6 = (f32[2,32,2048]{2,1,0:T(8,128)S(1)}, f32[2,32,2048]{2,1,0:T(8,128)S(1)}, u32[]{:S(2)}, u32[]{:S(2)}) collective-permute-start(f32[2,32,2048]{2,1,0:T(8,128)S(1)} %get-tuple-element.143), channel_id=1, source_target_pairs={{0,4},{4,8},{8,12},{1,5},{5,9},{9,13},{2,6},{6,10},{10,14},{3,7},{... | collective-permute-start | bytes 1572872 | tf_op jit(solution)/shard_map/ppermute | solution.py:36
  24.6 11.9 %collective-permute-start.7 = (f32[2,32,2048]{2,1,0:T(8,128)S(1)}, f32[2,32,2048]{2,1,0:T(8,128)}, u32[]{:S(2)}, u32[]{:S(2)}) collective-permute-start(f32[2,32,2048]{2,1,0:T(8,128)S(1)} %get-tuple-element.145), channel_id=1, source_target_pairs={{0,4},{4,8},{8,12},{1,5},{5,9},{9,13},{2,6},{6,10},{10,14},{3,7},{... | collective-permute-start | bytes 1572872 | tf_op jit(solution)/shard_map/ppermute | solution.py:36
  36.5 37.6 %collective-permute-start.8 = (f32[2,32,2048]{2,1,0:T(8,128)}, f32[2,32,2048]{2,1,0:T(8,128)}, u32[]{:S(2)}, u32[]{:S(2)}) collective-permute-start(f32[2,32,2048]{2,1,0:T(8,128)} %get-tuple-element.148), channel_id=1, source_target_pairs={{0,4},{4,8},{8,12},{1,5},{5,9},{9,13},{2,6},{6,10},{10,14},{3,7},{... | collective-permute-start | bytes 1572872 | tf_op jit(solution)/shard_map/ppermute | solution.py:36
  38.6 45.0 %collective-permute-start.10 = (f32[3,8,2048]{2,1,0:T(8,128)}, f32[3,8,2048]{2,1,0:T(8,128)S(1)}, u32[]{:S(2)}, u32[]{:S(2)}) collective-permute-start(f32[3,8,2048]{2,1,0:T(8,128)} %get-tuple-element.169), channel_id=1, source_target_pairs={{0,2},{1,3},{2,0},{3,1},{16,18},{17,19},{18,16},{19,17}} | collective-permute-start | bytes 589832 | tf_op jit(solution)/shard_map/ppermute | solution.py:491
  39.3 45.0 %collective-permute-start.11 = (f32[3,8,2048]{2,1,0:T(8,128)}, f32[3,8,2048]{2,1,0:T(8,128)S(1)}, u32[]{:S(2)}, u32[]{:S(2)}) collective-permute-start(f32[3,8,2048]{2,1,0:T(8,128)} %get-tuple-element.168), channel_id=1, source_target_pairs={{0,3},{1,0},{2,1},{3,2},{16,19},{17,16},{18,17},{19,18}} | collective-permute-start | bytes 589832 | tf_op jit(solution)/shard_map/ppermute | solution.py:491
  40.0 45.1 %collective-permute-start.9 = (f32[3,8,2048]{2,1,0:T(8,128)S(1)}, f32[3,8,2048]{2,1,0:T(8,128)S(1)}, u32[]{:S(2)}, u32[]{:S(2)}) collective-permute-start(f32[3,8,2048]{2,1,0:T(8,128)S(1)} %get-tuple-element.167), channel_id=1, source_target_pairs={{0,1},{1,2},{2,3},{3,0},{16,17},{17,18},{18,19},{19,16}} | collective-permute-start | bytes 589832 | tf_op jit(solution)/shard_map/ppermute | solution.py:491
  41.4 44.3 %collective-permute-start.12 = (f32[3,8,2048]{2,1,0:T(8,128)}, f32[3,8,2048]{2,1,0:T(8,128)S(1)}, u32[]{:S(2)}, u32[]{:S(2)}) collective-permute-start(f32[3,8,2048]{2,1,0:T(8,128)} %get-tuple-element.170), channel_id=1, source_target_pairs={{4,5},{5,6},{6,7},{7,4},{20,21},{21,22},{22,23},{23,20}} | collective-permute-start | bytes 589832 | tf_op jit(solution)/shard_map/ppermute | solution.py:491
  74.2 12.2 %collective-permute-start.13 = (f32[3,8,2048]{2,1,0:T(8,128)}, f32[3,8,2048]{2,1,0:T(8,128)S(1)}, u32[]{:S(2)}, u32[]{:S(2)}) collective-permute-start(f32[3,8,2048]{2,1,0:T(8,128)} %get-tuple-element.172), channel_id=1, source_target_pairs={{4,6},{5,7},{6,4},{7,5},{20,22},{21,23},{22,20},{23,21}} | collective-permute-start | bytes 589832 | tf_op jit(solution)/shard_map/ppermute | solution.py:491
  83.6 6.5 %collective-permute-start.14 = (f32[3,8,2048]{2,1,0:T(8,128)S(1)}, f32[3,8,2048]{2,1,0:T(8,128)S(1)}, u32[]{:S(2)}, u32[]{:S(2)}) collective-permute-start(f32[3,8,2048]{2,1,0:T(8,128)S(1)} %get-tuple-element.171), channel_id=1, source_target_pairs={{4,7},{5,4},{6,5},{7,6},{20,23},{21,20},{22,21},{23,22}} | collective-permute-start | bytes 589832 | tf_op jit(solution)/shard_map/ppermute | solution.py:491
  84.3 7.7 %collective-permute-start.15 = (f32[3,8,2048]{2,1,0:T(8,128)S(1)}, f32[3,8,2048]{2,1,0:T(8,128)S(1)}, u32[]{:S(2)}, u32[]{:S(2)}) collective-permute-start(f32[3,8,2048]{2,1,0:T(8,128)S(1)} %get-tuple-element.173), channel_id=1, source_target_pairs={{8,9},{9,10},{10,11},{11,8},{24,25},{25,26},{26,27},{27,24}} | collective-permute-start | bytes 589832 | tf_op jit(solution)/shard_map/ppermute | solution.py:491
  85.0 10.1 %collective-permute-start.16 = (f32[3,8,2048]{2,1,0:T(8,128)S(1)}, f32[3,8,2048]{2,1,0:T(8,128)S(1)}, u32[]{:S(2)}, u32[]{:S(2)}) collective-permute-start(f32[3,8,2048]{2,1,0:T(8,128)S(1)} %get-tuple-element.175), channel_id=1, source_target_pairs={{8,10},{9,11},{10,8},{11,9},{24,26},{25,27},{26,24},{27,25}} | collective-permute-start | bytes 589832 | tf_op jit(solution)/shard_map/ppermute | solution.py:491
  85.7 9.4 %collective-permute-start.17 = (f32[3,8,2048]{2,1,0:T(8,128)S(1)}, f32[3,8,2048]{2,1,0:T(8,128)S(1)}, u32[]{:S(2)}, u32[]{:S(2)}) collective-permute-start(f32[3,8,2048]{2,1,0:T(8,128)S(1)} %get-tuple-element.174), channel_id=1, source_target_pairs={{8,11},{9,8},{10,9},{11,10},{24,27},{25,24},{26,25},{27,26}} | collective-permute-start | bytes 589832 | tf_op jit(solution)/shard_map/ppermute | solution.py:491
  86.4 15.7 %collective-permute-start.18 = (f32[3,8,2048]{2,1,0:T(8,128)S(1)}, f32[3,8,2048]{2,1,0:T(8,128)S(1)}, u32[]{:S(2)}, u32[]{:S(2)}) collective-permute-start(f32[3,8,2048]{2,1,0:T(8,128)S(1)} %get-tuple-element.176), channel_id=1, source_target_pairs={{12,13},{13,14},{14,15},{15,12},{28,29},{29,30},{30,31},{31,28}} | collective-permute-start | bytes 589832 | tf_op jit(solution)/shard_map/ppermute | solution.py:491
  90.1 14.1 %collective-permute-start.19 = (f32[3,8,2048]{2,1,0:T(8,128)S(1)}, f32[3,8,2048]{2,1,0:T(8,128)S(1)}, u32[]{:S(2)}, u32[]{:S(2)}) collective-permute-start(f32[3,8,2048]{2,1,0:T(8,128)S(1)} %get-tuple-element.178), channel_id=1, source_target_pairs={{12,14},{13,15},{14,12},{15,13},{28,30},{29,31},{30,28},{31,29}} | collective-permute-start | bytes 589832 | tf_op jit(solution)/shard_map/ppermute | solution.py:491
  92.0 13.6 %collective-permute-start.20 = (f32[3,8,2048]{2,1,0:T(8,128)S(1)}, f32[3,8,2048]{2,1,0:T(8,128)S(1)}, u32[]{:S(2)}, u32[]{:S(2)}) collective-permute-start(f32[3,8,2048]{2,1,0:T(8,128)S(1)} %get-tuple-element.177), channel_id=1, source_target_pairs={{12,15},{13,12},{14,13},{15,14},{28,31},{29,28},{30,29},{31,30}} | collective-permute-start | bytes 589832 | tf_op jit(solution)/shard_map/ppermute | solution.py:491
  (1 other events, 0.7 us)

commit v2 on v1

--- a/solution.py
+++ b/solution.py
@@ -251,6 +251,7 @@
     rows = w_ref.shape[1]
     line_len = w_ref.shape[2]
     steps = rid_ref.shape[0]
+    strip_count, rows_here = img_ref.shape[0], img_ref.shape[2]
     chunks = rows // ROW_CHUNK
     inv_len = 1.0 / line_len
     wout_ref[...] = w_ref[...]
@@ -336,7 +337,8 @@
             new_im = here[1] + (lap[0] * gain + lap[1] * DAMPING)
             wout_ref[0, :, blk(a)] = new_re
             wout_ref[1, :, blk(a)] = new_im
-            img_ref[k, :, blk(a)] = new_re
+            for j in range(strip_count):
+                img_ref[j, k, :, blk(a)] = new_re[j * rows_here:(j + 1) * rows_here]
         return carry
 
     lax.fori_loop(0, steps, one_step, 0)
@@ -364,7 +366,7 @@
     return (halves(fwd), halves(inv), twiddle, kx_cd.astype(np.float32))
 
 
-def run_section(wave, regions, table, mult, consts):
+def run_section(wave, regions, table, mult, consts, strip_count):
     (fhi, flo), (ghi, glo), twiddle, _ = consts
     rows, line_len = wave.shape[1], wave.shape[2]
     steps = regions.shape[0]
@@ -375,7 +377,7 @@
         lambda *refs: section_kernel(*refs, table_len=table_len),
         out_shape=(
             jax.ShapeDtypeStruct(wave.shape, jnp.float32),
-            jax.ShapeDtypeStruct((steps, rows, line_len), jnp.float32),
+            jax.ShapeDtypeStruct((strip_count, steps, rows // strip_count, line_len), jnp.float32),
         ),
         in_specs=[pl.BlockSpec(memory_space=pltpu.SMEM)] + [vmem] * 8,
         out_specs=(vmem, vmem),
@@ -420,6 +422,7 @@
         freq_count == lax.axis_size("strip")
         and line_len == FFT_BLOCKS * LANE
         and rows % ROW_CHUNK == 0
+        and surface.shape[2] % ROW_CHUNK == 0
         and rows <= 64
         and region_speed.shape[0] <= 16
     )
@@ -454,46 +457,40 @@
         return shards_general(surface, omegas, region_speed, fd_coeff, region_index, ref_region)
     line_len = surface.shape[3]
     rows_here = surface.shape[2]
+    steps = region_index.shape[0]
     segment_no = lax.axis_index("depth")
     segment_count = lax.axis_size("depth")
     strip_no = lax.axis_index("strip")
     strip_count = lax.axis_size("strip")
+    rows = rows_here * strip_count
     consts = fast_constants(line_len)
-    mine = lax.dynamic_index_in_dim(surface, strip_no, 1, keepdims=False)
-    wave = jnp.zeros((2, rows_here * strip_count, line_len), jnp.float32)
-    wave = lax.dynamic_update_slice(wave, mine, (0, strip_no * rows_here, 0))
-    for shift in range(1, strip_count):
-        target = (strip_no + shift) % strip_count
-        piece = lax.dynamic_index_in_dim(surface, target, 1, keepdims=False)
-        got = lax.ppermute(piece, ("depth", "strip"), strip_pairs([0], strip_count, shift))
-        source = (strip_no - shift) % strip_count
-        wave = lax.dynamic_update_slice(wave, got, (0, source * rows_here, 0))
-    regions = gather_rows(region_index, range(segment_count), strip_no, strip_count, 1)
+    outgoing = jnp.concatenate(
+        [
+            jnp.broadcast_to(region_index.astype(jnp.float32)[None], (strip_count,) + region_index.shape),
+            jnp.transpose(surface, (1, 0, 2, 3)),
+        ],
+        axis=1,
+    )
+    incoming = lax.all_to_all(outgoing, "strip", 0, 0, tiled=True)
+    regions = jnp.transpose(incoming[:, :steps], (1, 0, 2, 3)).reshape(steps, rows, line_len)
+    regions = regions.astype(jnp.int32)
+    wave = jnp.transpose(incoming[:, steps:], (1, 0, 2, 3)).reshape(2, rows, line_len)
     omega = lax.dynamic_index_in_dim(omegas, strip_no, 0, keepdims=False)
     table, mult = section_tables(omega, region_speed, fd_coeff, ref_region, jnp.asarray(consts[3]))
-    image = jnp.zeros(regions.shape, jnp.float32)
+    image = jnp.zeros((strip_count, steps, rows_here, line_len), jnp.float32)
 
     def live(wave, image):
-        return run_section(wave, regions, table, mult, consts)
+        return run_section(wave, regions, table, mult, consts, strip_count)
 
     def idle(wave, image):
         return (wave, image)
 
-    arrived = []
     for tick_no in range(segment_count):
         wave, image = lax.cond(segment_no == tick_no, live, idle, wave, image)
         if tick_no + 1 < segment_count:
             wave = from_behind(wave, "depth", 1)
-        for shift in range(1, strip_count):
-            target = (strip_no + shift) % strip_count
-            piece = lax.dynamic_slice_in_dim(image, target * rows_here, rows_here, axis=1)
-            arrived.append(
-                lax.ppermute(piece, ("depth", "strip"), strip_pairs([tick_no], strip_count, shift))
-            )
-    total = lax.dynamic_slice_in_dim(image, strip_no * rows_here, rows_here, axis=1)
-    for piece in arrived:
-        total = total + piece
-    return total
+    parts = lax.all_to_all(image, "strip", 0, 0, tiled=True)
+    return jnp.sum(parts, axis=0)
 
 
 def solution(mesh):

time: 107 us -> 113 us (1.056)
  blocking collectives: 0 us -> 23.9 us
  starting transfers between devices: 24.3 us -> 8.75 us
  local copies, waits for them, and re-layouts: 8.2 us -> 2.58 us
  other arithmetic: 3.09 us -> 4.94 us
  waiting for transfers between devices: 61.3 us -> 63 us
    all_to_all x0 -> x1, waiting for transfers between devices: none -> 24 us  [shards(): incoming = lax.all_to_all(outgoing, 'strip', 0, 0, tiled=True)]
    all_to_all x0 -> x1, blocking collectives: none -> 23.9 us  [shards(): parts = lax.all_to_all(image, 'strip', 0, 0, tiled=True)]
    ppermute x18 -> x0, starting transfers between devices: 20.4 us -> none  [the longest x12 14.7 us: shards(): lax.ppermute(piece, ('depth', 'strip'), strip_pairs([tick_no], strip_coun...]
    ppermute x18 -> x0, waiting for transfers between devices: 16.3 us -> none  [the longest x12 10.5 us: shards(): lax.ppermute(piece, ('depth', 'strip'), strip_pairs([tick_no], strip_coun...]
    ppermute x3, waiting for transfers between devices: 45.1 us -> 39 us  [from_behind(): lax.ppermute(value, axis, [(source, source + steps) for source in range(f...]
    all_to_all x0 -> x1, starting transfers between devices: none -> 4.9 us  [shards(): incoming = lax.all_to_all(outgoing, 'strip', 0, 0, tiled=True)]
    unnamed x24 -> x21, local copies, waits for them, and re-layouts: 2.85 us -> 1.13 us
    dynamic_slice x4 -> x0, local copies, waits for them, and re-layouts: 1.68 us -> none  [shards(): lax.dynamic_slice_in_dim(image, target * rows_here, rows_here, axis=1)]
  transfers between devices with their start and end apart: 21 -> 4, of which waited for: 8 -> 4; matrix products, arithmetic and copies ran while one was open for 7% -> 3% of each run, Pallas kernels for 8% -> 0%
where the time goes in v2:
time: 113 us; the launch traced here: 112 us
  waiting for transfers between devices  63 us (56%)
  blocking collectives  23.9 us (21%)
  starting transfers between devices  8.75 us (8%)
  Pallas kernels  8.06 us (7%)
  other arithmetic  4.94 us (4%)
  local copies, waits for them, and re-layouts  2.58 us (2%)
    ppermute x3, waiting for transfers between devices, from_behind(): lax.ppermute(value, axis, [(source, source + steps) for source in range(f...  39 us
    all_to_all x1, waiting for transfers between devices, shards(): incoming = lax.all_to_all(outgoing, 'strip', 0, 0, tiled=True)  24 us
    all_to_all x1, blocking collectives, shards(): parts = lax.all_to_all(image, 'strip', 0, 0, tiled=True)  23.9 us
    pallas_call x1, Pallas kernels, run_section(): pl.pallas_call(lambda *refs: section_kernel(*refs, table_len=table_len),...  8.06 us
    all_to_all x1, starting transfers between devices, shards(): incoming = lax.all_to_all(outgoing, 'strip', 0, 0, tiled=True)  4.9 us
    ppermute x3, starting transfers between devices, from_behind(): lax.ppermute(value, axis, [(source, source + steps) for source in range(f...  3.85 us
  transfers between devices with their start and end apart: 4, of which 4 were waited for; matrix products, arithmetic and copies ran while one was open for 3% of the time, Pallas kernels for 0%

profile of v2, /device:TPU:11, one launch (start us, length us, event | category | flops | bytes accessed | tf_op | source)
XLA Modules:
  0.0 111.5 jit_solution(5911365932356823892)
XLA Ops:
  0.0 0.9 convert_element_type.28
  0.9 1.1 copy.24
  2.0 0.1 broadcast_in_dim.6
  2.1 1.2 %pad_maximum_fusion = f32[4,5,8,2048]{3,2,1,0:T(8,128)} fusion(f32[4,2,8,2048]{3,2,1,0:T(8,128)S(1)} %bitcast.12, f32[4,3,8,2048]{3,2,1,0:T(8,128)S(1)} %broadcast_in_dim.6), kind=kLoop, calls=%fused_computation.1 | loop fusion | flops 327680 | bytes 2621440 | tf_op jit(solution)/shard_map/concatenate | solution.py:467
  3.3 0.0 copy-start.4
  3.3 4.9 %all-to-all-start = ((f32[4,5,8,2048]{3,2,1,0:T(8,128)}), f32[4,5,8,2048]{3,2,1,0:T(8,128)S(1)}, u32[]{:S(2)}, u32[]{:S(2)}) async-start(f32[4,5,8,2048]{3,2,1,0:T(8,128)} %pad_maximum_fusion), calls=%async_computation | async-start | bytes 2621440 | tf_op jit(solution)/shard_map/all_to_all | solution.py:474
  8.2 0.6 dynamic_slice.4
  8.8 0.6 gather_fusion
  9.5 0.6 broadcast_divide_fusion
  10.0 0.7 fusion.11
  10.7 0.1 reshape.135
  10.8 0.6 multiply_multiply_fusion
  11.4 0.2 fusion.6
  11.6 0.0 copy-start.5
  11.6 0.0 copy-start.6
  11.6 0.0 copy-start.7
  11.6 0.0 copy-start.8
  11.7 0.0 copy-start.9
  11.7 24.0 %all-to-all-done = f32[4,5,8,2048]{3,2,1,0:T(8,128)S(1)} async-done(((f32[4,5,8,2048]{3,2,1,0:T(8,128)}), f32[4,5,8,2048]{3,2,1,0:T(8,128)S(1)}, u32[]{:S(2)}, u32[]{:S(2)}) %all-to-all-start) | async-done | bytes 1310752 | tf_op jit(solution)/shard_map/all_to_all | solution.py:474
  35.7 0.1 fusion
  35.8 0.1 conditional.4
  35.9 0.1 broadcast_in_dim.0
  35.9 1.3 %collective-permute-start = (f32[2,32,2048]{2,1,0:T(8,128)S(1)}, f32[2,32,2048]{2,1,0:T(8,128)S(1)}, u32[]{:S(2)}, u32[]{:S(2)}) collective-permute-start(f32[2,32,2048]{2,1,0:T(8,128)S(1)} %get-tuple-element.138), channel_id=1, source_target_pairs={{0,4},{4,8},{8,12},{1,5},{5,9},{9,13},{2,6},{6,10},{10,14},{3,7},{... | collective-permute-start | bytes 1572872 | tf_op jit(solution)/shard_map/ppermute | solution.py:36
  37.2 3.9 %collective-permute-done = f32[2,32,2048]{2,1,0:T(8,128)S(1)} collective-permute-done((f32[2,32,2048]{2,1,0:T(8,128)S(1)}, f32[2,32,2048]{2,1,0:T(8,128)S(1)}, u32[]{:S(2)}, u32[]{:S(2)}) %collective-permute-start) | collective-permute-done | bytes 524320 | tf_op jit(solution)/shard_map/ppermute | solution.py:36
  41.1 1.3 %collective-permute-start.1 = (f32[2,32,2048]{2,1,0:T(8,128)S(1)}, f32[2,32,2048]{2,1,0:T(8,128)S(1)}, u32[]{:S(2)}, u32[]{:S(2)}) collective-permute-start(f32[2,32,2048]{2,1,0:T(8,128)S(1)} %get-tuple-element.140), channel_id=1, source_target_pairs={{0,4},{4,8},{8,12},{1,5},{5,9},{9,13},{2,6},{6,10},{10,14},{3,7},{... | collective-permute-start | bytes 1572872 | tf_op jit(solution)/shard_map/ppermute | solution.py:36
  42.4 9.2 %collective-permute-done.1 = f32[2,32,2048]{2,1,0:T(8,128)S(1)} collective-permute-done((f32[2,32,2048]{2,1,0:T(8,128)S(1)}, f32[2,32,2048]{2,1,0:T(8,128)S(1)}, u32[]{:S(2)}, u32[]{:S(2)}) %collective-permute-start.1) | collective-permute-done | bytes 524320 | tf_op jit(solution)/shard_map/ppermute | solution.py:36
  51.6 1.3 %collective-permute-start.2 = (f32[2,32,2048]{2,1,0:T(8,128)S(1)}, f32[2,32,2048]{2,1,0:T(8,128)S(1)}, u32[]{:S(2)}, u32[]{:S(2)}) collective-permute-start(f32[2,32,2048]{2,1,0:T(8,128)S(1)} %get-tuple-element.143), channel_id=1, source_target_pairs={{0,4},{4,8},{8,12},{1,5},{5,9},{9,13},{2,6},{6,10},{10,14},{3,7},{... | collective-permute-start | bytes 1572872 | tf_op jit(solution)/shard_map/ppermute | solution.py:36
  52.9 26.0 %collective-permute-done.2 = f32[2,32,2048]{2,1,0:T(8,128)S(1)} collective-permute-done((f32[2,32,2048]{2,1,0:T(8,128)S(1)}, f32[2,32,2048]{2,1,0:T(8,128)S(1)}, u32[]{:S(2)}, u32[]{:S(2)}) %collective-permute-start.2) | collective-permute-done | bytes 524320 | tf_op jit(solution)/shard_map/ppermute | solution.py:36
  78.9 8.1 %conditional.7 = (f32[4,3,8,2048]{3,2,1,0:T(8,128)S(1)}) conditional(s32[]{:T(128)} %convert_element_type.24, f32[4,3,8,2048]{3,2,1,0:T(8,128)S(1)} %get-tuple-element.142, (f32[72]{0:T(128)S(1)}, f32[2,32,2048]{2,1,0:T(8,128)S(1)}, s32[3,32,2048]{2,1,0:T(8,128)S(1)}, f32[3,2,16,128]{3,2,1,0:T(8,128)S(1)}, f32[2,16,128]{2,1,0:T(8,128)S(1)}, ...), branch_computations={%region_6.7_spmd, %region_7.8_spmd} | conditional | flops 1286602752 | bytes 4718600 | solution.py:489
  78.9 8.1 %branch_1_fun.7 = (f32[2,32,2048]{2,1,0:T(8,128)}, f32[4,3,8,2048]{3,2,1,0:T(8,128)S(1)}) custom-call(f32[72]{0:T(128)S(1)} %get-tuple-element.122.refs_0_, f32[2,32,2048]{2,1,0:T(8,128)S(1)} %get-tuple-element.123.refs_1_, s32[3,32,2048]{2,1,0:T(8,128)S(1)} %get-tuple-element.124.refs_2_, f32[3,2,16,128]{3,2,1,0:T(8,128)S(1)} %get-tuple-element.125.refs_3_, ...), custom_call_target="tpu_custom_call" | custom-call | flops 1286602752 | bytes 4718592 | tf_op jit(solution)/shard_map/cond/branch_1_fun/pallas_call | solution.py:376
  86.9 23.9 %all_to_all.10 = f32[4,3,8,2048]{3,2,1,0:T(8,128)S(1)} all-to-all(f32[4,3,8,2048]{3,2,1,0:T(8,128)S(1)} %get-tuple-element.163), channel_id=1, replica_groups=mesh['shots'=2,'depth'=4,'strip'=4] {'strip'}, dimensions={0} | all-to-all | bytes 1572864 | tf_op jit(solution)/shard_map/all_to_all | solution.py:492
  110.8 0.7 reduce_sum.9
  (23 shorter events, 0.1 us)
Async XLA Ops:
  3.3 4.9 %copy-start = (f32[4]{0:T(128)S(1)}, f32[4]{0:T(128)}, u32[]{:S(2)}) copy-start(f32[4]{0:T(128)} %param.21) | copy-start | bytes 52
  3.3 5.5 %copy-start.1 = (s32[3]{0:T(128)S(1)}, s32[3]{0:T(128)}, u32[]{:S(2)}) copy-start(s32[3]{0:T(128)} %param.25) | copy-start | bytes 40
  3.3 5.5 %copy-start.2 = (f32[8]{0:T(128)S(1)}, f32[8]{0:T(128)}, u32[]{:S(2)}) copy-start(f32[8]{0:T(128)} %param.22) | copy-start | bytes 100
  3.3 6.2 %copy-start.3 = (f32[8]{0:T(128)S(1)}, f32[8]{0:T(128)}, u32[]{:S(2)}) copy-start(f32[8]{0:T(128)} %param.23) | copy-start | bytes 100
  3.3 8.1 %copy-start.4 = (f32[16,128]{1,0:T(8,128)S(1)}, f32[16,128]{1,0:T(8,128)}, u32[]{:S(2)}) copy-start(f32[16,128]{1,0:T(8,128)} %constant.51) | copy-start | bytes 24580
  3.3 32.3 %all-to-all-start = ((f32[4,5,8,2048]{3,2,1,0:T(8,128)}), f32[4,5,8,2048]{3,2,1,0:T(8,128)S(1)}, u32[]{:S(2)}, u32[]{:S(2)}) async-start(f32[4,5,8,2048]{3,2,1,0:T(8,128)} %pad_maximum_fusion), calls=%async_computation | async-start | bytes 2621440 | tf_op jit(solution)/shard_map/all_to_all | solution.py:474
  11.6 24.2 %copy-start.5 = (bf16[256,256]{1,0:T(8,128)(2,1)S(1)}, bf16[256,256]{1,0:T(8,128)(2,1)}, u32[]{:S(2)}) copy-start(bf16[256,256]{1,0:T(8,128)(2,1)} %constant.44.clone) | copy-start | bytes 393220
  11.6 24.2 %copy-start.6 = (bf16[256,256]{1,0:T(8,128)(2,1)S(1)}, bf16[256,256]{1,0:T(8,128)(2,1)}, u32[]{:S(2)}) copy-start(bf16[256,256]{1,0:T(8,128)(2,1)} %constant.45.clone) | copy-start | bytes 393220
  11.6 24.2 %copy-start.7 = (bf16[256,256]{1,0:T(8,128)(2,1)S(1)}, bf16[256,256]{1,0:T(8,128)(2,1)}, u32[]{:S(2)}) copy-start(bf16[256,256]{1,0:T(8,128)(2,1)} %constant.46.clone) | copy-start | bytes 393220
  11.6 24.2 %copy-start.8 = (bf16[256,256]{1,0:T(8,128)(2,1)S(1)}, bf16[256,256]{1,0:T(8,128)(2,1)}, u32[]{:S(2)}) copy-start(bf16[256,256]{1,0:T(8,128)(2,1)} %constant.47.clone) | copy-start | bytes 393220
  11.7 24.2 %copy-start.9 = (f32[2,16,128]{2,1,0:T(8,128)S(1)}, f32[2,16,128]{2,1,0:T(8,128)}, u32[]{:S(2)}) copy-start(f32[2,16,128]{2,1,0:T(8,128)} %constant.43.clone) | copy-start | bytes 49156
  35.9 5.2 %collective-permute-start = (f32[2,32,2048]{2,1,0:T(8,128)S(1)}, f32[2,32,2048]{2,1,0:T(8,128)S(1)}, u32[]{:S(2)}, u32[]{:S(2)}) collective-permute-start(f32[2,32,2048]{2,1,0:T(8,128)S(1)} %get-tuple-element.138), channel_id=1, source_target_pairs={{0,4},{4,8},{8,12},{1,5},{5,9},{9,13},{2,6},{6,10},{10,14},{3,7},{... | collective-permute-start | bytes 1572872 | tf_op jit(solution)/shard_map/ppermute | solution.py:36
  41.1 10.5 %collective-permute-start.1 = (f32[2,32,2048]{2,1,0:T(8,128)S(1)}, f32[2,32,2048]{2,1,0:T(8,128)S(1)}, u32[]{:S(2)}, u32[]{:S(2)}) collective-permute-start(f32[2,32,2048]{2,1,0:T(8,128)S(1)} %get-tuple-element.140), channel_id=1, source_target_pairs={{0,4},{4,8},{8,12},{1,5},{5,9},{9,13},{2,6},{6,10},{10,14},{3,7},{... | collective-permute-start | bytes 1572872 | tf_op jit(solution)/shard_map/ppermute | solution.py:36
  51.6 27.3 %collective-permute-start.2 = (f32[2,32,2048]{2,1,0:T(8,128)S(1)}, f32[2,32,2048]{2,1,0:T(8,128)S(1)}, u32[]{:S(2)}, u32[]{:S(2)}) collective-permute-start(f32[2,32,2048]{2,1,0:T(8,128)S(1)} %get-tuple-element.143), channel_id=1, source_target_pairs={{0,4},{4,8},{8,12},{1,5},{5,9},{9,13},{2,6},{6,10},{10,14},{3,7},{... | collective-permute-start | bytes 1572872 | tf_op jit(solution)/shard_map/ppermute | solution.py:36

commit v3 on v2

--- a/solution.py
+++ b/solution.py
@@ -463,18 +463,24 @@
     strip_no = lax.axis_index("strip")
     strip_count = lax.axis_size("strip")
     rows = rows_here * strip_count
+    every_depth = range(segment_count)
     consts = fast_constants(line_len)
-    outgoing = jnp.concatenate(
-        [
-            jnp.broadcast_to(region_index.astype(jnp.float32)[None], (strip_count,) + region_index.shape),
-            jnp.transpose(surface, (1, 0, 2, 3)),
-        ],
-        axis=1,
-    )
-    incoming = lax.all_to_all(outgoing, "strip", 0, 0, tiled=True)
-    regions = jnp.transpose(incoming[:, :steps], (1, 0, 2, 3)).reshape(steps, rows, line_len)
-    regions = regions.astype(jnp.int32)
-    wave = jnp.transpose(incoming[:, steps:], (1, 0, 2, 3)).reshape(2, rows, line_len)
+    region_f = region_index.astype(jnp.float32)
+    mine = lax.dynamic_index_in_dim(surface, strip_no, 1, keepdims=False)
+    gathered = jnp.zeros((steps + 2, rows, line_len), jnp.float32)
+    gathered = lax.dynamic_update_slice(
+        gathered, jnp.concatenate([region_f, mine], axis=0), (0, strip_no * rows_here, 0)
+    )
+    for shift in range(1, strip_count):
+        target = (strip_no + shift) % strip_count
+        piece = jnp.concatenate(
+            [region_f, lax.dynamic_index_in_dim(surface, target, 1, keepdims=False)], axis=0
+        )
+        got = lax.ppermute(piece, ("depth", "strip"), strip_pairs(every_depth, strip_count, shift))
+        source = (strip_no - shift) % strip_count
+        gathered = lax.dynamic_update_slice(gathered, got, (0, source * rows_here, 0))
+    regions = gathered[:steps].astype(jnp.int32)
+    wave = gathered[steps:]
     omega = lax.dynamic_index_in_dim(omegas, strip_no, 0, keepdims=False)
     table, mult = section_tables(omega, region_speed, fd_coeff, ref_region, jnp.asarray(consts[3]))
     image = jnp.zeros((strip_count, steps, rows_here, line_len), jnp.float32)
@@ -489,8 +495,14 @@
         wave, image = lax.cond(segment_no == tick_no, live, idle, wave, image)
         if tick_no + 1 < segment_count:
             wave = from_behind(wave, "depth", 1)
-    parts = lax.all_to_all(image, "strip", 0, 0, tiled=True)
-    return jnp.sum(parts, axis=0)
+    total = lax.dynamic_index_in_dim(image, strip_no, 0, keepdims=False)
+    for shift in range(1, strip_count):
+        target = (strip_no + shift) % strip_count
+        piece = lax.dynamic_index_in_dim(image, target, 0, keepdims=False)
+        total = total + lax.ppermute(
+            piece, ("depth", "strip"), strip_pairs(every_depth, strip_count, shift)
+        )
+    return total
 
 
 def solution(mesh):

time: 113 us -> 105 us (0.929)
  blocking collectives: 23.9 us -> 0 us
  waiting for transfers between devices: 63 us -> 77.6 us
  starting transfers between devices: 8.75 us -> 10.5 us
  local copies, waits for them, and re-layouts: 2.58 us -> 3.77 us
    ppermute x0 -> x6, waiting for transfers between devices: none -> 40 us  [shards(): lax.ppermute(piece, ('depth', 'strip'), strip_pairs(every_depth, strip_co...]
    all_to_all x1 -> x0, waiting for transfers between devices: 24 us -> none  [shards(): incoming = lax.all_to_all(outgoing, 'strip', 0, 0, tiled=True)]
    all_to_all x1 -> x0, blocking collectives: 23.9 us -> none  [shards(): parts = lax.all_to_all(image, 'strip', 0, 0, tiled=True)]
    ppermute x0 -> x6, starting transfers between devices: none -> 6.69 us  [shards(): lax.ppermute(piece, ('depth', 'strip'), strip_pairs(every_depth, strip_co...]
    all_to_all x1 -> x0, starting transfers between devices: 4.9 us -> none  [shards(): incoming = lax.all_to_all(outgoing, 'strip', 0, 0, tiled=True)]
    ppermute x3, waiting for transfers between devices: 39 us -> 37.6 us  [from_behind(): lax.ppermute(value, axis, [(source, source + steps) for source in range(f...]
    squeeze x0 -> x2, local copies, waits for them, and re-layouts: none -> 1.18 us  [the longest x1 1.14 us: shards(): lax.dynamic_index_in_dim(surface, target, 1, keepdims=False)]
  transfers between devices with their start and end apart: 4 -> 9, of which waited for: 4 -> 9; matrix products, arithmetic and copies ran while one was open for 3% -> 4% of each run, Pallas kernels for 0% -> 0%
where the time goes in v3:
time: 105 us; the launch traced here: 104 us
  waiting for transfers between devices  77.6 us (74%)
  starting transfers between devices  10.5 us (10%)
  Pallas kernels  8.04 us (8%)
  other arithmetic  4.17 us (4%)
  local copies, waits for them, and re-layouts  3.77 us (4%)
    ppermute x6, waiting for transfers between devices, shards(): lax.ppermute(piece, ('depth', 'strip'), strip_pairs(every_depth, strip_co...  40 us
    ppermute x3, waiting for transfers between devices, from_behind(): lax.ppermute(value, axis, [(source, source + steps) for source in range(f...  37.6 us
    pallas_call x1, Pallas kernels, run_section(): pl.pallas_call(lambda *refs: section_kernel(*refs, table_len=table_len),...  8.04 us
    ppermute x6, starting transfers between devices, shards(): lax.ppermute(piece, ('depth', 'strip'), strip_pairs(every_depth, strip_co...  6.69 us
    ppermute x3, starting transfers between devices, from_behind(): lax.ppermute(value, axis, [(source, source + steps) for source in range(f...  3.85 us
  transfers between devices with their start and end apart: 9, of which 9 were waited for; matrix products, arithmetic and copies ran while one was open for 4% of the time, Pallas kernels for 0%

profile of v3, /device:TPU:11, one launch (start us, length us, event | category | flops | bytes accessed | tf_op | source)
XLA Modules:
  0.0 104.4 jit_solution(3711015888063189954)
XLA Ops:
  0.0 0.9 convert_element_type.22
  1.0 1.1 %dynamic-slice_bitcast_fusion.3 = (f32[2,8,2048]{2,1,0:T(8,128)S(1)}, f32[2,8,2048]{2,1,0:T(8,128)S(1)}, f32[2,8,2048]{2,1,0:T(8,128)S(1)}, f32[2,8,2048]{2,1,0:T(8,128)S(1)}) fusion(f32[2,4,8,2048]{3,2,1,0:T(8,128)} %param.20, s32[]{:T(128)S(6)} %select_n.79, s32[]{:T(128)S(6)} %select_n.71, s32[]{:T(128)S(6)} %select_n.68, s32[]{:T(128)S(6)} %select_n.75), kind=kLoop, calls=%fused_computation.13 | loop fusion | bytes 1048592 | tf_op jit(solution)/shard_map/jit(dynamic_index_in_dim)/squeeze | solution.py:477
  2.1 0.1 broadcast_in_dim.6
  2.3 0.1 pad_maximum_fusion
  2.4 1.3 %collective-permute-start = (f32[5,8,2048]{2,1,0:T(8,128)S(1)}, f32[5,8,2048]{2,1,0:T(8,128)S(1)}, u32[]{:S(2)}, u32[]{:S(2)}) collective-permute-start(f32[5,8,2048]{2,1,0:T(8,128)S(1)} %get-tuple-element.152), channel_id=1, source_target_pairs={{0,1},{1,2},{2,3},{3,0},{4,5},{5,6},{6,7},{7,4},{8,9},{9,10},{10,1... | collective-permute-start | bytes 983048 | tf_op jit(solution)/shard_map/ppermute | solution.py:479
  3.8 1.1 %collective-permute-start.1 = (f32[5,8,2048]{2,1,0:T(8,128)S(1)}, f32[5,8,2048]{2,1,0:T(8,128)S(1)}, u32[]{:S(2)}, u32[]{:S(2)}) collective-permute-start(f32[5,8,2048]{2,1,0:T(8,128)S(1)} %get-tuple-element.153), channel_id=1, source_target_pairs={{0,2},{1,3},{2,0},{3,1},{4,6},{5,7},{6,4},{7,5},{8,10},{9,11},{10,... | collective-permute-start | bytes 983048 | tf_op jit(solution)/shard_map/ppermute | solution.py:479
  4.9 1.4 %collective-permute-start.2 = (f32[5,8,2048]{2,1,0:T(8,128)S(1)}, f32[5,8,2048]{2,1,0:T(8,128)S(1)}, u32[]{:S(2)}, u32[]{:S(2)}) collective-permute-start(f32[5,8,2048]{2,1,0:T(8,128)S(1)} %get-tuple-element.151), channel_id=1, source_target_pairs={{0,3},{1,0},{2,1},{3,2},{4,7},{5,4},{6,5},{7,6},{8,11},{9,8},{10,9... | collective-permute-start | bytes 983048 | tf_op jit(solution)/shard_map/ppermute | solution.py:479
  6.3 0.6 dynamic_slice.34
  6.9 0.6 gather_fusion
  7.5 0.8 fusion.13
  8.3 0.7 multiply_multiply_fusion
  9.0 0.7 broadcast_divide_fusion
  9.7 0.1 reshape.125
  9.8 0.2 fusion.8
  10.0 1.1 %collective-permute-done = f32[5,8,2048]{2,1,0:T(8,128)S(1)} collective-permute-done((f32[5,8,2048]{2,1,0:T(8,128)S(1)}, f32[5,8,2048]{2,1,0:T(8,128)S(1)}, u32[]{:S(2)}, u32[]{:S(2)}) %collective-permute-start) | collective-permute-done | bytes 327712 | tf_op jit(solution)/shard_map/ppermute | solution.py:479
  11.1 20.1 %collective-permute-done.1 = f32[5,8,2048]{2,1,0:T(8,128)S(1)} collective-permute-done((f32[5,8,2048]{2,1,0:T(8,128)S(1)}, f32[5,8,2048]{2,1,0:T(8,128)S(1)}, u32[]{:S(2)}, u32[]{:S(2)}) %collective-permute-start.1) | collective-permute-done | bytes 327712 | tf_op jit(solution)/shard_map/ppermute | solution.py:479
  31.3 2.8 %collective-permute-done.2 = f32[5,8,2048]{2,1,0:T(8,128)S(1)} collective-permute-done((f32[5,8,2048]{2,1,0:T(8,128)S(1)}, f32[5,8,2048]{2,1,0:T(8,128)S(1)}, u32[]{:S(2)}, u32[]{:S(2)}) %collective-permute-start.2) | collective-permute-done | bytes 327712 | tf_op jit(solution)/shard_map/ppermute | solution.py:479
  34.3 0.7 copy-done.5
  35.3 1.3 %collective-permute-start.3 = (f32[2,32,2048]{2,1,0:T(8,128)S(1)}, f32[2,32,2048]{2,1,0:T(8,128)S(1)}, u32[]{:S(2)}, u32[]{:S(2)}) collective-permute-start(f32[2,32,2048]{2,1,0:T(8,128)S(1)} %get-tuple-element.138), channel_id=1, source_target_pairs={{0,4},{4,8},{8,12},{1,5},{5,9},{9,13},{2,6},{6,10},{10,14},{3,7},{... | collective-permute-start | bytes 1572872 | tf_op jit(solution)/shard_map/ppermute | solution.py:36
  36.6 2.5 %collective-permute-done.3 = f32[2,32,2048]{2,1,0:T(8,128)S(1)} collective-permute-done((f32[2,32,2048]{2,1,0:T(8,128)S(1)}, f32[2,32,2048]{2,1,0:T(8,128)S(1)}, u32[]{:S(2)}, u32[]{:S(2)}) %collective-permute-start.3) | collective-permute-done | bytes 524320 | tf_op jit(solution)/shard_map/ppermute | solution.py:36
  39.1 1.3 %collective-permute-start.4 = (f32[2,32,2048]{2,1,0:T(8,128)S(1)}, f32[2,32,2048]{2,1,0:T(8,128)S(1)}, u32[]{:S(2)}, u32[]{:S(2)}) collective-permute-start(f32[2,32,2048]{2,1,0:T(8,128)S(1)} %get-tuple-element.140), channel_id=1, source_target_pairs={{0,4},{4,8},{8,12},{1,5},{5,9},{9,13},{2,6},{6,10},{10,14},{3,7},{... | collective-permute-start | bytes 1572872 | tf_op jit(solution)/shard_map/ppermute | solution.py:36
  40.4 9.2 %collective-permute-done.4 = f32[2,32,2048]{2,1,0:T(8,128)S(1)} collective-permute-done((f32[2,32,2048]{2,1,0:T(8,128)S(1)}, f32[2,32,2048]{2,1,0:T(8,128)S(1)}, u32[]{:S(2)}, u32[]{:S(2)}) %collective-permute-start.4) | collective-permute-done | bytes 524320 | tf_op jit(solution)/shard_map/ppermute | solution.py:36
  49.6 1.3 %collective-permute-start.5 = (f32[2,32,2048]{2,1,0:T(8,128)S(1)}, f32[2,32,2048]{2,1,0:T(8,128)S(1)}, u32[]{:S(2)}, u32[]{:S(2)}) collective-permute-start(f32[2,32,2048]{2,1,0:T(8,128)S(1)} %get-tuple-element.143), channel_id=1, source_target_pairs={{0,4},{4,8},{8,12},{1,5},{5,9},{9,13},{2,6},{6,10},{10,14},{3,7},{... | collective-permute-start | bytes 1572872 | tf_op jit(solution)/shard_map/ppermute | solution.py:36
  50.9 25.9 %collective-permute-done.5 = f32[2,32,2048]{2,1,0:T(8,128)S(1)} collective-permute-done((f32[2,32,2048]{2,1,0:T(8,128)S(1)}, f32[2,32,2048]{2,1,0:T(8,128)S(1)}, u32[]{:S(2)}, u32[]{:S(2)}) %collective-permute-start.5) | collective-permute-done | bytes 524320 | tf_op jit(solution)/shard_map/ppermute | solution.py:36
  76.8 8.0 %conditional.7 = (f32[4,3,8,2048]{3,2,1,0:T(8,128)S(1)}) conditional(s32[]{:T(128)} %convert_element_type.18, f32[4,3,8,2048]{3,2,1,0:T(8,128)S(1)} %get-tuple-element.142, (f32[72]{0:T(128)S(1)}, f32[2,32,2048]{2,1,0:T(8,128)S(1)}, s32[3,32,2048]{2,1,0:T(8,128)S(1)}, f32[3,2,16,128]{3,2,1,0:T(8,128)S(1)}, f32[2,16,128]{2,1,0:T(8,128)S(1)}, ...), branch_computations={%region_6.7_spmd, %region_7.8_spmd} | conditional | flops 1286602752 | bytes 4718600 | solution.py:495
  76.8 8.0 %branch_1_fun.7 = (f32[2,32,2048]{2,1,0:T(8,128)}, f32[4,3,8,2048]{3,2,1,0:T(8,128)S(1)}) custom-call(f32[72]{0:T(128)S(1)} %get-tuple-element.122.refs_0_, f32[2,32,2048]{2,1,0:T(8,128)S(1)} %get-tuple-element.123.refs_1_, s32[3,32,2048]{2,1,0:T(8,128)S(1)} %get-tuple-element.124.refs_2_, f32[3,2,16,128]{3,2,1,0:T(8,128)S(1)} %get-tuple-element.125.refs_3_, ...), custom_call_target="tpu_custom_call" | custom-call | flops 1286602752 | bytes 4718592 | tf_op jit(solution)/shard_map/cond/branch_1_fun/pallas_call | solution.py:376
  85.0 1.4 %collective-permute-start.7 = (f32[3,8,2048]{2,1,0:T(8,128)S(1)}, f32[3,8,2048]{2,1,0:T(8,128)S(1)}, u32[]{:S(2)}, u32[]{:S(2)}) collective-permute-start(f32[3,8,2048]{2,1,0:T(8,128)S(1)} %get-tuple-element.146), channel_id=1, source_target_pairs={{0,2},{1,3},{2,0},{3,1},{4,6},{5,7},{6,4},{7,5},{8,10},{9,11},{10,... | collective-permute-start | bytes 589832 | tf_op jit(solution)/shard_map/ppermute | solution.py:502
  86.4 1.4 %collective-permute-start.8 = (f32[3,8,2048]{2,1,0:T(8,128)S(1)}, f32[3,8,2048]{2,1,0:T(8,128)S(1)}, u32[]{:S(2)}, u32[]{:S(2)}) collective-permute-start(f32[3,8,2048]{2,1,0:T(8,128)S(1)} %get-tuple-element.145), channel_id=1, source_target_pairs={{0,3},{1,0},{2,1},{3,2},{4,7},{5,4},{6,5},{7,6},{8,11},{9,8},{10,9... | collective-permute-start | bytes 589832 | tf_op jit(solution)/shard_map/ppermute | solution.py:502
  87.8 4.0 %collective-permute-done.6 = f32[3,8,2048]{2,1,0:T(8,128)S(1)} collective-permute-done((f32[3,8,2048]{2,1,0:T(8,128)S(1)}, f32[3,8,2048]{2,1,0:T(8,128)S(1)}, u32[]{:S(2)}, u32[]{:S(2)}) %collective-permute-start.6) | collective-permute-done | bytes 196640 | tf_op jit(solution)/shard_map/ppermute | solution.py:502
  91.8 9.9 %collective-permute-done.7 = f32[3,8,2048]{2,1,0:T(8,128)S(1)} collective-permute-done((f32[3,8,2048]{2,1,0:T(8,128)S(1)}, f32[3,8,2048]{2,1,0:T(8,128)S(1)}, u32[]{:S(2)}, u32[]{:S(2)}) %collective-permute-start.7) | collective-permute-done | bytes 196640 | tf_op jit(solution)/shard_map/ppermute | solution.py:502
  101.6 2.1 %collective-permute-done.8 = f32[3,8,2048]{2,1,0:T(8,128)S(1)} collective-permute-done((f32[3,8,2048]{2,1,0:T(8,128)S(1)}, f32[3,8,2048]{2,1,0:T(8,128)S(1)}, u32[]{:S(2)}, u32[]{:S(2)}) %collective-permute-start.8) | collective-permute-done | bytes 196640 | tf_op jit(solution)/shard_map/ppermute | solution.py:502
  103.7 0.7 fusion.2
  (36 shorter events, 0.7 us)
Async XLA Ops:
  2.2 4.0 %copy-start = (f32[4]{0:T(128)S(1)}, f32[4]{0:T(128)}, u32[]{:S(2)}) copy-start(f32[4]{0:T(128)} %param.21) | copy-start | bytes 52
  2.3 4.6 %copy-start.1 = (f32[8]{0:T(128)S(1)}, f32[8]{0:T(128)}, u32[]{:S(2)}) copy-start(f32[8]{0:T(128)} %param.22) | copy-start | bytes 100
  2.3 4.6 %copy-start.2 = (s32[3]{0:T(128)S(1)}, s32[3]{0:T(128)}, u32[]{:S(2)}) copy-start(s32[3]{0:T(128)} %param.25) | copy-start | bytes 40
  2.3 6.7 %copy-start.3 = (f32[8]{0:T(128)S(1)}, f32[8]{0:T(128)}, u32[]{:S(2)}) copy-start(f32[8]{0:T(128)} %param.23) | copy-start | bytes 100
  2.3 7.5 %copy-start.4 = (f32[16,128]{1,0:T(8,128)S(1)}, f32[16,128]{1,0:T(8,128)}, u32[]{:S(2)}) copy-start(f32[16,128]{1,0:T(8,128)} %constant.116) | copy-start | bytes 24580
  2.4 8.6 %collective-permute-start = (f32[5,8,2048]{2,1,0:T(8,128)S(1)}, f32[5,8,2048]{2,1,0:T(8,128)S(1)}, u32[]{:S(2)}, u32[]{:S(2)}) collective-permute-start(f32[5,8,2048]{2,1,0:T(8,128)S(1)} %get-tuple-element.152), channel_id=1, source_target_pairs={{0,1},{1,2},{2,3},{3,0},{4,5},{5,6},{6,7},{7,4},{8,9},{9,10},{10,1... | collective-permute-start | bytes 983048 | tf_op jit(solution)/shard_map/ppermute | solution.py:479
  3.8 27.4 %collective-permute-start.1 = (f32[5,8,2048]{2,1,0:T(8,128)S(1)}, f32[5,8,2048]{2,1,0:T(8,128)S(1)}, u32[]{:S(2)}, u32[]{:S(2)}) collective-permute-start(f32[5,8,2048]{2,1,0:T(8,128)S(1)} %get-tuple-element.153), channel_id=1, source_target_pairs={{0,2},{1,3},{2,0},{3,1},{4,6},{5,7},{6,4},{7,5},{8,10},{9,11},{10,... | collective-permute-start | bytes 983048 | tf_op jit(solution)/shard_map/ppermute | solution.py:479
  4.9 29.2 %collective-permute-start.2 = (f32[5,8,2048]{2,1,0:T(8,128)S(1)}, f32[5,8,2048]{2,1,0:T(8,128)S(1)}, u32[]{:S(2)}, u32[]{:S(2)}) collective-permute-start(f32[5,8,2048]{2,1,0:T(8,128)S(1)} %get-tuple-element.151), channel_id=1, source_target_pairs={{0,3},{1,0},{2,1},{3,2},{4,7},{5,4},{6,5},{7,6},{8,11},{9,8},{10,9... | collective-permute-start | bytes 983048 | tf_op jit(solution)/shard_map/ppermute | solution.py:479
  34.1 0.9 copy-start.5
  34.1 1.0 copy-start.6
  34.1 1.0 copy-start.7
  34.2 1.1 %copy-start.8 = (bf16[256,256]{1,0:T(8,128)(2,1)S(1)}, bf16[256,256]{1,0:T(8,128)(2,1)}, u32[]{:S(2)}) copy-start(bf16[256,256]{1,0:T(8,128)(2,1)} %constant.112.clone) | copy-start | bytes 393220
  34.2 1.1 %copy-start.9 = (f32[2,16,128]{2,1,0:T(8,128)S(1)}, f32[2,16,128]{2,1,0:T(8,128)}, u32[]{:S(2)}) copy-start(f32[2,16,128]{2,1,0:T(8,128)} %constant.108.clone) | copy-start | bytes 49156
  35.3 3.8 %collective-permute-start.3 = (f32[2,32,2048]{2,1,0:T(8,128)S(1)}, f32[2,32,2048]{2,1,0:T(8,128)S(1)}, u32[]{:S(2)}, u32[]{:S(2)}) collective-permute-start(f32[2,32,2048]{2,1,0:T(8,128)S(1)} %get-tuple-element.138), channel_id=1, source_target_pairs={{0,4},{4,8},{8,12},{1,5},{5,9},{9,13},{2,6},{6,10},{10,14},{3,7},{... | collective-permute-start | bytes 1572872 | tf_op jit(solution)/shard_map/ppermute | solution.py:36
  39.1 10.5 %collective-permute-start.4 = (f32[2,32,2048]{2,1,0:T(8,128)S(1)}, f32[2,32,2048]{2,1,0:T(8,128)S(1)}, u32[]{:S(2)}, u32[]{:S(2)}) collective-permute-start(f32[2,32,2048]{2,1,0:T(8,128)S(1)} %get-tuple-element.140), channel_id=1, source_target_pairs={{0,4},{4,8},{8,12},{1,5},{5,9},{9,13},{2,6},{6,10},{10,14},{3,7},{... | collective-permute-start | bytes 1572872 | tf_op jit(solution)/shard_map/ppermute | solution.py:36
  49.6 27.2 %collective-permute-start.5 = (f32[2,32,2048]{2,1,0:T(8,128)S(1)}, f32[2,32,2048]{2,1,0:T(8,128)S(1)}, u32[]{:S(2)}, u32[]{:S(2)}) collective-permute-start(f32[2,32,2048]{2,1,0:T(8,128)S(1)} %get-tuple-element.143), channel_id=1, source_target_pairs={{0,4},{4,8},{8,12},{1,5},{5,9},{9,13},{2,6},{6,10},{10,14},{3,7},{... | collective-permute-start | bytes 1572872 | tf_op jit(solution)/shard_map/ppermute | solution.py:36
  84.9 6.9 %collective-permute-start.6 = (f32[3,8,2048]{2,1,0:T(8,128)S(1)}, f32[3,8,2048]{2,1,0:T(8,128)S(1)}, u32[]{:S(2)}, u32[]{:S(2)}) collective-permute-start(f32[3,8,2048]{2,1,0:T(8,128)S(1)} %get-tuple-element.144), channel_id=1, source_target_pairs={{0,1},{1,2},{2,3},{3,0},{4,5},{5,6},{6,7},{7,4},{8,9},{9,10},{10,1... | collective-permute-start | bytes 589832 | tf_op jit(solution)/shard_map/ppermute | solution.py:502
  85.0 16.7 %collective-permute-start.7 = (f32[3,8,2048]{2,1,0:T(8,128)S(1)}, f32[3,8,2048]{2,1,0:T(8,128)S(1)}, u32[]{:S(2)}, u32[]{:S(2)}) collective-permute-start(f32[3,8,2048]{2,1,0:T(8,128)S(1)} %get-tuple-element.146), channel_id=1, source_target_pairs={{0,2},{1,3},{2,0},{3,1},{4,6},{5,7},{6,4},{7,5},{8,10},{9,11},{10,... | collective-permute-start | bytes 589832 | tf_op jit(solution)/shard_map/ppermute | solution.py:502
  86.4 17.3 %collective-permute-start.8 = (f32[3,8,2048]{2,1,0:T(8,128)S(1)}, f32[3,8,2048]{2,1,0:T(8,128)S(1)}, u32[]{:S(2)}, u32[]{:S(2)}) collective-permute-start(f32[3,8,2048]{2,1,0:T(8,128)S(1)} %get-tuple-element.145), channel_id=1, source_target_pairs={{0,3},{1,0},{2,1},{3,2},{4,7},{5,4},{6,5},{7,6},{8,11},{9,8},{10,9... | collective-permute-start | bytes 589832 | tf_op jit(solution)/shard_map/ppermute | solution.py:502

commit v4 on v3

--- a/solution.py
+++ b/solution.py
@@ -463,7 +463,6 @@
     strip_no = lax.axis_index("strip")
     strip_count = lax.axis_size("strip")
     rows = rows_here * strip_count
-    every_depth = range(segment_count)
     consts = fast_constants(line_len)
     region_f = region_index.astype(jnp.float32)
     mine = lax.dynamic_index_in_dim(surface, strip_no, 1, keepdims=False)
@@ -476,7 +475,9 @@
         piece = jnp.concatenate(
             [region_f, lax.dynamic_index_in_dim(surface, target, 1, keepdims=False)], axis=0
         )
-        got = lax.ppermute(piece, ("depth", "strip"), strip_pairs(every_depth, strip_count, shift))
+        got = lax.ppermute(
+            piece, ("depth", "strip"), strip_pairs(range(segment_count), strip_count, shift)
+        )
         source = (strip_no - shift) % strip_count
         gathered = lax.dynamic_update_slice(gathered, got, (0, source * rows_here, 0))
     regions = gathered[:steps].astype(jnp.int32)
@@ -484,6 +485,7 @@
     omega = lax.dynamic_index_in_dim(omegas, strip_no, 0, keepdims=False)
     table, mult = section_tables(omega, region_speed, fd_coeff, ref_region, jnp.asarray(consts[3]))
     image = jnp.zeros((strip_count, steps, rows_here, line_len), jnp.float32)
+    total = jnp.zeros((steps, rows_here, line_len), jnp.float32)
 
     def live(wave, image):
         return run_section(wave, regions, table, mult, consts, strip_count)
@@ -494,15 +496,17 @@
     for tick_no in range(segment_count):
         wave, image = lax.cond(segment_no == tick_no, live, idle, wave, image)
         if tick_no + 1 < segment_count:
-            wave = from_behind(wave, "depth", 1)
-    total = lax.dynamic_index_in_dim(image, strip_no, 0, keepdims=False)
-    for shift in range(1, strip_count):
-        target = (strip_no + shift) % strip_count
-        piece = lax.dynamic_index_in_dim(image, target, 0, keepdims=False)
-        total = total + lax.ppermute(
-            piece, ("depth", "strip"), strip_pairs(every_depth, strip_count, shift)
-        )
-    return total
+            wave = lax.ppermute(wave, "depth", [(tick_no, tick_no + 1)])
+            wave, image = lax.optimization_barrier((wave, image))
+        for shift in range(1, strip_count):
+            target = (strip_no + shift) % strip_count
+            piece = lax.dynamic_index_in_dim(image, target, 0, keepdims=False)
+            total = total + lax.ppermute(
+                piece, ("depth", "strip"), strip_pairs([tick_no], strip_count, shift)
+            )
+        if tick_no + 1 < segment_count:
+            wave, total = lax.optimization_barrier((wave, total))
+    return total + lax.dynamic_index_in_dim(image, strip_no, 0, keepdims=False)
 
 
 def solution(mesh):

time: 105 us -> 109 us (1.038); the launches traced: 104 us -> 107 us
  starting transfers between devices: 10.5 us -> 22 us
  waiting for transfers between devices: 77.6 us -> 66.7 us
  other arithmetic: 4.17 us -> 5.29 us
    ppermute x9 -> x18, starting transfers between devices: 10.5 us -> 22 us  [the longest x12 15.3 us: shards(): lax.ppermute(piece, ('depth', 'strip'), strip_pairs([tick_no], strip_coun...]
    ppermute x9 -> x18, waiting for transfers between devices: 77.6 us -> 66.7 us  [the longest x3 37.7 us: shards(): wave = lax.ppermute(wave, 'depth', [(tick_no, tick_no + 1)])]
    add x1 -> x4, other arithmetic: 0.73 us -> 1.85 us  [the longest x3 1.1 us: shards(): total + lax.ppermute(piece, ('depth', 'strip'), strip_pairs([tick_no], st...]
  transfers between devices with their start and end apart: 9 -> 18, of which waited for: 9 -> 6; matrix products, arithmetic and copies ran while one was open for 4% -> 3% of each run, Pallas kernels for 0% -> 0%
where the time goes in v4:
time: 109 us; the launch traced here: 107 us
  waiting for transfers between devices  66.7 us (61%)
  starting transfers between devices  22 us (20%)
  Pallas kernels  8.68 us (8%)
  other arithmetic  5.29 us (5%)
  local copies, waits for them, and re-layouts  4 us (4%)
    ppermute x3, waiting for transfers between devices, shards(): wave = lax.ppermute(wave, 'depth', [(tick_no, tick_no + 1)])  37.7 us
    ppermute x3, waiting for transfers between devices, shards(): lax.ppermute(piece, ('depth', 'strip'), strip_pairs(range(segment_count),...  24.1 us
    ppermute x12, starting transfers between devices, shards(): lax.ppermute(piece, ('depth', 'strip'), strip_pairs([tick_no], strip_coun...  15.3 us
    pallas_call x1, Pallas kernels, run_section(): pl.pallas_call(lambda *refs: section_kernel(*refs, table_len=table_len),...  8.68 us
    ppermute x12, waiting for transfers between devices, shards(): lax.ppermute(piece, ('depth', 'strip'), strip_pairs([tick_no], strip_coun...  4.92 us
    ppermute x3, starting transfers between devices, shards(): lax.ppermute(piece, ('depth', 'strip'), strip_pairs(range(segment_count),...  3.83 us
    ppermute x3, starting transfers between devices, shards(): wave = lax.ppermute(wave, 'depth', [(tick_no, tick_no + 1)])  2.94 us
  transfers between devices with their start and end apart: 18, of which 6 were waited for; matrix products, arithmetic and copies ran while one was open for 3% of the time, Pallas kernels for 0%

profile of v4, /device:TPU:11, one launch (start us, length us, event | category | flops | bytes accessed | tf_op | source)
XLA Modules:
  0.0 107.3 jit_solution(13710319359991409808)
XLA Ops:
  0.0 0.9 convert_element_type.21
  1.0 1.1 %dynamic-slice_bitcast_fusion.12 = (f32[2,8,2048]{2,1,0:T(8,128)S(1)}, f32[2,8,2048]{2,1,0:T(8,128)S(1)}, f32[2,8,2048]{2,1,0:T(8,128)S(1)}, f32[2,8,2048]{2,1,0:T(8,128)S(1)}) fusion(f32[2,4,8,2048]{3,2,1,0:T(8,128)} %param.20, s32[]{:T(128)S(6)} %select_n.106, s32[]{:T(128)S(6)} %select_n.98, s32[]{:T(128)S(6)} %select_n.95, s32[]{:T(128)S(6)} %select_n.102), kind=kLoop, calls=%fused_computation.23 | loop fusion | bytes 1048592 | tf_op jit(solution)/shard_map/jit(dynamic_index_in_dim)/squeeze | solution.py:476
  2.4 1.3 %collective-permute-start = (f32[5,8,2048]{2,1,0:T(8,128)S(1)}, f32[5,8,2048]{2,1,0:T(8,128)S(1)}, u32[]{:S(2)}, u32[]{:S(2)}) collective-permute-start(f32[5,8,2048]{2,1,0:T(8,128)S(1)} %get-tuple-element.180), channel_id=1, source_target_pairs={{0,1},{1,2},{2,3},{3,0},{4,5},{5,6},{6,7},{7,4},{8,9},{9,10},{10,1... | collective-permute-start | bytes 983048 | tf_op jit(solution)/shard_map/ppermute | solution.py:478
  3.8 1.1 %collective-permute-start.1 = (f32[5,8,2048]{2,1,0:T(8,128)S(1)}, f32[5,8,2048]{2,1,0:T(8,128)S(1)}, u32[]{:S(2)}, u32[]{:S(2)}) collective-permute-start(f32[5,8,2048]{2,1,0:T(8,128)S(1)} %get-tuple-element.181), channel_id=1, source_target_pairs={{0,2},{1,3},{2,0},{3,1},{4,6},{5,7},{6,4},{7,5},{8,10},{9,11},{10,... | collective-permute-start | bytes 983048 | tf_op jit(solution)/shard_map/ppermute | solution.py:478
  4.9 1.4 %collective-permute-start.2 = (f32[5,8,2048]{2,1,0:T(8,128)S(1)}, f32[5,8,2048]{2,1,0:T(8,128)S(1)}, u32[]{:S(2)}, u32[]{:S(2)}) collective-permute-start(f32[5,8,2048]{2,1,0:T(8,128)S(1)} %get-tuple-element.179), channel_id=1, source_target_pairs={{0,3},{1,0},{2,1},{3,2},{4,7},{5,4},{6,5},{7,6},{8,11},{9,8},{10,9... | collective-permute-start | bytes 983048 | tf_op jit(solution)/shard_map/ppermute | solution.py:478
  7.5 0.8 fusion.11
  10.0 1.1 %collective-permute-done = f32[5,8,2048]{2,1,0:T(8,128)S(1)} collective-permute-done((f32[5,8,2048]{2,1,0:T(8,128)S(1)}, f32[5,8,2048]{2,1,0:T(8,128)S(1)}, u32[]{:S(2)}, u32[]{:S(2)}) %collective-permute-start) | collective-permute-done | bytes 327712 | tf_op jit(solution)/shard_map/ppermute | solution.py:478
  11.1 20.1 %collective-permute-done.1 = f32[5,8,2048]{2,1,0:T(8,128)S(1)} collective-permute-done((f32[5,8,2048]{2,1,0:T(8,128)S(1)}, f32[5,8,2048]{2,1,0:T(8,128)S(1)}, u32[]{:S(2)}, u32[]{:S(2)}) %collective-permute-start.1) | collective-permute-done | bytes 327712 | tf_op jit(solution)/shard_map/ppermute | solution.py:478
  31.3 2.8 %collective-permute-done.2 = f32[5,8,2048]{2,1,0:T(8,128)S(1)} collective-permute-done((f32[5,8,2048]{2,1,0:T(8,128)S(1)}, f32[5,8,2048]{2,1,0:T(8,128)S(1)}, u32[]{:S(2)}, u32[]{:S(2)}) %collective-permute-start.2) | collective-permute-done | bytes 327712 | tf_op jit(solution)/shard_map/ppermute | solution.py:478
  34.3 0.7 copy-done.6
  35.3 0.7 collective-permute-start.3
  36.1 0.7 collective-permute-start.4
  36.8 0.7 collective-permute-start.5
  37.4 0.7 collective-permute-start.6
  38.2 0.8 collective-permute-start.7
  39.1 0.7 collective-permute-start.10
  39.8 0.7 collective-permute-start.8
  40.5 1.4 %collective-permute-start.9 = (f32[3,8,2048]{2,1,0:T(8,128)S(1)}, f32[3,8,2048]{2,1,0:T(8,128)}, u32[]{:S(2)}, u32[]{:S(2)}) collective-permute-start(f32[3,8,2048]{2,1,0:T(8,128)S(1)} %get-tuple-element.171), channel_id=1, source_target_pairs={{4,6},{5,7},{6,4},{7,5},{20,22},{21,23},{22,20},{23,21}} | collective-permute-start | bytes 589832 | tf_op jit(solution)/shard_map/ppermute | solution.py:504
  41.9 1.0 add_add_fusion.1
  42.9 1.4 %collective-permute-start.11 = (f32[2,32,2048]{2,1,0:T(8,128)S(1)}, f32[2,32,2048]{2,1,0:T(8,128)S(1)}, u32[]{:S(2)}, u32[]{:S(2)}) collective-permute-start(f32[2,32,2048]{2,1,0:T(8,128)S(1)} %get-tuple-element.156), channel_id=1, source_target_pairs={{8,12},{9,13},{10,14},{11,15},{24,28},{25,29},{26,30},{27,31}} | collective-permute-start | bytes 1572872 | tf_op jit(solution)/shard_map/ppermute | solution.py:499
  44.3 37.7 %collective-permute-done.11 = f32[2,32,2048]{2,1,0:T(8,128)S(1)} collective-permute-done((f32[2,32,2048]{2,1,0:T(8,128)S(1)}, f32[2,32,2048]{2,1,0:T(8,128)S(1)}, u32[]{:S(2)}, u32[]{:S(2)}) %collective-permute-start.11) | collective-permute-done | bytes 524320 | tf_op jit(solution)/shard_map/ppermute | solution.py:499
  82.1 0.7 collective-permute-start.12
  82.9 0.7 collective-permute-start.13
  83.5 0.7 collective-permute-start.14
  84.3 8.7 %conditional.7 = (f32[4,3,8,2048]{3,2,1,0:T(8,128)S(1)}) conditional(s32[]{:T(128)} %convert_element_type.23, f32[4,3,8,2048]{3,2,1,0:T(8,128)S(1)} %get-tuple-element.160, (f32[72]{0:T(128)S(1)}, f32[2,32,2048]{2,1,0:T(8,128)}, s32[3,32,2048]{2,1,0:T(8,128)S(1)}, f32[3,2,16,128]{3,2,1,0:T(8,128)S(1)}, f32[2,16,128]{2,1,0:T(8,128)S(1)}, ...), branch_computations={%region_6.7_spmd, %region_7.8_spmd} | conditional | flops 1286602752 | bytes 4718600 | solution.py:497
  84.4 8.7 %branch_1_fun.7 = (f32[2,32,2048]{2,1,0:T(8,128)}, f32[4,3,8,2048]{3,2,1,0:T(8,128)S(1)}) custom-call(f32[72]{0:T(128)S(1)} %get-tuple-element.117.refs_0_, f32[2,32,2048]{2,1,0:T(8,128)} %get-tuple-element.118.refs_1_, s32[3,32,2048]{2,1,0:T(8,128)S(1)} %get-tuple-element.119.refs_2_, f32[3,2,16,128]{3,2,1,0:T(8,128)S(1)} %get-tuple-element.120.refs_3_, ...), custom_call_target="tpu_custom_call" | custom-call | flops 1286602752 | bytes 4718592 | tf_op jit(solution)/shard_map/cond/branch_1_fun/pallas_call | solution.py:376
  93.1 1.9 %collective-permute-start.15 = (f32[3,8,2048]{2,1,0:T(8,128)S(1)}, f32[3,8,2048]{2,1,0:T(8,128)S(1)}, u32[]{:S(2)}, u32[]{:S(2)}) collective-permute-start(f32[3,8,2048]{2,1,0:T(8,128)S(1)} %get-tuple-element.163), channel_id=1, source_target_pairs={{12,13},{13,14},{14,15},{15,12},{28,29},{29,30},{30,31},{31,28}} | collective-permute-start | bytes 589832 | tf_op jit(solution)/shard_map/ppermute | solution.py:504
  95.0 3.3 %collective-permute-start.16 = (f32[3,8,2048]{2,1,0:T(8,128)S(1)}, f32[3,8,2048]{2,1,0:T(8,128)S(1)}, u32[]{:S(2)}, u32[]{:S(2)}) collective-permute-start(f32[3,8,2048]{2,1,0:T(8,128)S(1)} %get-tuple-element.165), channel_id=1, source_target_pairs={{12,14},{13,15},{14,12},{15,13},{28,30},{29,31},{30,28},{31,29}} | collective-permute-start | bytes 589832 | tf_op jit(solution)/shard_map/ppermute | solution.py:504
  98.3 3.4 %collective-permute-start.17 = (f32[3,8,2048]{2,1,0:T(8,128)S(1)}, f32[3,8,2048]{2,1,0:T(8,128)S(1)}, u32[]{:S(2)}, u32[]{:S(2)}) collective-permute-start(f32[3,8,2048]{2,1,0:T(8,128)S(1)} %get-tuple-element.164), channel_id=1, source_target_pairs={{12,15},{13,12},{14,13},{15,14},{28,31},{29,28},{30,29},{31,30}} | collective-permute-start | bytes 589832 | tf_op jit(solution)/shard_map/ppermute | solution.py:504
  101.7 3.4 %collective-permute-done.16 = f32[3,8,2048]{2,1,0:T(8,128)S(1)} collective-permute-done((f32[3,8,2048]{2,1,0:T(8,128)S(1)}, f32[3,8,2048]{2,1,0:T(8,128)S(1)}, u32[]{:S(2)}, u32[]{:S(2)}) %collective-permute-start.16) | collective-permute-done | bytes 196640 | tf_op jit(solution)/shard_map/ppermute | solution.py:504
  105.1 1.5 %collective-permute-done.17 = f32[3,8,2048]{2,1,0:T(8,128)S(1)} collective-permute-done((f32[3,8,2048]{2,1,0:T(8,128)S(1)}, f32[3,8,2048]{2,1,0:T(8,128)S(1)}, u32[]{:S(2)}, u32[]{:S(2)}) %collective-permute-start.17) | collective-permute-done | bytes 196640 | tf_op jit(solution)/shard_map/ppermute | solution.py:504
  106.5 0.7 bitcast_add_fusion
  (68 shorter events, 4.1 us)
Async XLA Ops:
  2.2 4.0 %copy-start.1 = (f32[4]{0:T(128)S(1)}, f32[4]{0:T(128)}, u32[]{:S(2)}) copy-start(f32[4]{0:T(128)} %param.21) | copy-start | bytes 52
  2.3 4.6 %copy-start.2 = (f32[8]{0:T(128)S(1)}, f32[8]{0:T(128)}, u32[]{:S(2)}) copy-start(f32[8]{0:T(128)} %param.22) | copy-start | bytes 100
  2.3 4.6 %copy-start.3 = (s32[3]{0:T(128)S(1)}, s32[3]{0:T(128)}, u32[]{:S(2)}) copy-start(s32[3]{0:T(128)} %param.25) | copy-start | bytes 40
  2.3 6.7 %copy-start.4 = (f32[8]{0:T(128)S(1)}, f32[8]{0:T(128)}, u32[]{:S(2)}) copy-start(f32[8]{0:T(128)} %param.23) | copy-start | bytes 100
  2.3 7.5 %copy-start.5 = (f32[16,128]{1,0:T(8,128)S(1)}, f32[16,128]{1,0:T(8,128)}, u32[]{:S(2)}) copy-start(f32[16,128]{1,0:T(8,128)} %constant.152) | copy-start | bytes 24580
  2.4 8.6 %collective-permute-start = (f32[5,8,2048]{2,1,0:T(8,128)S(1)}, f32[5,8,2048]{2,1,0:T(8,128)S(1)}, u32[]{:S(2)}, u32[]{:S(2)}) collective-permute-start(f32[5,8,2048]{2,1,0:T(8,128)S(1)} %get-tuple-element.180), channel_id=1, source_target_pairs={{0,1},{1,2},{2,3},{3,0},{4,5},{5,6},{6,7},{7,4},{8,9},{9,10},{10,1... | collective-permute-start | bytes 983048 | tf_op jit(solution)/shard_map/ppermute | solution.py:478
  3.8 27.4 %collective-permute-start.1 = (f32[5,8,2048]{2,1,0:T(8,128)S(1)}, f32[5,8,2048]{2,1,0:T(8,128)S(1)}, u32[]{:S(2)}, u32[]{:S(2)}) collective-permute-start(f32[5,8,2048]{2,1,0:T(8,128)S(1)} %get-tuple-element.181), channel_id=1, source_target_pairs={{0,2},{1,3},{2,0},{3,1},{4,6},{5,7},{6,4},{7,5},{8,10},{9,11},{10,... | collective-permute-start | bytes 983048 | tf_op jit(solution)/shard_map/ppermute | solution.py:478
  4.9 29.2 %collective-permute-start.2 = (f32[5,8,2048]{2,1,0:T(8,128)S(1)}, f32[5,8,2048]{2,1,0:T(8,128)S(1)}, u32[]{:S(2)}, u32[]{:S(2)}) collective-permute-start(f32[5,8,2048]{2,1,0:T(8,128)S(1)} %get-tuple-element.179), channel_id=1, source_target_pairs={{0,3},{1,0},{2,1},{3,2},{4,7},{5,4},{6,5},{7,6},{8,11},{9,8},{10,9... | collective-permute-start | bytes 983048 | tf_op jit(solution)/shard_map/ppermute | solution.py:478
  34.1 0.9 copy-start.6
  34.1 1.0 copy-start.9
  34.1 1.0 copy-start.11
  34.2 1.1 copy-start.12
  34.2 1.1 copy-start.13
  35.3 0.7 collective-permute-start.3
  36.1 2.1 %collective-permute-start.4 = (f32[3,8,2048]{2,1,0:T(8,128)S(1)}, f32[3,8,2048]{2,1,0:T(8,128)S(1)}, u32[]{:S(2)}, u32[]{:S(2)}) collective-permute-start(f32[3,8,2048]{2,1,0:T(8,128)S(1)} %get-tuple-element.174), channel_id=1, source_target_pairs={{0,1},{1,2},{2,3},{3,0},{16,17},{17,18},{18,19},{19,16}} | collective-permute-start | bytes 589832 | tf_op jit(solution)/shard_map/ppermute | solution.py:504
  36.8 1.4 %collective-permute-start.5 = (f32[3,8,2048]{2,1,0:T(8,128)S(1)}, f32[3,8,2048]{2,1,0:T(8,128)S(1)}, u32[]{:S(2)}, u32[]{:S(2)}) collective-permute-start(f32[3,8,2048]{2,1,0:T(8,128)S(1)} %get-tuple-element.172), channel_id=1, source_target_pairs={{0,2},{1,3},{2,0},{3,1},{16,18},{17,19},{18,16},{19,17}} | collective-permute-start | bytes 589832 | tf_op jit(solution)/shard_map/ppermute | solution.py:504
  37.4 0.7 collective-permute-start.6
  38.2 4.6 %copy-start.7 = (bf16[256,256]{1,0:T(8,128)(2,1)S(1)}, bf16[256,256]{1,0:T(8,128)(2,1)}, u32[]{:S(2)}) copy-start(bf16[256,256]{1,0:T(8,128)(2,1)} %constant.145.clone) | copy-start | bytes 393220
  38.2 0.8 collective-permute-start.7
  39.1 2.7 %collective-permute-start.10 = (f32[3,8,2048]{2,1,0:T(8,128)S(1)}, f32[3,8,2048]{2,1,0:T(8,128)S(1)}, u32[]{:S(2)}, u32[]{:S(2)}) collective-permute-start(f32[3,8,2048]{2,1,0:T(8,128)S(1)} %get-tuple-element.170), channel_id=1, source_target_pairs={{4,7},{5,4},{6,5},{7,6},{20,23},{21,20},{22,21},{23,22}} | collective-permute-start | bytes 589832 | tf_op jit(solution)/shard_map/ppermute | solution.py:504
  39.8 2.0 %collective-permute-start.8 = (f32[3,8,2048]{2,1,0:T(8,128)S(1)}, f32[3,8,2048]{2,1,0:T(8,128)S(1)}, u32[]{:S(2)}, u32[]{:S(2)}) collective-permute-start(f32[3,8,2048]{2,1,0:T(8,128)S(1)} %get-tuple-element.169), channel_id=1, source_target_pairs={{4,5},{5,6},{6,7},{7,4},{20,21},{21,22},{22,23},{23,20}} | collective-permute-start | bytes 589832 | tf_op jit(solution)/shard_map/ppermute | solution.py:504
  40.5 1.4 %collective-permute-start.9 = (f32[3,8,2048]{2,1,0:T(8,128)S(1)}, f32[3,8,2048]{2,1,0:T(8,128)}, u32[]{:S(2)}, u32[]{:S(2)}) collective-permute-start(f32[3,8,2048]{2,1,0:T(8,128)S(1)} %get-tuple-element.171), channel_id=1, source_target_pairs={{4,6},{5,7},{6,4},{7,5},{20,22},{21,23},{22,20},{23,21}} | collective-permute-start | bytes 589832 | tf_op jit(solution)/shard_map/ppermute | solution.py:504
  42.9 41.4 %copy-start.8 = (bf16[256,256]{1,0:T(8,128)(2,1)S(1)}, bf16[256,256]{1,0:T(8,128)(2,1)}, u32[]{:S(2)}) copy-start(bf16[256,256]{1,0:T(8,128)(2,1)} %constant.145.clone) | copy-start | bytes 393220
  42.9 41.4 %copy-start.10 = (bf16[256,256]{1,0:T(8,128)(2,1)S(1)}, bf16[256,256]{1,0:T(8,128)(2,1)}, u32[]{:S(2)}) copy-start(bf16[256,256]{1,0:T(8,128)(2,1)} %constant.146.clone) | copy-start | bytes 393220
  42.9 39.2 %collective-permute-start.11 = (f32[2,32,2048]{2,1,0:T(8,128)S(1)}, f32[2,32,2048]{2,1,0:T(8,128)S(1)}, u32[]{:S(2)}, u32[]{:S(2)}) collective-permute-start(f32[2,32,2048]{2,1,0:T(8,128)S(1)} %get-tuple-element.156), channel_id=1, source_target_pairs={{8,12},{9,13},{10,14},{11,15},{24,28},{25,29},{26,30},{27,31}} | collective-permute-start | bytes 1572872 | tf_op jit(solution)/shard_map/ppermute | solution.py:499
  82.1 0.8 copy-start
  82.1 2.1 %collective-permute-start.12 = (f32[3,8,2048]{2,1,0:T(8,128)S(1)}, f32[3,8,2048]{2,1,0:T(8,128)S(1)}, u32[]{:S(2)}, u32[]{:S(2)}) collective-permute-start(f32[3,8,2048]{2,1,0:T(8,128)S(1)} %get-tuple-element.166), channel_id=1, source_target_pairs={{8,9},{9,10},{10,11},{11,8},{24,25},{25,26},{26,27},{27,24}} | collective-permute-start | bytes 589832 | tf_op jit(solution)/shard_map/ppermute | solution.py:504
  82.9 1.4 %collective-permute-start.13 = (f32[3,8,2048]{2,1,0:T(8,128)S(1)}, f32[3,8,2048]{2,1,0:T(8,128)S(1)}, u32[]{:S(2)}, u32[]{:S(2)}) collective-permute-start(f32[3,8,2048]{2,1,0:T(8,128)S(1)} %get-tuple-element.168), channel_id=1, source_target_pairs={{8,10},{9,11},{10,8},{11,9},{24,26},{25,27},{26,24},{27,25}} | collective-permute-start | bytes 589832 | tf_op jit(solution)/shard_map/ppermute | solution.py:504
  83.5 0.7 collective-permute-start.14
  93.1 8.6 %collective-permute-start.15 = (f32[3,8,2048]{2,1,0:T(8,128)S(1)}, f32[3,8,2048]{2,1,0:T(8,128)S(1)}, u32[]{:S(2)}, u32[]{:S(2)}) collective-permute-start(f32[3,8,2048]{2,1,0:T(8,128)S(1)} %get-tuple-element.163), channel_id=1, source_target_pairs={{12,13},{13,14},{14,15},{15,12},{28,29},{29,30},{30,31},{31,28}} | collective-permute-start | bytes 589832 | tf_op jit(solution)/shard_map/ppermute | solution.py:504
  95.0 10.1 %collective-permute-start.16 = (f32[3,8,2048]{2,1,0:T(8,128)S(1)}, f32[3,8,2048]{2,1,0:T(8,128)S(1)}, u32[]{:S(2)}, u32[]{:S(2)}) collective-permute-start(f32[3,8,2048]{2,1,0:T(8,128)S(1)} %get-tuple-element.165), channel_id=1, source_target_pairs={{12,14},{13,15},{14,12},{15,13},{28,30},{29,31},{30,28},{31,29}} | collective-permute-start | bytes 589832 | tf_op jit(solution)/shard_map/ppermute | solution.py:504
  98.3 8.3 %collective-permute-start.17 = (f32[3,8,2048]{2,1,0:T(8,128)S(1)}, f32[3,8,2048]{2,1,0:T(8,128)S(1)}, u32[]{:S(2)}, u32[]{:S(2)}) collective-permute-start(f32[3,8,2048]{2,1,0:T(8,128)S(1)} %get-tuple-element.164), channel_id=1, source_target_pairs={{12,15},{13,12},{14,13},{15,14},{28,31},{29,28},{30,29},{31,30}} | collective-permute-start | bytes 589832 | tf_op jit(solution)/shard_map/ppermute | solution.py:504

commit v5 on v2

--- a/solution.py
+++ b/solution.py
@@ -452,6 +452,22 @@
     return full
 
 
+def gather_strips(piece_of, local, depths, strip_no, strip_count, rows_here):
+    rows = rows_here * strip_count
+    shape = (local.shape[0], rows, local.shape[2])
+    full = lax.dynamic_update_slice(
+        jnp.zeros(shape, jnp.float32), local, (0, strip_no * rows_here, 0)
+    )
+    for shift in range(1, strip_count):
+        target = (strip_no + shift) % strip_count
+        got = lax.ppermute(
+            piece_of(target), ("depth", "strip"), strip_pairs(depths, strip_count, shift)
+        )
+        source = (strip_no - shift) % strip_count
+        full = lax.dynamic_update_slice(full, got, (0, source * rows_here, 0))
+    return full
+
+
 def shards(surface, omegas, region_speed, fd_coeff, region_index, ref_region):
     if not fast_fits(surface, region_index, region_speed):
         return shards_general(surface, omegas, region_speed, fd_coeff, region_index, ref_region)
@@ -462,35 +478,66 @@
     segment_count = lax.axis_size("depth")
     strip_no = lax.axis_index("strip")
     strip_count = lax.axis_size("strip")
-    rows = rows_here * strip_count
     consts = fast_constants(line_len)
-    outgoing = jnp.concatenate(
-        [
-            jnp.broadcast_to(region_index.astype(jnp.float32)[None], (strip_count,) + region_index.shape),
-            jnp.transpose(surface, (1, 0, 2, 3)),
-        ],
-        axis=1,
-    )
-    incoming = lax.all_to_all(outgoing, "strip", 0, 0, tiled=True)
-    regions = jnp.transpose(incoming[:, :steps], (1, 0, 2, 3)).reshape(steps, rows, line_len)
-    regions = regions.astype(jnp.int32)
-    wave = jnp.transpose(incoming[:, steps:], (1, 0, 2, 3)).reshape(2, rows, line_len)
+    region_f = region_index.astype(jnp.float32)
+    early = [d for d in range(segment_count) if d != 1]
+
+    def with_surface(target):
+        return jnp.concatenate(
+            [region_f, lax.dynamic_index_in_dim(surface, target, 1, keepdims=False)], axis=0
+        )
+
+    gathered = gather_strips(
+        with_surface, with_surface(strip_no), early, strip_no, strip_count, rows_here
+    )
+    regions_a = gathered[:steps].astype(jnp.int32)
+    wave = gathered[steps:]
     omega = lax.dynamic_index_in_dim(omegas, strip_no, 0, keepdims=False)
     table, mult = section_tables(omega, region_speed, fd_coeff, ref_region, jnp.asarray(consts[3]))
     image = jnp.zeros((strip_count, steps, rows_here, line_len), jnp.float32)
-
-    def live(wave, image):
-        return run_section(wave, regions, table, mult, consts, strip_count)
+    regions_b = regions_a
+    if segment_count > 1:
+        token = lax.ppermute(gathered[0, 0:8, 0:LANE], "depth", [(0, 1)])
+
+    def sweep(regions):
+        def live(wave, image):
+            return run_section(wave, regions, table, mult, consts, strip_count)
+
+        return live
 
     def idle(wave, image):
         return (wave, image)
 
+    def freq_sum(image, depths):
+        parts = []
+        for shift in range(1, strip_count):
+            target = (strip_no + shift) % strip_count
+            piece = lax.dynamic_index_in_dim(image, target, 0, keepdims=False)
+            parts.append(
+                lax.ppermute(piece, ("depth", "strip"), strip_pairs(depths, strip_count, shift))
+            )
+        return parts
+
+    arrived = []
     for tick_no in range(segment_count):
-        wave, image = lax.cond(segment_no == tick_no, live, idle, wave, image)
+        regions = regions_b if tick_no == 1 else regions_a
+        wave, image = lax.cond(segment_no == tick_no, sweep(regions), idle, wave, image)
         if tick_no + 1 < segment_count:
-            wave = from_behind(wave, "depth", 1)
-    parts = lax.all_to_all(image, "strip", 0, 0, tiled=True)
-    return jnp.sum(parts, axis=0)
+            wave = lax.ppermute(wave, "depth", [(tick_no, tick_no + 1)])
+        if tick_no == 0 and segment_count > 1:
+            held, token, _ = lax.optimization_barrier((region_f, token, image))
+            held = held + 0.0 * token[0, 0]
+            regions_b = gather_strips(
+                lambda target: held, held, [1], strip_no, strip_count, rows_here
+            ).astype(jnp.int32)
+        if tick_no == segment_count - 2:
+            wave, image = lax.optimization_barrier((wave, image))
+            arrived += freq_sum(image, range(segment_count - 1))
+    arrived += freq_sum(image, [segment_count - 1])
+    total = lax.dynamic_index_in_dim(image, strip_no, 0, keepdims=False)
+    for piece in arrived:
+        total = total + piece
+    return total
 
 
 def solution(mesh):

time: 113 us -> 101 us (0.89)
  blocking collectives: 23.9 us -> 0 us
  starting transfers between devices: 8.75 us -> 27.3 us
  waiting for transfers between devices: 63 us -> 53.3 us
  local copies, waits for them, and re-layouts: 2.58 us -> 4.57 us
    all_to_all x1 -> x0, waiting for transfers between devices: 24 us -> none  [shards(): incoming = lax.all_to_all(outgoing, 'strip', 0, 0, tiled=True)]
    all_to_all x1 -> x0, blocking collectives: 23.9 us -> none  [shards(): parts = lax.all_to_all(image, 'strip', 0, 0, tiled=True)]
    ppermute x3 -> x16, starting transfers between devices: 3.85 us -> 27.3 us  [the longest x6 11.5 us: freq_sum(): lax.ppermute(piece, ('depth', 'strip'), strip_pairs(depths, strip_count,...]
    ppermute x3 -> x16, waiting for transfers between devices: 39 us -> 53.3 us  [the longest x3 28.5 us: shards(): wave = lax.ppermute(wave, 'depth', [(tick_no, tick_no + 1)])]
    all_to_all x1 -> x0, starting transfers between devices: 4.9 us -> none  [shards(): incoming = lax.all_to_all(outgoing, 'strip', 0, 0, tiled=True)]
    squeeze x0 -> x4, local copies, waits for them, and re-layouts: none -> 1.23 us  [the longest x1 1.14 us: with_surface(): lax.dynamic_index_in_dim(surface, target, 1, keepdims=False)]
  transfers between devices with their start and end apart: 4 -> 16, of which waited for: 4 -> 6; matrix products, arithmetic and copies ran while one was open for 3% -> 6% of each run, Pallas kernels for 0% -> 0%
where the time goes in v5:
time: 101 us; the launch traced here: 100 us
  waiting for transfers between devices  53.3 us (53%)
  starting transfers between devices  27.3 us (27%)
  Pallas kernels  8.47 us (8%)
  other arithmetic  5.21 us (5%)
  local copies, waits for them, and re-layouts  4.57 us (5%)
  between operations  1.23 us (1%)
    ppermute x3, waiting for transfers between devices, shards(): wave = lax.ppermute(wave, 'depth', [(tick_no, tick_no + 1)])  28.5 us
    ppermute x6, waiting for transfers between devices, gather_strips(): lax.ppermute(piece_of(target), ('depth', 'strip'), strip_pairs(depths, st...  19.1 us
    ppermute x6, starting transfers between devices, freq_sum(): lax.ppermute(piece, ('depth', 'strip'), strip_pairs(depths, strip_count,...  11.5 us
    ppermute x6, starting transfers between devices, gather_strips(): lax.ppermute(piece_of(target), ('depth', 'strip'), strip_pairs(depths, st...  11.5 us
    pallas_call x1, Pallas kernels, run_section(): pl.pallas_call(lambda *refs: section_kernel(*refs, table_len=table_len),...  8.47 us
    ppermute x6, waiting for transfers between devices, freq_sum(): lax.ppermute(piece, ('depth', 'strip'), strip_pairs(depths, strip_count,...  5.67 us
    ppermute x3, starting transfers between devices, shards(): wave = lax.ppermute(wave, 'depth', [(tick_no, tick_no + 1)])  3.44 us
  transfers between devices with their start and end apart: 16, of which 6 were waited for; matrix products, arithmetic and copies ran while one was open for 6% of the time, Pallas kernels for 0%

profile of v5, /device:TPU:11, one launch (start us, length us, event | category | flops | bytes accessed | tf_op | source)
XLA Modules:
  0.0 100.1 jit_solution(7405786587942437838)
XLA Ops:
  0.0 0.9 convert_element_type.25
  1.0 1.1 %dynamic-slice_bitcast_fusion.6 = (f32[2,8,2048]{2,1,0:T(8,128)S(1)}, f32[2,8,2048]{2,1,0:T(8,128)S(1)}, f32[2,8,2048]{2,1,0:T(8,128)S(1)}, f32[2,8,2048]{2,1,0:T(8,128)S(1)}) fusion(f32[2,4,8,2048]{3,2,1,0:T(8,128)} %param.20, s32[]{:T(128)S(6)} %select_n.98, s32[]{:T(128)S(6)} %select_n.90, s32[]{:T(128)S(6)} %select_n.87, s32[]{:T(128)S(6)} %select_n.94), kind=kLoop, calls=%fused_computation.19 | loop fusion | bytes 1048592 | tf_op jit(solution)/shard_map/jit(dynamic_index_in_dim)/squeeze | solution.py:487
  2.4 3.2 %collective-permute-start = (f32[5,8,2048]{2,1,0:T(8,128)S(1)}, f32[5,8,2048]{2,1,0:T(8,128)}, u32[]{:S(2)}, u32[]{:S(2)}) collective-permute-start(f32[5,8,2048]{2,1,0:T(8,128)S(1)} %get-tuple-element.160), channel_id=1, source_target_pairs={{0,1},{1,2},{2,3},{3,0},{8,9},{9,10},{10,11},{11,8},{12,13},{13,14... | collective-permute-start | bytes 983048 | tf_op jit(solution)/shard_map/ppermute | solution.py:463
  5.6 2.9 %collective-permute-start.1 = (f32[5,8,2048]{2,1,0:T(8,128)S(1)}, f32[5,8,2048]{2,1,0:T(8,128)S(1)}, u32[]{:S(2)}, u32[]{:S(2)}) collective-permute-start(f32[5,8,2048]{2,1,0:T(8,128)S(1)} %get-tuple-element.161), channel_id=1, source_target_pairs={{0,2},{1,3},{2,0},{3,1},{8,10},{9,11},{10,8},{11,9},{12,14},{13,15... | collective-permute-start | bytes 983048 | tf_op jit(solution)/shard_map/ppermute | solution.py:463
  8.6 3.4 %collective-permute-start.2 = (f32[5,8,2048]{2,1,0:T(8,128)S(1)}, f32[5,8,2048]{2,1,0:T(8,128)S(1)}, u32[]{:S(2)}, u32[]{:S(2)}) collective-permute-start(f32[5,8,2048]{2,1,0:T(8,128)S(1)} %get-tuple-element.159), channel_id=1, source_target_pairs={{0,3},{1,0},{2,1},{3,2},{8,11},{9,8},{10,9},{11,10},{12,15},{13,12... | collective-permute-start | bytes 983048 | tf_op jit(solution)/shard_map/ppermute | solution.py:463
  12.7 0.6 gather_fusion
  13.3 0.8 fusion.16
  14.1 0.7 multiply_multiply_fusion
  14.7 0.7 broadcast_divide_fusion
  15.7 1.0 %constant_dynamic-update-slice_fusion.6 = f32[5,32,2048]{2,1,0:T(8,128)S(1)} fusion(f32[5,32,2048]{2,1,0:T(8,128)S(1)} %get-tuple-element.162, f32[5,8,2048]{2,1,0:T(8,128)} %collective-permute-done, s32[]{:T(128)S(6)} %select_n.92), kind=kLoop, calls=%fused_computation.43 | loop fusion | bytes 655364 | tf_op jit(solution)/shard_map/dynamic_update_slice | solution.py:467
  16.7 16.3 %collective-permute-done.1 = f32[5,8,2048]{2,1,0:T(8,128)S(1)} collective-permute-done((f32[5,8,2048]{2,1,0:T(8,128)S(1)}, f32[5,8,2048]{2,1,0:T(8,128)S(1)}, u32[]{:S(2)}, u32[]{:S(2)}) %collective-permute-start.1) | collective-permute-done | bytes 327712 | tf_op jit(solution)/shard_map/ppermute | solution.py:463
  33.1 2.8 %collective-permute-done.2 = f32[5,8,2048]{2,1,0:T(8,128)S(1)} collective-permute-done((f32[5,8,2048]{2,1,0:T(8,128)S(1)}, f32[5,8,2048]{2,1,0:T(8,128)S(1)}, u32[]{:S(2)}, u32[]{:S(2)}) %collective-permute-start.2) | collective-permute-done | bytes 327712 | tf_op jit(solution)/shard_map/ppermute | solution.py:463
  36.0 0.8 collective-permute-start.4
  38.3 0.7 collective-permute-start.5
  39.0 1.5 %collective-permute-start.3 = (f32[2,32,2048]{2,1,0:T(8,128)S(1)}, f32[2,32,2048]{2,1,0:T(8,128)}, u32[]{:S(2)}, u32[]{:S(2)}) collective-permute-start(f32[2,32,2048]{2,1,0:T(8,128)S(1)} %get-tuple-element.137), channel_id=1, source_target_pairs={{0,4},{1,5},{2,6},{3,7},{16,20},{17,21},{18,22},{19,23}} | collective-permute-start | bytes 1572872 | tf_op jit(solution)/shard_map/ppermute | solution.py:526
  40.5 0.7 collective-permute-start.6
  41.1 0.7 collective-permute-start.7
  42.0 1.0 convert_element_type.27
  42.9 0.7 collective-permute-start.8
  43.7 1.3 %collective-permute-start.9 = (f32[2,32,2048]{2,1,0:T(8,128)S(1)}, f32[2,32,2048]{2,1,0:T(8,128)S(1)}, u32[]{:S(2)}, u32[]{:S(2)}) collective-permute-start(f32[2,32,2048]{2,1,0:T(8,128)S(1)} %get-tuple-element.143), channel_id=1, source_target_pairs={{8,12},{9,13},{10,14},{11,15},{24,28},{25,29},{26,30},{27,31}} | collective-permute-start | bytes 1572872 | tf_op jit(solution)/shard_map/ppermute | solution.py:526
  45.0 28.5 %collective-permute-done.9 = f32[2,32,2048]{2,1,0:T(8,128)S(1)} collective-permute-done((f32[2,32,2048]{2,1,0:T(8,128)S(1)}, f32[2,32,2048]{2,1,0:T(8,128)S(1)}, u32[]{:S(2)}, u32[]{:S(2)}) %collective-permute-start.9) | collective-permute-done | bytes 524320 | tf_op jit(solution)/shard_map/ppermute | solution.py:526
  73.5 8.5 %conditional.7 = (f32[4,3,8,2048]{3,2,1,0:T(8,128)S(1)}) conditional(s32[]{:T(128)} %convert_element_type.21, f32[4,3,8,2048]{3,2,1,0:T(8,128)S(1)} %get-tuple-element.145, (f32[72]{0:T(128)S(1)}, f32[2,32,2048]{2,1,0:T(8,128)S(1)}, s32[3,32,2048]{2,1,0:T(8,128)S(1)}, f32[3,2,16,128]{3,2,1,0:T(8,128)S(1)}, f32[2,16,128]{2,1,0:T(8,128)S(1)}, ...), branch_computations={%region_6.7_spmd, %region_7.8_spmd} | conditional | flops 1286602752 | bytes 4718600 | solution.py:524
  73.5 8.5 %branch_1_fun.7 = (f32[2,32,2048]{2,1,0:T(8,128)}, f32[4,3,8,2048]{3,2,1,0:T(8,128)S(1)}) custom-call(f32[72]{0:T(128)S(1)} %get-tuple-element.117.refs_0_, f32[2,32,2048]{2,1,0:T(8,128)S(1)} %get-tuple-element.118.refs_1_, s32[3,32,2048]{2,1,0:T(8,128)S(1)} %get-tuple-element.119.refs_2_, f32[3,2,16,128]{3,2,1,0:T(8,128)S(1)} %get-tuple-element.120.refs_3_, ...), custom_call_target="tpu_custom_call" | custom-call | flops 1286602752 | bytes 4718592 | tf_op jit(solution)/shard_map/cond/branch_1_fun/pallas_call | solution.py:376
  82.0 1.9 %collective-permute-start.13 = (f32[3,8,2048]{2,1,0:T(8,128)S(1)}, f32[3,8,2048]{2,1,0:T(8,128)S(1)}, u32[]{:S(2)}, u32[]{:S(2)}) collective-permute-start(f32[3,8,2048]{2,1,0:T(8,128)S(1)} %get-tuple-element.152), channel_id=1, source_target_pairs={{12,13},{13,14},{14,15},{15,12},{28,29},{29,30},{30,31},{31,28}} | collective-permute-start | bytes 589832 | tf_op jit(solution)/shard_map/ppermute | solution.py:517
  83.9 5.2 %collective-permute-start.14 = (f32[3,8,2048]{2,1,0:T(8,128)S(1)}, f32[3,8,2048]{2,1,0:T(8,128)S(1)}, u32[]{:S(2)}, u32[]{:S(2)}) collective-permute-start(f32[3,8,2048]{2,1,0:T(8,128)S(1)} %get-tuple-element.154), channel_id=1, source_target_pairs={{12,14},{13,15},{14,12},{15,13},{28,30},{29,31},{30,28},{31,29}} | collective-permute-start | bytes 589832 | tf_op jit(solution)/shard_map/ppermute | solution.py:517
  89.1 2.4 %collective-permute-start.15 = (f32[3,8,2048]{2,1,0:T(8,128)S(1)}, f32[3,8,2048]{2,1,0:T(8,128)S(1)}, u32[]{:S(2)}, u32[]{:S(2)}) collective-permute-start(f32[3,8,2048]{2,1,0:T(8,128)S(1)} %get-tuple-element.153), channel_id=1, source_target_pairs={{12,15},{13,12},{14,13},{15,14},{28,31},{29,28},{30,29},{31,30}} | collective-permute-start | bytes 589832 | tf_op jit(solution)/shard_map/ppermute | solution.py:517
  91.6 0.7 collective-permute-start.10
  92.3 0.7 collective-permute-start.11
  92.9 3.8 %collective-permute-done.13 = f32[3,8,2048]{2,1,0:T(8,128)S(1)} collective-permute-done((f32[3,8,2048]{2,1,0:T(8,128)S(1)}, f32[3,8,2048]{2,1,0:T(8,128)S(1)}, u32[]{:S(2)}, u32[]{:S(2)}) %collective-permute-start.13) | collective-permute-done | bytes 196640 | tf_op jit(solution)/shard_map/ppermute | solution.py:517
  96.8 0.7 collective-permute-start.12
  97.5 1.4 %collective-permute-done.14 = f32[3,8,2048]{2,1,0:T(8,128)S(1)} collective-permute-done((f32[3,8,2048]{2,1,0:T(8,128)S(1)}, f32[3,8,2048]{2,1,0:T(8,128)S(1)}, u32[]{:S(2)}, u32[]{:S(2)}) %collective-permute-start.14) | collective-permute-done | bytes 196640 | tf_op jit(solution)/shard_map/ppermute | solution.py:517
  99.3 0.8 fusion.5
  (59 shorter events, 2.7 us)
Async XLA Ops:
  2.2 9.8 %copy-start = (f32[4]{0:T(128)S(1)}, f32[4]{0:T(128)}, u32[]{:S(2)}) copy-start(f32[4]{0:T(128)} %param.21) | copy-start | bytes 52
  2.3 10.4 %copy-start.1 = (f32[8]{0:T(128)S(1)}, f32[8]{0:T(128)}, u32[]{:S(2)}) copy-start(f32[8]{0:T(128)} %param.22) | copy-start | bytes 100
  2.3 10.4 %copy-start.2 = (s32[3]{0:T(128)S(1)}, s32[3]{0:T(128)}, u32[]{:S(2)}) copy-start(s32[3]{0:T(128)} %param.25) | copy-start | bytes 40
  2.3 12.5 %copy-start.3 = (f32[8]{0:T(128)S(1)}, f32[8]{0:T(128)}, u32[]{:S(2)}) copy-start(f32[8]{0:T(128)} %param.23) | copy-start | bytes 100
  2.3 13.2 %copy-start.4 = (f32[16,128]{1,0:T(8,128)S(1)}, f32[16,128]{1,0:T(8,128)}, u32[]{:S(2)}) copy-start(f32[16,128]{1,0:T(8,128)} %constant.138) | copy-start | bytes 24580
  2.4 13.3 %collective-permute-start = (f32[5,8,2048]{2,1,0:T(8,128)S(1)}, f32[5,8,2048]{2,1,0:T(8,128)}, u32[]{:S(2)}, u32[]{:S(2)}) collective-permute-start(f32[5,8,2048]{2,1,0:T(8,128)S(1)} %get-tuple-element.160), channel_id=1, source_target_pairs={{0,1},{1,2},{2,3},{3,0},{8,9},{9,10},{10,11},{11,8},{12,13},{13,14... | collective-permute-start | bytes 983048 | tf_op jit(solution)/shard_map/ppermute | solution.py:463
  5.6 27.4 %collective-permute-start.1 = (f32[5,8,2048]{2,1,0:T(8,128)S(1)}, f32[5,8,2048]{2,1,0:T(8,128)S(1)}, u32[]{:S(2)}, u32[]{:S(2)}) collective-permute-start(f32[5,8,2048]{2,1,0:T(8,128)S(1)} %get-tuple-element.161), channel_id=1, source_target_pairs={{0,2},{1,3},{2,0},{3,1},{8,10},{9,11},{10,8},{11,9},{12,14},{13,15... | collective-permute-start | bytes 983048 | tf_op jit(solution)/shard_map/ppermute | solution.py:463
  8.6 27.3 %collective-permute-start.2 = (f32[5,8,2048]{2,1,0:T(8,128)S(1)}, f32[5,8,2048]{2,1,0:T(8,128)S(1)}, u32[]{:S(2)}, u32[]{:S(2)}) collective-permute-start(f32[5,8,2048]{2,1,0:T(8,128)S(1)} %get-tuple-element.159), channel_id=1, source_target_pairs={{0,3},{1,0},{2,1},{3,2},{8,11},{9,8},{10,9},{11,10},{12,15},{13,12... | collective-permute-start | bytes 983048 | tf_op jit(solution)/shard_map/ppermute | solution.py:463
  35.9 1.0 copy-start.5
  35.9 1.0 copy-start.6
  35.9 1.0 %copy-start.8 = (bf16[256,256]{1,0:T(8,128)(2,1)S(1)}, bf16[256,256]{1,0:T(8,128)(2,1)}, u32[]{:S(2)}) copy-start(bf16[256,256]{1,0:T(8,128)(2,1)} %constant.133.clone) | copy-start | bytes 393220
  36.0 1.0 %copy-start.9 = (f32[2,16,128]{2,1,0:T(8,128)S(1)}, f32[2,16,128]{2,1,0:T(8,128)}, u32[]{:S(2)}) copy-start(f32[2,16,128]{2,1,0:T(8,128)} %constant.130.clone) | copy-start | bytes 49156
  36.0 1.1 %collective-permute-start.4 = (f32[8,128]{1,0:T(8,128)S(1)}, f32[8,128]{1,0:T(8,128)S(1)}, u32[]{:S(2)}, u32[]{:S(2)}) collective-permute-start(f32[8,128]{1,0:T(8,128)S(1)} %slice_bitcast_fusion), channel_id=1, source_target_pairs={{0,4},{1,5},{2,6},{3,7},{16,20},{17,21},{18,22},{19,23}} | collective-permute-start | bytes 12296 | tf_op jit(solution)/shard_map/ppermute | solution.py:500
  38.3 3.5 %collective-permute-start.5 = (f32[3,8,2048]{2,1,0:T(8,128)S(1)}, f32[3,8,2048]{2,1,0:T(8,128)S(1)}, u32[]{:S(2)}, u32[]{:S(2)}) collective-permute-start(f32[3,8,2048]{2,1,0:T(8,128)S(1)} %get-tuple-element.148), channel_id=1, source_target_pairs={{4,5},{5,6},{6,7},{7,4},{20,21},{21,22},{22,23},{23,20}} | collective-permute-start | bytes 589832 | tf_op jit(solution)/shard_map/ppermute | solution.py:463
  39.0 3.9 %collective-permute-start.3 = (f32[2,32,2048]{2,1,0:T(8,128)S(1)}, f32[2,32,2048]{2,1,0:T(8,128)}, u32[]{:S(2)}, u32[]{:S(2)}) collective-permute-start(f32[2,32,2048]{2,1,0:T(8,128)S(1)} %get-tuple-element.137), channel_id=1, source_target_pairs={{0,4},{1,5},{2,6},{3,7},{16,20},{17,21},{18,22},{19,23}} | collective-permute-start | bytes 1572872 | tf_op jit(solution)/shard_map/ppermute | solution.py:526
  40.5 1.4 %collective-permute-start.6 = (f32[3,8,2048]{2,1,0:T(8,128)S(1)}, f32[3,8,2048]{2,1,0:T(8,128)S(1)}, u32[]{:S(2)}, u32[]{:S(2)}) collective-permute-start(f32[3,8,2048]{2,1,0:T(8,128)S(1)} %get-tuple-element.148), channel_id=1, source_target_pairs={{4,6},{5,7},{6,4},{7,5},{20,22},{21,23},{22,20},{23,21}} | collective-permute-start | bytes 589832 | tf_op jit(solution)/shard_map/ppermute | solution.py:463
  41.1 0.8 collective-permute-start.7
  41.9 1.1 %copy-start.7 = (bf16[256,256]{1,0:T(8,128)(2,1)S(1)}, bf16[256,256]{1,0:T(8,128)(2,1)}, u32[]{:S(2)}) copy-start(bf16[256,256]{1,0:T(8,128)(2,1)} %constant.132.clone) | copy-start | bytes 393220
  42.9 0.7 collective-permute-start.8
  43.7 29.8 %collective-permute-start.9 = (f32[2,32,2048]{2,1,0:T(8,128)S(1)}, f32[2,32,2048]{2,1,0:T(8,128)S(1)}, u32[]{:S(2)}, u32[]{:S(2)}) collective-permute-start(f32[2,32,2048]{2,1,0:T(8,128)S(1)} %get-tuple-element.143), channel_id=1, source_target_pairs={{8,12},{9,13},{10,14},{11,15},{24,28},{25,29},{26,30},{27,31}} | collective-permute-start | bytes 1572872 | tf_op jit(solution)/shard_map/ppermute | solution.py:526
  82.0 14.8 %collective-permute-start.13 = (f32[3,8,2048]{2,1,0:T(8,128)S(1)}, f32[3,8,2048]{2,1,0:T(8,128)S(1)}, u32[]{:S(2)}, u32[]{:S(2)}) collective-permute-start(f32[3,8,2048]{2,1,0:T(8,128)S(1)} %get-tuple-element.152), channel_id=1, source_target_pairs={{12,13},{13,14},{14,15},{15,12},{28,29},{29,30},{30,31},{31,28}} | collective-permute-start | bytes 589832 | tf_op jit(solution)/shard_map/ppermute | solution.py:517
  83.9 15.0 %collective-permute-start.14 = (f32[3,8,2048]{2,1,0:T(8,128)S(1)}, f32[3,8,2048]{2,1,0:T(8,128)S(1)}, u32[]{:S(2)}, u32[]{:S(2)}) collective-permute-start(f32[3,8,2048]{2,1,0:T(8,128)S(1)} %get-tuple-element.154), channel_id=1, source_target_pairs={{12,14},{13,15},{14,12},{15,13},{28,30},{29,31},{30,28},{31,29}} | collective-permute-start | bytes 589832 | tf_op jit(solution)/shard_map/ppermute | solution.py:517
  89.1 10.2 %collective-permute-start.15 = (f32[3,8,2048]{2,1,0:T(8,128)S(1)}, f32[3,8,2048]{2,1,0:T(8,128)S(1)}, u32[]{:S(2)}, u32[]{:S(2)}) collective-permute-start(f32[3,8,2048]{2,1,0:T(8,128)S(1)} %get-tuple-element.153), channel_id=1, source_target_pairs={{12,15},{13,12},{14,13},{15,14},{28,31},{29,28},{30,29},{31,30}} | collective-permute-start | bytes 589832 | tf_op jit(solution)/shard_map/ppermute | solution.py:517
  91.6 7.7 %collective-permute-start.10 = (f32[3,8,2048]{2,1,0:T(8,128)S(1)}, f32[3,8,2048]{2,1,0:T(8,128)S(1)}, u32[]{:S(2)}, u32[]{:S(2)}) collective-permute-start(f32[3,8,2048]{2,1,0:T(8,128)S(1)} %get-tuple-element.149), channel_id=1, source_target_pairs={{0,1},{1,2},{2,3},{3,0},{4,5},{5,6},{6,7},{7,4},{8,9},{9,10},{10,1... | collective-permute-start | bytes 589832 | tf_op jit(solution)/shard_map/ppermute | solution.py:517
  92.3 7.0 %collective-permute-start.11 = (f32[3,8,2048]{2,1,0:T(8,128)S(1)}, f32[3,8,2048]{2,1,0:T(8,128)S(1)}, u32[]{:S(2)}, u32[]{:S(2)}) collective-permute-start(f32[3,8,2048]{2,1,0:T(8,128)S(1)} %get-tuple-element.151), channel_id=1, source_target_pairs={{0,2},{1,3},{2,0},{3,1},{4,6},{5,7},{6,4},{7,5},{8,10},{9,11},{10,... | collective-permute-start | bytes 589832 | tf_op jit(solution)/shard_map/ppermute | solution.py:517
  96.8 2.5 %collective-permute-start.12 = (f32[3,8,2048]{2,1,0:T(8,128)S(1)}, f32[3,8,2048]{2,1,0:T(8,128)S(1)}, u32[]{:S(2)}, u32[]{:S(2)}) collective-permute-start(f32[3,8,2048]{2,1,0:T(8,128)S(1)} %get-tuple-element.150), channel_id=1, source_target_pairs={{0,3},{1,0},{2,1},{3,2},{4,7},{5,4},{6,5},{7,6},{8,11},{9,8},{10,9... | collective-permute-start | bytes 589832 | tf_op jit(solution)/shard_map/ppermute | solution.py:517

commit v6 on v5

--- a/solution.py
+++ b/solution.py
@@ -254,7 +254,7 @@
     strip_count, rows_here = img_ref.shape[0], img_ref.shape[2]
     chunks = rows // ROW_CHUNK
     inv_len = 1.0 / line_len
-    wout_ref[...] = w_ref[...]
+    pltpu.sync_copy(w_ref, wout_ref)
 
     def blk(a):
         return slice(a * LANE, (a + 1) * LANE)
@@ -305,7 +305,7 @@
             for a in range(FFT_BLOCKS):
                 ur = back[a][0] * inv_len
                 ui = back[a][1] * inv_len
-                regions = rid_ref[k, pl.ds(y0, ROW_CHUNK), blk(a)]
+                regions = rid_ref[k, pl.ds(y0, ROW_CHUNK), blk(a)].astype(jnp.int32)
                 cs = pick(regions, cos_t)
                 sn = pick(regions, sin_t)
                 v_ref[0, pl.ds(y0, ROW_CHUNK), blk(a)] = ur * cs - ui * sn
@@ -332,7 +332,7 @@
                 )
                 lap.append(above + below + left + right - 4.0 * v)
                 here.append(v)
-            gain = pick(rid_ref[k, :, blk(a)], gain_t)
+            gain = pick(rid_ref[k, :, blk(a)].astype(jnp.int32), gain_t)
             new_re = here[0] + (lap[0] * DAMPING - lap[1] * gain)
             new_im = here[1] + (lap[0] * gain + lap[1] * DAMPING)
             wout_ref[0, :, blk(a)] = new_re
@@ -379,7 +379,8 @@
             jax.ShapeDtypeStruct(wave.shape, jnp.float32),
             jax.ShapeDtypeStruct((strip_count, steps, rows // strip_count, line_len), jnp.float32),
         ),
-        in_specs=[pl.BlockSpec(memory_space=pltpu.SMEM)] + [vmem] * 8,
+        in_specs=[pl.BlockSpec(memory_space=pltpu.SMEM), pl.BlockSpec(memory_space=pl.ANY)]
+        + [vmem] * 7,
         out_specs=(vmem, vmem),
         scratch_shapes=[
             pltpu.VMEM((FFT_BLOCKS * rows, 2 * LANE), jnp.float32),
@@ -490,7 +491,7 @@
     gathered = gather_strips(
         with_surface, with_surface(strip_no), early, strip_no, strip_count, rows_here
     )
-    regions_a = gathered[:steps].astype(jnp.int32)
+    regions_a = gathered[:steps]
     wave = gathered[steps:]
     omega = lax.dynamic_index_in_dim(omegas, strip_no, 0, keepdims=False)
     table, mult = section_tables(omega, region_speed, fd_coeff, ref_region, jnp.asarray(consts[3]))
@@ -529,7 +530,7 @@
             held = held + 0.0 * token[0, 0]
             regions_b = gather_strips(
                 lambda target: held, held, [1], strip_no, strip_count, rows_here
-            ).astype(jnp.int32)
+            )
         if tick_no == segment_count - 2:
             wave, image = lax.optimization_barrier((wave, image))
             arrived += freq_sum(image, range(segment_count - 1))

time: 101 us -> 102 us (level)
  starting transfers between devices: 27.3 us -> 26.2 us
    ppermute x3, waiting for transfers between devices: 28.5 us -> 30.1 us  [shards(): wave = lax.ppermute(wave, 'depth', [(tick_no, tick_no + 1)])]
    convert_element_type x2 -> x0, other arithmetic: 1.05 us -> none  [the longest x1 0.98 us: shards(): regions_b = gather_strips(lambda target: held, held, [1], strip_no, strip...]
where the time goes in v6:
time: 102 us; the launch traced here: 101 us
  waiting for transfers between devices  54.3 us (53%)
  starting transfers between devices  26.2 us (26%)
  Pallas kernels  8.7 us (9%)
  local copies, waits for them, and re-layouts  5.38 us (5%)
  other arithmetic  4.77 us (5%)
  between operations  1.21 us (1%)
    ppermute x3, waiting for transfers between devices, shards(): wave = lax.ppermute(wave, 'depth', [(tick_no, tick_no + 1)])  30.1 us
    ppermute x6, waiting for transfers between devices, gather_strips(): lax.ppermute(piece_of(target), ('depth', 'strip'), strip_pairs(depths, st...  18.6 us
    ppermute x6, starting transfers between devices, gather_strips(): lax.ppermute(piece_of(target), ('depth', 'strip'), strip_pairs(depths, st...  11.5 us
    ppermute x6, starting transfers between devices, freq_sum(): lax.ppermute(piece, ('depth', 'strip'), strip_pairs(depths, strip_count,...  11.4 us
    pallas_call x1, Pallas kernels, run_section(): pl.pallas_call(lambda *refs: section_kernel(*refs, table_len=table_len),...  8.7 us
    ppermute x6, waiting for transfers between devices, freq_sum(): lax.ppermute(piece, ('depth', 'strip'), strip_pairs(depths, strip_count,...  5.58 us
    ppermute x3, starting transfers between devices, shards(): wave = lax.ppermute(wave, 'depth', [(tick_no, tick_no + 1)])  2.68 us
  transfers between devices with their start and end apart: 16, of which 6 were waited for; matrix products, arithmetic and copies ran while one was open for 6% of the time, Pallas kernels for 0%

profile of v6, /device:TPU:11, one launch (start us, length us, event | category | flops | bytes accessed | tf_op | source)
XLA Modules:
  0.0 100.6 jit_solution(3298801003812951393)
XLA Ops:
  0.0 0.9 convert_element_type.19
  1.0 1.1 %dynamic-slice_bitcast_fusion.6 = (f32[2,8,2048]{2,1,0:T(8,128)S(1)}, f32[2,8,2048]{2,1,0:T(8,128)S(1)}, f32[2,8,2048]{2,1,0:T(8,128)S(1)}, f32[2,8,2048]{2,1,0:T(8,128)S(1)}) fusion(f32[2,4,8,2048]{3,2,1,0:T(8,128)} %param.20, s32[]{:T(128)S(6)} %select_n.98, s32[]{:T(128)S(6)} %select_n.90, s32[]{:T(128)S(6)} %select_n.87, s32[]{:T(128)S(6)} %select_n.94), kind=kLoop, calls=%fused_computation.18 | loop fusion | bytes 1048592 | tf_op jit(solution)/shard_map/jit(dynamic_index_in_dim)/squeeze | solution.py:488
  2.4 3.2 %collective-permute-start = (f32[5,8,2048]{2,1,0:T(8,128)S(1)}, f32[5,8,2048]{2,1,0:T(8,128)}, u32[]{:S(2)}, u32[]{:S(2)}) collective-permute-start(f32[5,8,2048]{2,1,0:T(8,128)S(1)} %get-tuple-element.246), channel_id=1, source_target_pairs={{0,1},{1,2},{2,3},{3,0},{8,9},{9,10},{10,11},{11,8},{12,13},{13,14... | collective-permute-start | bytes 983048 | tf_op jit(solution)/shard_map/ppermute | solution.py:464
  5.7 2.9 %collective-permute-start.1 = (f32[5,8,2048]{2,1,0:T(8,128)S(1)}, f32[5,8,2048]{2,1,0:T(8,128)S(1)}, u32[]{:S(2)}, u32[]{:S(2)}) collective-permute-start(f32[5,8,2048]{2,1,0:T(8,128)S(1)} %get-tuple-element.247), channel_id=1, source_target_pairs={{0,2},{1,3},{2,0},{3,1},{8,10},{9,11},{10,8},{11,9},{12,14},{13,15... | collective-permute-start | bytes 983048 | tf_op jit(solution)/shard_map/ppermute | solution.py:464
  8.6 3.4 %collective-permute-start.2 = (f32[5,8,2048]{2,1,0:T(8,128)S(1)}, f32[5,8,2048]{2,1,0:T(8,128)S(1)}, u32[]{:S(2)}, u32[]{:S(2)}) collective-permute-start(f32[5,8,2048]{2,1,0:T(8,128)S(1)} %get-tuple-element.245), channel_id=1, source_target_pairs={{0,3},{1,0},{2,1},{3,2},{8,11},{9,8},{10,9},{11,10},{12,15},{13,12... | collective-permute-start | bytes 983048 | tf_op jit(solution)/shard_map/ppermute | solution.py:464
  12.7 0.6 gather_fusion
  13.3 0.8 fusion.16
  14.1 0.7 multiply_multiply_fusion
  15.0 0.7 broadcast_divide_fusion
  16.3 1.0 constant_dynamic-update-slice_fusion.2
  17.2 15.8 %collective-permute-done.1 = f32[5,8,2048]{2,1,0:T(8,128)S(1)} collective-permute-done((f32[5,8,2048]{2,1,0:T(8,128)S(1)}, f32[5,8,2048]{2,1,0:T(8,128)S(1)}, u32[]{:S(2)}, u32[]{:S(2)}) %collective-permute-start.1) | collective-permute-done | bytes 327712 | tf_op jit(solution)/shard_map/ppermute | solution.py:464
  33.1 2.8 %collective-permute-done.2 = f32[5,8,2048]{2,1,0:T(8,128)S(1)} collective-permute-done((f32[5,8,2048]{2,1,0:T(8,128)S(1)}, f32[5,8,2048]{2,1,0:T(8,128)S(1)}, u32[]{:S(2)}, u32[]{:S(2)}) %collective-permute-start.2) | collective-permute-done | bytes 327712 | tf_op jit(solution)/shard_map/ppermute | solution.py:464
  35.9 0.7 collective-permute-start.4
  36.9 0.8 copy-done.8
  37.9 0.7 collective-permute-start.3
  39.8 0.7 collective-permute-start.5
  40.5 0.7 collective-permute-start.6
  41.2 0.7 collective-permute-start.7
  41.9 0.7 collective-permute-start.8
  42.6 1.3 %collective-permute-start.9 = (f32[2,32,2048]{2,1,0:T(8,128)S(1)}, f32[2,32,2048]{2,1,0:T(8,128)S(1)}, u32[]{:S(2)}, u32[]{:S(2)}) collective-permute-start(f32[2,32,2048]{2,1,0:T(8,128)S(1)} %get-tuple-element.231), channel_id=1, source_target_pairs={{8,12},{9,13},{10,14},{11,15},{24,28},{25,29},{26,30},{27,31}} | collective-permute-start | bytes 1572872 | tf_op jit(solution)/shard_map/ppermute | solution.py:527
  43.9 30.1 %collective-permute-done.9 = f32[2,32,2048]{2,1,0:T(8,128)S(1)} collective-permute-done((f32[2,32,2048]{2,1,0:T(8,128)S(1)}, f32[2,32,2048]{2,1,0:T(8,128)S(1)}, u32[]{:S(2)}, u32[]{:S(2)}) %collective-permute-start.9) | collective-permute-done | bytes 524320 | tf_op jit(solution)/shard_map/ppermute | solution.py:527
  74.0 8.7 %conditional.7 = (f32[4,3,8,2048]{3,2,1,0:T(8,128)S(1)}) conditional(s32[]{:T(128)} %convert_element_type.15, f32[4,3,8,2048]{3,2,1,0:T(8,128)S(1)} %get-tuple-element.233, (f32[72]{0:T(128)S(1)}, f32[2,32,2048]{2,1,0:T(8,128)S(1)}, f32[3,32,2048]{2,1,0:T(8,128)S(1)}, f32[3,2,16,128]{3,2,1,0:T(8,128)}, f32[2,16,128]{2,1,0:T(8,128)}, ...), branch_computations={%region_6.7_spmd, %region_7.8_spmd} | conditional | flops 1286602752 | bytes 4718600 | solution.py:525
  74.0 8.7 %branch_1_fun.9 = (f32[2,32,2048]{2,1,0:T(8,128)}, f32[4,3,8,2048]{3,2,1,0:T(8,128)S(1)}) custom-call(f32[72]{0:T(128)S(1)} %get-tuple-element.205.refs_0_, f32[2,32,2048]{2,1,0:T(8,128)S(1)} %get-tuple-element.206.refs_1_, f32[3,32,2048]{2,1,0:T(8,128)S(1)} %get-tuple-element.207.refs_2_, f32[3,2,16,128]{3,2,1,0:T(8,128)} %get-tuple-element.208.refs_3_, ...), custom_call_target="tpu_custom_call" | custom-call | flops 1286602752 | bytes 4718592 | tf_op jit(solution)/shard_map/cond/branch_1_fun/pallas_call | solution.py:376
  82.8 1.9 %collective-permute-start.13 = (f32[3,8,2048]{2,1,0:T(8,128)S(1)}, f32[3,8,2048]{2,1,0:T(8,128)S(1)}, u32[]{:S(2)}, u32[]{:S(2)}) collective-permute-start(f32[3,8,2048]{2,1,0:T(8,128)S(1)} %get-tuple-element.238), channel_id=1, source_target_pairs={{12,13},{13,14},{14,15},{15,12},{28,29},{29,30},{30,31},{31,28}} | collective-permute-start | bytes 589832 | tf_op jit(solution)/shard_map/ppermute | solution.py:518
  84.7 5.2 %collective-permute-start.14 = (f32[3,8,2048]{2,1,0:T(8,128)S(1)}, f32[3,8,2048]{2,1,0:T(8,128)S(1)}, u32[]{:S(2)}, u32[]{:S(2)}) collective-permute-start(f32[3,8,2048]{2,1,0:T(8,128)S(1)} %get-tuple-element.240), channel_id=1, source_target_pairs={{12,14},{13,15},{14,12},{15,13},{28,30},{29,31},{30,28},{31,29}} | collective-permute-start | bytes 589832 | tf_op jit(solution)/shard_map/ppermute | solution.py:518
  89.9 2.3 %collective-permute-start.15 = (f32[3,8,2048]{2,1,0:T(8,128)S(1)}, f32[3,8,2048]{2,1,0:T(8,128)S(1)}, u32[]{:S(2)}, u32[]{:S(2)}) collective-permute-start(f32[3,8,2048]{2,1,0:T(8,128)S(1)} %get-tuple-element.239), channel_id=1, source_target_pairs={{12,15},{13,12},{14,13},{15,14},{28,31},{29,28},{30,29},{31,30}} | collective-permute-start | bytes 589832 | tf_op jit(solution)/shard_map/ppermute | solution.py:518
  92.2 0.7 collective-permute-start.10
  92.9 0.7 collective-permute-start.11
  93.6 3.8 %collective-permute-done.13 = f32[3,8,2048]{2,1,0:T(8,128)S(1)} collective-permute-done((f32[3,8,2048]{2,1,0:T(8,128)S(1)}, f32[3,8,2048]{2,1,0:T(8,128)S(1)}, u32[]{:S(2)}, u32[]{:S(2)}) %collective-permute-start.13) | collective-permute-done | bytes 196640 | tf_op jit(solution)/shard_map/ppermute | solution.py:518
  97.4 0.7 collective-permute-start.12
  98.0 1.4 %collective-permute-done.14 = f32[3,8,2048]{2,1,0:T(8,128)S(1)} collective-permute-done((f32[3,8,2048]{2,1,0:T(8,128)S(1)}, f32[3,8,2048]{2,1,0:T(8,128)S(1)}, u32[]{:S(2)}, u32[]{:S(2)}) %collective-permute-start.14) | collective-permute-done | bytes 196640 | tf_op jit(solution)/shard_map/ppermute | solution.py:518
  99.9 0.8 fusion.5
  (54 shorter events, 3.3 us)
Async XLA Ops:
  2.2 9.8 %copy-start.3 = (f32[4]{0:T(128)S(1)}, f32[4]{0:T(128)}, u32[]{:S(2)}) copy-start(f32[4]{0:T(128)} %param.21) | copy-start | bytes 52
  2.3 10.4 %copy-start.4 = (f32[8]{0:T(128)S(1)}, f32[8]{0:T(128)}, u32[]{:S(2)}) copy-start(f32[8]{0:T(128)} %param.22) | copy-start | bytes 100
  2.3 10.4 %copy-start.5 = (s32[3]{0:T(128)S(1)}, s32[3]{0:T(128)}, u32[]{:S(2)}) copy-start(s32[3]{0:T(128)} %param.25) | copy-start | bytes 40
  2.3 12.5 %copy-start.7 = (f32[16,128]{1,0:T(8,128)S(1)}, f32[16,128]{1,0:T(8,128)}, u32[]{:S(2)}) copy-start(f32[16,128]{1,0:T(8,128)} %constant.152) | copy-start | bytes 24580
  2.3 12.7 %copy-start.6 = (f32[8]{0:T(128)S(1)}, f32[8]{0:T(128)}, u32[]{:S(2)}) copy-start(f32[8]{0:T(128)} %param.23) | copy-start | bytes 100
  2.4 13.8 %collective-permute-start = (f32[5,8,2048]{2,1,0:T(8,128)S(1)}, f32[5,8,2048]{2,1,0:T(8,128)}, u32[]{:S(2)}, u32[]{:S(2)}) collective-permute-start(f32[5,8,2048]{2,1,0:T(8,128)S(1)} %get-tuple-element.246), channel_id=1, source_target_pairs={{0,1},{1,2},{2,3},{3,0},{8,9},{9,10},{10,11},{11,8},{12,13},{13,14... | collective-permute-start | bytes 983048 | tf_op jit(solution)/shard_map/ppermute | solution.py:464
  5.7 27.4 %collective-permute-start.1 = (f32[5,8,2048]{2,1,0:T(8,128)S(1)}, f32[5,8,2048]{2,1,0:T(8,128)S(1)}, u32[]{:S(2)}, u32[]{:S(2)}) collective-permute-start(f32[5,8,2048]{2,1,0:T(8,128)S(1)} %get-tuple-element.247), channel_id=1, source_target_pairs={{0,2},{1,3},{2,0},{3,1},{8,10},{9,11},{10,8},{11,9},{12,14},{13,15... | collective-permute-start | bytes 983048 | tf_op jit(solution)/shard_map/ppermute | solution.py:464
  8.6 27.3 %collective-permute-start.2 = (f32[5,8,2048]{2,1,0:T(8,128)S(1)}, f32[5,8,2048]{2,1,0:T(8,128)S(1)}, u32[]{:S(2)}, u32[]{:S(2)}) collective-permute-start(f32[5,8,2048]{2,1,0:T(8,128)S(1)} %get-tuple-element.245), channel_id=1, source_target_pairs={{0,3},{1,0},{2,1},{3,2},{8,11},{9,8},{10,9},{11,10},{12,15},{13,12... | collective-permute-start | bytes 983048 | tf_op jit(solution)/shard_map/ppermute | solution.py:464
  35.9 2.7 %collective-permute-start.4 = (f32[8,128]{1,0:T(8,128)S(1)}, f32[8,128]{1,0:T(8,128)S(1)}, u32[]{:S(2)}, u32[]{:S(2)}) collective-permute-start(f32[8,128]{1,0:T(8,128)S(1)} %slice_bitcast_fusion), channel_id=1, source_target_pairs={{0,4},{1,5},{2,6},{3,7},{16,20},{17,21},{18,22},{19,23}} | collective-permute-start | bytes 12296 | tf_op jit(solution)/shard_map/ppermute | solution.py:501
  36.7 0.9 copy-start.8
  36.7 1.0 copy-start.10
  36.7 1.0 %copy-start.11 = (bf16[256,256]{1,0:T(8,128)(2,1)S(1)}, bf16[256,256]{1,0:T(8,128)(2,1)}, u32[]{:S(2)}) copy-start(bf16[256,256]{1,0:T(8,128)(2,1)} %constant.147.clone) | copy-start | bytes 393220
  36.7 1.1 %copy-start.12 = (bf16[256,256]{1,0:T(8,128)(2,1)S(1)}, bf16[256,256]{1,0:T(8,128)(2,1)}, u32[]{:S(2)}) copy-start(bf16[256,256]{1,0:T(8,128)(2,1)} %constant.148.clone) | copy-start | bytes 393220
  36.8 1.1 %copy-start.13 = (f32[2,16,128]{2,1,0:T(8,128)S(1)}, f32[2,16,128]{2,1,0:T(8,128)}, u32[]{:S(2)}) copy-start(f32[2,16,128]{2,1,0:T(8,128)} %constant.144.clone) | copy-start | bytes 49156
  37.9 4.0 %collective-permute-start.3 = (f32[2,32,2048]{2,1,0:T(8,128)S(1)}, f32[2,32,2048]{2,1,0:T(8,128)S(1)}, u32[]{:S(2)}, u32[]{:S(2)}) collective-permute-start(f32[2,32,2048]{2,1,0:T(8,128)S(1)} %get-tuple-element.225), channel_id=1, source_target_pairs={{0,4},{1,5},{2,6},{3,7},{16,20},{17,21},{18,22},{19,23}} | collective-permute-start | bytes 1572872 | tf_op jit(solution)/shard_map/ppermute | solution.py:527
  39.8 2.1 %collective-permute-start.5 = (f32[3,8,2048]{2,1,0:T(8,128)S(1)}, f32[3,8,2048]{2,1,0:T(8,128)S(1)}, u32[]{:S(2)}, u32[]{:S(2)}) collective-permute-start(f32[3,8,2048]{2,1,0:T(8,128)S(1)} %broadcast_add_fusion), channel_id=1, source_target_pairs={{4,5},{5,6},{6,7},{7,4},{20,21},{21,22},{22,23},{23,20}} | collective-permute-start | bytes 589832 | tf_op jit(solution)/shard_map/ppermute | solution.py:464
  40.5 1.4 %collective-permute-start.6 = (f32[3,8,2048]{2,1,0:T(8,128)S(1)}, f32[3,8,2048]{2,1,0:T(8,128)S(1)}, u32[]{:S(2)}, u32[]{:S(2)}) collective-permute-start(f32[3,8,2048]{2,1,0:T(8,128)S(1)} %broadcast_add_fusion), channel_id=1, source_target_pairs={{4,6},{5,7},{6,4},{7,5},{20,22},{21,23},{22,20},{23,21}} | collective-permute-start | bytes 589832 | tf_op jit(solution)/shard_map/ppermute | solution.py:464
  41.2 0.7 collective-permute-start.7
  41.9 0.7 collective-permute-start.8
  42.6 31.4 %collective-permute-start.9 = (f32[2,32,2048]{2,1,0:T(8,128)S(1)}, f32[2,32,2048]{2,1,0:T(8,128)S(1)}, u32[]{:S(2)}, u32[]{:S(2)}) collective-permute-start(f32[2,32,2048]{2,1,0:T(8,128)S(1)} %get-tuple-element.231), channel_id=1, source_target_pairs={{8,12},{9,13},{10,14},{11,15},{24,28},{25,29},{26,30},{27,31}} | collective-permute-start | bytes 1572872 | tf_op jit(solution)/shard_map/ppermute | solution.py:527
  82.8 14.6 %collective-permute-start.13 = (f32[3,8,2048]{2,1,0:T(8,128)S(1)}, f32[3,8,2048]{2,1,0:T(8,128)S(1)}, u32[]{:S(2)}, u32[]{:S(2)}) collective-permute-start(f32[3,8,2048]{2,1,0:T(8,128)S(1)} %get-tuple-element.238), channel_id=1, source_target_pairs={{12,13},{13,14},{14,15},{15,12},{28,29},{29,30},{30,31},{31,28}} | collective-permute-start | bytes 589832 | tf_op jit(solution)/shard_map/ppermute | solution.py:518
  84.7 14.8 %collective-permute-start.14 = (f32[3,8,2048]{2,1,0:T(8,128)S(1)}, f32[3,8,2048]{2,1,0:T(8,128)S(1)}, u32[]{:S(2)}, u32[]{:S(2)}) collective-permute-start(f32[3,8,2048]{2,1,0:T(8,128)S(1)} %get-tuple-element.240), channel_id=1, source_target_pairs={{12,14},{13,15},{14,12},{15,13},{28,30},{29,31},{30,28},{31,29}} | collective-permute-start | bytes 589832 | tf_op jit(solution)/shard_map/ppermute | solution.py:518
  89.9 10.0 %collective-permute-start.15 = (f32[3,8,2048]{2,1,0:T(8,128)S(1)}, f32[3,8,2048]{2,1,0:T(8,128)S(1)}, u32[]{:S(2)}, u32[]{:S(2)}) collective-permute-start(f32[3,8,2048]{2,1,0:T(8,128)S(1)} %get-tuple-element.239), channel_id=1, source_target_pairs={{12,15},{13,12},{14,13},{15,14},{28,31},{29,28},{30,29},{31,30}} | collective-permute-start | bytes 589832 | tf_op jit(solution)/shard_map/ppermute | solution.py:518
  92.2 7.6 %collective-permute-start.10 = (f32[3,8,2048]{2,1,0:T(8,128)S(1)}, f32[3,8,2048]{2,1,0:T(8,128)S(1)}, u32[]{:S(2)}, u32[]{:S(2)}) collective-permute-start(f32[3,8,2048]{2,1,0:T(8,128)S(1)} %get-tuple-element.235), channel_id=1, source_target_pairs={{0,1},{1,2},{2,3},{3,0},{4,5},{5,6},{6,7},{7,4},{8,9},{9,10},{10,1... | collective-permute-start | bytes 589832 | tf_op jit(solution)/shard_map/ppermute | solution.py:518
  92.9 6.9 %collective-permute-start.11 = (f32[3,8,2048]{2,1,0:T(8,128)S(1)}, f32[3,8,2048]{2,1,0:T(8,128)S(1)}, u32[]{:S(2)}, u32[]{:S(2)}) collective-permute-start(f32[3,8,2048]{2,1,0:T(8,128)S(1)} %get-tuple-element.237), channel_id=1, source_target_pairs={{0,2},{1,3},{2,0},{3,1},{4,6},{5,7},{6,4},{7,5},{8,10},{9,11},{10,... | collective-permute-start | bytes 589832 | tf_op jit(solution)/shard_map/ppermute | solution.py:518
  97.4 2.5 %collective-permute-start.12 = (f32[3,8,2048]{2,1,0:T(8,128)S(1)}, f32[3,8,2048]{2,1,0:T(8,128)S(1)}, u32[]{:S(2)}, u32[]{:S(2)}) collective-permute-start(f32[3,8,2048]{2,1,0:T(8,128)S(1)} %get-tuple-element.236), channel_id=1, source_target_pairs={{0,3},{1,0},{2,1},{3,2},{4,7},{5,4},{6,5},{7,6},{8,11},{9,8},{10,9... | collective-permute-start | bytes 589832 | tf_op jit(solution)/shard_map/ppermute | solution.py:518

commit v7 on v5

--- a/solution.py
+++ b/solution.py
@@ -315,21 +315,26 @@
         lax.fori_loop(0, chunks, inverse_chunk, 0)
         row_id = lax.broadcasted_iota(jnp.int32, (rows, LANE), 0)
         lane_id = lax.broadcasted_iota(jnp.int32, (rows, LANE), 1)
+        cache = {}
+
+        def cell(part, a):
+            key = (part, a % FFT_BLOCKS)
+            if key not in cache:
+                v = v_ref[part, :, blk(a % FFT_BLOCKS)]
+                cache[key] = (v, pltpu.roll(v, 1, 1), pltpu.roll(v, LANE - 1, 1))
+            return cache[key]
+
         for a in range(FFT_BLOCKS):
-            prev_b = blk((a - 1) % FFT_BLOCKS)
-            next_b = blk((a + 1) % FFT_BLOCKS)
             lap = []
             here = []
             for part in range(2):
-                v = v_ref[part, :, blk(a)]
-                vp = v_ref[part, :, prev_b]
-                vn = v_ref[part, :, next_b]
+                v, from_left, from_right = cell(part, a)
+                prev_left = cell(part, a - 1)[1]
+                next_right = cell(part, a + 1)[2]
                 above = jnp.where(row_id == 0, 0.0, pltpu.roll(v, 1, 0))
                 below = jnp.where(row_id == rows - 1, 0.0, pltpu.roll(v, rows - 1, 0))
-                left = jnp.where(lane_id == 0, pltpu.roll(vp, 1, 1), pltpu.roll(v, 1, 1))
-                right = jnp.where(
-                    lane_id == LANE - 1, pltpu.roll(vn, LANE - 1, 1), pltpu.roll(v, LANE - 1, 1)
-                )
+                left = jnp.where(lane_id == 0, prev_left, from_left)
+                right = jnp.where(lane_id == LANE - 1, next_right, from_right)
                 lap.append(above + below + left + right - 4.0 * v)
                 here.append(v)
             gain = pick(rid_ref[k, :, blk(a)], gain_t)

time: 101 us -> 99.8 us (0.988)
    ppermute x3, waiting for transfers between devices: 28.5 us -> 27.4 us  [shards(): wave = lax.ppermute(wave, 'depth', [(tick_no, tick_no + 1)])]
where the time goes in v7:
time: 99.8 us; the launch traced here: 99 us
  waiting for transfers between devices  52.8 us (53%)
  starting transfers between devices  27.3 us (27%)
  Pallas kernels  7.92 us (8%)
  other arithmetic  5.21 us (5%)
  local copies, waits for them, and re-layouts  4.57 us (5%)
  between operations  1.23 us (1%)
    ppermute x3, waiting for transfers between devices, shards(): wave = lax.ppermute(wave, 'depth', [(tick_no, tick_no + 1)])  27.4 us
    ppermute x6, waiting for transfers between devices, gather_strips(): lax.ppermute(piece_of(target), ('depth', 'strip'), strip_pairs(depths, st...  19.1 us
    ppermute x6, starting transfers between devices, freq_sum(): lax.ppermute(piece, ('depth', 'strip'), strip_pairs(depths, strip_count,...  11.5 us
    ppermute x6, starting transfers between devices, gather_strips(): lax.ppermute(piece_of(target), ('depth', 'strip'), strip_pairs(depths, st...  11.5 us
    pallas_call x1, Pallas kernels, run_section(): pl.pallas_call(lambda *refs: section_kernel(*refs, table_len=table_len),...  7.92 us
    ppermute x6, waiting for transfers between devices, freq_sum(): lax.ppermute(piece, ('depth', 'strip'), strip_pairs(depths, strip_count,...  6.23 us
    ppermute x3, starting transfers between devices, shards(): wave = lax.ppermute(wave, 'depth', [(tick_no, tick_no + 1)])  3.44 us
  transfers between devices with their start and end apart: 16, of which 6 were waited for; matrix products, arithmetic and copies ran while one was open for 6% of the time, Pallas kernels for 0%

profile of v7, /device:TPU:11, one launch (start us, length us, event | category | flops | bytes accessed | tf_op | source)
XLA Modules:
  0.0 99.0 jit_solution(9954614993354114380)
XLA Ops:
  0.0 0.9 convert_element_type.25
  1.0 1.1 %dynamic-slice_bitcast_fusion.6 = (f32[2,8,2048]{2,1,0:T(8,128)S(1)}, f32[2,8,2048]{2,1,0:T(8,128)S(1)}, f32[2,8,2048]{2,1,0:T(8,128)S(1)}, f32[2,8,2048]{2,1,0:T(8,128)S(1)}) fusion(f32[2,4,8,2048]{3,2,1,0:T(8,128)} %param.20, s32[]{:T(128)S(6)} %select_n.98, s32[]{:T(128)S(6)} %select_n.90, s32[]{:T(128)S(6)} %select_n.87, s32[]{:T(128)S(6)} %select_n.94), kind=kLoop, calls=%fused_computation.19 | loop fusion | bytes 1048592 | tf_op jit(solution)/shard_map/jit(dynamic_index_in_dim)/squeeze | solution.py:492
  2.4 3.2 %collective-permute-start = (f32[5,8,2048]{2,1,0:T(8,128)S(1)}, f32[5,8,2048]{2,1,0:T(8,128)}, u32[]{:S(2)}, u32[]{:S(2)}) collective-permute-start(f32[5,8,2048]{2,1,0:T(8,128)S(1)} %get-tuple-element.160), channel_id=1, source_target_pairs={{0,1},{1,2},{2,3},{3,0},{8,9},{9,10},{10,11},{11,8},{12,13},{13,14... | collective-permute-start | bytes 983048 | tf_op jit(solution)/shard_map/ppermute | solution.py:468
  5.6 2.9 %collective-permute-start.1 = (f32[5,8,2048]{2,1,0:T(8,128)S(1)}, f32[5,8,2048]{2,1,0:T(8,128)S(1)}, u32[]{:S(2)}, u32[]{:S(2)}) collective-permute-start(f32[5,8,2048]{2,1,0:T(8,128)S(1)} %get-tuple-element.161), channel_id=1, source_target_pairs={{0,2},{1,3},{2,0},{3,1},{8,10},{9,11},{10,8},{11,9},{12,14},{13,15... | collective-permute-start | bytes 983048 | tf_op jit(solution)/shard_map/ppermute | solution.py:468
  8.6 3.4 %collective-permute-start.2 = (f32[5,8,2048]{2,1,0:T(8,128)S(1)}, f32[5,8,2048]{2,1,0:T(8,128)S(1)}, u32[]{:S(2)}, u32[]{:S(2)}) collective-permute-start(f32[5,8,2048]{2,1,0:T(8,128)S(1)} %get-tuple-element.159), channel_id=1, source_target_pairs={{0,3},{1,0},{2,1},{3,2},{8,11},{9,8},{10,9},{11,10},{12,15},{13,12... | collective-permute-start | bytes 983048 | tf_op jit(solution)/shard_map/ppermute | solution.py:468
  13.3 0.8 fusion.16
  14.1 0.7 multiply_multiply_fusion
  14.7 0.7 broadcast_divide_fusion
  15.7 1.0 %constant_dynamic-update-slice_fusion.6 = f32[5,32,2048]{2,1,0:T(8,128)S(1)} fusion(f32[5,32,2048]{2,1,0:T(8,128)S(1)} %get-tuple-element.162, f32[5,8,2048]{2,1,0:T(8,128)} %collective-permute-done, s32[]{:T(128)S(6)} %select_n.92), kind=kLoop, calls=%fused_computation.43 | loop fusion | bytes 655364 | tf_op jit(solution)/shard_map/dynamic_update_slice | solution.py:472
  16.7 16.3 %collective-permute-done.1 = f32[5,8,2048]{2,1,0:T(8,128)S(1)} collective-permute-done((f32[5,8,2048]{2,1,0:T(8,128)S(1)}, f32[5,8,2048]{2,1,0:T(8,128)S(1)}, u32[]{:S(2)}, u32[]{:S(2)}) %collective-permute-start.1) | collective-permute-done | bytes 327712 | tf_op jit(solution)/shard_map/ppermute | solution.py:468
  33.1 2.8 %collective-permute-done.2 = f32[5,8,2048]{2,1,0:T(8,128)S(1)} collective-permute-done((f32[5,8,2048]{2,1,0:T(8,128)S(1)}, f32[5,8,2048]{2,1,0:T(8,128)S(1)}, u32[]{:S(2)}, u32[]{:S(2)}) %collective-permute-start.2) | collective-permute-done | bytes 327712 | tf_op jit(solution)/shard_map/ppermute | solution.py:468
  36.0 0.8 collective-permute-start.4
  38.3 0.7 collective-permute-start.5
  39.0 1.5 %collective-permute-start.3 = (f32[2,32,2048]{2,1,0:T(8,128)S(1)}, f32[2,32,2048]{2,1,0:T(8,128)}, u32[]{:S(2)}, u32[]{:S(2)}) collective-permute-start(f32[2,32,2048]{2,1,0:T(8,128)S(1)} %get-tuple-element.137), channel_id=1, source_target_pairs={{0,4},{1,5},{2,6},{3,7},{16,20},{17,21},{18,22},{19,23}} | collective-permute-start | bytes 1572872 | tf_op jit(solution)/shard_map/ppermute | solution.py:531
  40.5 0.7 collective-permute-start.6
  41.1 0.7 collective-permute-start.7
  42.0 1.0 convert_element_type.27
  42.9 0.7 collective-permute-start.8
  43.7 1.3 %collective-permute-start.9 = (f32[2,32,2048]{2,1,0:T(8,128)S(1)}, f32[2,32,2048]{2,1,0:T(8,128)S(1)}, u32[]{:S(2)}, u32[]{:S(2)}) collective-permute-start(f32[2,32,2048]{2,1,0:T(8,128)S(1)} %get-tuple-element.143), channel_id=1, source_target_pairs={{8,12},{9,13},{10,14},{11,15},{24,28},{25,29},{26,30},{27,31}} | collective-permute-start | bytes 1572872 | tf_op jit(solution)/shard_map/ppermute | solution.py:531
  45.0 27.4 %collective-permute-done.9 = f32[2,32,2048]{2,1,0:T(8,128)S(1)} collective-permute-done((f32[2,32,2048]{2,1,0:T(8,128)S(1)}, f32[2,32,2048]{2,1,0:T(8,128)S(1)}, u32[]{:S(2)}, u32[]{:S(2)}) %collective-permute-start.9) | collective-permute-done | bytes 524320 | tf_op jit(solution)/shard_map/ppermute | solution.py:531
  72.4 7.9 %conditional.7 = (f32[4,3,8,2048]{3,2,1,0:T(8,128)S(1)}) conditional(s32[]{:T(128)} %convert_element_type.21, f32[4,3,8,2048]{3,2,1,0:T(8,128)S(1)} %get-tuple-element.145, (f32[72]{0:T(128)S(1)}, f32[2,32,2048]{2,1,0:T(8,128)S(1)}, s32[3,32,2048]{2,1,0:T(8,128)S(1)}, f32[3,2,16,128]{3,2,1,0:T(8,128)S(1)}, f32[2,16,128]{2,1,0:T(8,128)S(1)}, ...), branch_computations={%region_6.7_spmd, %region_7.8_spmd} | conditional | flops 1286602752 | bytes 4718600 | solution.py:529
  72.4 7.9 %branch_1_fun.7 = (f32[2,32,2048]{2,1,0:T(8,128)}, f32[4,3,8,2048]{3,2,1,0:T(8,128)S(1)}) custom-call(f32[72]{0:T(128)S(1)} %get-tuple-element.117.refs_0_, f32[2,32,2048]{2,1,0:T(8,128)S(1)} %get-tuple-element.118.refs_1_, s32[3,32,2048]{2,1,0:T(8,128)S(1)} %get-tuple-element.119.refs_2_, f32[3,2,16,128]{3,2,1,0:T(8,128)S(1)} %get-tuple-element.120.refs_3_, ...), custom_call_target="tpu_custom_call" | custom-call | flops 1286602752 | bytes 4718592 | tf_op jit(solution)/shard_map/cond/branch_1_fun/pallas_call | solution.py:381
  80.3 1.9 %collective-permute-start.13 = (f32[3,8,2048]{2,1,0:T(8,128)S(1)}, f32[3,8,2048]{2,1,0:T(8,128)S(1)}, u32[]{:S(2)}, u32[]{:S(2)}) collective-permute-start(f32[3,8,2048]{2,1,0:T(8,128)S(1)} %get-tuple-element.152), channel_id=1, source_target_pairs={{12,13},{13,14},{14,15},{15,12},{28,29},{29,30},{30,31},{31,28}} | collective-permute-start | bytes 589832 | tf_op jit(solution)/shard_map/ppermute | solution.py:522
  82.3 5.2 %collective-permute-start.14 = (f32[3,8,2048]{2,1,0:T(8,128)S(1)}, f32[3,8,2048]{2,1,0:T(8,128)S(1)}, u32[]{:S(2)}, u32[]{:S(2)}) collective-permute-start(f32[3,8,2048]{2,1,0:T(8,128)S(1)} %get-tuple-element.154), channel_id=1, source_target_pairs={{12,14},{13,15},{14,12},{15,13},{28,30},{29,31},{30,28},{31,29}} | collective-permute-start | bytes 589832 | tf_op jit(solution)/shard_map/ppermute | solution.py:522
  87.4 2.4 %collective-permute-start.15 = (f32[3,8,2048]{2,1,0:T(8,128)S(1)}, f32[3,8,2048]{2,1,0:T(8,128)S(1)}, u32[]{:S(2)}, u32[]{:S(2)}) collective-permute-start(f32[3,8,2048]{2,1,0:T(8,128)S(1)} %get-tuple-element.153), channel_id=1, source_target_pairs={{12,15},{13,12},{14,13},{15,14},{28,31},{29,28},{30,29},{31,30}} | collective-permute-start | bytes 589832 | tf_op jit(solution)/shard_map/ppermute | solution.py:522
  89.9 0.7 collective-permute-start.10
  90.6 0.7 collective-permute-start.11
  91.3 3.8 %collective-permute-done.13 = f32[3,8,2048]{2,1,0:T(8,128)S(1)} collective-permute-done((f32[3,8,2048]{2,1,0:T(8,128)S(1)}, f32[3,8,2048]{2,1,0:T(8,128)S(1)}, u32[]{:S(2)}, u32[]{:S(2)}) %collective-permute-start.13) | collective-permute-done | bytes 196640 | tf_op jit(solution)/shard_map/ppermute | solution.py:522
  95.1 0.7 collective-permute-start.12
  95.7 1.7 %collective-permute-done.14 = f32[3,8,2048]{2,1,0:T(8,128)S(1)} collective-permute-done((f32[3,8,2048]{2,1,0:T(8,128)S(1)}, f32[3,8,2048]{2,1,0:T(8,128)S(1)}, u32[]{:S(2)}, u32[]{:S(2)}) %collective-permute-start.14) | collective-permute-done | bytes 196640 | tf_op jit(solution)/shard_map/ppermute | solution.py:522
  97.5 0.7 collective-permute-done.15
  98.2 0.8 fusion.5
  (59 shorter events, 3.0 us)
Async XLA Ops:
  2.2 9.8 %copy-start = (f32[4]{0:T(128)S(1)}, f32[4]{0:T(128)}, u32[]{:S(2)}) copy-start(f32[4]{0:T(128)} %param.21) | copy-start | bytes 52
  2.3 10.4 %copy-start.1 = (f32[8]{0:T(128)S(1)}, f32[8]{0:T(128)}, u32[]{:S(2)}) copy-start(f32[8]{0:T(128)} %param.22) | copy-start | bytes 100
  2.3 10.4 %copy-start.2 = (s32[3]{0:T(128)S(1)}, s32[3]{0:T(128)}, u32[]{:S(2)}) copy-start(s32[3]{0:T(128)} %param.25) | copy-start | bytes 40
  2.3 12.5 %copy-start.3 = (f32[8]{0:T(128)S(1)}, f32[8]{0:T(128)}, u32[]{:S(2)}) copy-start(f32[8]{0:T(128)} %param.23) | copy-start | bytes 100
  2.3 13.2 %copy-start.4 = (f32[16,128]{1,0:T(8,128)S(1)}, f32[16,128]{1,0:T(8,128)}, u32[]{:S(2)}) copy-start(f32[16,128]{1,0:T(8,128)} %constant.138) | copy-start | bytes 24580
  2.4 13.3 %collective-permute-start = (f32[5,8,2048]{2,1,0:T(8,128)S(1)}, f32[5,8,2048]{2,1,0:T(8,128)}, u32[]{:S(2)}, u32[]{:S(2)}) collective-permute-start(f32[5,8,2048]{2,1,0:T(8,128)S(1)} %get-tuple-element.160), channel_id=1, source_target_pairs={{0,1},{1,2},{2,3},{3,0},{8,9},{9,10},{10,11},{11,8},{12,13},{13,14... | collective-permute-start | bytes 983048 | tf_op jit(solution)/shard_map/ppermute | solution.py:468
  5.6 27.4 %collective-permute-start.1 = (f32[5,8,2048]{2,1,0:T(8,128)S(1)}, f32[5,8,2048]{2,1,0:T(8,128)S(1)}, u32[]{:S(2)}, u32[]{:S(2)}) collective-permute-start(f32[5,8,2048]{2,1,0:T(8,128)S(1)} %get-tuple-element.161), channel_id=1, source_target_pairs={{0,2},{1,3},{2,0},{3,1},{8,10},{9,11},{10,8},{11,9},{12,14},{13,15... | collective-permute-start | bytes 983048 | tf_op jit(solution)/shard_map/ppermute | solution.py:468
  8.6 27.3 %collective-permute-start.2 = (f32[5,8,2048]{2,1,0:T(8,128)S(1)}, f32[5,8,2048]{2,1,0:T(8,128)S(1)}, u32[]{:S(2)}, u32[]{:S(2)}) collective-permute-start(f32[5,8,2048]{2,1,0:T(8,128)S(1)} %get-tuple-element.159), channel_id=1, source_target_pairs={{0,3},{1,0},{2,1},{3,2},{8,11},{9,8},{10,9},{11,10},{12,15},{13,12... | collective-permute-start | bytes 983048 | tf_op jit(solution)/shard_map/ppermute | solution.py:468
  35.9 1.0 copy-start.5
  35.9 1.0 copy-start.6
  35.9 1.0 %copy-start.8 = (bf16[256,256]{1,0:T(8,128)(2,1)S(1)}, bf16[256,256]{1,0:T(8,128)(2,1)}, u32[]{:S(2)}) copy-start(bf16[256,256]{1,0:T(8,128)(2,1)} %constant.133.clone) | copy-start | bytes 393220
  36.0 1.0 %copy-start.9 = (f32[2,16,128]{2,1,0:T(8,128)S(1)}, f32[2,16,128]{2,1,0:T(8,128)}, u32[]{:S(2)}) copy-start(f32[2,16,128]{2,1,0:T(8,128)} %constant.130.clone) | copy-start | bytes 49156
  36.0 1.1 %collective-permute-start.4 = (f32[8,128]{1,0:T(8,128)S(1)}, f32[8,128]{1,0:T(8,128)S(1)}, u32[]{:S(2)}, u32[]{:S(2)}) collective-permute-start(f32[8,128]{1,0:T(8,128)S(1)} %slice_bitcast_fusion), channel_id=1, source_target_pairs={{0,4},{1,5},{2,6},{3,7},{16,20},{17,21},{18,22},{19,23}} | collective-permute-start | bytes 12296 | tf_op jit(solution)/shard_map/ppermute | solution.py:505
  38.3 3.5 %collective-permute-start.5 = (f32[3,8,2048]{2,1,0:T(8,128)S(1)}, f32[3,8,2048]{2,1,0:T(8,128)S(1)}, u32[]{:S(2)}, u32[]{:S(2)}) collective-permute-start(f32[3,8,2048]{2,1,0:T(8,128)S(1)} %get-tuple-element.148), channel_id=1, source_target_pairs={{4,5},{5,6},{6,7},{7,4},{20,21},{21,22},{22,23},{23,20}} | collective-permute-start | bytes 589832 | tf_op jit(solution)/shard_map/ppermute | solution.py:468
  39.0 3.9 %collective-permute-start.3 = (f32[2,32,2048]{2,1,0:T(8,128)S(1)}, f32[2,32,2048]{2,1,0:T(8,128)}, u32[]{:S(2)}, u32[]{:S(2)}) collective-permute-start(f32[2,32,2048]{2,1,0:T(8,128)S(1)} %get-tuple-element.137), channel_id=1, source_target_pairs={{0,4},{1,5},{2,6},{3,7},{16,20},{17,21},{18,22},{19,23}} | collective-permute-start | bytes 1572872 | tf_op jit(solution)/shard_map/ppermute | solution.py:531
  40.5 1.4 %collective-permute-start.6 = (f32[3,8,2048]{2,1,0:T(8,128)S(1)}, f32[3,8,2048]{2,1,0:T(8,128)S(1)}, u32[]{:S(2)}, u32[]{:S(2)}) collective-permute-start(f32[3,8,2048]{2,1,0:T(8,128)S(1)} %get-tuple-element.148), channel_id=1, source_target_pairs={{4,6},{5,7},{6,4},{7,5},{20,22},{21,23},{22,20},{23,21}} | collective-permute-start | bytes 589832 | tf_op jit(solution)/shard_map/ppermute | solution.py:468
  41.1 0.8 collective-permute-start.7
  41.9 1.1 %copy-start.7 = (bf16[256,256]{1,0:T(8,128)(2,1)S(1)}, bf16[256,256]{1,0:T(8,128)(2,1)}, u32[]{:S(2)}) copy-start(bf16[256,256]{1,0:T(8,128)(2,1)} %constant.132.clone) | copy-start | bytes 393220
  42.9 0.7 collective-permute-start.8
  43.7 28.7 %collective-permute-start.9 = (f32[2,32,2048]{2,1,0:T(8,128)S(1)}, f32[2,32,2048]{2,1,0:T(8,128)S(1)}, u32[]{:S(2)}, u32[]{:S(2)}) collective-permute-start(f32[2,32,2048]{2,1,0:T(8,128)S(1)} %get-tuple-element.143), channel_id=1, source_target_pairs={{8,12},{9,13},{10,14},{11,15},{24,28},{25,29},{26,30},{27,31}} | collective-permute-start | bytes 1572872 | tf_op jit(solution)/shard_map/ppermute | solution.py:531
  80.3 14.7 %collective-permute-start.13 = (f32[3,8,2048]{2,1,0:T(8,128)S(1)}, f32[3,8,2048]{2,1,0:T(8,128)S(1)}, u32[]{:S(2)}, u32[]{:S(2)}) collective-permute-start(f32[3,8,2048]{2,1,0:T(8,128)S(1)} %get-tuple-element.152), channel_id=1, source_target_pairs={{12,13},{13,14},{14,15},{15,12},{28,29},{29,30},{30,31},{31,28}} | collective-permute-start | bytes 589832 | tf_op jit(solution)/shard_map/ppermute | solution.py:522
  82.3 15.2 %collective-permute-start.14 = (f32[3,8,2048]{2,1,0:T(8,128)S(1)}, f32[3,8,2048]{2,1,0:T(8,128)S(1)}, u32[]{:S(2)}, u32[]{:S(2)}) collective-permute-start(f32[3,8,2048]{2,1,0:T(8,128)S(1)} %get-tuple-element.154), channel_id=1, source_target_pairs={{12,14},{13,15},{14,12},{15,13},{28,30},{29,31},{30,28},{31,29}} | collective-permute-start | bytes 589832 | tf_op jit(solution)/shard_map/ppermute | solution.py:522
  87.4 10.8 %collective-permute-start.15 = (f32[3,8,2048]{2,1,0:T(8,128)S(1)}, f32[3,8,2048]{2,1,0:T(8,128)S(1)}, u32[]{:S(2)}, u32[]{:S(2)}) collective-permute-start(f32[3,8,2048]{2,1,0:T(8,128)S(1)} %get-tuple-element.153), channel_id=1, source_target_pairs={{12,15},{13,12},{14,13},{15,14},{28,31},{29,28},{30,29},{31,30}} | collective-permute-start | bytes 589832 | tf_op jit(solution)/shard_map/ppermute | solution.py:522
  89.9 8.3 %collective-permute-start.10 = (f32[3,8,2048]{2,1,0:T(8,128)S(1)}, f32[3,8,2048]{2,1,0:T(8,128)S(1)}, u32[]{:S(2)}, u32[]{:S(2)}) collective-permute-start(f32[3,8,2048]{2,1,0:T(8,128)S(1)} %get-tuple-element.149), channel_id=1, source_target_pairs={{0,1},{1,2},{2,3},{3,0},{4,5},{5,6},{6,7},{7,4},{8,9},{9,10},{10,1... | collective-permute-start | bytes 589832 | tf_op jit(solution)/shard_map/ppermute | solution.py:522
  90.6 7.6 %collective-permute-start.11 = (f32[3,8,2048]{2,1,0:T(8,128)S(1)}, f32[3,8,2048]{2,1,0:T(8,128)S(1)}, u32[]{:S(2)}, u32[]{:S(2)}) collective-permute-start(f32[3,8,2048]{2,1,0:T(8,128)S(1)} %get-tuple-element.151), channel_id=1, source_target_pairs={{0,2},{1,3},{2,0},{3,1},{4,6},{5,7},{6,4},{7,5},{8,10},{9,11},{10,... | collective-permute-start | bytes 589832 | tf_op jit(solution)/shard_map/ppermute | solution.py:522
  95.1 3.1 %collective-permute-start.12 = (f32[3,8,2048]{2,1,0:T(8,128)S(1)}, f32[3,8,2048]{2,1,0:T(8,128)S(1)}, u32[]{:S(2)}, u32[]{:S(2)}) collective-permute-start(f32[3,8,2048]{2,1,0:T(8,128)S(1)} %get-tuple-element.150), channel_id=1, source_target_pairs={{0,3},{1,0},{2,1},{3,2},{4,7},{5,4},{6,5},{7,6},{8,11},{9,8},{10,9... | collective-permute-start | bytes 589832 | tf_op jit(solution)/shard_map/ppermute | solution.py:522

commit v8 on v7

--- a/solution.py
+++ b/solution.py
@@ -234,6 +234,12 @@
     return jnp.broadcast_to(level[0], regions.shape)
 
 
+def full_dot(values, mat_ref):
+    return jnp.dot(
+        values, mat_ref[...], precision=lax.Precision.HIGHEST, preferred_element_type=jnp.float32
+    )
+
+
 def split_dot(values, hi_ref, lo_ref):
     high = values.astype(jnp.bfloat16)
     low = (values - high.astype(jnp.float32)).astype(jnp.bfloat16)
@@ -281,7 +287,7 @@
             return c
 
         lax.fori_loop(0, chunks, forward_chunk, 0)
-        y_ref[...] = split_dot(a_ref[...], fhi_ref, flo_ref)
+        y_ref[...] = full_dot(a_ref[...], fhi_ref)
         for cc in range(FFT_BLOCKS):
             band = slice(cc * rows, (cc + 1) * rows)
             yr = y_ref[band, 0:LANE]
@@ -290,7 +296,7 @@
             mi = mult_ref[k, 1, cc:cc + 1, :]
             a_ref[band, 0:LANE] = yr * mr - yi * mi
             a_ref[band, LANE:2 * LANE] = yr * mi + yi * mr
-        y_ref[...] = split_dot(a_ref[...], ghi_ref, glo_ref)
+        y_ref[...] = full_dot(a_ref[...], ghi_ref)
 
         def inverse_chunk(i, c):
             y0 = pl.multiple_of(i * ROW_CHUNK, ROW_CHUNK)
@@ -368,7 +374,7 @@
     q = c[:, None] + outer * b[None, :]
     signed = np.where(q >= line_len // 2, q - line_len, q).astype(np.float32)
     kx_cd = signed * np.float32(2.0 * math.pi / line_len)
-    return (halves(fwd), halves(inv), twiddle, kx_cd.astype(np.float32))
+    return ((fwd.astype(np.float32), fwd.astype(np.float32)), (inv.astype(np.float32), inv.astype(np.float32)), twiddle, kx_cd.astype(np.float32))
 
 
 def run_section(wave, regions, table, mult, consts, strip_count):

time: 99.8 us -> 106 us (1.062)
  Pallas kernels: 7.92 us -> 10.7 us
  waiting for transfers between devices: 52.8 us -> 55.5 us
    ppermute x3, waiting for transfers between devices: 27.4 us -> 32.9 us  [shards(): wave = lax.ppermute(wave, 'depth', [(tick_no, tick_no + 1)])]
    ppermute x6, waiting for transfers between devices: 6.23 us -> 3.48 us  [freq_sum(): lax.ppermute(piece, ('depth', 'strip'), strip_pairs(depths, strip_count,...]
    pallas_call x1, Pallas kernels: 7.92 us -> 10.7 us  [run_section(): pl.pallas_call(lambda *refs: section_kernel(*refs, table_len=table_len),...]
  transfers between devices with their start and end apart: 16 -> 16, of which waited for: 6 -> 5; matrix products, arithmetic and copies ran while one was open for 6% -> 6% of each run, Pallas kernels for 0% -> 0%
where the time goes in v8:
time: 106 us; the launch traced here: 104 us
  waiting for transfers between devices  55.5 us (52%)
  starting transfers between devices  27.1 us (26%)
  Pallas kernels  10.7 us (10%)
  other arithmetic  5.2 us (5%)
  local copies, waits for them, and re-layouts  4.5 us (4%)
  between operations  1.2 us (1%)
    ppermute x3, waiting for transfers between devices, shards(): wave = lax.ppermute(wave, 'depth', [(tick_no, tick_no + 1)])  32.9 us
    ppermute x6, waiting for transfers between devices, gather_strips(): lax.ppermute(piece_of(target), ('depth', 'strip'), strip_pairs(depths, st...  19.1 us
    ppermute x6, starting transfers between devices, freq_sum(): lax.ppermute(piece, ('depth', 'strip'), strip_pairs(depths, strip_count,...  11.5 us
    ppermute x6, starting transfers between devices, gather_strips(): lax.ppermute(piece_of(target), ('depth', 'strip'), strip_pairs(depths, st...  11.5 us
    pallas_call x1, Pallas kernels, run_section(): pl.pallas_call(lambda *refs: section_kernel(*refs, table_len=table_len),...  10.7 us
    ppermute x6, waiting for transfers between devices, freq_sum(): lax.ppermute(piece, ('depth', 'strip'), strip_pairs(depths, strip_count,...  3.48 us
    ppermute x3, starting transfers between devices, shards(): wave = lax.ppermute(wave, 'depth', [(tick_no, tick_no + 1)])  3.43 us
  transfers between devices with their start and end apart: 16, of which 5 were waited for; matrix products, arithmetic and copies ran while one was open for 6% of the time, Pallas kernels for 0%

profile of v8, /device:TPU:11, one launch (start us, length us, event | category | flops | bytes accessed | tf_op | source)
XLA Modules:
  0.0 104.3 jit_solution(15501951333762944734)
XLA Ops:
  0.0 0.9 convert_element_type.25
  1.0 1.1 %dynamic-slice_bitcast_fusion.6 = (f32[2,8,2048]{2,1,0:T(8,128)S(1)}, f32[2,8,2048]{2,1,0:T(8,128)S(1)}, f32[2,8,2048]{2,1,0:T(8,128)S(1)}, f32[2,8,2048]{2,1,0:T(8,128)S(1)}) fusion(f32[2,4,8,2048]{3,2,1,0:T(8,128)} %param.20, s32[]{:T(128)S(6)} %select_n.98, s32[]{:T(128)S(6)} %select_n.90, s32[]{:T(128)S(6)} %select_n.87, s32[]{:T(128)S(6)} %select_n.94), kind=kLoop, calls=%fused_computation.19 | loop fusion | bytes 1048592 | tf_op jit(solution)/shard_map/jit(dynamic_index_in_dim)/squeeze | solution.py:498
  2.4 3.2 %collective-permute-start = (f32[5,8,2048]{2,1,0:T(8,128)S(1)}, f32[5,8,2048]{2,1,0:T(8,128)}, u32[]{:S(2)}, u32[]{:S(2)}) collective-permute-start(f32[5,8,2048]{2,1,0:T(8,128)S(1)} %get-tuple-element.160), channel_id=1, source_target_pairs={{0,1},{1,2},{2,3},{3,0},{8,9},{9,10},{10,11},{11,8},{12,13},{13,14... | collective-permute-start | bytes 983048 | tf_op jit(solution)/shard_map/ppermute | solution.py:474
  5.6 2.9 %collective-permute-start.1 = (f32[5,8,2048]{2,1,0:T(8,128)S(1)}, f32[5,8,2048]{2,1,0:T(8,128)S(1)}, u32[]{:S(2)}, u32[]{:S(2)}) collective-permute-start(f32[5,8,2048]{2,1,0:T(8,128)S(1)} %get-tuple-element.161), channel_id=1, source_target_pairs={{0,2},{1,3},{2,0},{3,1},{8,10},{9,11},{10,8},{11,9},{12,14},{13,15... | collective-permute-start | bytes 983048 | tf_op jit(solution)/shard_map/ppermute | solution.py:474
  8.6 3.4 %collective-permute-start.2 = (f32[5,8,2048]{2,1,0:T(8,128)S(1)}, f32[5,8,2048]{2,1,0:T(8,128)S(1)}, u32[]{:S(2)}, u32[]{:S(2)}) collective-permute-start(f32[5,8,2048]{2,1,0:T(8,128)S(1)} %get-tuple-element.159), channel_id=1, source_target_pairs={{0,3},{1,0},{2,1},{3,2},{8,11},{9,8},{10,9},{11,10},{12,15},{13,12... | collective-permute-start | bytes 983048 | tf_op jit(solution)/shard_map/ppermute | solution.py:474
  12.0 0.6 dynamic_slice.43
  12.7 0.6 gather_fusion
  13.3 0.8 fusion.16
  14.1 0.7 multiply_multiply_fusion
  14.7 0.7 broadcast_divide_fusion
  15.7 1.0 constant_dynamic-update-slice_fusion.6
  16.7 16.3 %collective-permute-done.1 = f32[5,8,2048]{2,1,0:T(8,128)S(1)} collective-permute-done((f32[5,8,2048]{2,1,0:T(8,128)S(1)}, f32[5,8,2048]{2,1,0:T(8,128)S(1)}, u32[]{:S(2)}, u32[]{:S(2)}) %collective-permute-start.1) | collective-permute-done | bytes 327712 | tf_op jit(solution)/shard_map/ppermute | solution.py:474
  33.1 2.8 %collective-permute-done.2 = f32[5,8,2048]{2,1,0:T(8,128)S(1)} collective-permute-done((f32[5,8,2048]{2,1,0:T(8,128)S(1)}, f32[5,8,2048]{2,1,0:T(8,128)S(1)}, u32[]{:S(2)}, u32[]{:S(2)}) %collective-permute-start.2) | collective-permute-done | bytes 327712 | tf_op jit(solution)/shard_map/ppermute | solution.py:474
  35.9 0.7 collective-permute-start.4
  38.1 0.7 collective-permute-start.5
  38.8 1.5 %collective-permute-start.3 = (f32[2,32,2048]{2,1,0:T(8,128)S(1)}, f32[2,32,2048]{2,1,0:T(8,128)}, u32[]{:S(2)}, u32[]{:S(2)}) collective-permute-start(f32[2,32,2048]{2,1,0:T(8,128)S(1)} %get-tuple-element.137), channel_id=1, source_target_pairs={{0,4},{1,5},{2,6},{3,7},{16,20},{17,21},{18,22},{19,23}} | collective-permute-start | bytes 1572872 | tf_op jit(solution)/shard_map/ppermute | solution.py:537
  40.3 0.7 collective-permute-start.6
  40.9 0.7 collective-permute-start.7
  41.7 1.0 convert_element_type.27
  42.7 0.7 collective-permute-start.8
  43.4 1.3 %collective-permute-start.9 = (f32[2,32,2048]{2,1,0:T(8,128)S(1)}, f32[2,32,2048]{2,1,0:T(8,128)S(1)}, u32[]{:S(2)}, u32[]{:S(2)}) collective-permute-start(f32[2,32,2048]{2,1,0:T(8,128)S(1)} %get-tuple-element.143), channel_id=1, source_target_pairs={{8,12},{9,13},{10,14},{11,15},{24,28},{25,29},{26,30},{27,31}} | collective-permute-start | bytes 1572872 | tf_op jit(solution)/shard_map/ppermute | solution.py:537
  44.7 32.9 %collective-permute-done.9 = f32[2,32,2048]{2,1,0:T(8,128)S(1)} collective-permute-done((f32[2,32,2048]{2,1,0:T(8,128)S(1)}, f32[2,32,2048]{2,1,0:T(8,128)S(1)}, u32[]{:S(2)}, u32[]{:S(2)}) %collective-permute-start.9) | collective-permute-done | bytes 524320 | tf_op jit(solution)/shard_map/ppermute | solution.py:537
  77.6 10.7 %conditional.7 = (f32[4,3,8,2048]{3,2,1,0:T(8,128)S(1)}) conditional(s32[]{:T(128)} %convert_element_type.21, f32[4,3,8,2048]{3,2,1,0:T(8,128)S(1)} %get-tuple-element.145, (f32[72]{0:T(128)S(1)}, f32[2,32,2048]{2,1,0:T(8,128)S(1)}, s32[3,32,2048]{2,1,0:T(8,128)S(1)}, f32[3,2,16,128]{3,2,1,0:T(8,128)S(1)}, f32[2,16,128]{2,1,0:T(8,128)S(1)}, ...), branch_computations={%region_6.7_spmd, %region_7.8_spmd} | conditional | flops 1286602752 | bytes 4718600 | solution.py:535
  77.6 10.7 %branch_1_fun.7 = (f32[2,32,2048]{2,1,0:T(8,128)}, f32[4,3,8,2048]{3,2,1,0:T(8,128)S(1)}) custom-call(f32[72]{0:T(128)S(1)} %get-tuple-element.117.refs_0_, f32[2,32,2048]{2,1,0:T(8,128)S(1)} %get-tuple-element.118.refs_1_, s32[3,32,2048]{2,1,0:T(8,128)S(1)} %get-tuple-element.119.refs_2_, f32[3,2,16,128]{3,2,1,0:T(8,128)S(1)} %get-tuple-element.120.refs_3_, ...), custom_call_target="tpu_custom_call" | custom-call | flops 1286602752 | bytes 4718592 | tf_op jit(solution)/shard_map/cond/branch_1_fun/pallas_call | solution.py:387
  88.3 1.9 %collective-permute-start.13 = (f32[3,8,2048]{2,1,0:T(8,128)S(1)}, f32[3,8,2048]{2,1,0:T(8,128)S(1)}, u32[]{:S(2)}, u32[]{:S(2)}) collective-permute-start(f32[3,8,2048]{2,1,0:T(8,128)S(1)} %get-tuple-element.152), channel_id=1, source_target_pairs={{12,13},{13,14},{14,15},{15,12},{28,29},{29,30},{30,31},{31,28}} | collective-permute-start | bytes 589832 | tf_op jit(solution)/shard_map/ppermute | solution.py:528
  90.3 5.2 %collective-permute-start.14 = (f32[3,8,2048]{2,1,0:T(8,128)S(1)}, f32[3,8,2048]{2,1,0:T(8,128)S(1)}, u32[]{:S(2)}, u32[]{:S(2)}) collective-permute-start(f32[3,8,2048]{2,1,0:T(8,128)S(1)} %get-tuple-element.154), channel_id=1, source_target_pairs={{12,14},{13,15},{14,12},{15,13},{28,30},{29,31},{30,28},{31,29}} | collective-permute-start | bytes 589832 | tf_op jit(solution)/shard_map/ppermute | solution.py:528
  95.4 2.4 %collective-permute-start.15 = (f32[3,8,2048]{2,1,0:T(8,128)S(1)}, f32[3,8,2048]{2,1,0:T(8,128)S(1)}, u32[]{:S(2)}, u32[]{:S(2)}) collective-permute-start(f32[3,8,2048]{2,1,0:T(8,128)S(1)} %get-tuple-element.153), channel_id=1, source_target_pairs={{12,15},{13,12},{14,13},{15,14},{28,31},{29,28},{30,29},{31,30}} | collective-permute-start | bytes 589832 | tf_op jit(solution)/shard_map/ppermute | solution.py:528
  97.9 0.7 collective-permute-start.10
  98.6 0.7 collective-permute-start.11
  99.3 0.7 collective-permute-start.12
  100.0 3.1 %collective-permute-done.14 = f32[3,8,2048]{2,1,0:T(8,128)S(1)} collective-permute-done((f32[3,8,2048]{2,1,0:T(8,128)S(1)}, f32[3,8,2048]{2,1,0:T(8,128)S(1)}, u32[]{:S(2)}, u32[]{:S(2)}) %collective-permute-start.14) | collective-permute-done | bytes 196640 | tf_op jit(solution)/shard_map/ppermute | solution.py:528
  103.5 0.8 fusion.5
  (51 shorter events, 2.1 us)
Async XLA Ops:
  2.2 9.8 %copy-start = (f32[4]{0:T(128)S(1)}, f32[4]{0:T(128)}, u32[]{:S(2)}) copy-start(f32[4]{0:T(128)} %param.21) | copy-start | bytes 52
  2.3 10.4 %copy-start.1 = (f32[8]{0:T(128)S(1)}, f32[8]{0:T(128)}, u32[]{:S(2)}) copy-start(f32[8]{0:T(128)} %param.22) | copy-start | bytes 100
  2.3 10.4 %copy-start.2 = (s32[3]{0:T(128)S(1)}, s32[3]{0:T(128)}, u32[]{:S(2)}) copy-start(s32[3]{0:T(128)} %param.25) | copy-start | bytes 40
  2.3 12.5 %copy-start.3 = (f32[8]{0:T(128)S(1)}, f32[8]{0:T(128)}, u32[]{:S(2)}) copy-start(f32[8]{0:T(128)} %param.23) | copy-start | bytes 100
  2.3 13.2 %copy-start.4 = (f32[16,128]{1,0:T(8,128)S(1)}, f32[16,128]{1,0:T(8,128)}, u32[]{:S(2)}) copy-start(f32[16,128]{1,0:T(8,128)} %constant.132) | copy-start | bytes 24580
  2.4 13.3 %collective-permute-start = (f32[5,8,2048]{2,1,0:T(8,128)S(1)}, f32[5,8,2048]{2,1,0:T(8,128)}, u32[]{:S(2)}, u32[]{:S(2)}) collective-permute-start(f32[5,8,2048]{2,1,0:T(8,128)S(1)} %get-tuple-element.160), channel_id=1, source_target_pairs={{0,1},{1,2},{2,3},{3,0},{8,9},{9,10},{10,11},{11,8},{12,13},{13,14... | collective-permute-start | bytes 983048 | tf_op jit(solution)/shard_map/ppermute | solution.py:474
  5.6 27.4 %collective-permute-start.1 = (f32[5,8,2048]{2,1,0:T(8,128)S(1)}, f32[5,8,2048]{2,1,0:T(8,128)S(1)}, u32[]{:S(2)}, u32[]{:S(2)}) collective-permute-start(f32[5,8,2048]{2,1,0:T(8,128)S(1)} %get-tuple-element.161), channel_id=1, source_target_pairs={{0,2},{1,3},{2,0},{3,1},{8,10},{9,11},{10,8},{11,9},{12,14},{13,15... | collective-permute-start | bytes 983048 | tf_op jit(solution)/shard_map/ppermute | solution.py:474
  8.6 27.3 %collective-permute-start.2 = (f32[5,8,2048]{2,1,0:T(8,128)S(1)}, f32[5,8,2048]{2,1,0:T(8,128)S(1)}, u32[]{:S(2)}, u32[]{:S(2)}) collective-permute-start(f32[5,8,2048]{2,1,0:T(8,128)S(1)} %get-tuple-element.159), channel_id=1, source_target_pairs={{0,3},{1,0},{2,1},{3,2},{8,11},{9,8},{10,9},{11,10},{12,15},{13,12... | collective-permute-start | bytes 983048 | tf_op jit(solution)/shard_map/ppermute | solution.py:474
  35.9 0.8 copy-start.5
  35.9 0.9 collective-permute-start.4
  38.1 3.5 %collective-permute-start.5 = (f32[3,8,2048]{2,1,0:T(8,128)S(1)}, f32[3,8,2048]{2,1,0:T(8,128)S(1)}, u32[]{:S(2)}, u32[]{:S(2)}) collective-permute-start(f32[3,8,2048]{2,1,0:T(8,128)S(1)} %get-tuple-element.148), channel_id=1, source_target_pairs={{4,5},{5,6},{6,7},{7,4},{20,21},{21,22},{22,23},{23,20}} | collective-permute-start | bytes 589832 | tf_op jit(solution)/shard_map/ppermute | solution.py:474
  38.8 3.9 %collective-permute-start.3 = (f32[2,32,2048]{2,1,0:T(8,128)S(1)}, f32[2,32,2048]{2,1,0:T(8,128)}, u32[]{:S(2)}, u32[]{:S(2)}) collective-permute-start(f32[2,32,2048]{2,1,0:T(8,128)S(1)} %get-tuple-element.137), channel_id=1, source_target_pairs={{0,4},{1,5},{2,6},{3,7},{16,20},{17,21},{18,22},{19,23}} | collective-permute-start | bytes 1572872 | tf_op jit(solution)/shard_map/ppermute | solution.py:537
  40.3 1.4 %collective-permute-start.6 = (f32[3,8,2048]{2,1,0:T(8,128)S(1)}, f32[3,8,2048]{2,1,0:T(8,128)S(1)}, u32[]{:S(2)}, u32[]{:S(2)}) collective-permute-start(f32[3,8,2048]{2,1,0:T(8,128)S(1)} %get-tuple-element.148), channel_id=1, source_target_pairs={{4,6},{5,7},{6,4},{7,5},{20,22},{21,23},{22,20},{23,21}} | collective-permute-start | bytes 589832 | tf_op jit(solution)/shard_map/ppermute | solution.py:474
  40.9 0.8 collective-permute-start.7
  42.7 0.7 collective-permute-start.8
  43.4 34.2 %collective-permute-start.9 = (f32[2,32,2048]{2,1,0:T(8,128)S(1)}, f32[2,32,2048]{2,1,0:T(8,128)S(1)}, u32[]{:S(2)}, u32[]{:S(2)}) collective-permute-start(f32[2,32,2048]{2,1,0:T(8,128)S(1)} %get-tuple-element.143), channel_id=1, source_target_pairs={{8,12},{9,13},{10,14},{11,15},{24,28},{25,29},{26,30},{27,31}} | collective-permute-start | bytes 1572872 | tf_op jit(solution)/shard_map/ppermute | solution.py:537
  88.3 11.0 %collective-permute-start.13 = (f32[3,8,2048]{2,1,0:T(8,128)S(1)}, f32[3,8,2048]{2,1,0:T(8,128)S(1)}, u32[]{:S(2)}, u32[]{:S(2)}) collective-permute-start(f32[3,8,2048]{2,1,0:T(8,128)S(1)} %get-tuple-element.152), channel_id=1, source_target_pairs={{12,13},{13,14},{14,15},{15,12},{28,29},{29,30},{30,31},{31,28}} | collective-permute-start | bytes 589832 | tf_op jit(solution)/shard_map/ppermute | solution.py:528
  90.3 12.8 %collective-permute-start.14 = (f32[3,8,2048]{2,1,0:T(8,128)S(1)}, f32[3,8,2048]{2,1,0:T(8,128)S(1)}, u32[]{:S(2)}, u32[]{:S(2)}) collective-permute-start(f32[3,8,2048]{2,1,0:T(8,128)S(1)} %get-tuple-element.154), channel_id=1, source_target_pairs={{12,14},{13,15},{14,12},{15,13},{28,30},{29,31},{30,28},{31,29}} | collective-permute-start | bytes 589832 | tf_op jit(solution)/shard_map/ppermute | solution.py:528
  95.4 8.0 %collective-permute-start.15 = (f32[3,8,2048]{2,1,0:T(8,128)S(1)}, f32[3,8,2048]{2,1,0:T(8,128)S(1)}, u32[]{:S(2)}, u32[]{:S(2)}) collective-permute-start(f32[3,8,2048]{2,1,0:T(8,128)S(1)} %get-tuple-element.153), channel_id=1, source_target_pairs={{12,15},{13,12},{14,13},{15,14},{28,31},{29,28},{30,29},{31,30}} | collective-permute-start | bytes 589832 | tf_op jit(solution)/shard_map/ppermute | solution.py:528
  97.9 5.5 %collective-permute-start.10 = (f32[3,8,2048]{2,1,0:T(8,128)S(1)}, f32[3,8,2048]{2,1,0:T(8,128)S(1)}, u32[]{:S(2)}, u32[]{:S(2)}) collective-permute-start(f32[3,8,2048]{2,1,0:T(8,128)S(1)} %get-tuple-element.149), channel_id=1, source_target_pairs={{0,1},{1,2},{2,3},{3,0},{4,5},{5,6},{6,7},{7,4},{8,9},{9,10},{10,1... | collective-permute-start | bytes 589832 | tf_op jit(solution)/shard_map/ppermute | solution.py:528
  98.6 4.8 %collective-permute-start.11 = (f32[3,8,2048]{2,1,0:T(8,128)S(1)}, f32[3,8,2048]{2,1,0:T(8,128)S(1)}, u32[]{:S(2)}, u32[]{:S(2)}) collective-permute-start(f32[3,8,2048]{2,1,0:T(8,128)S(1)} %get-tuple-element.151), channel_id=1, source_target_pairs={{0,2},{1,3},{2,0},{3,1},{4,6},{5,7},{6,4},{7,5},{8,10},{9,11},{10,... | collective-permute-start | bytes 589832 | tf_op jit(solution)/shard_map/ppermute | solution.py:528
  99.3 4.2 %collective-permute-start.12 = (f32[3,8,2048]{2,1,0:T(8,128)S(1)}, f32[3,8,2048]{2,1,0:T(8,128)S(1)}, u32[]{:S(2)}, u32[]{:S(2)}) collective-permute-start(f32[3,8,2048]{2,1,0:T(8,128)S(1)} %get-tuple-element.150), channel_id=1, source_target_pairs={{0,3},{1,0},{2,1},{3,2},{4,7},{5,4},{6,5},{7,6},{8,11},{9,8},{10,9... | collective-permute-start | bytes 589832 | tf_op jit(solution)/shard_map/ppermute | solution.py:528

commit v9 on v7

--- a/solution.py
+++ b/solution.py
@@ -234,6 +234,13 @@
     return jnp.broadcast_to(level[0], regions.shape)
 
 
+def pick_bits(bits, values):
+    level = list(values)
+    for chosen in bits:
+        level = [jnp.where(chosen, level[i + 1], level[i]) for i in range(0, len(level), 2)]
+    return jnp.broadcast_to(level[0], bits[0].shape)
+
+
 def split_dot(values, hi_ref, lo_ref):
     high = values.astype(jnp.bfloat16)
     low = (values - high.astype(jnp.float32)).astype(jnp.bfloat16)
@@ -246,7 +253,7 @@
 
 def section_kernel(
     tab_ref, w_ref, rid_ref, mult_ref, tw_ref, fhi_ref, flo_ref, ghi_ref, glo_ref,
-    wout_ref, img_ref, a_ref, y_ref, v_ref, *, table_len
+    wout_ref, img_ref, a_ref, y_ref, v_ref, cs_ref, sn_ref, gn_ref, *, table_len
 ):
     rows = w_ref.shape[1]
     line_len = w_ref.shape[2]
@@ -281,7 +288,14 @@
             return c
 
         lax.fori_loop(0, chunks, forward_chunk, 0)
-        y_ref[...] = split_dot(a_ref[...], fhi_ref, flo_ref)
+        spectrum = split_dot(a_ref[...], fhi_ref, flo_ref)
+        for a in range(FFT_BLOCKS):
+            regions = rid_ref[k, :, blk(a)]
+            bits = [(regions & (1 << b)) != 0 for b in range(max(1, (table_len - 1).bit_length()))]
+            cs_ref[:, blk(a)] = pick_bits(bits, cos_t)
+            sn_ref[:, blk(a)] = pick_bits(bits, sin_t)
+            gn_ref[:, blk(a)] = pick_bits(bits, gain_t)
+        y_ref[...] = spectrum
         for cc in range(FFT_BLOCKS):
             band = slice(cc * rows, (cc + 1) * rows)
             yr = y_ref[band, 0:LANE]
@@ -305,9 +319,8 @@
             for a in range(FFT_BLOCKS):
                 ur = back[a][0] * inv_len
                 ui = back[a][1] * inv_len
-                regions = rid_ref[k, pl.ds(y0, ROW_CHUNK), blk(a)]
-                cs = pick(regions, cos_t)
-                sn = pick(regions, sin_t)
+                cs = cs_ref[pl.ds(y0, ROW_CHUNK), blk(a)]
+                sn = sn_ref[pl.ds(y0, ROW_CHUNK), blk(a)]
                 v_ref[0, pl.ds(y0, ROW_CHUNK), blk(a)] = ur * cs - ui * sn
                 v_ref[1, pl.ds(y0, ROW_CHUNK), blk(a)] = ur * sn + ui * cs
             return c
@@ -337,7 +350,7 @@
                 right = jnp.where(lane_id == LANE - 1, next_right, from_right)
                 lap.append(above + below + left + right - 4.0 * v)
                 here.append(v)
-            gain = pick(rid_ref[k, :, blk(a)], gain_t)
+            gain = gn_ref[:, blk(a)]
             new_re = here[0] + (lap[0] * DAMPING - lap[1] * gain)
             new_im = here[1] + (lap[0] * gain + lap[1] * DAMPING)
             wout_ref[0, :, blk(a)] = new_re
@@ -390,6 +403,9 @@
             pltpu.VMEM((FFT_BLOCKS * rows, 2 * LANE), jnp.float32),
             pltpu.VMEM((FFT_BLOCKS * rows, 2 * LANE), jnp.float32),
             pltpu.VMEM((2, rows, line_len), jnp.float32),
+            pltpu.VMEM((rows, line_len), jnp.float32),
+            pltpu.VMEM((rows, line_len), jnp.float32),
+            pltpu.VMEM((rows, line_len), jnp.float32),
         ],
         cost_estimate=pl.CostEstimate(
             flops=flops, transcendentals=0, bytes_accessed=4 * rows * line_len * 6 * steps

time: 99.8 us -> 99.3 us (level)
  no operation moved by 1% of the time
where the time goes in v9:
time: 99.3 us; the launch traced here: 98.6 us
  waiting for transfers between devices  52.5 us (53%)
  starting transfers between devices  27.3 us (27%)
  Pallas kernels  7.71 us (8%)
  other arithmetic  5.21 us (5%)
  local copies, waits for them, and re-layouts  4.57 us (5%)
  between operations  1.23 us (1%)
    ppermute x3, waiting for transfers between devices, shards(): wave = lax.ppermute(wave, 'depth', [(tick_no, tick_no + 1)])  27 us
    ppermute x6, waiting for transfers between devices, gather_strips(): lax.ppermute(piece_of(target), ('depth', 'strip'), strip_pairs(depths, st...  19.1 us
    ppermute x6, starting transfers between devices, freq_sum(): lax.ppermute(piece, ('depth', 'strip'), strip_pairs(depths, strip_count,...  11.5 us
    ppermute x6, starting transfers between devices, gather_strips(): lax.ppermute(piece_of(target), ('depth', 'strip'), strip_pairs(depths, st...  11.5 us
    pallas_call x1, Pallas kernels, run_section(): pl.pallas_call(lambda *refs: section_kernel(*refs, table_len=table_len),...  7.71 us
    ppermute x6, waiting for transfers between devices, freq_sum(): lax.ppermute(piece, ('depth', 'strip'), strip_pairs(depths, strip_count,...  6.44 us
    ppermute x3, starting transfers between devices, shards(): wave = lax.ppermute(wave, 'depth', [(tick_no, tick_no + 1)])  3.44 us
  transfers between devices with their start and end apart: 16, of which 6 were waited for; matrix products, arithmetic and copies ran while one was open for 6% of the time, Pallas kernels for 0%

profile of v9, /device:TPU:11, one launch (start us, length us, event | category | flops | bytes accessed | tf_op | source)
XLA Modules:
  0.0 98.6 jit_solution(10585119539175564694)
XLA Ops:
  0.0 0.9 convert_element_type.25
  1.0 1.1 %dynamic-slice_bitcast_fusion.6 = (f32[2,8,2048]{2,1,0:T(8,128)S(1)}, f32[2,8,2048]{2,1,0:T(8,128)S(1)}, f32[2,8,2048]{2,1,0:T(8,128)S(1)}, f32[2,8,2048]{2,1,0:T(8,128)S(1)}) fusion(f32[2,4,8,2048]{3,2,1,0:T(8,128)} %param.20, s32[]{:T(128)S(6)} %select_n.98, s32[]{:T(128)S(6)} %select_n.90, s32[]{:T(128)S(6)} %select_n.87, s32[]{:T(128)S(6)} %select_n.94), kind=kLoop, calls=%fused_computation.19 | loop fusion | bytes 1048592 | tf_op jit(solution)/shard_map/jit(dynamic_index_in_dim)/squeeze | solution.py:508
  2.4 3.2 %collective-permute-start = (f32[5,8,2048]{2,1,0:T(8,128)S(1)}, f32[5,8,2048]{2,1,0:T(8,128)}, u32[]{:S(2)}, u32[]{:S(2)}) collective-permute-start(f32[5,8,2048]{2,1,0:T(8,128)S(1)} %get-tuple-element.160), channel_id=1, source_target_pairs={{0,1},{1,2},{2,3},{3,0},{8,9},{9,10},{10,11},{11,8},{12,13},{13,14... | collective-permute-start | bytes 983048 | tf_op jit(solution)/shard_map/ppermute | solution.py:484
  5.6 2.9 %collective-permute-start.1 = (f32[5,8,2048]{2,1,0:T(8,128)S(1)}, f32[5,8,2048]{2,1,0:T(8,128)S(1)}, u32[]{:S(2)}, u32[]{:S(2)}) collective-permute-start(f32[5,8,2048]{2,1,0:T(8,128)S(1)} %get-tuple-element.161), channel_id=1, source_target_pairs={{0,2},{1,3},{2,0},{3,1},{8,10},{9,11},{10,8},{11,9},{12,14},{13,15... | collective-permute-start | bytes 983048 | tf_op jit(solution)/shard_map/ppermute | solution.py:484
  8.6 3.4 %collective-permute-start.2 = (f32[5,8,2048]{2,1,0:T(8,128)S(1)}, f32[5,8,2048]{2,1,0:T(8,128)S(1)}, u32[]{:S(2)}, u32[]{:S(2)}) collective-permute-start(f32[5,8,2048]{2,1,0:T(8,128)S(1)} %get-tuple-element.159), channel_id=1, source_target_pairs={{0,3},{1,0},{2,1},{3,2},{8,11},{9,8},{10,9},{11,10},{12,15},{13,12... | collective-permute-start | bytes 983048 | tf_op jit(solution)/shard_map/ppermute | solution.py:484
  13.3 0.8 fusion.16
  14.1 0.7 multiply_multiply_fusion
  14.7 0.7 broadcast_divide_fusion
  15.7 1.0 %constant_dynamic-update-slice_fusion.6 = f32[5,32,2048]{2,1,0:T(8,128)S(1)} fusion(f32[5,32,2048]{2,1,0:T(8,128)S(1)} %get-tuple-element.162, f32[5,8,2048]{2,1,0:T(8,128)} %collective-permute-done, s32[]{:T(128)S(6)} %select_n.92), kind=kLoop, calls=%fused_computation.43 | loop fusion | bytes 655364 | tf_op jit(solution)/shard_map/dynamic_update_slice | solution.py:488
  16.7 16.3 %collective-permute-done.1 = f32[5,8,2048]{2,1,0:T(8,128)S(1)} collective-permute-done((f32[5,8,2048]{2,1,0:T(8,128)S(1)}, f32[5,8,2048]{2,1,0:T(8,128)S(1)}, u32[]{:S(2)}, u32[]{:S(2)}) %collective-permute-start.1) | collective-permute-done | bytes 327712 | tf_op jit(solution)/shard_map/ppermute | solution.py:484
  33.1 2.8 %collective-permute-done.2 = f32[5,8,2048]{2,1,0:T(8,128)S(1)} collective-permute-done((f32[5,8,2048]{2,1,0:T(8,128)S(1)}, f32[5,8,2048]{2,1,0:T(8,128)S(1)}, u32[]{:S(2)}, u32[]{:S(2)}) %collective-permute-start.2) | collective-permute-done | bytes 327712 | tf_op jit(solution)/shard_map/ppermute | solution.py:484
  36.0 0.8 collective-permute-start.4
  38.3 0.7 collective-permute-start.5
  39.0 1.5 %collective-permute-start.3 = (f32[2,32,2048]{2,1,0:T(8,128)S(1)}, f32[2,32,2048]{2,1,0:T(8,128)}, u32[]{:S(2)}, u32[]{:S(2)}) collective-permute-start(f32[2,32,2048]{2,1,0:T(8,128)S(1)} %get-tuple-element.137), channel_id=1, source_target_pairs={{0,4},{1,5},{2,6},{3,7},{16,20},{17,21},{18,22},{19,23}} | collective-permute-start | bytes 1572872 | tf_op jit(solution)/shard_map/ppermute | solution.py:547
  40.5 0.7 collective-permute-start.6
  41.1 0.7 collective-permute-start.7
  42.0 1.0 convert_element_type.27
  42.9 0.7 collective-permute-start.8
  43.7 1.3 %collective-permute-start.9 = (f32[2,32,2048]{2,1,0:T(8,128)S(1)}, f32[2,32,2048]{2,1,0:T(8,128)S(1)}, u32[]{:S(2)}, u32[]{:S(2)}) collective-permute-start(f32[2,32,2048]{2,1,0:T(8,128)S(1)} %get-tuple-element.143), channel_id=1, source_target_pairs={{8,12},{9,13},{10,14},{11,15},{24,28},{25,29},{26,30},{27,31}} | collective-permute-start | bytes 1572872 | tf_op jit(solution)/shard_map/ppermute | solution.py:547
  45.0 27.0 %collective-permute-done.9 = f32[2,32,2048]{2,1,0:T(8,128)S(1)} collective-permute-done((f32[2,32,2048]{2,1,0:T(8,128)S(1)}, f32[2,32,2048]{2,1,0:T(8,128)S(1)}, u32[]{:S(2)}, u32[]{:S(2)}) %collective-permute-start.9) | collective-permute-done | bytes 524320 | tf_op jit(solution)/shard_map/ppermute | solution.py:547
  71.9 7.7 %conditional.7 = (f32[4,3,8,2048]{3,2,1,0:T(8,128)S(1)}) conditional(s32[]{:T(128)} %convert_element_type.21, f32[4,3,8,2048]{3,2,1,0:T(8,128)S(1)} %get-tuple-element.145, (f32[72]{0:T(128)S(1)}, f32[2,32,2048]{2,1,0:T(8,128)S(1)}, s32[3,32,2048]{2,1,0:T(8,128)S(1)}, f32[3,2,16,128]{3,2,1,0:T(8,128)S(1)}, f32[2,16,128]{2,1,0:T(8,128)S(1)}, ...), branch_computations={%region_6.7_spmd, %region_7.8_spmd} | conditional | flops 1286602752 | bytes 4718600 | solution.py:545
  71.9 7.7 %branch_1_fun.7 = (f32[2,32,2048]{2,1,0:T(8,128)}, f32[4,3,8,2048]{3,2,1,0:T(8,128)S(1)}) custom-call(f32[72]{0:T(128)S(1)} %get-tuple-element.117.refs_0_, f32[2,32,2048]{2,1,0:T(8,128)S(1)} %get-tuple-element.118.refs_1_, s32[3,32,2048]{2,1,0:T(8,128)S(1)} %get-tuple-element.119.refs_2_, f32[3,2,16,128]{3,2,1,0:T(8,128)S(1)} %get-tuple-element.120.refs_3_, ...), custom_call_target="tpu_custom_call" | custom-call | flops 1286602752 | bytes 4718592 | tf_op jit(solution)/shard_map/cond/branch_1_fun/pallas_call | solution.py:394
  79.7 1.9 %collective-permute-start.13 = (f32[3,8,2048]{2,1,0:T(8,128)S(1)}, f32[3,8,2048]{2,1,0:T(8,128)S(1)}, u32[]{:S(2)}, u32[]{:S(2)}) collective-permute-start(f32[3,8,2048]{2,1,0:T(8,128)S(1)} %get-tuple-element.152), channel_id=1, source_target_pairs={{12,13},{13,14},{14,15},{15,12},{28,29},{29,30},{30,31},{31,28}} | collective-permute-start | bytes 589832 | tf_op jit(solution)/shard_map/ppermute | solution.py:538
  81.6 5.2 %collective-permute-start.14 = (f32[3,8,2048]{2,1,0:T(8,128)S(1)}, f32[3,8,2048]{2,1,0:T(8,128)S(1)}, u32[]{:S(2)}, u32[]{:S(2)}) collective-permute-start(f32[3,8,2048]{2,1,0:T(8,128)S(1)} %get-tuple-element.154), channel_id=1, source_target_pairs={{12,14},{13,15},{14,12},{15,13},{28,30},{29,31},{30,28},{31,29}} | collective-permute-start | bytes 589832 | tf_op jit(solution)/shard_map/ppermute | solution.py:538
  86.8 2.4 %collective-permute-start.15 = (f32[3,8,2048]{2,1,0:T(8,128)S(1)}, f32[3,8,2048]{2,1,0:T(8,128)S(1)}, u32[]{:S(2)}, u32[]{:S(2)}) collective-permute-start(f32[3,8,2048]{2,1,0:T(8,128)S(1)} %get-tuple-element.153), channel_id=1, source_target_pairs={{12,15},{13,12},{14,13},{15,14},{28,31},{29,28},{30,29},{31,30}} | collective-permute-start | bytes 589832 | tf_op jit(solution)/shard_map/ppermute | solution.py:538
  89.3 0.7 collective-permute-start.10
  90.0 0.7 collective-permute-start.11
  90.7 3.6 %collective-permute-done.13 = f32[3,8,2048]{2,1,0:T(8,128)S(1)} collective-permute-done((f32[3,8,2048]{2,1,0:T(8,128)S(1)}, f32[3,8,2048]{2,1,0:T(8,128)S(1)}, u32[]{:S(2)}, u32[]{:S(2)}) %collective-permute-start.13) | collective-permute-done | bytes 196640 | tf_op jit(solution)/shard_map/ppermute | solution.py:538
  94.3 0.7 collective-permute-start.12
  95.0 1.9 %collective-permute-done.14 = f32[3,8,2048]{2,1,0:T(8,128)S(1)} collective-permute-done((f32[3,8,2048]{2,1,0:T(8,128)S(1)}, f32[3,8,2048]{2,1,0:T(8,128)S(1)}, u32[]{:S(2)}, u32[]{:S(2)}) %collective-permute-start.14) | collective-permute-done | bytes 196640 | tf_op jit(solution)/shard_map/ppermute | solution.py:538
  96.9 0.9 collective-permute-done.15
  97.8 0.8 fusion.5
  (59 shorter events, 3.0 us)
Async XLA Ops:
  2.2 9.8 %copy-start = (f32[4]{0:T(128)S(1)}, f32[4]{0:T(128)}, u32[]{:S(2)}) copy-start(f32[4]{0:T(128)} %param.21) | copy-start | bytes 52
  2.3 10.4 %copy-start.1 = (f32[8]{0:T(128)S(1)}, f32[8]{0:T(128)}, u32[]{:S(2)}) copy-start(f32[8]{0:T(128)} %param.22) | copy-start | bytes 100
  2.3 10.4 %copy-start.2 = (s32[3]{0:T(128)S(1)}, s32[3]{0:T(128)}, u32[]{:S(2)}) copy-start(s32[3]{0:T(128)} %param.25) | copy-start | bytes 40
  2.3 12.5 %copy-start.3 = (f32[8]{0:T(128)S(1)}, f32[8]{0:T(128)}, u32[]{:S(2)}) copy-start(f32[8]{0:T(128)} %param.23) | copy-start | bytes 100
  2.3 13.2 %copy-start.4 = (f32[16,128]{1,0:T(8,128)S(1)}, f32[16,128]{1,0:T(8,128)}, u32[]{:S(2)}) copy-start(f32[16,128]{1,0:T(8,128)} %constant.138) | copy-start | bytes 24580
  2.4 13.3 %collective-permute-start = (f32[5,8,2048]{2,1,0:T(8,128)S(1)}, f32[5,8,2048]{2,1,0:T(8,128)}, u32[]{:S(2)}, u32[]{:S(2)}) collective-permute-start(f32[5,8,2048]{2,1,0:T(8,128)S(1)} %get-tuple-element.160), channel_id=1, source_target_pairs={{0,1},{1,2},{2,3},{3,0},{8,9},{9,10},{10,11},{11,8},{12,13},{13,14... | collective-permute-start | bytes 983048 | tf_op jit(solution)/shard_map/ppermute | solution.py:484
  5.6 27.4 %collective-permute-start.1 = (f32[5,8,2048]{2,1,0:T(8,128)S(1)}, f32[5,8,2048]{2,1,0:T(8,128)S(1)}, u32[]{:S(2)}, u32[]{:S(2)}) collective-permute-start(f32[5,8,2048]{2,1,0:T(8,128)S(1)} %get-tuple-element.161), channel_id=1, source_target_pairs={{0,2},{1,3},{2,0},{3,1},{8,10},{9,11},{10,8},{11,9},{12,14},{13,15... | collective-permute-start | bytes 983048 | tf_op jit(solution)/shard_map/ppermute | solution.py:484
  8.6 27.3 %collective-permute-start.2 = (f32[5,8,2048]{2,1,0:T(8,128)S(1)}, f32[5,8,2048]{2,1,0:T(8,128)S(1)}, u32[]{:S(2)}, u32[]{:S(2)}) collective-permute-start(f32[5,8,2048]{2,1,0:T(8,128)S(1)} %get-tuple-element.159), channel_id=1, source_target_pairs={{0,3},{1,0},{2,1},{3,2},{8,11},{9,8},{10,9},{11,10},{12,15},{13,12... | collective-permute-start | bytes 983048 | tf_op jit(solution)/shard_map/ppermute | solution.py:484
  35.9 1.0 copy-start.5
  35.9 1.0 copy-start.6
  35.9 1.0 %copy-start.8 = (bf16[256,256]{1,0:T(8,128)(2,1)S(1)}, bf16[256,256]{1,0:T(8,128)(2,1)}, u32[]{:S(2)}) copy-start(bf16[256,256]{1,0:T(8,128)(2,1)} %constant.133.clone) | copy-start | bytes 393220
  36.0 1.0 %copy-start.9 = (f32[2,16,128]{2,1,0:T(8,128)S(1)}, f32[2,16,128]{2,1,0:T(8,128)}, u32[]{:S(2)}) copy-start(f32[2,16,128]{2,1,0:T(8,128)} %constant.130.clone) | copy-start | bytes 49156
  36.0 1.1 %collective-permute-start.4 = (f32[8,128]{1,0:T(8,128)S(1)}, f32[8,128]{1,0:T(8,128)S(1)}, u32[]{:S(2)}, u32[]{:S(2)}) collective-permute-start(f32[8,128]{1,0:T(8,128)S(1)} %slice_bitcast_fusion), channel_id=1, source_target_pairs={{0,4},{1,5},{2,6},{3,7},{16,20},{17,21},{18,22},{19,23}} | collective-permute-start | bytes 12296 | tf_op jit(solution)/shard_map/ppermute | solution.py:521
  38.3 3.5 %collective-permute-start.5 = (f32[3,8,2048]{2,1,0:T(8,128)S(1)}, f32[3,8,2048]{2,1,0:T(8,128)S(1)}, u32[]{:S(2)}, u32[]{:S(2)}) collective-permute-start(f32[3,8,2048]{2,1,0:T(8,128)S(1)} %get-tuple-element.148), channel_id=1, source_target_pairs={{4,5},{5,6},{6,7},{7,4},{20,21},{21,22},{22,23},{23,20}} | collective-permute-start | bytes 589832 | tf_op jit(solution)/shard_map/ppermute | solution.py:484
  39.0 3.9 %collective-permute-start.3 = (f32[2,32,2048]{2,1,0:T(8,128)S(1)}, f32[2,32,2048]{2,1,0:T(8,128)}, u32[]{:S(2)}, u32[]{:S(2)}) collective-permute-start(f32[2,32,2048]{2,1,0:T(8,128)S(1)} %get-tuple-element.137), channel_id=1, source_target_pairs={{0,4},{1,5},{2,6},{3,7},{16,20},{17,21},{18,22},{19,23}} | collective-permute-start | bytes 1572872 | tf_op jit(solution)/shard_map/ppermute | solution.py:547
  40.5 1.4 %collective-permute-start.6 = (f32[3,8,2048]{2,1,0:T(8,128)S(1)}, f32[3,8,2048]{2,1,0:T(8,128)S(1)}, u32[]{:S(2)}, u32[]{:S(2)}) collective-permute-start(f32[3,8,2048]{2,1,0:T(8,128)S(1)} %get-tuple-element.148), channel_id=1, source_target_pairs={{4,6},{5,7},{6,4},{7,5},{20,22},{21,23},{22,20},{23,21}} | collective-permute-start | bytes 589832 | tf_op jit(solution)/shard_map/ppermute | solution.py:484
  41.1 0.8 collective-permute-start.7
  41.9 1.1 %copy-start.7 = (bf16[256,256]{1,0:T(8,128)(2,1)S(1)}, bf16[256,256]{1,0:T(8,128)(2,1)}, u32[]{:S(2)}) copy-start(bf16[256,256]{1,0:T(8,128)(2,1)} %constant.132.clone) | copy-start | bytes 393220
  42.9 0.7 collective-permute-start.8
  43.7 28.3 %collective-permute-start.9 = (f32[2,32,2048]{2,1,0:T(8,128)S(1)}, f32[2,32,2048]{2,1,0:T(8,128)S(1)}, u32[]{:S(2)}, u32[]{:S(2)}) collective-permute-start(f32[2,32,2048]{2,1,0:T(8,128)S(1)} %get-tuple-element.143), channel_id=1, source_target_pairs={{8,12},{9,13},{10,14},{11,15},{24,28},{25,29},{26,30},{27,31}} | collective-permute-start | bytes 1572872 | tf_op jit(solution)/shard_map/ppermute | solution.py:547
  79.7 14.6 %collective-permute-start.13 = (f32[3,8,2048]{2,1,0:T(8,128)S(1)}, f32[3,8,2048]{2,1,0:T(8,128)S(1)}, u32[]{:S(2)}, u32[]{:S(2)}) collective-permute-start(f32[3,8,2048]{2,1,0:T(8,128)S(1)} %get-tuple-element.152), channel_id=1, source_target_pairs={{12,13},{13,14},{14,15},{15,12},{28,29},{29,30},{30,31},{31,28}} | collective-permute-start | bytes 589832 | tf_op jit(solution)/shard_map/ppermute | solution.py:538
  81.6 15.2 %collective-permute-start.14 = (f32[3,8,2048]{2,1,0:T(8,128)S(1)}, f32[3,8,2048]{2,1,0:T(8,128)S(1)}, u32[]{:S(2)}, u32[]{:S(2)}) collective-permute-start(f32[3,8,2048]{2,1,0:T(8,128)S(1)} %get-tuple-element.154), channel_id=1, source_target_pairs={{12,14},{13,15},{14,12},{15,13},{28,30},{29,31},{30,28},{31,29}} | collective-permute-start | bytes 589832 | tf_op jit(solution)/shard_map/ppermute | solution.py:538
  86.8 11.0 %collective-permute-start.15 = (f32[3,8,2048]{2,1,0:T(8,128)S(1)}, f32[3,8,2048]{2,1,0:T(8,128)S(1)}, u32[]{:S(2)}, u32[]{:S(2)}) collective-permute-start(f32[3,8,2048]{2,1,0:T(8,128)S(1)} %get-tuple-element.153), channel_id=1, source_target_pairs={{12,15},{13,12},{14,13},{15,14},{28,31},{29,28},{30,29},{31,30}} | collective-permute-start | bytes 589832 | tf_op jit(solution)/shard_map/ppermute | solution.py:538
  89.3 8.5 %collective-permute-start.10 = (f32[3,8,2048]{2,1,0:T(8,128)S(1)}, f32[3,8,2048]{2,1,0:T(8,128)S(1)}, u32[]{:S(2)}, u32[]{:S(2)}) collective-permute-start(f32[3,8,2048]{2,1,0:T(8,128)S(1)} %get-tuple-element.149), channel_id=1, source_target_pairs={{0,1},{1,2},{2,3},{3,0},{4,5},{5,6},{6,7},{7,4},{8,9},{9,10},{10,1... | collective-permute-start | bytes 589832 | tf_op jit(solution)/shard_map/ppermute | solution.py:538
  90.0 7.8 %collective-permute-start.11 = (f32[3,8,2048]{2,1,0:T(8,128)S(1)}, f32[3,8,2048]{2,1,0:T(8,128)S(1)}, u32[]{:S(2)}, u32[]{:S(2)}) collective-permute-start(f32[3,8,2048]{2,1,0:T(8,128)S(1)} %get-tuple-element.151), channel_id=1, source_target_pairs={{0,2},{1,3},{2,0},{3,1},{4,6},{5,7},{6,4},{7,5},{8,10},{9,11},{10,... | collective-permute-start | bytes 589832 | tf_op jit(solution)/shard_map/ppermute | solution.py:538
  94.3 3.5 %collective-permute-start.12 = (f32[3,8,2048]{2,1,0:T(8,128)S(1)}, f32[3,8,2048]{2,1,0:T(8,128)S(1)}, u32[]{:S(2)}, u32[]{:S(2)}) collective-permute-start(f32[3,8,2048]{2,1,0:T(8,128)S(1)} %get-tuple-element.150), channel_id=1, source_target_pairs={{0,3},{1,0},{2,1},{3,2},{4,7},{5,4},{6,5},{7,6},{8,11},{9,8},{10,9... | collective-permute-start | bytes 589832 | tf_op jit(solution)/shard_map/ppermute | solution.py:538

commit v10 on v9

--- a/solution.py
+++ b/solution.py
@@ -501,7 +501,7 @@
     strip_count = lax.axis_size("strip")
     consts = fast_constants(line_len)
     region_f = region_index.astype(jnp.float32)
-    early = [d for d in range(segment_count) if d != 1]
+    early = list(range(segment_count))
 
     def with_surface(target):
         return jnp.concatenate(
@@ -516,9 +516,6 @@
     omega = lax.dynamic_index_in_dim(omegas, strip_no, 0, keepdims=False)
     table, mult = section_tables(omega, region_speed, fd_coeff, ref_region, jnp.asarray(consts[3]))
     image = jnp.zeros((strip_count, steps, rows_here, line_len), jnp.float32)
-    regions_b = regions_a
-    if segment_count > 1:
-        token = lax.ppermute(gathered[0, 0:8, 0:LANE], "depth", [(0, 1)])
 
     def sweep(regions):
         def live(wave, image):
@@ -541,16 +538,9 @@
 
     arrived = []
     for tick_no in range(segment_count):
-        regions = regions_b if tick_no == 1 else regions_a
-        wave, image = lax.cond(segment_no == tick_no, sweep(regions), idle, wave, image)
+        wave, image = lax.cond(segment_no == tick_no, sweep(regions_a), idle, wave, image)
         if tick_no + 1 < segment_count:
             wave = lax.ppermute(wave, "depth", [(tick_no, tick_no + 1)])
-        if tick_no == 0 and segment_count > 1:
-            held, token, _ = lax.optimization_barrier((region_f, token, image))
-            held = held + 0.0 * token[0, 0]
-            regions_b = gather_strips(
-                lambda target: held, held, [1], strip_no, strip_count, rows_here
-            ).astype(jnp.int32)
         if tick_no == segment_count - 2:
             wave, image = lax.optimization_barrier((wave, image))
             arrived += freq_sum(image, range(segment_count - 1))

time: 99.3 us -> 99.4 us (level)
  waiting for transfers between devices: 52.5 us -> 65.7 us
  starting transfers between devices: 27.3 us -> 17.1 us
  other arithmetic: 5.21 us -> 4.21 us
    ppermute x3, waiting for transfers between devices: 27 us -> 35.3 us  [shards(): wave = lax.ppermute(wave, 'depth', [(tick_no, tick_no + 1)])]
    ppermute x6 -> x3, starting transfers between devices: 11.5 us -> 3.83 us  [gather_strips(): lax.ppermute(piece_of(target), ('depth', 'strip'), strip_pairs(depths, st...]
    ppermute x6 -> x3, waiting for transfers between devices: 19.1 us -> 24.1 us  [gather_strips(): lax.ppermute(piece_of(target), ('depth', 'strip'), strip_pairs(depths, st...]
    dynamic_update_slice x6 -> x3, local copies, waits for them, and re-layouts: 1.11 us -> 0.08 us  [gather_strips(): full = lax.dynamic_update_slice(full, got, (0, source * rows_here, 0))]
  transfers between devices with their start and end apart: 16 -> 12, of which waited for: 6 -> 6; matrix products, arithmetic and copies ran while one was open for 6% -> 4% of each run, Pallas kernels for 0% -> 0%
where the time goes in v10:
time: 99.4 us; the launch traced here: 99 us
  waiting for transfers between devices  65.7 us (66%)
  starting transfers between devices  17.1 us (17%)
  Pallas kernels  7.72 us (8%)
  other arithmetic  4.21 us (4%)
  local copies, waits for them, and re-layouts  3.82 us (4%)
    ppermute x3, waiting for transfers between devices, shards(): wave = lax.ppermute(wave, 'depth', [(tick_no, tick_no + 1)])  35.3 us
    ppermute x3, waiting for transfers between devices, gather_strips(): lax.ppermute(piece_of(target), ('depth', 'strip'), strip_pairs(depths, st...  24.1 us
    ppermute x6, starting transfers between devices, freq_sum(): lax.ppermute(piece, ('depth', 'strip'), strip_pairs(depths, strip_count,...  10.5 us
    pallas_call x1, Pallas kernels, run_section(): pl.pallas_call(lambda *refs: section_kernel(*refs, table_len=table_len),...  7.72 us
    ppermute x6, waiting for transfers between devices, freq_sum(): lax.ppermute(piece, ('depth', 'strip'), strip_pairs(depths, strip_count,...  6.4 us
    ppermute x3, starting transfers between devices, gather_strips(): lax.ppermute(piece_of(target), ('depth', 'strip'), strip_pairs(depths, st...  3.83 us
    ppermute x3, starting transfers between devices, shards(): wave = lax.ppermute(wave, 'depth', [(tick_no, tick_no + 1)])  2.68 us
  transfers between devices with their start and end apart: 12, of which 6 were waited for; matrix products, arithmetic and copies ran while one was open for 4% of the time, Pallas kernels for 0%

profile of v10, /device:TPU:11, one launch (start us, length us, event | category | flops | bytes accessed | tf_op | source)
XLA Modules:
  0.0 99.0 jit_solution(8369310057432415751)
XLA Ops:
  0.0 0.9 convert_element_type.22
  1.0 1.1 %dynamic-slice_bitcast_fusion.6 = (f32[2,8,2048]{2,1,0:T(8,128)S(1)}, f32[2,8,2048]{2,1,0:T(8,128)S(1)}, f32[2,8,2048]{2,1,0:T(8,128)S(1)}, f32[2,8,2048]{2,1,0:T(8,128)S(1)}) fusion(f32[2,4,8,2048]{3,2,1,0:T(8,128)} %param.20, s32[]{:T(128)S(6)} %select_n.88, s32[]{:T(128)S(6)} %select_n.80, s32[]{:T(128)S(6)} %select_n.77, s32[]{:T(128)S(6)} %select_n.84), kind=kLoop, calls=%fused_computation.19 | loop fusion | bytes 1048592 | tf_op jit(solution)/shard_map/jit(dynamic_index_in_dim)/squeeze | solution.py:508
  2.1 0.1 broadcast_in_dim.6
  2.3 0.1 pad_maximum_fusion
  2.4 1.3 %collective-permute-start = (f32[5,8,2048]{2,1,0:T(8,128)S(1)}, f32[5,8,2048]{2,1,0:T(8,128)S(1)}, u32[]{:S(2)}, u32[]{:S(2)}) collective-permute-start(f32[5,8,2048]{2,1,0:T(8,128)S(1)} %get-tuple-element.154), channel_id=1, source_target_pairs={{0,1},{1,2},{2,3},{3,0},{4,5},{5,6},{6,7},{7,4},{8,9},{9,10},{10,1... | collective-permute-start | bytes 983048 | tf_op jit(solution)/shard_map/ppermute | solution.py:484
  3.8 1.1 %collective-permute-start.1 = (f32[5,8,2048]{2,1,0:T(8,128)S(1)}, f32[5,8,2048]{2,1,0:T(8,128)S(1)}, u32[]{:S(2)}, u32[]{:S(2)}) collective-permute-start(f32[5,8,2048]{2,1,0:T(8,128)S(1)} %get-tuple-element.155), channel_id=1, source_target_pairs={{0,2},{1,3},{2,0},{3,1},{4,6},{5,7},{6,4},{7,5},{8,10},{9,11},{10,... | collective-permute-start | bytes 983048 | tf_op jit(solution)/shard_map/ppermute | solution.py:484
  4.9 1.4 %collective-permute-start.2 = (f32[5,8,2048]{2,1,0:T(8,128)S(1)}, f32[5,8,2048]{2,1,0:T(8,128)S(1)}, u32[]{:S(2)}, u32[]{:S(2)}) collective-permute-start(f32[5,8,2048]{2,1,0:T(8,128)S(1)} %get-tuple-element.153), channel_id=1, source_target_pairs={{0,3},{1,0},{2,1},{3,2},{4,7},{5,4},{6,5},{7,6},{8,11},{9,8},{10,9... | collective-permute-start | bytes 983048 | tf_op jit(solution)/shard_map/ppermute | solution.py:484
  6.3 0.6 dynamic_slice.43
  6.9 0.6 gather_fusion
  7.5 0.8 fusion.16
  8.3 0.7 multiply_multiply_fusion
  9.0 0.7 broadcast_divide_fusion
  9.8 0.2 fusion.11
  10.0 1.1 %collective-permute-done = f32[5,8,2048]{2,1,0:T(8,128)S(1)} collective-permute-done((f32[5,8,2048]{2,1,0:T(8,128)S(1)}, f32[5,8,2048]{2,1,0:T(8,128)S(1)}, u32[]{:S(2)}, u32[]{:S(2)}) %collective-permute-start) | collective-permute-done | bytes 327712 | tf_op jit(solution)/shard_map/ppermute | solution.py:484
  11.1 20.1 %collective-permute-done.1 = f32[5,8,2048]{2,1,0:T(8,128)S(1)} collective-permute-done((f32[5,8,2048]{2,1,0:T(8,128)S(1)}, f32[5,8,2048]{2,1,0:T(8,128)S(1)}, u32[]{:S(2)}, u32[]{:S(2)}) %collective-permute-start.1) | collective-permute-done | bytes 327712 | tf_op jit(solution)/shard_map/ppermute | solution.py:484
  31.3 2.8 %collective-permute-done.2 = f32[5,8,2048]{2,1,0:T(8,128)S(1)} collective-permute-done((f32[5,8,2048]{2,1,0:T(8,128)S(1)}, f32[5,8,2048]{2,1,0:T(8,128)S(1)}, u32[]{:S(2)}, u32[]{:S(2)}) %collective-permute-start.2) | collective-permute-done | bytes 327712 | tf_op jit(solution)/shard_map/ppermute | solution.py:484
  34.3 0.7 copy-done.5
  35.3 0.7 collective-permute-start.3
  36.0 0.7 collective-permute-start.4
  36.8 1.3 %collective-permute-start.5 = (f32[2,32,2048]{2,1,0:T(8,128)S(1)}, f32[2,32,2048]{2,1,0:T(8,128)S(1)}, u32[]{:S(2)}, u32[]{:S(2)}) collective-permute-start(f32[2,32,2048]{2,1,0:T(8,128)S(1)} %get-tuple-element.139), channel_id=1, source_target_pairs={{8,12},{9,13},{10,14},{11,15},{24,28},{25,29},{26,30},{27,31}} | collective-permute-start | bytes 1572872 | tf_op jit(solution)/shard_map/ppermute | solution.py:543
  38.1 35.3 %collective-permute-done.5 = f32[2,32,2048]{2,1,0:T(8,128)S(1)} collective-permute-done((f32[2,32,2048]{2,1,0:T(8,128)S(1)}, f32[2,32,2048]{2,1,0:T(8,128)S(1)}, u32[]{:S(2)}, u32[]{:S(2)}) %collective-permute-start.5) | collective-permute-done | bytes 524320 | tf_op jit(solution)/shard_map/ppermute | solution.py:543
  73.4 7.7 %conditional.7 = (f32[4,3,8,2048]{3,2,1,0:T(8,128)S(1)}) conditional(s32[]{:T(128)} %convert_element_type.18, f32[4,3,8,2048]{3,2,1,0:T(8,128)S(1)} %get-tuple-element.141, (f32[72]{0:T(128)S(1)}, f32[2,32,2048]{2,1,0:T(8,128)S(1)}, s32[3,32,2048]{2,1,0:T(8,128)S(1)}, f32[3,2,16,128]{3,2,1,0:T(8,128)S(1)}, f32[2,16,128]{2,1,0:T(8,128)S(1)}, ...), branch_computations={%region_6.7_spmd, %region_7.8_spmd} | conditional | flops 1286602752 | bytes 4718600 | solution.py:541
  73.4 7.7 %branch_1_fun.7 = (f32[2,32,2048]{2,1,0:T(8,128)}, f32[4,3,8,2048]{3,2,1,0:T(8,128)S(1)}) custom-call(f32[72]{0:T(128)S(1)} %get-tuple-element.117.refs_0_, f32[2,32,2048]{2,1,0:T(8,128)S(1)} %get-tuple-element.118.refs_1_, s32[3,32,2048]{2,1,0:T(8,128)S(1)} %get-tuple-element.119.refs_2_, f32[3,2,16,128]{3,2,1,0:T(8,128)S(1)} %get-tuple-element.120.refs_3_, ...), custom_call_target="tpu_custom_call" | custom-call | flops 1286602752 | bytes 4718592 | tf_op jit(solution)/shard_map/cond/branch_1_fun/pallas_call | solution.py:394
  81.1 3.3 %collective-permute-start.10 = (f32[3,8,2048]{2,1,0:T(8,128)S(1)}, f32[3,8,2048]{2,1,0:T(8,128)S(1)}, u32[]{:S(2)}, u32[]{:S(2)}) collective-permute-start(f32[3,8,2048]{2,1,0:T(8,128)S(1)} %get-tuple-element.148), channel_id=1, source_target_pairs={{12,14},{13,15},{14,12},{15,13},{28,30},{29,31},{30,28},{31,29}} | collective-permute-start | bytes 589832 | tf_op jit(solution)/shard_map/ppermute | solution.py:535
  84.4 1.9 %collective-permute-start.11 = (f32[3,8,2048]{2,1,0:T(8,128)S(1)}, f32[3,8,2048]{2,1,0:T(8,128)S(1)}, u32[]{:S(2)}, u32[]{:S(2)}) collective-permute-start(f32[3,8,2048]{2,1,0:T(8,128)S(1)} %get-tuple-element.147), channel_id=1, source_target_pairs={{12,15},{13,12},{14,13},{15,14},{28,31},{29,28},{30,29},{31,30}} | collective-permute-start | bytes 589832 | tf_op jit(solution)/shard_map/ppermute | solution.py:535
  86.3 3.4 %collective-permute-start.9 = (f32[3,8,2048]{2,1,0:T(8,128)S(1)}, f32[3,8,2048]{2,1,0:T(8,128)S(1)}, u32[]{:S(2)}, u32[]{:S(2)}) collective-permute-start(f32[3,8,2048]{2,1,0:T(8,128)S(1)} %get-tuple-element.146), channel_id=1, source_target_pairs={{12,13},{13,14},{14,15},{15,12},{28,29},{29,30},{30,31},{31,28}} | collective-permute-start | bytes 589832 | tf_op jit(solution)/shard_map/ppermute | solution.py:535
  89.8 0.7 collective-permute-start.6
  90.4 0.7 collective-permute-start.7
  91.1 3.4 %collective-permute-done.10 = f32[3,8,2048]{2,1,0:T(8,128)S(1)} collective-permute-done((f32[3,8,2048]{2,1,0:T(8,128)S(1)}, f32[3,8,2048]{2,1,0:T(8,128)S(1)}, u32[]{:S(2)}, u32[]{:S(2)}) %collective-permute-start.10) | collective-permute-done | bytes 196640 | tf_op jit(solution)/shard_map/ppermute | solution.py:535
  94.5 0.7 collective-permute-start.8
  95.2 3.0 %collective-permute-done.11 = f32[3,8,2048]{2,1,0:T(8,128)S(1)} collective-permute-done((f32[3,8,2048]{2,1,0:T(8,128)S(1)}, f32[3,8,2048]{2,1,0:T(8,128)S(1)}, u32[]{:S(2)}, u32[]{:S(2)}) %collective-permute-start.11) | collective-permute-done | bytes 196640 | tf_op jit(solution)/shard_map/ppermute | solution.py:535
  98.2 0.8 fusion.5
  (43 shorter events, 0.8 us)
Async XLA Ops:
  2.2 4.0 %copy-start = (f32[4]{0:T(128)S(1)}, f32[4]{0:T(128)}, u32[]{:S(2)}) copy-start(f32[4]{0:T(128)} %param.21) | copy-start | bytes 52
  2.3 4.6 %copy-start.1 = (f32[8]{0:T(128)S(1)}, f32[8]{0:T(128)}, u32[]{:S(2)}) copy-start(f32[8]{0:T(128)} %param.22) | copy-start | bytes 100
  2.3 4.6 %copy-start.2 = (s32[3]{0:T(128)S(1)}, s32[3]{0:T(128)}, u32[]{:S(2)}) copy-start(s32[3]{0:T(128)} %param.25) | copy-start | bytes 40
  2.3 6.7 %copy-start.3 = (f32[8]{0:T(128)S(1)}, f32[8]{0:T(128)}, u32[]{:S(2)}) copy-start(f32[8]{0:T(128)} %param.23) | copy-start | bytes 100
  2.3 7.5 %copy-start.4 = (f32[16,128]{1,0:T(8,128)S(1)}, f32[16,128]{1,0:T(8,128)}, u32[]{:S(2)}) copy-start(f32[16,128]{1,0:T(8,128)} %constant.128) | copy-start | bytes 24580
  2.4 8.6 %collective-permute-start = (f32[5,8,2048]{2,1,0:T(8,128)S(1)}, f32[5,8,2048]{2,1,0:T(8,128)S(1)}, u32[]{:S(2)}, u32[]{:S(2)}) collective-permute-start(f32[5,8,2048]{2,1,0:T(8,128)S(1)} %get-tuple-element.154), channel_id=1, source_target_pairs={{0,1},{1,2},{2,3},{3,0},{4,5},{5,6},{6,7},{7,4},{8,9},{9,10},{10,1... | collective-permute-start | bytes 983048 | tf_op jit(solution)/shard_map/ppermute | solution.py:484
  3.8 27.4 %collective-permute-start.1 = (f32[5,8,2048]{2,1,0:T(8,128)S(1)}, f32[5,8,2048]{2,1,0:T(8,128)S(1)}, u32[]{:S(2)}, u32[]{:S(2)}) collective-permute-start(f32[5,8,2048]{2,1,0:T(8,128)S(1)} %get-tuple-element.155), channel_id=1, source_target_pairs={{0,2},{1,3},{2,0},{3,1},{4,6},{5,7},{6,4},{7,5},{8,10},{9,11},{10,... | collective-permute-start | bytes 983048 | tf_op jit(solution)/shard_map/ppermute | solution.py:484
  4.9 29.2 %collective-permute-start.2 = (f32[5,8,2048]{2,1,0:T(8,128)S(1)}, f32[5,8,2048]{2,1,0:T(8,128)S(1)}, u32[]{:S(2)}, u32[]{:S(2)}) collective-permute-start(f32[5,8,2048]{2,1,0:T(8,128)S(1)} %get-tuple-element.153), channel_id=1, source_target_pairs={{0,3},{1,0},{2,1},{3,2},{4,7},{5,4},{6,5},{7,6},{8,11},{9,8},{10,9... | collective-permute-start | bytes 983048 | tf_op jit(solution)/shard_map/ppermute | solution.py:484
  34.1 0.9 copy-start.5
  34.1 1.0 copy-start.6
  34.1 1.0 %copy-start.7 = (bf16[256,256]{1,0:T(8,128)(2,1)S(1)}, bf16[256,256]{1,0:T(8,128)(2,1)}, u32[]{:S(2)}) copy-start(bf16[256,256]{1,0:T(8,128)(2,1)} %constant.123.clone) | copy-start | bytes 393220
  34.2 1.1 %copy-start.8 = (bf16[256,256]{1,0:T(8,128)(2,1)S(1)}, bf16[256,256]{1,0:T(8,128)(2,1)}, u32[]{:S(2)}) copy-start(bf16[256,256]{1,0:T(8,128)(2,1)} %constant.124.clone) | copy-start | bytes 393220
  34.2 1.1 %copy-start.9 = (f32[2,16,128]{2,1,0:T(8,128)S(1)}, f32[2,16,128]{2,1,0:T(8,128)}, u32[]{:S(2)}) copy-start(f32[2,16,128]{2,1,0:T(8,128)} %constant.120.clone) | copy-start | bytes 49156
  35.3 0.7 collective-permute-start.3
  36.0 0.7 collective-permute-start.4
  36.8 36.6 %collective-permute-start.5 = (f32[2,32,2048]{2,1,0:T(8,128)S(1)}, f32[2,32,2048]{2,1,0:T(8,128)S(1)}, u32[]{:S(2)}, u32[]{:S(2)}) collective-permute-start(f32[2,32,2048]{2,1,0:T(8,128)S(1)} %get-tuple-element.139), channel_id=1, source_target_pairs={{8,12},{9,13},{10,14},{11,15},{24,28},{25,29},{26,30},{27,31}} | collective-permute-start | bytes 1572872 | tf_op jit(solution)/shard_map/ppermute | solution.py:543
  81.1 13.4 %collective-permute-start.10 = (f32[3,8,2048]{2,1,0:T(8,128)S(1)}, f32[3,8,2048]{2,1,0:T(8,128)S(1)}, u32[]{:S(2)}, u32[]{:S(2)}) collective-permute-start(f32[3,8,2048]{2,1,0:T(8,128)S(1)} %get-tuple-element.148), channel_id=1, source_target_pairs={{12,14},{13,15},{14,12},{15,13},{28,30},{29,31},{30,28},{31,29}} | collective-permute-start | bytes 589832 | tf_op jit(solution)/shard_map/ppermute | solution.py:535
  84.4 13.8 %collective-permute-start.11 = (f32[3,8,2048]{2,1,0:T(8,128)S(1)}, f32[3,8,2048]{2,1,0:T(8,128)S(1)}, u32[]{:S(2)}, u32[]{:S(2)}) collective-permute-start(f32[3,8,2048]{2,1,0:T(8,128)S(1)} %get-tuple-element.147), channel_id=1, source_target_pairs={{12,15},{13,12},{14,13},{15,14},{28,31},{29,28},{30,29},{31,30}} | collective-permute-start | bytes 589832 | tf_op jit(solution)/shard_map/ppermute | solution.py:535
  86.3 11.8 %collective-permute-start.9 = (f32[3,8,2048]{2,1,0:T(8,128)S(1)}, f32[3,8,2048]{2,1,0:T(8,128)S(1)}, u32[]{:S(2)}, u32[]{:S(2)}) collective-permute-start(f32[3,8,2048]{2,1,0:T(8,128)S(1)} %get-tuple-element.146), channel_id=1, source_target_pairs={{12,13},{13,14},{14,15},{15,12},{28,29},{29,30},{30,31},{31,28}} | collective-permute-start | bytes 589832 | tf_op jit(solution)/shard_map/ppermute | solution.py:535
  89.8 8.4 %collective-permute-start.6 = (f32[3,8,2048]{2,1,0:T(8,128)S(1)}, f32[3,8,2048]{2,1,0:T(8,128)S(1)}, u32[]{:S(2)}, u32[]{:S(2)}) collective-permute-start(f32[3,8,2048]{2,1,0:T(8,128)S(1)} %get-tuple-element.143), channel_id=1, source_target_pairs={{0,1},{1,2},{2,3},{3,0},{4,5},{5,6},{6,7},{7,4},{8,9},{9,10},{10,1... | collective-permute-start | bytes 589832 | tf_op jit(solution)/shard_map/ppermute | solution.py:535
  90.4 7.7 %collective-permute-start.7 = (f32[3,8,2048]{2,1,0:T(8,128)S(1)}, f32[3,8,2048]{2,1,0:T(8,128)S(1)}, u32[]{:S(2)}, u32[]{:S(2)}) collective-permute-start(f32[3,8,2048]{2,1,0:T(8,128)S(1)} %get-tuple-element.145), channel_id=1, source_target_pairs={{0,2},{1,3},{2,0},{3,1},{4,6},{5,7},{6,4},{7,5},{8,10},{9,11},{10,... | collective-permute-start | bytes 589832 | tf_op jit(solution)/shard_map/ppermute | solution.py:535
  94.5 3.6 %collective-permute-start.8 = (f32[3,8,2048]{2,1,0:T(8,128)S(1)}, f32[3,8,2048]{2,1,0:T(8,128)S(1)}, u32[]{:S(2)}, u32[]{:S(2)}) collective-permute-start(f32[3,8,2048]{2,1,0:T(8,128)S(1)} %get-tuple-element.144), channel_id=1, source_target_pairs={{0,3},{1,0},{2,1},{3,2},{4,7},{5,4},{6,5},{7,6},{8,11},{9,8},{10,9... | collective-permute-start | bytes 589832 | tf_op jit(solution)/shard_map/ppermute | solution.py:535

commit v11 on v10

--- a/solution.py
+++ b/solution.py
@@ -543,7 +543,9 @@
             wave = lax.ppermute(wave, "depth", [(tick_no, tick_no + 1)])
         if tick_no == segment_count - 2:
             wave, image = lax.optimization_barrier((wave, image))
-            arrived += freq_sum(image, range(segment_count - 1))
+            group = freq_sum(image, range(segment_count - 1))
+            wave, group = lax.optimization_barrier((wave, group))
+            arrived += list(group)
     arrived += freq_sum(image, [segment_count - 1])
     total = lax.dynamic_index_in_dim(image, strip_no, 0, keepdims=False)
     for piece in arrived:

time: 99.4 us -> 99.9 us (level)
  the two profiles are of different devices: /device:TPU:11 before, /device:TPU:3 now
where the time goes in v11:
time: 99.9 us; the launch traced here: 99.5 us
  waiting for transfers between devices  58.9 us (59%)
  starting transfers between devices  24.4 us (24%)
  Pallas kernels  7.79 us (8%)
  other arithmetic  4.2 us (4%)
  local copies, waits for them, and re-layouts  3.81 us (4%)
    ppermute x3, waiting for transfers between devices, shards(): wave = lax.ppermute(wave, 'depth', [(tick_no, tick_no + 1)])  35.4 us
    ppermute x3, waiting for transfers between devices, gather_strips(): lax.ppermute(piece_of(target), ('depth', 'strip'), strip_pairs(depths, st...  17.2 us
    ppermute x6, starting transfers between devices, freq_sum(): lax.ppermute(piece, ('depth', 'strip'), strip_pairs(depths, strip_count,...  17 us
    pallas_call x1, Pallas kernels, run_section(): pl.pallas_call(lambda *refs: section_kernel(*refs, table_len=table_len),...  7.79 us
    ppermute x6, waiting for transfers between devices, freq_sum(): lax.ppermute(piece, ('depth', 'strip'), strip_pairs(depths, strip_count,...  6.29 us
    ppermute x3, starting transfers between devices, gather_strips(): lax.ppermute(piece_of(target), ('depth', 'strip'), strip_pairs(depths, st...  4.73 us
    ppermute x3, starting transfers between devices, shards(): wave = lax.ppermute(wave, 'depth', [(tick_no, tick_no + 1)])  2.68 us
  transfers between devices with their start and end apart: 12, of which 6 were waited for; matrix products, arithmetic and copies ran while one was open for 4% of the time, Pallas kernels for 0%

profile of v11, /device:TPU:3, one launch (start us, length us, event | category | flops | bytes accessed | tf_op | source)
XLA Modules:
  0.0 99.5 jit_solution(18419841543428567231)
XLA Ops:
  0.0 0.9 convert_element_type.22
  1.0 1.1 %dynamic-slice_bitcast_fusion.6 = (f32[2,8,2048]{2,1,0:T(8,128)S(1)}, f32[2,8,2048]{2,1,0:T(8,128)S(1)}, f32[2,8,2048]{2,1,0:T(8,128)S(1)}, f32[2,8,2048]{2,1,0:T(8,128)S(1)}) fusion(f32[2,4,8,2048]{3,2,1,0:T(8,128)} %param.20, s32[]{:T(128)S(6)} %select_n.88, s32[]{:T(128)S(6)} %select_n.80, s32[]{:T(128)S(6)} %select_n.77, s32[]{:T(128)S(6)} %select_n.84), kind=kLoop, calls=%fused_computation.19 | loop fusion | bytes 1048592 | tf_op jit(solution)/shard_map/jit(dynamic_index_in_dim)/squeeze | solution.py:508
  2.1 0.1 broadcast_in_dim.6
  2.3 0.1 pad_maximum_fusion
  2.4 1.3 %collective-permute-start = (f32[5,8,2048]{2,1,0:T(8,128)S(1)}, f32[5,8,2048]{2,1,0:T(8,128)S(1)}, u32[]{:S(2)}, u32[]{:S(2)}) collective-permute-start(f32[5,8,2048]{2,1,0:T(8,128)S(1)} %get-tuple-element.162), channel_id=1, source_target_pairs={{0,1},{1,2},{2,3},{3,0},{4,5},{5,6},{6,7},{7,4},{8,9},{9,10},{10,1... | collective-permute-start | bytes 983048 | tf_op jit(solution)/shard_map/ppermute | solution.py:484
  3.8 2.3 %collective-permute-start.1 = (f32[5,8,2048]{2,1,0:T(8,128)S(1)}, f32[5,8,2048]{2,1,0:T(8,128)S(1)}, u32[]{:S(2)}, u32[]{:S(2)}) collective-permute-start(f32[5,8,2048]{2,1,0:T(8,128)S(1)} %get-tuple-element.163), channel_id=1, source_target_pairs={{0,2},{1,3},{2,0},{3,1},{4,6},{5,7},{6,4},{7,5},{8,10},{9,11},{10,... | collective-permute-start | bytes 983048 | tf_op jit(solution)/shard_map/ppermute | solution.py:484
  6.1 1.1 %collective-permute-start.2 = (f32[5,8,2048]{2,1,0:T(8,128)S(1)}, f32[5,8,2048]{2,1,0:T(8,128)S(1)}, u32[]{:S(2)}, u32[]{:S(2)}) collective-permute-start(f32[5,8,2048]{2,1,0:T(8,128)S(1)} %get-tuple-element.161), channel_id=1, source_target_pairs={{0,3},{1,0},{2,1},{3,2},{4,7},{5,4},{6,5},{7,6},{8,11},{9,8},{10,9... | collective-permute-start | bytes 983048 | tf_op jit(solution)/shard_map/ppermute | solution.py:484
  7.2 0.6 dynamic_slice.43
  7.8 0.6 gather_fusion
  8.4 0.8 fusion.16
  9.2 0.7 multiply_multiply_fusion
  9.9 0.7 broadcast_divide_fusion
  10.7 0.2 fusion.11
  10.9 2.2 %collective-permute-done = f32[5,8,2048]{2,1,0:T(8,128)S(1)} collective-permute-done((f32[5,8,2048]{2,1,0:T(8,128)S(1)}, f32[5,8,2048]{2,1,0:T(8,128)S(1)}, u32[]{:S(2)}, u32[]{:S(2)}) %collective-permute-start) | collective-permute-done | bytes 327712 | tf_op jit(solution)/shard_map/ppermute | solution.py:484
  13.1 15.0 %collective-permute-done.1 = f32[5,8,2048]{2,1,0:T(8,128)S(1)} collective-permute-done((f32[5,8,2048]{2,1,0:T(8,128)S(1)}, f32[5,8,2048]{2,1,0:T(8,128)S(1)}, u32[]{:S(2)}, u32[]{:S(2)}) %collective-permute-start.1) | collective-permute-done | bytes 327712 | tf_op jit(solution)/shard_map/ppermute | solution.py:484
  28.3 0.7 copy-done.5
  29.3 0.7 collective-permute-start.3
  30.1 0.7 collective-permute-start.4
  30.8 1.3 %collective-permute-start.5 = (f32[2,32,2048]{2,1,0:T(8,128)S(1)}, f32[2,32,2048]{2,1,0:T(8,128)S(1)}, u32[]{:S(2)}, u32[]{:S(2)}) collective-permute-start(f32[2,32,2048]{2,1,0:T(8,128)S(1)} %get-tuple-element.143), channel_id=1, source_target_pairs={{8,12},{9,13},{10,14},{11,15},{24,28},{25,29},{26,30},{27,31}} | collective-permute-start | bytes 1572872 | tf_op jit(solution)/shard_map/ppermute | solution.py:543
  32.1 35.4 %collective-permute-done.5 = f32[2,32,2048]{2,1,0:T(8,128)S(1)} collective-permute-done((f32[2,32,2048]{2,1,0:T(8,128)S(1)}, f32[2,32,2048]{2,1,0:T(8,128)S(1)}, u32[]{:S(2)}, u32[]{:S(2)}) %collective-permute-start.5) | collective-permute-done | bytes 524320 | tf_op jit(solution)/shard_map/ppermute | solution.py:543
  67.5 0.7 collective-permute-start.6
  68.2 0.7 collective-permute-start.7
  68.9 0.7 collective-permute-start.8
  69.6 7.8 %conditional.7 = (f32[4,3,8,2048]{3,2,1,0:T(8,128)S(1)}) conditional(s32[]{:T(128)} %convert_element_type.18, f32[4,3,8,2048]{3,2,1,0:T(8,128)S(1)} %get-tuple-element.145, (f32[72]{0:T(128)S(1)}, f32[2,32,2048]{2,1,0:T(8,128)S(1)}, s32[3,32,2048]{2,1,0:T(8,128)S(1)}, f32[3,2,16,128]{3,2,1,0:T(8,128)S(1)}, f32[2,16,128]{2,1,0:T(8,128)S(1)}, ...), branch_computations={%region_6.7_spmd, %region_7.8_spmd} | conditional | flops 1286602752 | bytes 4718600 | solution.py:541
  69.6 7.8 %branch_1_fun.7 = (f32[2,32,2048]{2,1,0:T(8,128)}, f32[4,3,8,2048]{3,2,1,0:T(8,128)S(1)}) custom-call(f32[72]{0:T(128)S(1)} %get-tuple-element.117.refs_0_, f32[2,32,2048]{2,1,0:T(8,128)S(1)} %get-tuple-element.118.refs_1_, s32[3,32,2048]{2,1,0:T(8,128)S(1)} %get-tuple-element.119.refs_2_, f32[3,2,16,128]{3,2,1,0:T(8,128)S(1)} %get-tuple-element.120.refs_3_, ...), custom_call_target="tpu_custom_call" | custom-call | flops 1286602752 | bytes 4718592 | tf_op jit(solution)/shard_map/cond/branch_1_fun/pallas_call | solution.py:394
  77.5 8.1 %collective-permute-start.10 = (f32[3,8,2048]{2,1,0:T(8,128)S(1)}, f32[3,8,2048]{2,1,0:T(8,128)S(1)}, u32[]{:S(2)}, u32[]{:S(2)}) collective-permute-start(f32[3,8,2048]{2,1,0:T(8,128)S(1)} %get-tuple-element.153), channel_id=1, source_target_pairs={{12,14},{13,15},{14,12},{15,13},{28,30},{29,31},{30,28},{31,29}} | collective-permute-start | bytes 589832 | tf_op jit(solution)/shard_map/ppermute | solution.py:535
  85.6 5.0 %collective-permute-start.11 = (f32[3,8,2048]{2,1,0:T(8,128)S(1)}, f32[3,8,2048]{2,1,0:T(8,128)S(1)}, u32[]{:S(2)}, u32[]{:S(2)}) collective-permute-start(f32[3,8,2048]{2,1,0:T(8,128)S(1)} %get-tuple-element.152), channel_id=1, source_target_pairs={{12,15},{13,12},{14,13},{15,14},{28,31},{29,28},{30,29},{31,30}} | collective-permute-start | bytes 589832 | tf_op jit(solution)/shard_map/ppermute | solution.py:535
  90.6 1.9 %collective-permute-start.9 = (f32[3,8,2048]{2,1,0:T(8,128)S(1)}, f32[3,8,2048]{2,1,0:T(8,128)S(1)}, u32[]{:S(2)}, u32[]{:S(2)}) collective-permute-start(f32[3,8,2048]{2,1,0:T(8,128)S(1)} %get-tuple-element.151), channel_id=1, source_target_pairs={{12,13},{13,14},{14,15},{15,12},{28,29},{29,30},{30,31},{31,28}} | collective-permute-start | bytes 589832 | tf_op jit(solution)/shard_map/ppermute | solution.py:535
  92.5 0.3 collective-permute-done.10
  92.8 0.6 collective-permute-done.11
  93.4 5.4 %collective-permute-done.9 = f32[3,8,2048]{2,1,0:T(8,128)S(1)} collective-permute-done((f32[3,8,2048]{2,1,0:T(8,128)S(1)}, f32[3,8,2048]{2,1,0:T(8,128)S(1)}, u32[]{:S(2)}, u32[]{:S(2)}) %collective-permute-start.9) | collective-permute-done | bytes 196640 | tf_op jit(solution)/shard_map/ppermute | solution.py:535
  98.8 0.8 fusion.5
  (43 shorter events, 0.8 us)
Async XLA Ops:
  2.2 4.9 %copy-start = (f32[4]{0:T(128)S(1)}, f32[4]{0:T(128)}, u32[]{:S(2)}) copy-start(f32[4]{0:T(128)} %param.21) | copy-start | bytes 52
  2.3 5.5 %copy-start.1 = (f32[8]{0:T(128)S(1)}, f32[8]{0:T(128)}, u32[]{:S(2)}) copy-start(f32[8]{0:T(128)} %param.22) | copy-start | bytes 100
  2.3 5.5 %copy-start.2 = (s32[3]{0:T(128)S(1)}, s32[3]{0:T(128)}, u32[]{:S(2)}) copy-start(s32[3]{0:T(128)} %param.25) | copy-start | bytes 40
  2.3 7.6 %copy-start.3 = (f32[8]{0:T(128)S(1)}, f32[8]{0:T(128)}, u32[]{:S(2)}) copy-start(f32[8]{0:T(128)} %param.23) | copy-start | bytes 100
  2.3 8.4 %copy-start.4 = (f32[16,128]{1,0:T(8,128)S(1)}, f32[16,128]{1,0:T(8,128)}, u32[]{:S(2)}) copy-start(f32[16,128]{1,0:T(8,128)} %constant.128) | copy-start | bytes 24580
  2.4 10.7 %collective-permute-start = (f32[5,8,2048]{2,1,0:T(8,128)S(1)}, f32[5,8,2048]{2,1,0:T(8,128)S(1)}, u32[]{:S(2)}, u32[]{:S(2)}) collective-permute-start(f32[5,8,2048]{2,1,0:T(8,128)S(1)} %get-tuple-element.162), channel_id=1, source_target_pairs={{0,1},{1,2},{2,3},{3,0},{4,5},{5,6},{6,7},{7,4},{8,9},{9,10},{10,1... | collective-permute-start | bytes 983048 | tf_op jit(solution)/shard_map/ppermute | solution.py:484
  3.8 24.3 %collective-permute-start.1 = (f32[5,8,2048]{2,1,0:T(8,128)S(1)}, f32[5,8,2048]{2,1,0:T(8,128)S(1)}, u32[]{:S(2)}, u32[]{:S(2)}) collective-permute-start(f32[5,8,2048]{2,1,0:T(8,128)S(1)} %get-tuple-element.163), channel_id=1, source_target_pairs={{0,2},{1,3},{2,0},{3,1},{4,6},{5,7},{6,4},{7,5},{8,10},{9,11},{10,... | collective-permute-start | bytes 983048 | tf_op jit(solution)/shard_map/ppermute | solution.py:484
  6.1 22.0 %collective-permute-start.2 = (f32[5,8,2048]{2,1,0:T(8,128)S(1)}, f32[5,8,2048]{2,1,0:T(8,128)S(1)}, u32[]{:S(2)}, u32[]{:S(2)}) collective-permute-start(f32[5,8,2048]{2,1,0:T(8,128)S(1)} %get-tuple-element.161), channel_id=1, source_target_pairs={{0,3},{1,0},{2,1},{3,2},{4,7},{5,4},{6,5},{7,6},{8,11},{9,8},{10,9... | collective-permute-start | bytes 983048 | tf_op jit(solution)/shard_map/ppermute | solution.py:484
  28.2 0.9 copy-start.5
  28.2 1.0 copy-start.6
  28.2 1.0 %copy-start.7 = (bf16[256,256]{1,0:T(8,128)(2,1)S(1)}, bf16[256,256]{1,0:T(8,128)(2,1)}, u32[]{:S(2)}) copy-start(bf16[256,256]{1,0:T(8,128)(2,1)} %constant.123.clone) | copy-start | bytes 393220
  28.2 1.1 %copy-start.8 = (bf16[256,256]{1,0:T(8,128)(2,1)S(1)}, bf16[256,256]{1,0:T(8,128)(2,1)}, u32[]{:S(2)}) copy-start(bf16[256,256]{1,0:T(8,128)(2,1)} %constant.124.clone) | copy-start | bytes 393220
  28.2 1.1 %copy-start.9 = (f32[2,16,128]{2,1,0:T(8,128)S(1)}, f32[2,16,128]{2,1,0:T(8,128)}, u32[]{:S(2)}) copy-start(f32[2,16,128]{2,1,0:T(8,128)} %constant.120.clone) | copy-start | bytes 49156
  29.3 0.7 collective-permute-start.3
  30.1 0.7 collective-permute-start.4
  30.8 36.7 %collective-permute-start.5 = (f32[2,32,2048]{2,1,0:T(8,128)S(1)}, f32[2,32,2048]{2,1,0:T(8,128)S(1)}, u32[]{:S(2)}, u32[]{:S(2)}) collective-permute-start(f32[2,32,2048]{2,1,0:T(8,128)S(1)} %get-tuple-element.143), channel_id=1, source_target_pairs={{8,12},{9,13},{10,14},{11,15},{24,28},{25,29},{26,30},{27,31}} | collective-permute-start | bytes 1572872 | tf_op jit(solution)/shard_map/ppermute | solution.py:543
  67.5 2.1 %collective-permute-start.6 = (f32[3,8,2048]{2,1,0:T(8,128)S(1)}, f32[3,8,2048]{2,1,0:T(8,128)S(1)}, u32[]{:S(2)}, u32[]{:S(2)}) collective-permute-start(f32[3,8,2048]{2,1,0:T(8,128)S(1)} %get-tuple-element.156), channel_id=1, source_target_pairs={{0,1},{1,2},{2,3},{3,0},{4,5},{5,6},{6,7},{7,4},{8,9},{9,10},{10,1... | collective-permute-start | bytes 589832 | tf_op jit(solution)/shard_map/ppermute | solution.py:535
  68.2 1.4 %collective-permute-start.7 = (f32[3,8,2048]{2,1,0:T(8,128)S(1)}, f32[3,8,2048]{2,1,0:T(8,128)S(1)}, u32[]{:S(2)}, u32[]{:S(2)}) collective-permute-start(f32[3,8,2048]{2,1,0:T(8,128)S(1)} %get-tuple-element.155), channel_id=1, source_target_pairs={{0,2},{1,3},{2,0},{3,1},{4,6},{5,7},{6,4},{7,5},{8,10},{9,11},{10,... | collective-permute-start | bytes 589832 | tf_op jit(solution)/shard_map/ppermute | solution.py:535
  68.9 0.7 collective-permute-start.8
  77.5 15.3 %collective-permute-start.10 = (f32[3,8,2048]{2,1,0:T(8,128)S(1)}, f32[3,8,2048]{2,1,0:T(8,128)S(1)}, u32[]{:S(2)}, u32[]{:S(2)}) collective-permute-start(f32[3,8,2048]{2,1,0:T(8,128)S(1)} %get-tuple-element.153), channel_id=1, source_target_pairs={{12,14},{13,15},{14,12},{15,13},{28,30},{29,31},{30,28},{31,29}} | collective-permute-start | bytes 589832 | tf_op jit(solution)/shard_map/ppermute | solution.py:535
  85.6 7.9 %collective-permute-start.11 = (f32[3,8,2048]{2,1,0:T(8,128)S(1)}, f32[3,8,2048]{2,1,0:T(8,128)S(1)}, u32[]{:S(2)}, u32[]{:S(2)}) collective-permute-start(f32[3,8,2048]{2,1,0:T(8,128)S(1)} %get-tuple-element.152), channel_id=1, source_target_pairs={{12,15},{13,12},{14,13},{15,14},{28,31},{29,28},{30,29},{31,30}} | collective-permute-start | bytes 589832 | tf_op jit(solution)/shard_map/ppermute | solution.py:535
  90.6 8.2 %collective-permute-start.9 = (f32[3,8,2048]{2,1,0:T(8,128)S(1)}, f32[3,8,2048]{2,1,0:T(8,128)S(1)}, u32[]{:S(2)}, u32[]{:S(2)}) collective-permute-start(f32[3,8,2048]{2,1,0:T(8,128)S(1)} %get-tuple-element.151), channel_id=1, source_target_pairs={{12,13},{13,14},{14,15},{15,12},{28,29},{29,30},{30,31},{31,28}} | collective-permute-start | bytes 589832 | tf_op jit(solution)/shard_map/ppermute | solution.py:535

commit v12 on v9

--- a/solution.py
+++ b/solution.py
@@ -517,8 +517,6 @@
     table, mult = section_tables(omega, region_speed, fd_coeff, ref_region, jnp.asarray(consts[3]))
     image = jnp.zeros((strip_count, steps, rows_here, line_len), jnp.float32)
     regions_b = regions_a
-    if segment_count > 1:
-        token = lax.ppermute(gathered[0, 0:8, 0:LANE], "depth", [(0, 1)])
 
     def sweep(regions):
         def live(wave, image):
@@ -546,8 +544,7 @@
         if tick_no + 1 < segment_count:
             wave = lax.ppermute(wave, "depth", [(tick_no, tick_no + 1)])
         if tick_no == 0 and segment_count > 1:
-            held, token, _ = lax.optimization_barrier((region_f, token, image))
-            held = held + 0.0 * token[0, 0]
+            held, _ = lax.optimization_barrier((region_f, image))
             regions_b = gather_strips(
                 lambda target: held, held, [1], strip_no, strip_count, rows_here
             ).astype(jnp.int32)

time: 99.3 us -> 97.7 us (0.984)
  starting transfers between devices: 27.3 us -> 23.5 us
  waiting for transfers between devices: 52.5 us -> 55 us
    ppermute x3, waiting for transfers between devices: 27 us -> 29.5 us  [shards(): wave = lax.ppermute(wave, 'depth', [(tick_no, tick_no + 1)])]
    ppermute x6, starting transfers between devices: 11.5 us -> 9.21 us  [freq_sum(): lax.ppermute(piece, ('depth', 'strip'), strip_pairs(depths, strip_count,...]
  transfers between devices with their start and end apart: 16 -> 15, of which waited for: 6 -> 6; matrix products, arithmetic and copies ran while one was open for 6% -> 6% of each run, Pallas kernels for 0% -> 0%
where the time goes in v12:
time: 97.7 us; the launch traced here: 96.9 us
  waiting for transfers between devices  55 us (56%)
  starting transfers between devices  23.5 us (24%)
  Pallas kernels  7.71 us (8%)
  other arithmetic  5.2 us (5%)
  local copies, waits for them, and re-layouts  4.95 us (5%)
    ppermute x3, waiting for transfers between devices, shards(): wave = lax.ppermute(wave, 'depth', [(tick_no, tick_no + 1)])  29.5 us
    ppermute x6, waiting for transfers between devices, gather_strips(): lax.ppermute(piece_of(target), ('depth', 'strip'), strip_pairs(depths, st...  19.1 us
    ppermute x6, starting transfers between devices, gather_strips(): lax.ppermute(piece_of(target), ('depth', 'strip'), strip_pairs(depths, st...  11.5 us
    ppermute x6, starting transfers between devices, freq_sum(): lax.ppermute(piece, ('depth', 'strip'), strip_pairs(depths, strip_count,...  9.21 us
    pallas_call x1, Pallas kernels, run_section(): pl.pallas_call(lambda *refs: section_kernel(*refs, table_len=table_len),...  7.71 us
    ppermute x6, waiting for transfers between devices, freq_sum(): lax.ppermute(piece, ('depth', 'strip'), strip_pairs(depths, strip_count,...  6.29 us
    ppermute x3, starting transfers between devices, shards(): wave = lax.ppermute(wave, 'depth', [(tick_no, tick_no + 1)])  2.8 us
  transfers between devices with their start and end apart: 15, of which 6 were waited for; matrix products, arithmetic and copies ran while one was open for 6% of the time, Pallas kernels for 0%

profile of v12, /device:TPU:11, one launch (start us, length us, event | category | flops | bytes accessed | tf_op | source)
XLA Modules:
  0.0 96.9 jit_solution(4044328642694212498)
XLA Ops:
  0.0 0.9 convert_element_type.25
  1.0 1.1 %dynamic-slice_bitcast_fusion.6 = (f32[2,8,2048]{2,1,0:T(8,128)S(1)}, f32[2,8,2048]{2,1,0:T(8,128)S(1)}, f32[2,8,2048]{2,1,0:T(8,128)S(1)}, f32[2,8,2048]{2,1,0:T(8,128)S(1)}) fusion(f32[2,4,8,2048]{3,2,1,0:T(8,128)} %param.20, s32[]{:T(128)S(6)} %select_n.98, s32[]{:T(128)S(6)} %select_n.90, s32[]{:T(128)S(6)} %select_n.87, s32[]{:T(128)S(6)} %select_n.94), kind=kLoop, calls=%fused_computation.19 | loop fusion | bytes 1048592 | tf_op jit(solution)/shard_map/jit(dynamic_index_in_dim)/squeeze | solution.py:508
  2.4 3.2 %collective-permute-start = (f32[5,8,2048]{2,1,0:T(8,128)S(1)}, f32[5,8,2048]{2,1,0:T(8,128)}, u32[]{:S(2)}, u32[]{:S(2)}) collective-permute-start(f32[5,8,2048]{2,1,0:T(8,128)S(1)} %get-tuple-element.156), channel_id=1, source_target_pairs={{0,1},{1,2},{2,3},{3,0},{8,9},{9,10},{10,11},{11,8},{12,13},{13,14... | collective-permute-start | bytes 983048 | tf_op jit(solution)/shard_map/ppermute | solution.py:484
  5.7 2.9 %collective-permute-start.1 = (f32[5,8,2048]{2,1,0:T(8,128)S(1)}, f32[5,8,2048]{2,1,0:T(8,128)S(1)}, u32[]{:S(2)}, u32[]{:S(2)}) collective-permute-start(f32[5,8,2048]{2,1,0:T(8,128)S(1)} %get-tuple-element.157), channel_id=1, source_target_pairs={{0,2},{1,3},{2,0},{3,1},{8,10},{9,11},{10,8},{11,9},{12,14},{13,15... | collective-permute-start | bytes 983048 | tf_op jit(solution)/shard_map/ppermute | solution.py:484
  8.6 3.4 %collective-permute-start.2 = (f32[5,8,2048]{2,1,0:T(8,128)S(1)}, f32[5,8,2048]{2,1,0:T(8,128)S(1)}, u32[]{:S(2)}, u32[]{:S(2)}) collective-permute-start(f32[5,8,2048]{2,1,0:T(8,128)S(1)} %get-tuple-element.155), channel_id=1, source_target_pairs={{0,3},{1,0},{2,1},{3,2},{8,11},{9,8},{10,9},{11,10},{12,15},{13,12... | collective-permute-start | bytes 983048 | tf_op jit(solution)/shard_map/ppermute | solution.py:484
  12.0 0.6 dynamic_slice.43
  12.7 0.6 gather_fusion
  13.3 0.8 fusion.16
  14.1 0.7 multiply_multiply_fusion
  14.8 0.7 broadcast_divide_fusion
  15.8 1.0 %constant_dynamic-update-slice_fusion.6 = f32[5,32,2048]{2,1,0:T(8,128)S(1)} fusion(f32[5,32,2048]{2,1,0:T(8,128)S(1)} %get-tuple-element.158, f32[5,8,2048]{2,1,0:T(8,128)} %collective-permute-done, s32[]{:T(128)S(6)} %select_n.92), kind=kLoop, calls=%fused_computation.42 | loop fusion | bytes 655364 | tf_op jit(solution)/shard_map/dynamic_update_slice | solution.py:488
  16.8 16.3 %collective-permute-done.1 = f32[5,8,2048]{2,1,0:T(8,128)S(1)} collective-permute-done((f32[5,8,2048]{2,1,0:T(8,128)S(1)}, f32[5,8,2048]{2,1,0:T(8,128)S(1)}, u32[]{:S(2)}, u32[]{:S(2)}) %collective-permute-start.1) | collective-permute-done | bytes 327712 | tf_op jit(solution)/shard_map/ppermute | solution.py:484
  33.1 2.8 %collective-permute-done.2 = f32[5,8,2048]{2,1,0:T(8,128)S(1)} collective-permute-done((f32[5,8,2048]{2,1,0:T(8,128)S(1)}, f32[5,8,2048]{2,1,0:T(8,128)S(1)}, u32[]{:S(2)}, u32[]{:S(2)}) %collective-permute-start.2) | collective-permute-done | bytes 327712 | tf_op jit(solution)/shard_map/ppermute | solution.py:484
  36.1 0.7 copy-done.5
  37.1 0.7 collective-permute-start.4
  37.8 0.7 collective-permute-start.5
  38.5 0.7 collective-permute-start.6
  39.2 0.7 collective-permute-start.3
  40.1 1.0 %convert_element_type.27 = s32[3,32,2048]{2,1,0:T(8,128)} convert(f32[3,32,2048]{2,1,0:T(8,128)S(1)} %constant_dynamic-update-slice_fusion) | non-fusion elementwise | flops 196608 | bytes 1572864 | tf_op jit(solution)/shard_map/convert_element_type | solution.py:550
  41.1 0.7 collective-permute-start.7
  41.8 1.4 %collective-permute-start.8 = (f32[2,32,2048]{2,1,0:T(8,128)S(1)}, f32[2,32,2048]{2,1,0:T(8,128)S(1)}, u32[]{:S(2)}, u32[]{:S(2)}) collective-permute-start(f32[2,32,2048]{2,1,0:T(8,128)S(1)} %get-tuple-element.141), channel_id=1, source_target_pairs={{8,12},{9,13},{10,14},{11,15},{24,28},{25,29},{26,30},{27,31}} | collective-permute-start | bytes 1572872 | tf_op jit(solution)/shard_map/ppermute | solution.py:545
  43.2 29.5 %collective-permute-done.8 = f32[2,32,2048]{2,1,0:T(8,128)S(1)} collective-permute-done((f32[2,32,2048]{2,1,0:T(8,128)S(1)}, f32[2,32,2048]{2,1,0:T(8,128)S(1)}, u32[]{:S(2)}, u32[]{:S(2)}) %collective-permute-start.8) | collective-permute-done | bytes 524320 | tf_op jit(solution)/shard_map/ppermute | solution.py:545
  72.8 7.7 %conditional.7 = (f32[4,3,8,2048]{3,2,1,0:T(8,128)S(1)}) conditional(s32[]{:T(128)} %convert_element_type.21, f32[4,3,8,2048]{3,2,1,0:T(8,128)S(1)} %get-tuple-element.143, (f32[72]{0:T(128)S(1)}, f32[2,32,2048]{2,1,0:T(8,128)S(1)}, s32[3,32,2048]{2,1,0:T(8,128)S(1)}, f32[3,2,16,128]{3,2,1,0:T(8,128)S(1)}, f32[2,16,128]{2,1,0:T(8,128)S(1)}, ...), branch_computations={%region_6.7_spmd, %region_7.8_spmd} | conditional | flops 1286602752 | bytes 4718600 | solution.py:543
  72.8 7.7 %branch_1_fun.7 = (f32[2,32,2048]{2,1,0:T(8,128)}, f32[4,3,8,2048]{3,2,1,0:T(8,128)S(1)}) custom-call(f32[72]{0:T(128)S(1)} %get-tuple-element.117.refs_0_, f32[2,32,2048]{2,1,0:T(8,128)S(1)} %get-tuple-element.118.refs_1_, s32[3,32,2048]{2,1,0:T(8,128)S(1)} %get-tuple-element.119.refs_2_, f32[3,2,16,128]{3,2,1,0:T(8,128)S(1)} %get-tuple-element.120.refs_3_, ...), custom_call_target="tpu_custom_call" | custom-call | flops 1286602752 | bytes 4718592 | tf_op jit(solution)/shard_map/cond/branch_1_fun/pallas_call | solution.py:394
  80.5 1.9 %collective-permute-start.12 = (f32[3,8,2048]{2,1,0:T(8,128)S(1)}, f32[3,8,2048]{2,1,0:T(8,128)S(1)}, u32[]{:S(2)}, u32[]{:S(2)}) collective-permute-start(f32[3,8,2048]{2,1,0:T(8,128)S(1)} %get-tuple-element.148), channel_id=1, source_target_pairs={{12,13},{13,14},{14,15},{15,12},{28,29},{29,30},{30,31},{31,28}} | collective-permute-start | bytes 589832 | tf_op jit(solution)/shard_map/ppermute | solution.py:536
  82.5 1.9 %collective-permute-start.13 = (f32[3,8,2048]{2,1,0:T(8,128)S(1)}, f32[3,8,2048]{2,1,0:T(8,128)S(1)}, u32[]{:S(2)}, u32[]{:S(2)}) collective-permute-start(f32[3,8,2048]{2,1,0:T(8,128)S(1)} %get-tuple-element.150), channel_id=1, source_target_pairs={{12,14},{13,15},{14,12},{15,13},{28,30},{29,31},{30,28},{31,29}} | collective-permute-start | bytes 589832 | tf_op jit(solution)/shard_map/ppermute | solution.py:536
  84.4 3.4 %collective-permute-start.14 = (f32[3,8,2048]{2,1,0:T(8,128)S(1)}, f32[3,8,2048]{2,1,0:T(8,128)S(1)}, u32[]{:S(2)}, u32[]{:S(2)}) collective-permute-start(f32[3,8,2048]{2,1,0:T(8,128)S(1)} %get-tuple-element.149), channel_id=1, source_target_pairs={{12,15},{13,12},{14,13},{15,14},{28,31},{29,28},{30,29},{31,30}} | collective-permute-start | bytes 589832 | tf_op jit(solution)/shard_map/ppermute | solution.py:536
  87.8 0.7 collective-permute-start.10
  88.5 0.7 collective-permute-start.11
  89.3 0.7 collective-permute-start.9
  90.0 5.6 %collective-permute-done.13 = f32[3,8,2048]{2,1,0:T(8,128)S(1)} collective-permute-done((f32[3,8,2048]{2,1,0:T(8,128)S(1)}, f32[3,8,2048]{2,1,0:T(8,128)S(1)}, u32[]{:S(2)}, u32[]{:S(2)}) %collective-permute-start.13) | collective-permute-done | bytes 196640 | tf_op jit(solution)/shard_map/ppermute | solution.py:536
  96.2 0.8 fusion.5
  (57 shorter events, 2.1 us)
Async XLA Ops:
  2.2 9.8 %copy-start = (f32[4]{0:T(128)S(1)}, f32[4]{0:T(128)}, u32[]{:S(2)}) copy-start(f32[4]{0:T(128)} %param.21) | copy-start | bytes 52
  2.3 10.4 %copy-start.1 = (f32[8]{0:T(128)S(1)}, f32[8]{0:T(128)}, u32[]{:S(2)}) copy-start(f32[8]{0:T(128)} %param.22) | copy-start | bytes 100
  2.3 10.4 %copy-start.2 = (s32[3]{0:T(128)S(1)}, s32[3]{0:T(128)}, u32[]{:S(2)}) copy-start(s32[3]{0:T(128)} %param.25) | copy-start | bytes 40
  2.3 12.5 %copy-start.3 = (f32[8]{0:T(128)S(1)}, f32[8]{0:T(128)}, u32[]{:S(2)}) copy-start(f32[8]{0:T(128)} %param.23) | copy-start | bytes 100
  2.3 13.2 %copy-start.4 = (f32[16,128]{1,0:T(8,128)S(1)}, f32[16,128]{1,0:T(8,128)}, u32[]{:S(2)}) copy-start(f32[16,128]{1,0:T(8,128)} %constant.135) | copy-start | bytes 24580
  2.4 13.3 %collective-permute-start = (f32[5,8,2048]{2,1,0:T(8,128)S(1)}, f32[5,8,2048]{2,1,0:T(8,128)}, u32[]{:S(2)}, u32[]{:S(2)}) collective-permute-start(f32[5,8,2048]{2,1,0:T(8,128)S(1)} %get-tuple-element.156), channel_id=1, source_target_pairs={{0,1},{1,2},{2,3},{3,0},{8,9},{9,10},{10,11},{11,8},{12,13},{13,14... | collective-permute-start | bytes 983048 | tf_op jit(solution)/shard_map/ppermute | solution.py:484
  5.7 27.4 %collective-permute-start.1 = (f32[5,8,2048]{2,1,0:T(8,128)S(1)}, f32[5,8,2048]{2,1,0:T(8,128)S(1)}, u32[]{:S(2)}, u32[]{:S(2)}) collective-permute-start(f32[5,8,2048]{2,1,0:T(8,128)S(1)} %get-tuple-element.157), channel_id=1, source_target_pairs={{0,2},{1,3},{2,0},{3,1},{8,10},{9,11},{10,8},{11,9},{12,14},{13,15... | collective-permute-start | bytes 983048 | tf_op jit(solution)/shard_map/ppermute | solution.py:484
  8.6 27.3 %collective-permute-start.2 = (f32[5,8,2048]{2,1,0:T(8,128)S(1)}, f32[5,8,2048]{2,1,0:T(8,128)S(1)}, u32[]{:S(2)}, u32[]{:S(2)}) collective-permute-start(f32[5,8,2048]{2,1,0:T(8,128)S(1)} %get-tuple-element.155), channel_id=1, source_target_pairs={{0,3},{1,0},{2,1},{3,2},{8,11},{9,8},{10,9},{11,10},{12,15},{13,12... | collective-permute-start | bytes 983048 | tf_op jit(solution)/shard_map/ppermute | solution.py:484
  35.9 0.9 copy-start.5
  35.9 1.0 copy-start.6
  35.9 1.0 %copy-start.8 = (bf16[256,256]{1,0:T(8,128)(2,1)S(1)}, bf16[256,256]{1,0:T(8,128)(2,1)}, u32[]{:S(2)}) copy-start(bf16[256,256]{1,0:T(8,128)(2,1)} %constant.130.clone) | copy-start | bytes 393220
  36.0 1.1 %copy-start.9 = (bf16[256,256]{1,0:T(8,128)(2,1)S(1)}, bf16[256,256]{1,0:T(8,128)(2,1)}, u32[]{:S(2)}) copy-start(bf16[256,256]{1,0:T(8,128)(2,1)} %constant.131.clone) | copy-start | bytes 393220
  36.0 1.1 %copy-start.10 = (f32[2,16,128]{2,1,0:T(8,128)S(1)}, f32[2,16,128]{2,1,0:T(8,128)}, u32[]{:S(2)}) copy-start(f32[2,16,128]{2,1,0:T(8,128)} %constant.127.clone) | copy-start | bytes 49156
  37.1 2.8 %collective-permute-start.4 = (f32[3,8,2048]{2,1,0:T(8,128)S(1)}, f32[3,8,2048]{2,1,0:T(8,128)S(1)}, u32[]{:S(2)}, u32[]{:S(2)}) collective-permute-start(f32[3,8,2048]{2,1,0:T(8,128)S(1)} %convert_element_type.25), channel_id=1, source_target_pairs={{4,5},{5,6},{6,7},{7,4},{20,21},{21,22},{22,23},{23,20}} | collective-permute-start | bytes 589832 | tf_op jit(solution)/shard_map/ppermute | solution.py:484
  37.8 2.2 %collective-permute-start.5 = (f32[3,8,2048]{2,1,0:T(8,128)S(1)}, f32[3,8,2048]{2,1,0:T(8,128)S(1)}, u32[]{:S(2)}, u32[]{:S(2)}) collective-permute-start(f32[3,8,2048]{2,1,0:T(8,128)S(1)} %convert_element_type.25), channel_id=1, source_target_pairs={{4,6},{5,7},{6,4},{7,5},{20,22},{21,23},{22,20},{23,21}} | collective-permute-start | bytes 589832 | tf_op jit(solution)/shard_map/ppermute | solution.py:484
  38.5 1.6 %collective-permute-start.6 = (f32[3,8,2048]{2,1,0:T(8,128)S(1)}, f32[3,8,2048]{2,1,0:T(8,128)S(1)}, u32[]{:S(2)}, u32[]{:S(2)}) collective-permute-start(f32[3,8,2048]{2,1,0:T(8,128)S(1)} %convert_element_type.25), channel_id=1, source_target_pairs={{4,7},{5,4},{6,5},{7,6},{20,23},{21,20},{22,21},{23,22}} | collective-permute-start | bytes 589832 | tf_op jit(solution)/shard_map/ppermute | solution.py:484
  39.2 1.9 %collective-permute-start.3 = (f32[2,32,2048]{2,1,0:T(8,128)S(1)}, f32[2,32,2048]{2,1,0:T(8,128)S(1)}, u32[]{:S(2)}, u32[]{:S(2)}) collective-permute-start(f32[2,32,2048]{2,1,0:T(8,128)S(1)} %get-tuple-element.136), channel_id=1, source_target_pairs={{0,4},{1,5},{2,6},{3,7},{16,20},{17,21},{18,22},{19,23}} | collective-permute-start | bytes 1572872 | tf_op jit(solution)/shard_map/ppermute | solution.py:545
  41.1 0.7 collective-permute-start.7
  41.8 31.0 %copy-start.7 = (bf16[256,256]{1,0:T(8,128)(2,1)S(1)}, bf16[256,256]{1,0:T(8,128)(2,1)}, u32[]{:S(2)}) copy-start(bf16[256,256]{1,0:T(8,128)(2,1)} %constant.129.clone) | copy-start | bytes 393220
  41.8 31.0 %collective-permute-start.8 = (f32[2,32,2048]{2,1,0:T(8,128)S(1)}, f32[2,32,2048]{2,1,0:T(8,128)S(1)}, u32[]{:S(2)}, u32[]{:S(2)}) collective-permute-start(f32[2,32,2048]{2,1,0:T(8,128)S(1)} %get-tuple-element.141), channel_id=1, source_target_pairs={{8,12},{9,13},{10,14},{11,15},{24,28},{25,29},{26,30},{27,31}} | collective-permute-start | bytes 1572872 | tf_op jit(solution)/shard_map/ppermute | solution.py:545
  80.5 8.8 %collective-permute-start.12 = (f32[3,8,2048]{2,1,0:T(8,128)S(1)}, f32[3,8,2048]{2,1,0:T(8,128)S(1)}, u32[]{:S(2)}, u32[]{:S(2)}) collective-permute-start(f32[3,8,2048]{2,1,0:T(8,128)S(1)} %get-tuple-element.148), channel_id=1, source_target_pairs={{12,13},{13,14},{14,15},{15,12},{28,29},{29,30},{30,31},{31,28}} | collective-permute-start | bytes 589832 | tf_op jit(solution)/shard_map/ppermute | solution.py:536
  82.5 13.1 %collective-permute-start.13 = (f32[3,8,2048]{2,1,0:T(8,128)S(1)}, f32[3,8,2048]{2,1,0:T(8,128)S(1)}, u32[]{:S(2)}, u32[]{:S(2)}) collective-permute-start(f32[3,8,2048]{2,1,0:T(8,128)S(1)} %get-tuple-element.150), channel_id=1, source_target_pairs={{12,14},{13,15},{14,12},{15,13},{28,30},{29,31},{30,28},{31,29}} | collective-permute-start | bytes 589832 | tf_op jit(solution)/shard_map/ppermute | solution.py:536
  84.4 11.7 %collective-permute-start.14 = (f32[3,8,2048]{2,1,0:T(8,128)S(1)}, f32[3,8,2048]{2,1,0:T(8,128)S(1)}, u32[]{:S(2)}, u32[]{:S(2)}) collective-permute-start(f32[3,8,2048]{2,1,0:T(8,128)S(1)} %get-tuple-element.149), channel_id=1, source_target_pairs={{12,15},{13,12},{14,13},{15,14},{28,31},{29,28},{30,29},{31,30}} | collective-permute-start | bytes 589832 | tf_op jit(solution)/shard_map/ppermute | solution.py:536
  87.8 8.3 %collective-permute-start.10 = (f32[3,8,2048]{2,1,0:T(8,128)S(1)}, f32[3,8,2048]{2,1,0:T(8,128)S(1)}, u32[]{:S(2)}, u32[]{:S(2)}) collective-permute-start(f32[3,8,2048]{2,1,0:T(8,128)S(1)} %get-tuple-element.147), channel_id=1, source_target_pairs={{0,2},{1,3},{2,0},{3,1},{4,6},{5,7},{6,4},{7,5},{8,10},{9,11},{10,... | collective-permute-start | bytes 589832 | tf_op jit(solution)/shard_map/ppermute | solution.py:536
  88.5 7.6 %collective-permute-start.11 = (f32[3,8,2048]{2,1,0:T(8,128)S(1)}, f32[3,8,2048]{2,1,0:T(8,128)S(1)}, u32[]{:S(2)}, u32[]{:S(2)}) collective-permute-start(f32[3,8,2048]{2,1,0:T(8,128)S(1)} %get-tuple-element.146), channel_id=1, source_target_pairs={{0,3},{1,0},{2,1},{3,2},{4,7},{5,4},{6,5},{7,6},{8,11},{9,8},{10,9... | collective-permute-start | bytes 589832 | tf_op jit(solution)/shard_map/ppermute | solution.py:536
  89.3 6.8 %collective-permute-start.9 = (f32[3,8,2048]{2,1,0:T(8,128)S(1)}, f32[3,8,2048]{2,1,0:T(8,128)S(1)}, u32[]{:S(2)}, u32[]{:S(2)}) collective-permute-start(f32[3,8,2048]{2,1,0:T(8,128)S(1)} %get-tuple-element.145), channel_id=1, source_target_pairs={{0,1},{1,2},{2,3},{3,0},{4,5},{5,6},{6,7},{7,4},{8,9},{9,10},{10,1... | collective-permute-start | bytes 589832 | tf_op jit(solution)/shard_map/ppermute | solution.py:536

commit v13 on v12

--- a/solution.py
+++ b/solution.py
@@ -540,7 +540,10 @@
     arrived = []
     for tick_no in range(segment_count):
         regions = regions_b if tick_no == 1 else regions_a
-        wave, image = lax.cond(segment_no == tick_no, sweep(regions), idle, wave, image)
+        if tick_no == 0:
+            wave, image = sweep(regions)(wave, image)
+        else:
+            wave, image = lax.cond(segment_no == tick_no, sweep(regions), idle, wave, image)
         if tick_no + 1 < segment_count:
             wave = lax.ppermute(wave, "depth", [(tick_no, tick_no + 1)])
         if tick_no == 0 and segment_count > 1:

time: 97.7 us -> 94.9 us (0.971)
  waiting for transfers between devices: 55 us -> 43.6 us
  Pallas kernels: 7.71 us -> 15.5 us
  starting transfers between devices: 23.5 us -> 24.8 us
    ppermute x3, waiting for transfers between devices: 29.5 us -> 19.5 us  [shards(): wave = lax.ppermute(wave, 'depth', [(tick_no, tick_no + 1)])]
    pallas_call x1 -> x2, Pallas kernels: 7.71 us -> 15.5 us  [run_section(): pl.pallas_call(lambda *refs: section_kernel(*refs, table_len=table_len),...]
    ppermute x6, starting transfers between devices: 9.21 us -> 10.6 us  [freq_sum(): lax.ppermute(piece, ('depth', 'strip'), strip_pairs(depths, strip_count,...]
    ppermute x6, waiting for transfers between devices: 6.29 us -> 4.93 us  [freq_sum(): lax.ppermute(piece, ('depth', 'strip'), strip_pairs(depths, strip_count,...]
  transfers between devices with their start and end apart: 15 -> 15, of which waited for: 6 -> 5; matrix products, arithmetic and copies ran while one was open for 6% -> 5% of each run, Pallas kernels for 0% -> 0%
where the time goes in v13:
time: 94.9 us; the launch traced here: 93.8 us
  waiting for transfers between devices  43.6 us (46%)
  starting transfers between devices  24.8 us (26%)
  Pallas kernels  15.5 us (16%)
  local copies, waits for them, and re-layouts  5.03 us (5%)
  other arithmetic  4.27 us (4%)
    ppermute x3, waiting for transfers between devices, shards(): wave = lax.ppermute(wave, 'depth', [(tick_no, tick_no + 1)])  19.5 us
    ppermute x6, waiting for transfers between devices, gather_strips(): lax.ppermute(piece_of(target), ('depth', 'strip'), strip_pairs(depths, st...  19.1 us
    pallas_call x2, Pallas kernels, run_section(): pl.pallas_call(lambda *refs: section_kernel(*refs, table_len=table_len),...  15.5 us
    ppermute x6, starting transfers between devices, gather_strips(): lax.ppermute(piece_of(target), ('depth', 'strip'), strip_pairs(depths, st...  11.5 us
    ppermute x6, starting transfers between devices, freq_sum(): lax.ppermute(piece, ('depth', 'strip'), strip_pairs(depths, strip_count,...  10.6 us
    ppermute x6, waiting for transfers between devices, freq_sum(): lax.ppermute(piece, ('depth', 'strip'), strip_pairs(depths, strip_count,...  4.93 us
    ppermute x3, starting transfers between devices, shards(): wave = lax.ppermute(wave, 'depth', [(tick_no, tick_no + 1)])  2.68 us
  transfers between devices with their start and end apart: 15, of which 5 were waited for; matrix products, arithmetic and copies ran while one was open for 5% of the time, Pallas kernels for 0%

profile of v13, /device:TPU:11, one launch (start us, length us, event | category | flops | bytes accessed | tf_op | source)
XLA Modules:
  0.0 93.8 jit_solution(11459556570502137639)
XLA Ops:
  0.0 0.9 %convert_element_type.21 = f32[3,8,2048]{2,1,0:T(8,128)S(1)} convert(s32[3,8,2048]{2,1,0:T(8,128)} %param.22) | non-fusion elementwise | flops 49152 | bytes 393216 | tf_op jit(solution)/shard_map/convert_element_type | solution.py:503
  1.0 1.1 %dynamic-slice_bitcast_fusion.6 = (f32[2,8,2048]{2,1,0:T(8,128)S(1)}, f32[2,8,2048]{2,1,0:T(8,128)S(1)}, f32[2,8,2048]{2,1,0:T(8,128)S(1)}, f32[2,8,2048]{2,1,0:T(8,128)S(1)}) fusion(f32[2,4,8,2048]{3,2,1,0:T(8,128)} %param.18, s32[]{:T(128)S(6)} %select_n.99, s32[]{:T(128)S(6)} %select_n.91, s32[]{:T(128)S(6)} %select_n.87, s32[]{:T(128)S(6)} %select_n.95), kind=kLoop, calls=%fused_computation.19 | loop fusion | bytes 1048592 | tf_op jit(solution)/shard_map/jit(dynamic_index_in_dim)/squeeze | solution.py:508
  2.4 3.2 %collective-permute-start = (f32[5,8,2048]{2,1,0:T(8,128)S(1)}, f32[5,8,2048]{2,1,0:T(8,128)}, u32[]{:S(2)}, u32[]{:S(2)}) collective-permute-start(f32[5,8,2048]{2,1,0:T(8,128)S(1)} %get-tuple-element.128), channel_id=1, source_target_pairs={{0,1},{1,2},{2,3},{3,0},{8,9},{9,10},{10,11},{11,8},{12,13},{13,14... | collective-permute-start | bytes 983048 | tf_op jit(solution)/shard_map/ppermute | solution.py:484
  5.6 2.9 %collective-permute-start.1 = (f32[5,8,2048]{2,1,0:T(8,128)S(1)}, f32[5,8,2048]{2,1,0:T(8,128)S(1)}, u32[]{:S(2)}, u32[]{:S(2)}) collective-permute-start(f32[5,8,2048]{2,1,0:T(8,128)S(1)} %get-tuple-element.129), channel_id=1, source_target_pairs={{0,2},{1,3},{2,0},{3,1},{8,10},{9,11},{10,8},{11,9},{12,14},{13,15... | collective-permute-start | bytes 983048 | tf_op jit(solution)/shard_map/ppermute | solution.py:484
  8.6 3.4 %collective-permute-start.2 = (f32[5,8,2048]{2,1,0:T(8,128)S(1)}, f32[5,8,2048]{2,1,0:T(8,128)S(1)}, u32[]{:S(2)}, u32[]{:S(2)}) collective-permute-start(f32[5,8,2048]{2,1,0:T(8,128)S(1)} %get-tuple-element.127), channel_id=1, source_target_pairs={{0,3},{1,0},{2,1},{3,2},{8,11},{9,8},{10,9},{11,10},{12,15},{13,12... | collective-permute-start | bytes 983048 | tf_op jit(solution)/shard_map/ppermute | solution.py:484
  12.0 0.6 dynamic_slice.39
  12.7 0.6 gather_fusion
  13.3 0.8 fusion.16
  14.1 0.7 multiply_multiply_fusion
  14.7 0.7 broadcast_divide_fusion
  15.7 1.0 %constant_dynamic-update-slice_fusion.6 = f32[5,32,2048]{2,1,0:T(8,128)S(1)} fusion(f32[5,32,2048]{2,1,0:T(8,128)S(1)} %get-tuple-element.130, f32[5,8,2048]{2,1,0:T(8,128)} %collective-permute-done, s32[]{:T(128)S(6)} %select_n.93), kind=kLoop, calls=%fused_computation.42 | loop fusion | bytes 655364 | tf_op jit(solution)/shard_map/dynamic_update_slice | solution.py:488
  16.7 16.3 %collective-permute-done.1 = f32[5,8,2048]{2,1,0:T(8,128)S(1)} collective-permute-done((f32[5,8,2048]{2,1,0:T(8,128)S(1)}, f32[5,8,2048]{2,1,0:T(8,128)S(1)}, u32[]{:S(2)}, u32[]{:S(2)}) %collective-permute-start.1) | collective-permute-done | bytes 327712 | tf_op jit(solution)/shard_map/ppermute | solution.py:484
  33.1 2.8 %collective-permute-done.2 = f32[5,8,2048]{2,1,0:T(8,128)S(1)} collective-permute-done((f32[5,8,2048]{2,1,0:T(8,128)S(1)}, f32[5,8,2048]{2,1,0:T(8,128)S(1)}, u32[]{:S(2)}, u32[]{:S(2)}) %collective-permute-start.2) | collective-permute-done | bytes 327712 | tf_op jit(solution)/shard_map/ppermute | solution.py:484
  36.1 0.8 slice.10.refs_1_
  37.2 7.8 %shard_map.118 = (f32[2,32,2048]{2,1,0:T(8,128)}, f32[4,3,8,2048]{3,2,1,0:T(8,128)S(1)}) custom-call(f32[72]{0:T(128)S(1)} %reshape.125.refs_0_, f32[2,32,2048]{2,1,0:T(8,128)} %slice.10.refs_1_, s32[3,32,2048]{2,1,0:T(8,128)S(1)} %slice_convert_fusion.refs_2_, f32[3,2,16,128]{3,2,1,0:T(8,128)S(1)} %pad_maximum_fusion.4.refs_3_, ...), custom_call_target="tpu_custom_call" | custom-call | flops 1286602752 | bytes 4718592 | tf_op jit(solution)/shard_map/pallas_call | solution.py:394
  45.0 0.7 collective-permute-start.4
  45.6 0.7 collective-permute-start.5
  46.3 0.7 collective-permute-start.6
  47.0 0.7 collective-permute-start.3
  48.0 0.7 collective-permute-start.7
  48.8 1.3 %collective-permute-start.8 = (f32[2,32,2048]{2,1,0:T(8,128)S(1)}, f32[2,32,2048]{2,1,0:T(8,128)S(1)}, u32[]{:S(2)}, u32[]{:S(2)}) collective-permute-start(f32[2,32,2048]{2,1,0:T(8,128)S(1)} %get-tuple-element.113), channel_id=1, source_target_pairs={{8,12},{9,13},{10,14},{11,15},{24,28},{25,29},{26,30},{27,31}} | collective-permute-start | bytes 1572872 | tf_op jit(solution)/shard_map/ppermute | solution.py:548
  50.1 19.5 %collective-permute-done.8 = f32[2,32,2048]{2,1,0:T(8,128)S(1)} collective-permute-done((f32[2,32,2048]{2,1,0:T(8,128)S(1)}, f32[2,32,2048]{2,1,0:T(8,128)S(1)}, u32[]{:S(2)}, u32[]{:S(2)}) %collective-permute-start.8) | collective-permute-done | bytes 524320 | tf_op jit(solution)/shard_map/ppermute | solution.py:548
  69.6 7.7 %conditional.5 = (f32[4,3,8,2048]{3,2,1,0:T(8,128)S(1)}) conditional(s32[]{:T(128)} %convert_element_type.18, f32[4,3,8,2048]{3,2,1,0:T(8,128)S(1)} %get-tuple-element.115, (f32[72]{0:T(128)S(1)}, f32[2,32,2048]{2,1,0:T(8,128)S(1)}, s32[3,32,2048]{2,1,0:T(8,128)S(1)}, f32[3,2,16,128]{3,2,1,0:T(8,128)S(1)}, f32[2,16,128]{2,1,0:T(8,128)S(1)}, ...), branch_computations={%region_4.5_spmd, %region_5.6_spmd} | conditional | flops 1286602752 | bytes 4718600 | solution.py:546
  69.6 7.7 %branch_1_fun.5 = (f32[2,32,2048]{2,1,0:T(8,128)}, f32[4,3,8,2048]{3,2,1,0:T(8,128)S(1)}) custom-call(f32[72]{0:T(128)S(1)} %get-tuple-element.89.refs_0_, f32[2,32,2048]{2,1,0:T(8,128)S(1)} %get-tuple-element.90.refs_1_, s32[3,32,2048]{2,1,0:T(8,128)S(1)} %get-tuple-element.91.refs_2_, f32[3,2,16,128]{3,2,1,0:T(8,128)S(1)} %get-tuple-element.92.refs_3_, ...), custom_call_target="tpu_custom_call" | custom-call | flops 1286602752 | bytes 4718592 | tf_op jit(solution)/shard_map/cond/branch_1_fun/pallas_call | solution.py:394
  77.4 1.9 %collective-permute-start.12 = (f32[3,8,2048]{2,1,0:T(8,128)S(1)}, f32[3,8,2048]{2,1,0:T(8,128)S(1)}, u32[]{:S(2)}, u32[]{:S(2)}) collective-permute-start(f32[3,8,2048]{2,1,0:T(8,128)S(1)} %get-tuple-element.120), channel_id=1, source_target_pairs={{12,13},{13,14},{14,15},{15,12},{28,29},{29,30},{30,31},{31,28}} | collective-permute-start | bytes 589832 | tf_op jit(solution)/shard_map/ppermute | solution.py:536
  79.3 3.3 %collective-permute-start.13 = (f32[3,8,2048]{2,1,0:T(8,128)S(1)}, f32[3,8,2048]{2,1,0:T(8,128)S(1)}, u32[]{:S(2)}, u32[]{:S(2)}) collective-permute-start(f32[3,8,2048]{2,1,0:T(8,128)S(1)} %get-tuple-element.122), channel_id=1, source_target_pairs={{12,14},{13,15},{14,12},{15,13},{28,30},{29,31},{30,28},{31,29}} | collective-permute-start | bytes 589832 | tf_op jit(solution)/shard_map/ppermute | solution.py:536
  82.6 3.4 %collective-permute-start.14 = (f32[3,8,2048]{2,1,0:T(8,128)S(1)}, f32[3,8,2048]{2,1,0:T(8,128)S(1)}, u32[]{:S(2)}, u32[]{:S(2)}) collective-permute-start(f32[3,8,2048]{2,1,0:T(8,128)S(1)} %get-tuple-element.121), channel_id=1, source_target_pairs={{12,15},{13,12},{14,13},{15,14},{28,31},{29,28},{30,29},{31,30}} | collective-permute-start | bytes 589832 | tf_op jit(solution)/shard_map/ppermute | solution.py:536
  86.0 0.7 collective-permute-start.10
  86.7 0.7 collective-permute-start.11
  87.4 0.7 collective-permute-start.9
  88.1 4.3 %collective-permute-done.13 = f32[3,8,2048]{2,1,0:T(8,128)S(1)} collective-permute-done((f32[3,8,2048]{2,1,0:T(8,128)S(1)}, f32[3,8,2048]{2,1,0:T(8,128)S(1)}, u32[]{:S(2)}, u32[]{:S(2)}) %collective-permute-start.13) | collective-permute-done | bytes 196640 | tf_op jit(solution)/shard_map/ppermute | solution.py:536
  93.0 0.8 fusion.5
  (54 shorter events, 1.9 us)
Async XLA Ops:
  2.2 9.8 %copy-start = (f32[4]{0:T(128)S(1)}, f32[4]{0:T(128)}, u32[]{:S(2)}) copy-start(f32[4]{0:T(128)} %param.19) | copy-start | bytes 52
  2.3 10.4 %copy-start.1 = (f32[8]{0:T(128)S(1)}, f32[8]{0:T(128)}, u32[]{:S(2)}) copy-start(f32[8]{0:T(128)} %param.20) | copy-start | bytes 100
  2.3 10.4 %copy-start.2 = (s32[3]{0:T(128)S(1)}, s32[3]{0:T(128)}, u32[]{:S(2)}) copy-start(s32[3]{0:T(128)} %param.23) | copy-start | bytes 40
  2.3 12.5 %copy-start.3 = (f32[8]{0:T(128)S(1)}, f32[8]{0:T(128)}, u32[]{:S(2)}) copy-start(f32[8]{0:T(128)} %param.21) | copy-start | bytes 100
  2.3 13.2 %copy-start.4 = (f32[16,128]{1,0:T(8,128)S(1)}, f32[16,128]{1,0:T(8,128)}, u32[]{:S(2)}) copy-start(f32[16,128]{1,0:T(8,128)} %constant.133) | copy-start | bytes 24580
  2.4 13.3 %collective-permute-start = (f32[5,8,2048]{2,1,0:T(8,128)S(1)}, f32[5,8,2048]{2,1,0:T(8,128)}, u32[]{:S(2)}, u32[]{:S(2)}) collective-permute-start(f32[5,8,2048]{2,1,0:T(8,128)S(1)} %get-tuple-element.128), channel_id=1, source_target_pairs={{0,1},{1,2},{2,3},{3,0},{8,9},{9,10},{10,11},{11,8},{12,13},{13,14... | collective-permute-start | bytes 983048 | tf_op jit(solution)/shard_map/ppermute | solution.py:484
  5.6 27.4 %collective-permute-start.1 = (f32[5,8,2048]{2,1,0:T(8,128)S(1)}, f32[5,8,2048]{2,1,0:T(8,128)S(1)}, u32[]{:S(2)}, u32[]{:S(2)}) collective-permute-start(f32[5,8,2048]{2,1,0:T(8,128)S(1)} %get-tuple-element.129), channel_id=1, source_target_pairs={{0,2},{1,3},{2,0},{3,1},{8,10},{9,11},{10,8},{11,9},{12,14},{13,15... | collective-permute-start | bytes 983048 | tf_op jit(solution)/shard_map/ppermute | solution.py:484
  8.6 27.3 %collective-permute-start.2 = (f32[5,8,2048]{2,1,0:T(8,128)S(1)}, f32[5,8,2048]{2,1,0:T(8,128)S(1)}, u32[]{:S(2)}, u32[]{:S(2)}) collective-permute-start(f32[5,8,2048]{2,1,0:T(8,128)S(1)} %get-tuple-element.127), channel_id=1, source_target_pairs={{0,3},{1,0},{2,1},{3,2},{8,11},{9,8},{10,9},{11,10},{12,15},{13,12... | collective-permute-start | bytes 983048 | tf_op jit(solution)/shard_map/ppermute | solution.py:484
  35.9 1.0 %copy-start.5 = (bf16[256,256]{1,0:T(8,128)(2,1)S(1)}, bf16[256,256]{1,0:T(8,128)(2,1)}, u32[]{:S(2)}) copy-start(bf16[256,256]{1,0:T(8,128)(2,1)} %constant.126.clone.refs_5_) | copy-start | bytes 393220
  35.9 1.0 %copy-start.6 = (bf16[256,256]{1,0:T(8,128)(2,1)S(1)}, bf16[256,256]{1,0:T(8,128)(2,1)}, u32[]{:S(2)}) copy-start(bf16[256,256]{1,0:T(8,128)(2,1)} %constant.127.clone.refs_6_) | copy-start | bytes 393220
  35.9 1.0 %copy-start.7 = (bf16[256,256]{1,0:T(8,128)(2,1)S(1)}, bf16[256,256]{1,0:T(8,128)(2,1)}, u32[]{:S(2)}) copy-start(bf16[256,256]{1,0:T(8,128)(2,1)} %constant.128.clone.refs_7_) | copy-start | bytes 393220
  36.0 1.2 %copy-start.8 = (bf16[256,256]{1,0:T(8,128)(2,1)S(1)}, bf16[256,256]{1,0:T(8,128)(2,1)}, u32[]{:S(2)}) copy-start(bf16[256,256]{1,0:T(8,128)(2,1)} %constant.129.clone.refs_8_) | copy-start | bytes 393220
  36.0 1.2 %copy-start.9 = (f32[2,16,128]{2,1,0:T(8,128)S(1)}, f32[2,16,128]{2,1,0:T(8,128)}, u32[]{:S(2)}) copy-start(f32[2,16,128]{2,1,0:T(8,128)} %constant.125.clone.refs_4_) | copy-start | bytes 49156
  45.0 2.8 %collective-permute-start.4 = (f32[3,8,2048]{2,1,0:T(8,128)S(1)}, f32[3,8,2048]{2,1,0:T(8,128)S(1)}, u32[]{:S(2)}, u32[]{:S(2)}) collective-permute-start(f32[3,8,2048]{2,1,0:T(8,128)S(1)} %convert_element_type.21), channel_id=1, source_target_pairs={{4,5},{5,6},{6,7},{7,4},{20,21},{21,22},{22,23},{23,20}} | collective-permute-start | bytes 589832 | tf_op jit(solution)/shard_map/ppermute | solution.py:484
  45.6 2.2 %collective-permute-start.5 = (f32[3,8,2048]{2,1,0:T(8,128)S(1)}, f32[3,8,2048]{2,1,0:T(8,128)S(1)}, u32[]{:S(2)}, u32[]{:S(2)}) collective-permute-start(f32[3,8,2048]{2,1,0:T(8,128)S(1)} %convert_element_type.21), channel_id=1, source_target_pairs={{4,6},{5,7},{6,4},{7,5},{20,22},{21,23},{22,20},{23,21}} | collective-permute-start | bytes 589832 | tf_op jit(solution)/shard_map/ppermute | solution.py:484
  46.3 1.6 %collective-permute-start.6 = (f32[3,8,2048]{2,1,0:T(8,128)S(1)}, f32[3,8,2048]{2,1,0:T(8,128)S(1)}, u32[]{:S(2)}, u32[]{:S(2)}) collective-permute-start(f32[3,8,2048]{2,1,0:T(8,128)S(1)} %convert_element_type.21), channel_id=1, source_target_pairs={{4,7},{5,4},{6,5},{7,6},{20,23},{21,20},{22,21},{23,22}} | collective-permute-start | bytes 589832 | tf_op jit(solution)/shard_map/ppermute | solution.py:484
  47.0 1.0 %collective-permute-start.3 = (f32[2,32,2048]{2,1,0:T(8,128)}, f32[2,32,2048]{2,1,0:T(8,128)S(1)}, u32[]{:S(2)}, u32[]{:S(2)}) collective-permute-start(f32[2,32,2048]{2,1,0:T(8,128)} %get-tuple-element.108), channel_id=1, source_target_pairs={{0,4},{1,5},{2,6},{3,7},{16,20},{17,21},{18,22},{19,23}} | collective-permute-start | bytes 1572872 | tf_op jit(solution)/shard_map/ppermute | solution.py:548
  48.0 0.7 collective-permute-start.7
  48.8 20.8 %collective-permute-start.8 = (f32[2,32,2048]{2,1,0:T(8,128)S(1)}, f32[2,32,2048]{2,1,0:T(8,128)S(1)}, u32[]{:S(2)}, u32[]{:S(2)}) collective-permute-start(f32[2,32,2048]{2,1,0:T(8,128)S(1)} %get-tuple-element.113), channel_id=1, source_target_pairs={{8,12},{9,13},{10,14},{11,15},{24,28},{25,29},{26,30},{27,31}} | collective-permute-start | bytes 1572872 | tf_op jit(solution)/shard_map/ppermute | solution.py:548
  77.4 10.0 %collective-permute-start.12 = (f32[3,8,2048]{2,1,0:T(8,128)S(1)}, f32[3,8,2048]{2,1,0:T(8,128)S(1)}, u32[]{:S(2)}, u32[]{:S(2)}) collective-permute-start(f32[3,8,2048]{2,1,0:T(8,128)S(1)} %get-tuple-element.120), channel_id=1, source_target_pairs={{12,13},{13,14},{14,15},{15,12},{28,29},{29,30},{30,31},{31,28}} | collective-permute-start | bytes 589832 | tf_op jit(solution)/shard_map/ppermute | solution.py:536
  79.3 13.1 %collective-permute-start.13 = (f32[3,8,2048]{2,1,0:T(8,128)S(1)}, f32[3,8,2048]{2,1,0:T(8,128)S(1)}, u32[]{:S(2)}, u32[]{:S(2)}) collective-permute-start(f32[3,8,2048]{2,1,0:T(8,128)S(1)} %get-tuple-element.122), channel_id=1, source_target_pairs={{12,14},{13,15},{14,12},{15,13},{28,30},{29,31},{30,28},{31,29}} | collective-permute-start | bytes 589832 | tf_op jit(solution)/shard_map/ppermute | solution.py:536
  82.6 10.4 %collective-permute-start.14 = (f32[3,8,2048]{2,1,0:T(8,128)S(1)}, f32[3,8,2048]{2,1,0:T(8,128)S(1)}, u32[]{:S(2)}, u32[]{:S(2)}) collective-permute-start(f32[3,8,2048]{2,1,0:T(8,128)S(1)} %get-tuple-element.121), channel_id=1, source_target_pairs={{12,15},{13,12},{14,13},{15,14},{28,31},{29,28},{30,29},{31,30}} | collective-permute-start | bytes 589832 | tf_op jit(solution)/shard_map/ppermute | solution.py:536
  86.0 7.0 %collective-permute-start.10 = (f32[3,8,2048]{2,1,0:T(8,128)S(1)}, f32[3,8,2048]{2,1,0:T(8,128)S(1)}, u32[]{:S(2)}, u32[]{:S(2)}) collective-permute-start(f32[3,8,2048]{2,1,0:T(8,128)S(1)} %get-tuple-element.119), channel_id=1, source_target_pairs={{0,2},{1,3},{2,0},{3,1},{4,6},{5,7},{6,4},{7,5},{8,10},{9,11},{10,... | collective-permute-start | bytes 589832 | tf_op jit(solution)/shard_map/ppermute | solution.py:536
  86.7 6.3 %collective-permute-start.11 = (f32[3,8,2048]{2,1,0:T(8,128)S(1)}, f32[3,8,2048]{2,1,0:T(8,128)S(1)}, u32[]{:S(2)}, u32[]{:S(2)}) collective-permute-start(f32[3,8,2048]{2,1,0:T(8,128)S(1)} %get-tuple-element.118), channel_id=1, source_target_pairs={{0,3},{1,0},{2,1},{3,2},{4,7},{5,4},{6,5},{7,6},{8,11},{9,8},{10,9... | collective-permute-start | bytes 589832 | tf_op jit(solution)/shard_map/ppermute | solution.py:536
  87.4 5.6 %collective-permute-start.9 = (f32[3,8,2048]{2,1,0:T(8,128)S(1)}, f32[3,8,2048]{2,1,0:T(8,128)S(1)}, u32[]{:S(2)}, u32[]{:S(2)}) collective-permute-start(f32[3,8,2048]{2,1,0:T(8,128)S(1)} %get-tuple-element.117), channel_id=1, source_target_pairs={{0,1},{1,2},{2,3},{3,0},{4,5},{5,6},{6,7},{7,4},{8,9},{9,10},{10,1... | collective-permute-start | bytes 589832 | tf_op jit(solution)/shard_map/ppermute | solution.py:536

commit v14 on v12

--- a/solution.py
+++ b/solution.py
@@ -540,7 +540,8 @@
     arrived = []
     for tick_no in range(segment_count):
         regions = regions_b if tick_no == 1 else regions_a
-        wave, image = lax.cond(segment_no == tick_no, sweep(regions), idle, wave, image)
+        wave, fresh = sweep(regions)(wave, image)
+        image = fresh if tick_no == 0 else jnp.where(segment_no == tick_no, fresh, image)
         if tick_no + 1 < segment_count:
             wave = lax.ppermute(wave, "depth", [(tick_no, tick_no + 1)])
         if tick_no == 0 and segment_count > 1:

time: 97.7 us -> 117 us (1.20)
  Pallas kernels: 7.71 us -> 33.8 us
  waiting for transfers between devices: 55 us -> 40.8 us
  other arithmetic: 5.2 us -> 8.08 us
  starting transfers between devices: 23.5 us -> 25.7 us
  local copies, waits for them, and re-layouts: 4.95 us -> 6.64 us
    pallas_call x1 -> x4, Pallas kernels: 7.71 us -> 33.8 us  [run_section(): pl.pallas_call(lambda *refs: section_kernel(*refs, table_len=table_len),...]
    ppermute x3, waiting for transfers between devices: 29.5 us -> 11.9 us  [shards(): wave = lax.ppermute(wave, 'depth', [(tick_no, tick_no + 1)])]
    ppermute x6, waiting for transfers between devices: 6.29 us -> 9.88 us  [freq_sum(): lax.ppermute(piece, ('depth', 'strip'), strip_pairs(depths, strip_count,...]
    ppermute x6, starting transfers between devices: 9.21 us -> 11.5 us  [freq_sum(): lax.ppermute(piece, ('depth', 'strip'), strip_pairs(depths, strip_count,...]
    unnamed x22 -> x20, local copies, waits for them, and re-layouts: 0.98 us -> 2.41 us
    select_n x0 -> x2, other arithmetic: none -> 1.35 us  [shards(): jnp.where(segment_no == tick_no, fresh, image)]
  transfers between devices with their start and end apart: 15 -> 15, of which waited for: 6 -> 5; matrix products, arithmetic and copies ran while one was open for 6% -> 5% of each run, Pallas kernels for 0% -> 0%
where the time goes in v14:
time: 117 us; the launch traced here: 115 us
  waiting for transfers between devices  40.8 us (35%)
  Pallas kernels  33.8 us (29%)
  starting transfers between devices  25.7 us (22%)
  other arithmetic  8.08 us (7%)
  local copies, waits for them, and re-layouts  6.64 us (6%)
    pallas_call x4, Pallas kernels, run_section(): pl.pallas_call(lambda *refs: section_kernel(*refs, table_len=table_len),...  33.8 us
    ppermute x6, waiting for transfers between devices, gather_strips(): lax.ppermute(piece_of(target), ('depth', 'strip'), strip_pairs(depths, st...  19 us
    ppermute x3, waiting for transfers between devices, shards(): wave = lax.ppermute(wave, 'depth', [(tick_no, tick_no + 1)])  11.9 us
    ppermute x6, starting transfers between devices, gather_strips(): lax.ppermute(piece_of(target), ('depth', 'strip'), strip_pairs(depths, st...  11.5 us
    ppermute x6, starting transfers between devices, freq_sum(): lax.ppermute(piece, ('depth', 'strip'), strip_pairs(depths, strip_count,...  11.5 us
    ppermute x6, waiting for transfers between devices, freq_sum(): lax.ppermute(piece, ('depth', 'strip'), strip_pairs(depths, strip_count,...  9.88 us
    ppermute x3, starting transfers between devices, shards(): wave = lax.ppermute(wave, 'depth', [(tick_no, tick_no + 1)])  2.66 us
    unnamed x20, local copies, waits for them, and re-layouts  2.41 us
  transfers between devices with their start and end apart: 15, of which 5 were waited for; matrix products, arithmetic and copies ran while one was open for 5% of the time, Pallas kernels for 0%

profile of v14, /device:TPU:11, one launch (start us, length us, event | category | flops | bytes accessed | tf_op | source)
XLA Modules:
  0.0 115.5 jit_solution(15151651667898375240)
XLA Ops:
  0.0 0.9 convert_element_type.9
  1.0 1.1 dynamic-slice_bitcast_fusion.6
  2.4 3.2 %collective-permute-start = (f32[5,8,2048]{2,1,0:T(8,128)S(1)}, f32[5,8,2048]{2,1,0:T(8,128)S(1)}, u32[]{:S(2)}, u32[]{:S(2)}) collective-permute-start(f32[5,8,2048]{2,1,0:T(8,128)S(1)} %get-tuple-element.36), channel_id=1, source_target_pairs={{0,1},{1,2},{2,3},{3,0},{8,9},{9,10},{10,11},{11,8},{12,13},{13,14... | collective-permute-start | bytes 983048 | tf_op jit(solution)/shard_map/ppermute | solution.py:484
  5.7 2.9 %collective-permute-start.1 = (f32[5,8,2048]{2,1,0:T(8,128)S(1)}, f32[5,8,2048]{2,1,0:T(8,128)S(1)}, u32[]{:S(2)}, u32[]{:S(2)}) collective-permute-start(f32[5,8,2048]{2,1,0:T(8,128)S(1)} %get-tuple-element.37), channel_id=1, source_target_pairs={{0,2},{1,3},{2,0},{3,1},{8,10},{9,11},{10,8},{11,9},{12,14},{13,15... | collective-permute-start | bytes 983048 | tf_op jit(solution)/shard_map/ppermute | solution.py:484
  8.6 3.4 %collective-permute-start.2 = (f32[5,8,2048]{2,1,0:T(8,128)S(1)}, f32[5,8,2048]{2,1,0:T(8,128)S(1)}, u32[]{:S(2)}, u32[]{:S(2)}) collective-permute-start(f32[5,8,2048]{2,1,0:T(8,128)S(1)} %get-tuple-element.35), channel_id=1, source_target_pairs={{0,3},{1,0},{2,1},{3,2},{8,11},{9,8},{10,9},{11,10},{12,15},{13,12... | collective-permute-start | bytes 983048 | tf_op jit(solution)/shard_map/ppermute | solution.py:484
  13.3 0.8 fusion.16
  16.9 16.2 %collective-permute-done.1 = f32[5,8,2048]{2,1,0:T(8,128)S(1)} collective-permute-done((f32[5,8,2048]{2,1,0:T(8,128)S(1)}, f32[5,8,2048]{2,1,0:T(8,128)S(1)}, u32[]{:S(2)}, u32[]{:S(2)}) %collective-permute-start.1) | collective-permute-done | bytes 327712 | tf_op jit(solution)/shard_map/ppermute | solution.py:484
  33.1 2.8 %collective-permute-done.2 = f32[5,8,2048]{2,1,0:T(8,128)S(1)} collective-permute-done((f32[5,8,2048]{2,1,0:T(8,128)S(1)}, f32[5,8,2048]{2,1,0:T(8,128)S(1)}, u32[]{:S(2)}, u32[]{:S(2)}) %collective-permute-start.2) | collective-permute-done | bytes 327712 | tf_op jit(solution)/shard_map/ppermute | solution.py:484
  35.9 0.8 slice.10.refs_1_
  36.7 1.0 slice_convert_fusion.refs_2_
  37.7 8.5 %shard_map.118 = (f32[2,32,2048]{2,1,0:T(8,128)}, f32[4,3,8,2048]{3,2,1,0:T(8,128)}) custom-call(f32[72]{0:T(128)} %reshape.125.refs_0_, f32[2,32,2048]{2,1,0:T(8,128)} %slice.10.refs_1_, s32[3,32,2048]{2,1,0:T(8,128)} %slice_convert_fusion.refs_2_, f32[3,2,16,128]{3,2,1,0:T(8,128)} %pad_maximum_fusion.4.refs_3_, f32[2,16,128]{2,1,0:T(8,128)} %constant.125.clone.refs_4_, ...), custom_call_target="tpu_custom_call" | custom-call | flops 1286602752 | bytes 4718592 | tf_op jit(solution)/shard_map/pallas_call | solution.py:394
  46.9 0.7 collective-permute-start.5
  47.6 0.7 collective-permute-start.6
  48.2 0.7 collective-permute-start.3
  49.2 1.0 convert_element_type.11.refs_2_
  50.1 0.8 copy-done.2
  50.9 8.4 %shard_map.119 = (f32[2,32,2048]{2,1,0:T(8,128)}, f32[4,3,8,2048]{3,2,1,0:T(8,128)}) custom-call(f32[72]{0:T(128)} %reshape.125.refs_0_, f32[2,32,2048]{2,1,0:T(8,128)} %copy-done.2, s32[3,32,2048]{2,1,0:T(8,128)} %convert_element_type.11.refs_2_, f32[3,2,16,128]{3,2,1,0:T(8,128)} %pad_maximum_fusion.4.refs_3_, f32[2,16,128]{2,1,0:T(8,128)} %constant.125.clone.refs_4_, ...), custom_call_target="tpu_custom_call" | custom-call | flops 1286602752 | bytes 4718592 | tf_op jit(solution)/shard_map/pallas_call | solution.py:394
  59.4 0.7 collective-permute-start.7
  60.1 0.8 copy-done.4
  60.9 8.4 %shard_map.120 = (f32[2,32,2048]{2,1,0:T(8,128)}, f32[4,3,8,2048]{3,2,1,0:T(8,128)}) custom-call(f32[72]{0:T(128)} %reshape.125.refs_0_, f32[2,32,2048]{2,1,0:T(8,128)} %copy-done.4, s32[3,32,2048]{2,1,0:T(8,128)} %slice_convert_fusion.refs_2_, f32[3,2,16,128]{3,2,1,0:T(8,128)} %pad_maximum_fusion.4.refs_3_, f32[2,16,128]{2,1,0:T(8,128)} %constant.125.clone.refs_4_, ...), custom_call_target="tpu_custom_call" | custom-call | flops 1286602752 | bytes 4718592 | tf_op jit(solution)/shard_map/pallas_call | solution.py:394
  69.3 1.3 %collective-permute-start.8 = (f32[2,32,2048]{2,1,0:T(8,128)}, f32[2,32,2048]{2,1,0:T(8,128)S(1)}, u32[]{:S(2)}, u32[]{:S(2)}) collective-permute-start(f32[2,32,2048]{2,1,0:T(8,128)} %get-tuple-element.19), channel_id=1, source_target_pairs={{8,12},{9,13},{10,14},{11,15},{24,28},{25,29},{26,30},{27,31}} | collective-permute-start | bytes 1572872 | tf_op jit(solution)/shard_map/ppermute | solution.py:546
  70.8 11.9 %collective-permute-done.8.refs_1_ = f32[2,32,2048]{2,1,0:T(8,128)S(1)} collective-permute-done((f32[2,32,2048]{2,1,0:T(8,128)}, f32[2,32,2048]{2,1,0:T(8,128)S(1)}, u32[]{:S(2)}, u32[]{:S(2)}) %collective-permute-start.8) | collective-permute-done | bytes 524320 | tf_op jit(solution)/shard_map/ppermute | solution.py:546
  82.7 0.8 copy-done.3
  83.4 8.5 %shard_map.121 = (f32[2,32,2048]{2,1,0:T(8,128)}, f32[4,3,8,2048]{3,2,1,0:T(8,128)}) custom-call(f32[72]{0:T(128)} %reshape.125.refs_0_, f32[2,32,2048]{2,1,0:T(8,128)} %copy-done.3, s32[3,32,2048]{2,1,0:T(8,128)} %slice_convert_fusion.refs_2_, f32[3,2,16,128]{3,2,1,0:T(8,128)} %pad_maximum_fusion.4.refs_3_, f32[2,16,128]{2,1,0:T(8,128)} %constant.125.clone.refs_4_, ...), custom_call_target="tpu_custom_call" | custom-call | flops 1286602752 | bytes 4718592 | tf_op jit(solution)/shard_map/pallas_call | solution.py:394
  91.9 1.2 %broadcast_select_fusion = f32[4,3,8,2048]{3,2,1,0:T(8,128)S(1)} fusion(f32[4,3,8,2048]{3,2,1,0:T(8,128)} %get-tuple-element.23, f32[4,3,8,2048]{3,2,1,0:T(8,128)S(1)} %select_select_fusion, pred[]{:T(512)S(6)} %eq.25), kind=kLoop, calls=%fused_computation.7 | loop fusion | flops 196608 | bytes 2359297 | tf_op jit(solution)/shard_map/jit(_where)/select_n | solution.py:544
  93.2 1.9 %collective-permute-start.14 = (f32[3,8,2048]{2,1,0:T(8,128)S(1)}, f32[3,8,2048]{2,1,0:T(8,128)S(1)}, u32[]{:S(2)}, u32[]{:S(2)}) collective-permute-start(f32[3,8,2048]{2,1,0:T(8,128)S(1)} %get-tuple-element.29), channel_id=1, source_target_pairs={{12,15},{13,12},{14,13},{15,14},{28,31},{29,28},{30,29},{31,30}} | collective-permute-start | bytes 589832 | tf_op jit(solution)/shard_map/ppermute | solution.py:536
  95.1 3.3 %collective-permute-start.13 = (f32[3,8,2048]{2,1,0:T(8,128)S(1)}, f32[3,8,2048]{2,1,0:T(8,128)S(1)}, u32[]{:S(2)}, u32[]{:S(2)}) collective-permute-start(f32[3,8,2048]{2,1,0:T(8,128)S(1)} %get-tuple-element.30), channel_id=1, source_target_pairs={{12,14},{13,15},{14,12},{15,13},{28,30},{29,31},{30,28},{31,29}} | collective-permute-start | bytes 589832 | tf_op jit(solution)/shard_map/ppermute | solution.py:536
  98.4 4.3 %collective-permute-start.12 = (f32[3,8,2048]{2,1,0:T(8,128)S(1)}, f32[3,8,2048]{2,1,0:T(8,128)S(1)}, u32[]{:S(2)}, u32[]{:S(2)}) collective-permute-start(f32[3,8,2048]{2,1,0:T(8,128)S(1)} %get-tuple-element.28), channel_id=1, source_target_pairs={{12,13},{13,14},{14,15},{15,12},{28,29},{29,30},{30,31},{31,28}} | collective-permute-start | bytes 589832 | tf_op jit(solution)/shard_map/ppermute | solution.py:536
  102.8 0.7 collective-permute-start.11
  104.8 5.7 %collective-permute-done.13 = f32[3,8,2048]{2,1,0:T(8,128)S(1)} collective-permute-done((f32[3,8,2048]{2,1,0:T(8,128)S(1)}, f32[3,8,2048]{2,1,0:T(8,128)S(1)}, u32[]{:S(2)}, u32[]{:S(2)}) %collective-permute-start.13) | collective-permute-done | bytes 196640 | tf_op jit(solution)/shard_map/ppermute | solution.py:536
  110.5 4.2 %collective-permute-done.12 = f32[3,8,2048]{2,1,0:T(8,128)S(1)} collective-permute-done((f32[3,8,2048]{2,1,0:T(8,128)S(1)}, f32[3,8,2048]{2,1,0:T(8,128)S(1)}, u32[]{:S(2)}, u32[]{:S(2)}) %collective-permute-start.12) | collective-permute-done | bytes 196640 | tf_op jit(solution)/shard_map/ppermute | solution.py:536
  114.7 0.8 fusion.5
  (55 shorter events, 6.8 us)
Async XLA Ops:
  2.2 9.8 %copy-start.5 = (f32[4]{0:T(128)S(1)}, f32[4]{0:T(128)}, u32[]{:S(2)}) copy-start(f32[4]{0:T(128)} %param.13) | copy-start | bytes 52
  2.3 10.4 %copy-start.6 = (f32[8]{0:T(128)S(1)}, f32[8]{0:T(128)}, u32[]{:S(2)}) copy-start(f32[8]{0:T(128)} %param.14) | copy-start | bytes 100
  2.3 10.4 %copy-start.7 = (s32[3]{0:T(128)S(1)}, s32[3]{0:T(128)}, u32[]{:S(2)}) copy-start(s32[3]{0:T(128)} %param.17) | copy-start | bytes 40
  2.3 12.5 %copy-start.8 = (f32[8]{0:T(128)S(1)}, f32[8]{0:T(128)}, u32[]{:S(2)}) copy-start(f32[8]{0:T(128)} %param.15) | copy-start | bytes 100
  2.3 13.7 %copy-start.9 = (f32[16,128]{1,0:T(8,128)S(1)}, f32[16,128]{1,0:T(8,128)}, u32[]{:S(2)}) copy-start(f32[16,128]{1,0:T(8,128)} %constant.133) | copy-start | bytes 24580
  2.4 14.4 %collective-permute-start = (f32[5,8,2048]{2,1,0:T(8,128)S(1)}, f32[5,8,2048]{2,1,0:T(8,128)S(1)}, u32[]{:S(2)}, u32[]{:S(2)}) collective-permute-start(f32[5,8,2048]{2,1,0:T(8,128)S(1)} %get-tuple-element.36), channel_id=1, source_target_pairs={{0,1},{1,2},{2,3},{3,0},{8,9},{9,10},{10,11},{11,8},{12,13},{13,14... | collective-permute-start | bytes 983048 | tf_op jit(solution)/shard_map/ppermute | solution.py:484
  5.7 27.4 %collective-permute-start.1 = (f32[5,8,2048]{2,1,0:T(8,128)S(1)}, f32[5,8,2048]{2,1,0:T(8,128)S(1)}, u32[]{:S(2)}, u32[]{:S(2)}) collective-permute-start(f32[5,8,2048]{2,1,0:T(8,128)S(1)} %get-tuple-element.37), channel_id=1, source_target_pairs={{0,2},{1,3},{2,0},{3,1},{8,10},{9,11},{10,8},{11,9},{12,14},{13,15... | collective-permute-start | bytes 983048 | tf_op jit(solution)/shard_map/ppermute | solution.py:484
  8.6 27.3 %collective-permute-start.2 = (f32[5,8,2048]{2,1,0:T(8,128)S(1)}, f32[5,8,2048]{2,1,0:T(8,128)S(1)}, u32[]{:S(2)}, u32[]{:S(2)}) collective-permute-start(f32[5,8,2048]{2,1,0:T(8,128)S(1)} %get-tuple-element.35), channel_id=1, source_target_pairs={{0,3},{1,0},{2,1},{3,2},{8,11},{9,8},{10,9},{11,10},{12,15},{13,12... | collective-permute-start | bytes 983048 | tf_op jit(solution)/shard_map/ppermute | solution.py:484
  46.2 2.8 %collective-permute-start.4 = (f32[3,8,2048]{2,1,0:T(8,128)S(1)}, f32[3,8,2048]{2,1,0:T(8,128)S(1)}, u32[]{:S(2)}, u32[]{:S(2)}) collective-permute-start(f32[3,8,2048]{2,1,0:T(8,128)S(1)} %convert_element_type.9), channel_id=1, source_target_pairs={{4,5},{5,6},{6,7},{7,4},{20,21},{21,22},{22,23},{23,20}} | collective-permute-start | bytes 589832 | tf_op jit(solution)/shard_map/ppermute | solution.py:484
  46.9 2.2 %collective-permute-start.5 = (f32[3,8,2048]{2,1,0:T(8,128)S(1)}, f32[3,8,2048]{2,1,0:T(8,128)S(1)}, u32[]{:S(2)}, u32[]{:S(2)}) collective-permute-start(f32[3,8,2048]{2,1,0:T(8,128)S(1)} %convert_element_type.9), channel_id=1, source_target_pairs={{4,6},{5,7},{6,4},{7,5},{20,22},{21,23},{22,20},{23,21}} | collective-permute-start | bytes 589832 | tf_op jit(solution)/shard_map/ppermute | solution.py:484
  47.6 1.6 %collective-permute-start.6 = (f32[3,8,2048]{2,1,0:T(8,128)S(1)}, f32[3,8,2048]{2,1,0:T(8,128)S(1)}, u32[]{:S(2)}, u32[]{:S(2)}) collective-permute-start(f32[3,8,2048]{2,1,0:T(8,128)S(1)} %convert_element_type.9), channel_id=1, source_target_pairs={{4,7},{5,4},{6,5},{7,6},{20,23},{21,20},{22,21},{23,22}} | collective-permute-start | bytes 589832 | tf_op jit(solution)/shard_map/ppermute | solution.py:484
  48.2 1.9 %collective-permute-start.3 = (f32[2,32,2048]{2,1,0:T(8,128)}, f32[2,32,2048]{2,1,0:T(8,128)S(1)}, u32[]{:S(2)}, u32[]{:S(2)}) collective-permute-start(f32[2,32,2048]{2,1,0:T(8,128)} %get-tuple-element.15), channel_id=1, source_target_pairs={{0,4},{1,5},{2,6},{3,7},{16,20},{17,21},{18,22},{19,23}} | collective-permute-start | bytes 1572872 | tf_op jit(solution)/shard_map/ppermute | solution.py:546
  50.1 0.8 copy-start.2
  59.4 0.7 collective-permute-start.7
  60.1 10.5 %copy-start = (f32[4,3,8,2048]{3,2,1,0:T(8,128)S(1)}, f32[4,3,8,2048]{3,2,1,0:T(8,128)}, u32[]{:S(2)}) copy-start(f32[4,3,8,2048]{3,2,1,0:T(8,128)} %get-tuple-element.16) | copy-start | bytes 2359300
  60.1 10.5 %copy-start.1 = (f32[4,3,8,2048]{3,2,1,0:T(8,128)S(1)}, f32[4,3,8,2048]{3,2,1,0:T(8,128)}, u32[]{:S(2)}) copy-start(f32[4,3,8,2048]{3,2,1,0:T(8,128)} %get-tuple-element.21) | copy-start | bytes 2359300
  60.1 0.8 copy-start.4
  69.3 13.3 %collective-permute-start.8 = (f32[2,32,2048]{2,1,0:T(8,128)}, f32[2,32,2048]{2,1,0:T(8,128)S(1)}, u32[]{:S(2)}, u32[]{:S(2)}) collective-permute-start(f32[2,32,2048]{2,1,0:T(8,128)} %get-tuple-element.19), channel_id=1, source_target_pairs={{8,12},{9,13},{10,14},{11,15},{24,28},{25,29},{26,30},{27,31}} | collective-permute-start | bytes 1572872 | tf_op jit(solution)/shard_map/ppermute | solution.py:546
  82.7 0.8 copy-start.3
  93.2 10.9 %collective-permute-start.14 = (f32[3,8,2048]{2,1,0:T(8,128)S(1)}, f32[3,8,2048]{2,1,0:T(8,128)S(1)}, u32[]{:S(2)}, u32[]{:S(2)}) collective-permute-start(f32[3,8,2048]{2,1,0:T(8,128)S(1)} %get-tuple-element.29), channel_id=1, source_target_pairs={{12,15},{13,12},{14,13},{15,14},{28,31},{29,28},{30,29},{31,30}} | collective-permute-start | bytes 589832 | tf_op jit(solution)/shard_map/ppermute | solution.py:536
  95.1 15.3 %collective-permute-start.13 = (f32[3,8,2048]{2,1,0:T(8,128)S(1)}, f32[3,8,2048]{2,1,0:T(8,128)S(1)}, u32[]{:S(2)}, u32[]{:S(2)}) collective-permute-start(f32[3,8,2048]{2,1,0:T(8,128)S(1)} %get-tuple-element.30), channel_id=1, source_target_pairs={{12,14},{13,15},{14,12},{15,13},{28,30},{29,31},{30,28},{31,29}} | collective-permute-start | bytes 589832 | tf_op jit(solution)/shard_map/ppermute | solution.py:536
  98.4 16.3 %collective-permute-start.12 = (f32[3,8,2048]{2,1,0:T(8,128)S(1)}, f32[3,8,2048]{2,1,0:T(8,128)S(1)}, u32[]{:S(2)}, u32[]{:S(2)}) collective-permute-start(f32[3,8,2048]{2,1,0:T(8,128)S(1)} %get-tuple-element.28), channel_id=1, source_target_pairs={{12,13},{13,14},{14,15},{15,12},{28,29},{29,30},{30,31},{31,28}} | collective-permute-start | bytes 589832 | tf_op jit(solution)/shard_map/ppermute | solution.py:536
  102.8 11.9 %collective-permute-start.11 = (f32[3,8,2048]{2,1,0:T(8,128)S(1)}, f32[3,8,2048]{2,1,0:T(8,128)S(1)}, u32[]{:S(2)}, u32[]{:S(2)}) collective-permute-start(f32[3,8,2048]{2,1,0:T(8,128)S(1)} %get-tuple-element.26), channel_id=1, source_target_pairs={{0,3},{1,0},{2,1},{3,2},{4,7},{5,4},{6,5},{7,6},{8,11},{9,8},{10,9... | collective-permute-start | bytes 589832 | tf_op jit(solution)/shard_map/ppermute | solution.py:536
  103.5 11.3 %collective-permute-start.10 = (f32[3,8,2048]{2,1,0:T(8,128)S(1)}, f32[3,8,2048]{2,1,0:T(8,128)S(1)}, u32[]{:S(2)}, u32[]{:S(2)}) collective-permute-start(f32[3,8,2048]{2,1,0:T(8,128)S(1)} %get-tuple-element.27), channel_id=1, source_target_pairs={{0,2},{1,3},{2,0},{3,1},{4,6},{5,7},{6,4},{7,5},{8,10},{9,11},{10,... | collective-permute-start | bytes 589832 | tf_op jit(solution)/shard_map/ppermute | solution.py:536
  104.1 10.6 %collective-permute-start.9 = (f32[3,8,2048]{2,1,0:T(8,128)S(1)}, f32[3,8,2048]{2,1,0:T(8,128)S(1)}, u32[]{:S(2)}, u32[]{:S(2)}) collective-permute-start(f32[3,8,2048]{2,1,0:T(8,128)S(1)} %get-tuple-element.25), channel_id=1, source_target_pairs={{0,1},{1,2},{2,3},{3,0},{4,5},{5,6},{6,7},{7,4},{8,9},{9,10},{10,1... | collective-permute-start | bytes 589832 | tf_op jit(solution)/shard_map/ppermute | solution.py:536

commit v15 on v13

--- a/solution.py
+++ b/solution.py
@@ -252,7 +252,7 @@
 
 
 def section_kernel(
-    tab_ref, w_ref, rid_ref, mult_ref, tw_ref, fhi_ref, flo_ref, ghi_ref, glo_ref,
+    tab_ref, w_ref, rid_ref, mult_ref, tw_ref, fhi_ref, flo_ref, ghi_ref, glo_ref, pos_ref,
     wout_ref, img_ref, a_ref, y_ref, v_ref, cs_ref, sn_ref, gn_ref, *, table_len
 ):
     rows = w_ref.shape[1]
@@ -356,7 +356,8 @@
             wout_ref[0, :, blk(a)] = new_re
             wout_ref[1, :, blk(a)] = new_im
             for j in range(strip_count):
-                img_ref[j, k, :, blk(a)] = new_re[j * rows_here:(j + 1) * rows_here]
+                slot = (j - pos_ref[0] + strip_count) % strip_count
+                img_ref[slot, k, :, blk(a)] = new_re[j * rows_here:(j + 1) * rows_here]
         return carry
 
     lax.fori_loop(0, steps, one_step, 0)
@@ -384,7 +385,7 @@
     return (halves(fwd), halves(inv), twiddle, kx_cd.astype(np.float32))
 
 
-def run_section(wave, regions, table, mult, consts, strip_count):
+def run_section(wave, regions, table, mult, consts, strip_count, strip_no):
     (fhi, flo), (ghi, glo), twiddle, _ = consts
     rows, line_len = wave.shape[1], wave.shape[2]
     steps = regions.shape[0]
@@ -397,7 +398,8 @@
             jax.ShapeDtypeStruct(wave.shape, jnp.float32),
             jax.ShapeDtypeStruct((strip_count, steps, rows // strip_count, line_len), jnp.float32),
         ),
-        in_specs=[pl.BlockSpec(memory_space=pltpu.SMEM)] + [vmem] * 8,
+        in_specs=[pl.BlockSpec(memory_space=pltpu.SMEM)] + [vmem] * 8
+        + [pl.BlockSpec(memory_space=pltpu.SMEM)],
         out_specs=(vmem, vmem),
         scratch_shapes=[
             pltpu.VMEM((FFT_BLOCKS * rows, 2 * LANE), jnp.float32),
@@ -411,7 +413,7 @@
             flops=flops, transcendentals=0, bytes_accessed=4 * rows * line_len * 6 * steps
         ),
     )(table, wave, regions, mult, jnp.asarray(twiddle), jnp.asarray(fhi), jnp.asarray(flo),
-      jnp.asarray(ghi), jnp.asarray(glo))
+      jnp.asarray(ghi), jnp.asarray(glo), jnp.reshape(strip_no, (1,)).astype(jnp.int32))
 
 
 def section_tables(omega, region_speed, fd_coeff, ref_region, kx_cd):
@@ -520,7 +522,7 @@
 
     def sweep(regions):
         def live(wave, image):
-            return run_section(wave, regions, table, mult, consts, strip_count)
+            return run_section(wave, regions, table, mult, consts, strip_count, strip_no)
 
         return live
 
@@ -530,8 +532,7 @@
     def freq_sum(image, depths):
         parts = []
         for shift in range(1, strip_count):
-            target = (strip_no + shift) % strip_count
-            piece = lax.dynamic_index_in_dim(image, target, 0, keepdims=False)
+            piece = image[shift]
             parts.append(
                 lax.ppermute(piece, ("depth", "strip"), strip_pairs(depths, strip_count, shift))
             )
@@ -555,7 +556,7 @@
             wave, image = lax.optimization_barrier((wave, image))
             arrived += freq_sum(image, range(segment_count - 1))
     arrived += freq_sum(image, [segment_count - 1])
-    total = lax.dynamic_index_in_dim(image, strip_no, 0, keepdims=False)
+    total = image[0]
     for piece in arrived:
         total = total + piece
     return total

time: 94.9 us -> 94.8 us (level)
  no operation moved by 1% of the time
where the time goes in v15:
time: 94.8 us; the launch traced here: 93.7 us
  waiting for transfers between devices  43.6 us (46%)
  starting transfers between devices  24.8 us (26%)
  Pallas kernels  15.5 us (16%)
  local copies, waits for them, and re-layouts  5.02 us (5%)
  other arithmetic  4.26 us (4%)
    ppermute x3, waiting for transfers between devices, shards(): wave = lax.ppermute(wave, 'depth', [(tick_no, tick_no + 1)])  19.5 us
    ppermute x6, waiting for transfers between devices, gather_strips(): lax.ppermute(piece_of(target), ('depth', 'strip'), strip_pairs(depths, st...  19.1 us
    pallas_call x2, Pallas kernels, run_section(): pl.pallas_call(lambda *refs: section_kernel(*refs, table_len=table_len),...  15.5 us
    ppermute x6, starting transfers between devices, gather_strips(): lax.ppermute(piece_of(target), ('depth', 'strip'), strip_pairs(depths, st...  11.5 us
    ppermute x6, starting transfers between devices, freq_sum(): lax.ppermute(piece, ('depth', 'strip'), strip_pairs(depths, strip_count,...  10.6 us
    ppermute x6, waiting for transfers between devices, freq_sum(): lax.ppermute(piece, ('depth', 'strip'), strip_pairs(depths, strip_count,...  4.96 us
    ppermute x3, starting transfers between devices, shards(): wave = lax.ppermute(wave, 'depth', [(tick_no, tick_no + 1)])  2.68 us
  transfers between devices with their start and end apart: 15, of which 5 were waited for; matrix products, arithmetic and copies ran while one was open for 5% of the time, Pallas kernels for 0%

profile of v15, /device:TPU:11, one launch (start us, length us, event | category | flops | bytes accessed | tf_op | source)
XLA Modules:
  0.0 93.7 jit_solution(17260989094527133809)
XLA Ops:
  0.0 0.9 %convert_element_type.21 = f32[3,8,2048]{2,1,0:T(8,128)S(1)} convert(s32[3,8,2048]{2,1,0:T(8,128)} %param.22) | non-fusion elementwise | flops 49152 | bytes 393216 | tf_op jit(solution)/shard_map/convert_element_type | solution.py:505
  1.0 1.1 %dynamic-slice_bitcast_fusion = (f32[2,8,2048]{2,1,0:T(8,128)S(1)}, f32[2,8,2048]{2,1,0:T(8,128)S(1)}, f32[2,8,2048]{2,1,0:T(8,128)S(1)}, f32[2,8,2048]{2,1,0:T(8,128)S(1)}) fusion(f32[2,4,8,2048]{3,2,1,0:T(8,128)} %param.18, s32[]{:T(128)S(6)} %select_n.79, s32[]{:T(128)S(6)} %select_n.71, s32[]{:T(128)S(6)} %select_n.67, s32[]{:T(128)S(6)} %select_n.75), kind=kLoop, calls=%fused_computation.20 | loop fusion | bytes 1048592 | tf_op jit(solution)/shard_map/jit(dynamic_index_in_dim)/squeeze | solution.py:510
  2.4 3.2 %collective-permute-start = (f32[5,8,2048]{2,1,0:T(8,128)S(1)}, f32[5,8,2048]{2,1,0:T(8,128)}, u32[]{:S(2)}, u32[]{:S(2)}) collective-permute-start(f32[5,8,2048]{2,1,0:T(8,128)S(1)} %get-tuple-element.137), channel_id=1, source_target_pairs={{0,1},{1,2},{2,3},{3,0},{8,9},{9,10},{10,11},{11,8},{12,13},{13,14... | collective-permute-start | bytes 983048 | tf_op jit(solution)/shard_map/ppermute | solution.py:486
  5.6 2.9 %collective-permute-start.1 = (f32[5,8,2048]{2,1,0:T(8,128)S(1)}, f32[5,8,2048]{2,1,0:T(8,128)S(1)}, u32[]{:S(2)}, u32[]{:S(2)}) collective-permute-start(f32[5,8,2048]{2,1,0:T(8,128)S(1)} %get-tuple-element.138), channel_id=1, source_target_pairs={{0,2},{1,3},{2,0},{3,1},{8,10},{9,11},{10,8},{11,9},{12,14},{13,15... | collective-permute-start | bytes 983048 | tf_op jit(solution)/shard_map/ppermute | solution.py:486
  8.6 3.4 %collective-permute-start.2 = (f32[5,8,2048]{2,1,0:T(8,128)S(1)}, f32[5,8,2048]{2,1,0:T(8,128)S(1)}, u32[]{:S(2)}, u32[]{:S(2)}) collective-permute-start(f32[5,8,2048]{2,1,0:T(8,128)S(1)} %get-tuple-element.136), channel_id=1, source_target_pairs={{0,3},{1,0},{2,1},{3,2},{8,11},{9,8},{10,9},{11,10},{12,15},{13,12... | collective-permute-start | bytes 983048 | tf_op jit(solution)/shard_map/ppermute | solution.py:486
  12.7 0.6 gather_fusion
  13.3 0.8 fusion.17
  14.1 0.7 multiply_multiply_fusion
  14.7 0.7 broadcast_divide_fusion
  15.7 1.0 %constant_dynamic-update-slice_fusion.6 = f32[5,32,2048]{2,1,0:T(8,128)S(1)} fusion(f32[5,32,2048]{2,1,0:T(8,128)S(1)} %get-tuple-element.139, f32[5,8,2048]{2,1,0:T(8,128)} %collective-permute-done, s32[]{:T(128)S(6)} %select_n.73), kind=kLoop, calls=%fused_computation.44 | loop fusion | bytes 655364 | tf_op jit(solution)/shard_map/dynamic_update_slice | solution.py:490
  16.7 16.3 %collective-permute-done.1 = f32[5,8,2048]{2,1,0:T(8,128)S(1)} collective-permute-done((f32[5,8,2048]{2,1,0:T(8,128)S(1)}, f32[5,8,2048]{2,1,0:T(8,128)S(1)}, u32[]{:S(2)}, u32[]{:S(2)}) %collective-permute-start.1) | collective-permute-done | bytes 327712 | tf_op jit(solution)/shard_map/ppermute | solution.py:486
  33.1 2.8 %collective-permute-done.2 = f32[5,8,2048]{2,1,0:T(8,128)S(1)} collective-permute-done((f32[5,8,2048]{2,1,0:T(8,128)S(1)}, f32[5,8,2048]{2,1,0:T(8,128)S(1)}, u32[]{:S(2)}, u32[]{:S(2)}) %collective-permute-start.2) | collective-permute-done | bytes 327712 | tf_op jit(solution)/shard_map/ppermute | solution.py:486
  36.1 0.8 slice.38.refs_1_
  37.2 7.8 %shard_map.118 = (f32[2,32,2048]{2,1,0:T(8,128)}, f32[4,3,8,2048]{3,2,1,0:T(8,128)S(1)}) custom-call(f32[72]{0:T(128)S(1)} %reshape.137.refs_0_, f32[2,32,2048]{2,1,0:T(8,128)} %slice.38.refs_1_, s32[3,32,2048]{2,1,0:T(8,128)S(1)} %slice_convert_fusion.refs_2_, f32[3,2,16,128]{3,2,1,0:T(8,128)S(1)} %pad_maximum_fusion.4.refs_3_, ...), custom_call_target="tpu_custom_call" | custom-call | flops 1286602752 | bytes 4718592 | tf_op jit(solution)/shard_map/pallas_call | solution.py:395
  44.9 0.7 collective-permute-start.4
  45.6 0.7 collective-permute-start.5
  46.3 0.7 collective-permute-start.6
  47.0 0.7 collective-permute-start.3
  48.0 0.7 collective-permute-start.7
  48.7 1.3 %collective-permute-start.8 = (f32[2,32,2048]{2,1,0:T(8,128)S(1)}, f32[2,32,2048]{2,1,0:T(8,128)S(1)}, u32[]{:S(2)}, u32[]{:S(2)}) collective-permute-start(f32[2,32,2048]{2,1,0:T(8,128)S(1)} %get-tuple-element.122), channel_id=1, source_target_pairs={{8,12},{9,13},{10,14},{11,15},{24,28},{25,29},{26,30},{27,31}} | collective-permute-start | bytes 1572872 | tf_op jit(solution)/shard_map/ppermute | solution.py:549
  50.0 19.5 %collective-permute-done.8 = f32[2,32,2048]{2,1,0:T(8,128)S(1)} collective-permute-done((f32[2,32,2048]{2,1,0:T(8,128)S(1)}, f32[2,32,2048]{2,1,0:T(8,128)S(1)}, u32[]{:S(2)}, u32[]{:S(2)}) %collective-permute-start.8) | collective-permute-done | bytes 524320 | tf_op jit(solution)/shard_map/ppermute | solution.py:549
  69.5 7.7 %conditional.5 = (f32[4,3,8,2048]{3,2,1,0:T(8,128)S(1)}) conditional(s32[]{:T(128)} %convert_element_type.18, f32[4,3,8,2048]{3,2,1,0:T(8,128)S(1)} %get-tuple-element.124, (s32[]{:T(128)}, f32[72]{0:T(128)S(1)}, f32[2,32,2048]{2,1,0:T(8,128)S(1)}, s32[3,32,2048]{2,1,0:T(8,128)S(1)}, f32[3,2,16,128]{3,2,1,0:T(8,128)S(1)}, ...), branch_computations={%region_4.5_spmd, %region_5.6_spmd} | conditional | flops 1286602752 | bytes 4718600 | solution.py:547
  69.5 7.7 %branch_1_fun.5 = (f32[2,32,2048]{2,1,0:T(8,128)}, f32[4,3,8,2048]{3,2,1,0:T(8,128)S(1)}) custom-call(f32[72]{0:T(128)S(1)} %get-tuple-element.97.refs_0_, f32[2,32,2048]{2,1,0:T(8,128)S(1)} %get-tuple-element.98.refs_1_, s32[3,32,2048]{2,1,0:T(8,128)S(1)} %get-tuple-element.99.refs_2_, f32[3,2,16,128]{3,2,1,0:T(8,128)S(1)} %get-tuple-element.100.refs_3_, ...), custom_call_target="tpu_custom_call" | custom-call | flops 1286602752 | bytes 4718592 | tf_op jit(solution)/shard_map/cond/branch_1_fun/pallas_call | solution.py:395
  77.3 1.9 %collective-permute-start.12 = (f32[3,8,2048]{2,1,0:T(8,128)S(1)}, f32[3,8,2048]{2,1,0:T(8,128)S(1)}, u32[]{:S(2)}, u32[]{:S(2)}) collective-permute-start(f32[3,8,2048]{2,1,0:T(8,128)S(1)} %get-tuple-element.129), channel_id=1, source_target_pairs={{12,13},{13,14},{14,15},{15,12},{28,29},{29,30},{30,31},{31,28}} | collective-permute-start | bytes 589832 | tf_op jit(solution)/shard_map/ppermute | solution.py:537
  79.2 3.3 %collective-permute-start.13 = (f32[3,8,2048]{2,1,0:T(8,128)S(1)}, f32[3,8,2048]{2,1,0:T(8,128)S(1)}, u32[]{:S(2)}, u32[]{:S(2)}) collective-permute-start(f32[3,8,2048]{2,1,0:T(8,128)S(1)} %get-tuple-element.131), channel_id=1, source_target_pairs={{12,14},{13,15},{14,12},{15,13},{28,30},{29,31},{30,28},{31,29}} | collective-permute-start | bytes 589832 | tf_op jit(solution)/shard_map/ppermute | solution.py:537
  82.5 3.4 %collective-permute-start.14 = (f32[3,8,2048]{2,1,0:T(8,128)S(1)}, f32[3,8,2048]{2,1,0:T(8,128)S(1)}, u32[]{:S(2)}, u32[]{:S(2)}) collective-permute-start(f32[3,8,2048]{2,1,0:T(8,128)S(1)} %get-tuple-element.130), channel_id=1, source_target_pairs={{12,15},{13,12},{14,13},{15,14},{28,31},{29,28},{30,29},{31,30}} | collective-permute-start | bytes 589832 | tf_op jit(solution)/shard_map/ppermute | solution.py:537
  85.9 0.7 collective-permute-start.10
  86.6 0.7 collective-permute-start.11
  87.3 0.7 collective-permute-start.9
  88.0 4.3 %collective-permute-done.13 = f32[3,8,2048]{2,1,0:T(8,128)S(1)} collective-permute-done((f32[3,8,2048]{2,1,0:T(8,128)S(1)}, f32[3,8,2048]{2,1,0:T(8,128)S(1)}, u32[]{:S(2)}, u32[]{:S(2)}) %collective-permute-start.13) | collective-permute-done | bytes 196640 | tf_op jit(solution)/shard_map/ppermute | solution.py:537
  92.3 0.6 collective-permute-done.14
  92.9 0.8 fusion.6
  (54 shorter events, 1.9 us)
Async XLA Ops:
  2.2 9.8 %copy-start = (f32[4]{0:T(128)S(1)}, f32[4]{0:T(128)}, u32[]{:S(2)}) copy-start(f32[4]{0:T(128)} %param.19) | copy-start | bytes 52
  2.3 10.4 %copy-start.1 = (f32[8]{0:T(128)S(1)}, f32[8]{0:T(128)}, u32[]{:S(2)}) copy-start(f32[8]{0:T(128)} %param.20) | copy-start | bytes 100
  2.3 10.4 %copy-start.2 = (s32[3]{0:T(128)S(1)}, s32[3]{0:T(128)}, u32[]{:S(2)}) copy-start(s32[3]{0:T(128)} %param.23) | copy-start | bytes 40
  2.3 12.5 %copy-start.3 = (f32[8]{0:T(128)S(1)}, f32[8]{0:T(128)}, u32[]{:S(2)}) copy-start(f32[8]{0:T(128)} %param.21) | copy-start | bytes 100
  2.3 13.2 %copy-start.4 = (f32[16,128]{1,0:T(8,128)S(1)}, f32[16,128]{1,0:T(8,128)}, u32[]{:S(2)}) copy-start(f32[16,128]{1,0:T(8,128)} %constant.105) | copy-start | bytes 24580
  2.4 13.3 %collective-permute-start = (f32[5,8,2048]{2,1,0:T(8,128)S(1)}, f32[5,8,2048]{2,1,0:T(8,128)}, u32[]{:S(2)}, u32[]{:S(2)}) collective-permute-start(f32[5,8,2048]{2,1,0:T(8,128)S(1)} %get-tuple-element.137), channel_id=1, source_target_pairs={{0,1},{1,2},{2,3},{3,0},{8,9},{9,10},{10,11},{11,8},{12,13},{13,14... | collective-permute-start | bytes 983048 | tf_op jit(solution)/shard_map/ppermute | solution.py:486
  5.6 27.4 %collective-permute-start.1 = (f32[5,8,2048]{2,1,0:T(8,128)S(1)}, f32[5,8,2048]{2,1,0:T(8,128)S(1)}, u32[]{:S(2)}, u32[]{:S(2)}) collective-permute-start(f32[5,8,2048]{2,1,0:T(8,128)S(1)} %get-tuple-element.138), channel_id=1, source_target_pairs={{0,2},{1,3},{2,0},{3,1},{8,10},{9,11},{10,8},{11,9},{12,14},{13,15... | collective-permute-start | bytes 983048 | tf_op jit(solution)/shard_map/ppermute | solution.py:486
  8.6 27.3 %collective-permute-start.2 = (f32[5,8,2048]{2,1,0:T(8,128)S(1)}, f32[5,8,2048]{2,1,0:T(8,128)S(1)}, u32[]{:S(2)}, u32[]{:S(2)}) collective-permute-start(f32[5,8,2048]{2,1,0:T(8,128)S(1)} %get-tuple-element.136), channel_id=1, source_target_pairs={{0,3},{1,0},{2,1},{3,2},{8,11},{9,8},{10,9},{11,10},{12,15},{13,12... | collective-permute-start | bytes 983048 | tf_op jit(solution)/shard_map/ppermute | solution.py:486
  35.9 1.0 %copy-start.5 = (bf16[256,256]{1,0:T(8,128)(2,1)S(1)}, bf16[256,256]{1,0:T(8,128)(2,1)}, u32[]{:S(2)}) copy-start(bf16[256,256]{1,0:T(8,128)(2,1)} %constant.100.clone.refs_7_) | copy-start | bytes 393220
  35.9 1.0 %copy-start.6 = (bf16[256,256]{1,0:T(8,128)(2,1)S(1)}, bf16[256,256]{1,0:T(8,128)(2,1)}, u32[]{:S(2)}) copy-start(bf16[256,256]{1,0:T(8,128)(2,1)} %constant.101.clone.refs_8_) | copy-start | bytes 393220
  35.9 1.0 %copy-start.7 = (bf16[256,256]{1,0:T(8,128)(2,1)S(1)}, bf16[256,256]{1,0:T(8,128)(2,1)}, u32[]{:S(2)}) copy-start(bf16[256,256]{1,0:T(8,128)(2,1)} %constant.98.clone.refs_5_) | copy-start | bytes 393220
  35.9 1.2 %copy-start.8 = (bf16[256,256]{1,0:T(8,128)(2,1)S(1)}, bf16[256,256]{1,0:T(8,128)(2,1)}, u32[]{:S(2)}) copy-start(bf16[256,256]{1,0:T(8,128)(2,1)} %constant.99.clone.refs_6_) | copy-start | bytes 393220
  36.0 1.2 %copy-start.9 = (f32[2,16,128]{2,1,0:T(8,128)S(1)}, f32[2,16,128]{2,1,0:T(8,128)}, u32[]{:S(2)}) copy-start(f32[2,16,128]{2,1,0:T(8,128)} %constant.97.clone.refs_4_) | copy-start | bytes 49156
  44.9 2.8 %collective-permute-start.4 = (f32[3,8,2048]{2,1,0:T(8,128)S(1)}, f32[3,8,2048]{2,1,0:T(8,128)S(1)}, u32[]{:S(2)}, u32[]{:S(2)}) collective-permute-start(f32[3,8,2048]{2,1,0:T(8,128)S(1)} %convert_element_type.21), channel_id=1, source_target_pairs={{4,5},{5,6},{6,7},{7,4},{20,21},{21,22},{22,23},{23,20}} | collective-permute-start | bytes 589832 | tf_op jit(solution)/shard_map/ppermute | solution.py:486
  45.6 2.2 %collective-permute-start.5 = (f32[3,8,2048]{2,1,0:T(8,128)S(1)}, f32[3,8,2048]{2,1,0:T(8,128)S(1)}, u32[]{:S(2)}, u32[]{:S(2)}) collective-permute-start(f32[3,8,2048]{2,1,0:T(8,128)S(1)} %convert_element_type.21), channel_id=1, source_target_pairs={{4,6},{5,7},{6,4},{7,5},{20,22},{21,23},{22,20},{23,21}} | collective-permute-start | bytes 589832 | tf_op jit(solution)/shard_map/ppermute | solution.py:486
  46.3 1.6 %collective-permute-start.6 = (f32[3,8,2048]{2,1,0:T(8,128)S(1)}, f32[3,8,2048]{2,1,0:T(8,128)S(1)}, u32[]{:S(2)}, u32[]{:S(2)}) collective-permute-start(f32[3,8,2048]{2,1,0:T(8,128)S(1)} %convert_element_type.21), channel_id=1, source_target_pairs={{4,7},{5,4},{6,5},{7,6},{20,23},{21,20},{22,21},{23,22}} | collective-permute-start | bytes 589832 | tf_op jit(solution)/shard_map/ppermute | solution.py:486
  47.0 1.0 %collective-permute-start.3 = (f32[2,32,2048]{2,1,0:T(8,128)}, f32[2,32,2048]{2,1,0:T(8,128)S(1)}, u32[]{:S(2)}, u32[]{:S(2)}) collective-permute-start(f32[2,32,2048]{2,1,0:T(8,128)} %get-tuple-element.117), channel_id=1, source_target_pairs={{0,4},{1,5},{2,6},{3,7},{16,20},{17,21},{18,22},{19,23}} | collective-permute-start | bytes 1572872 | tf_op jit(solution)/shard_map/ppermute | solution.py:549
  48.0 0.7 collective-permute-start.7
  48.7 20.8 %collective-permute-start.8 = (f32[2,32,2048]{2,1,0:T(8,128)S(1)}, f32[2,32,2048]{2,1,0:T(8,128)S(1)}, u32[]{:S(2)}, u32[]{:S(2)}) collective-permute-start(f32[2,32,2048]{2,1,0:T(8,128)S(1)} %get-tuple-element.122), channel_id=1, source_target_pairs={{8,12},{9,13},{10,14},{11,15},{24,28},{25,29},{26,30},{27,31}} | collective-permute-start | bytes 1572872 | tf_op jit(solution)/shard_map/ppermute | solution.py:549
  77.3 10.0 %collective-permute-start.12 = (f32[3,8,2048]{2,1,0:T(8,128)S(1)}, f32[3,8,2048]{2,1,0:T(8,128)S(1)}, u32[]{:S(2)}, u32[]{:S(2)}) collective-permute-start(f32[3,8,2048]{2,1,0:T(8,128)S(1)} %get-tuple-element.129), channel_id=1, source_target_pairs={{12,13},{13,14},{14,15},{15,12},{28,29},{29,30},{30,31},{31,28}} | collective-permute-start | bytes 589832 | tf_op jit(solution)/shard_map/ppermute | solution.py:537
  79.2 13.1 %collective-permute-start.13 = (f32[3,8,2048]{2,1,0:T(8,128)S(1)}, f32[3,8,2048]{2,1,0:T(8,128)S(1)}, u32[]{:S(2)}, u32[]{:S(2)}) collective-permute-start(f32[3,8,2048]{2,1,0:T(8,128)S(1)} %get-tuple-element.131), channel_id=1, source_target_pairs={{12,14},{13,15},{14,12},{15,13},{28,30},{29,31},{30,28},{31,29}} | collective-permute-start | bytes 589832 | tf_op jit(solution)/shard_map/ppermute | solution.py:537
  82.5 10.4 %collective-permute-start.14 = (f32[3,8,2048]{2,1,0:T(8,128)S(1)}, f32[3,8,2048]{2,1,0:T(8,128)S(1)}, u32[]{:S(2)}, u32[]{:S(2)}) collective-permute-start(f32[3,8,2048]{2,1,0:T(8,128)S(1)} %get-tuple-element.130), channel_id=1, source_target_pairs={{12,15},{13,12},{14,13},{15,14},{28,31},{29,28},{30,29},{31,30}} | collective-permute-start | bytes 589832 | tf_op jit(solution)/shard_map/ppermute | solution.py:537
  85.9 7.0 %collective-permute-start.10 = (f32[3,8,2048]{2,1,0:T(8,128)S(1)}, f32[3,8,2048]{2,1,0:T(8,128)S(1)}, u32[]{:S(2)}, u32[]{:S(2)}) collective-permute-start(f32[3,8,2048]{2,1,0:T(8,128)S(1)} %get-tuple-element.128), channel_id=1, source_target_pairs={{0,2},{1,3},{2,0},{3,1},{4,6},{5,7},{6,4},{7,5},{8,10},{9,11},{10,... | collective-permute-start | bytes 589832 | tf_op jit(solution)/shard_map/ppermute | solution.py:537
  86.6 6.3 %collective-permute-start.11 = (f32[3,8,2048]{2,1,0:T(8,128)S(1)}, f32[3,8,2048]{2,1,0:T(8,128)S(1)}, u32[]{:S(2)}, u32[]{:S(2)}) collective-permute-start(f32[3,8,2048]{2,1,0:T(8,128)S(1)} %get-tuple-element.127), channel_id=1, source_target_pairs={{0,3},{1,0},{2,1},{3,2},{4,7},{5,4},{6,5},{7,6},{8,11},{9,8},{10,9... | collective-permute-start | bytes 589832 | tf_op jit(solution)/shard_map/ppermute | solution.py:537
  87.3 5.6 %collective-permute-start.9 = (f32[3,8,2048]{2,1,0:T(8,128)S(1)}, f32[3,8,2048]{2,1,0:T(8,128)S(1)}, u32[]{:S(2)}, u32[]{:S(2)}) collective-permute-start(f32[3,8,2048]{2,1,0:T(8,128)S(1)} %get-tuple-element.126), channel_id=1, source_target_pairs={{0,1},{1,2},{2,3},{3,0},{4,5},{5,6},{6,7},{7,4},{8,9},{9,10},{10,1... | collective-permute-start | bytes 589832 | tf_op jit(solution)/shard_map/ppermute | solution.py:537

commit v16 on v15

--- a/solution.py
+++ b/solution.py
@@ -510,11 +510,24 @@
             [region_f, lax.dynamic_index_in_dim(surface, target, 1, keepdims=False)], axis=0
         )
 
-    gathered = gather_strips(
-        with_surface, with_surface(strip_no), early, strip_no, strip_count, rows_here
-    )
-    regions_a = gathered[:steps].astype(jnp.int32)
-    wave = gathered[steps:]
+    rows = rows_here * strip_count
+    regions_a = lax.dynamic_update_slice(
+        jnp.zeros((steps, rows, line_len), jnp.float32), region_f, (0, strip_no * rows_here, 0)
+    )
+    wave = lax.dynamic_update_slice(
+        jnp.zeros((2, rows, line_len), jnp.float32),
+        lax.dynamic_index_in_dim(surface, strip_no, 1, keepdims=False),
+        (0, strip_no * rows_here, 0),
+    )
+    for shift in range(1, strip_count):
+        target = (strip_no + shift) % strip_count
+        got = lax.ppermute(
+            with_surface(target), ("depth", "strip"), strip_pairs(early, strip_count, shift)
+        )
+        start = (0, ((strip_no - shift) % strip_count) * rows_here, 0)
+        regions_a = lax.dynamic_update_slice(regions_a, got[:steps], start)
+        wave = lax.dynamic_update_slice(wave, got[steps:], start)
+    regions_a = regions_a.astype(jnp.int32)
     omega = lax.dynamic_index_in_dim(omegas, strip_no, 0, keepdims=False)
     table, mult = section_tables(omega, region_speed, fd_coeff, ref_region, jnp.asarray(consts[3]))
     image = jnp.zeros((strip_count, steps, rows_here, line_len), jnp.float32)

time: 94.8 us -> 98.1 us (1.035)
  local copies, waits for them, and re-layouts: 5.02 us -> 10.6 us
  waiting for transfers between devices: 43.6 us -> 40.4 us
    ppermute x6 -> x3, waiting for transfers between devices: 19.1 us -> 0.01 us  [gather_strips(): lax.ppermute(piece_of(target), ('depth', 'strip'), strip_pairs(depths, st...]
    ppermute x0 -> x3, waiting for transfers between devices: none -> 15.8 us  [shards(): lax.ppermute(with_surface(target), ('depth', 'strip'), strip_pairs(early,...]
    ppermute x6 -> x3, starting transfers between devices: 11.5 us -> 2.01 us  [gather_strips(): lax.ppermute(piece_of(target), ('depth', 'strip'), strip_pairs(depths, st...]
    ppermute x0 -> x3, starting transfers between devices: none -> 9.49 us  [shards(): lax.ppermute(with_surface(target), ('depth', 'strip'), strip_pairs(early,...]
    unnamed x20 -> x28, local copies, waits for them, and re-layouts: 0.32 us -> 5.83 us
    dynamic_update_slice x0 -> x7, local copies, waits for them, and re-layouts: none -> 2.04 us  [the longest x3 1.06 us: shards(): wave = lax.dynamic_update_slice(wave, got[steps:], start)]
    dynamic_update_slice x6 -> x3, local copies, waits for them, and re-layouts: 1.11 us -> 0.06 us  [gather_strips(): full = lax.dynamic_update_slice(full, got, (0, source * rows_here, 0))]
where the time goes in v16:
time: 98.1 us; the launch traced here: 96.8 us
  waiting for transfers between devices  40.4 us (41%)
  starting transfers between devices  24.7 us (25%)
  Pallas kernels  15.4 us (16%)
  local copies, waits for them, and re-layouts  10.6 us (11%)
  other arithmetic  5.09 us (5%)
    ppermute x3, waiting for transfers between devices, shards(): wave = lax.ppermute(wave, 'depth', [(tick_no, tick_no + 1)])  19.7 us
    ppermute x3, waiting for transfers between devices, shards(): lax.ppermute(with_surface(target), ('depth', 'strip'), strip_pairs(early,...  15.8 us
    pallas_call x2, Pallas kernels, run_section(): pl.pallas_call(lambda *refs: section_kernel(*refs, table_len=table_len),...  15.4 us
    ppermute x6, starting transfers between devices, freq_sum(): lax.ppermute(piece, ('depth', 'strip'), strip_pairs(depths, strip_count,...  10.6 us
    ppermute x3, starting transfers between devices, shards(): lax.ppermute(with_surface(target), ('depth', 'strip'), strip_pairs(early,...  9.49 us
    unnamed x28, local copies, waits for them, and re-layouts  5.83 us
    ppermute x6, waiting for transfers between devices, freq_sum(): lax.ppermute(piece, ('depth', 'strip'), strip_pairs(depths, strip_count,...  5 us
    ppermute x3, starting transfers between devices, shards(): wave = lax.ppermute(wave, 'depth', [(tick_no, tick_no + 1)])  2.67 us
  transfers between devices with their start and end apart: 15, of which 5 were waited for; matrix products, arithmetic and copies ran while one was open for 5% of the time, Pallas kernels for 0%

profile of v16, /device:TPU:11, one launch (start us, length us, event | category | flops | bytes accessed | tf_op | source)
XLA Modules:
  0.0 96.8 jit_solution(18120933371561101708)
XLA Ops:
  0.0 0.9 convert_element_type.21
  1.0 1.1 %dynamic-slice_bitcast_fusion = (f32[2,8,2048]{2,1,0:T(8,128)S(1)}, f32[2,8,2048]{2,1,0:T(8,128)S(1)}, f32[2,8,2048]{2,1,0:T(8,128)S(1)}) fusion(f32[2,4,8,2048]{3,2,1,0:T(8,128)} %param.18, s32[]{:T(128)S(6)} %select_n.83, s32[]{:T(128)S(6)} %select_n.75, s32[]{:T(128)S(6)} %select_n.79), kind=kLoop, calls=%fused_computation.24 | loop fusion | bytes 786444 | tf_op jit(solution)/shard_map/jit(dynamic_index_in_dim)/squeeze | solution.py:510
  2.0 0.9 pad_maximum_fusion
  3.0 3.2 %collective-permute-start = (f32[5,8,2048]{2,1,0:T(8,128)}, f32[5,8,2048]{2,1,0:T(8,128)S(1)}, u32[]{:S(2)}, u32[]{:S(2)}) collective-permute-start(f32[5,8,2048]{2,1,0:T(8,128)} %get-tuple-element.137), channel_id=1, source_target_pairs={{0,1},{1,2},{2,3},{3,0},{8,9},{9,10},{10,11},{11,8},{12,13},{13,14... | collective-permute-start | bytes 983048 | tf_op jit(solution)/shard_map/ppermute | solution.py:524
  6.2 2.9 %collective-permute-start.1 = (f32[5,8,2048]{2,1,0:T(8,128)}, f32[5,8,2048]{2,1,0:T(8,128)S(1)}, u32[]{:S(2)}, u32[]{:S(2)}) collective-permute-start(f32[5,8,2048]{2,1,0:T(8,128)} %get-tuple-element.136), channel_id=1, source_target_pairs={{0,2},{1,3},{2,0},{3,1},{8,10},{9,11},{10,8},{11,9},{12,14},{13,15... | collective-permute-start | bytes 983048 | tf_op jit(solution)/shard_map/ppermute | solution.py:524
  9.1 3.4 %collective-permute-start.2 = (f32[5,8,2048]{2,1,0:T(8,128)S(1)}, f32[5,8,2048]{2,1,0:T(8,128)S(1)}, u32[]{:S(2)}, u32[]{:S(2)}) collective-permute-start(f32[5,8,2048]{2,1,0:T(8,128)S(1)} %get-tuple-element.135), channel_id=1, source_target_pairs={{0,3},{1,0},{2,1},{3,2},{8,11},{9,8},{10,9},{11,10},{12,15},{13,12... | collective-permute-start | bytes 983048 | tf_op jit(solution)/shard_map/ppermute | solution.py:524
  15.7 0.8 fusion.16
  18.1 0.9 copy-done
  19.9 0.9 bitcast_dynamic-update-slice_fusion
  20.8 13.1 %collective-permute-done.1 = f32[5,8,2048]{2,1,0:T(8,128)S(1)} collective-permute-done((f32[5,8,2048]{2,1,0:T(8,128)}, f32[5,8,2048]{2,1,0:T(8,128)S(1)}, u32[]{:S(2)}, u32[]{:S(2)}) %collective-permute-start.1) | collective-permute-done | bytes 327712 | tf_op jit(solution)/shard_map/ppermute | solution.py:524
  33.9 2.7 %collective-permute-done.2 = f32[5,8,2048]{2,1,0:T(8,128)S(1)} collective-permute-done((f32[5,8,2048]{2,1,0:T(8,128)S(1)}, f32[5,8,2048]{2,1,0:T(8,128)S(1)}, u32[]{:S(2)}, u32[]{:S(2)}) %collective-permute-start.2) | collective-permute-done | bytes 327712 | tf_op jit(solution)/shard_map/ppermute | solution.py:524
  36.6 0.7 copy-done.2
  37.5 1.0 %slice_dynamic-update-slice_fusion.3.refs_1_ = f32[2,32,2048]{2,1,0:T(8,128)S(1)} fusion(f32[2,32,2048]{2,1,0:T(8,128)S(1)} %slice_dynamic-update-slice_fusion.4, s32[]{:T(128)S(6)} %select_n.85, f32[5,8,2048]{2,1,0:T(8,128)} %copy-done.2), kind=kLoop, calls=%fused_computation.20 | loop fusion | bytes 262148 | tf_op jit(solution)/shard_map/dynamic_update_slice | solution.py:529
  38.6 0.8 copy-done.1
  39.4 7.8 %shard_map.118 = (f32[2,32,2048]{2,1,0:T(8,128)}, f32[4,3,8,2048]{3,2,1,0:T(8,128)S(1)}) custom-call(f32[72]{0:T(128)S(1)} %reshape.137.refs_0_, f32[2,32,2048]{2,1,0:T(8,128)} %copy-done.1, s32[3,32,2048]{2,1,0:T(8,128)S(1)} %convert_element_type.22.refs_2_, f32[3,2,16,128]{3,2,1,0:T(8,128)S(1)} %pad_maximum_fusion.3.refs_3_, f32[2,16,128]{2,1,0:T(8,128)S(1)} %copy-done.14, ...), custom_call_target="tpu_custom_call" | custom-call | flops 1286602752 | bytes 4718592 | tf_op jit(solution)/shard_map/pallas_call | solution.py:395
  47.9 0.7 collective-permute-start.5
  48.5 0.7 collective-permute-start.6
  49.2 0.7 collective-permute-start.3
  50.2 0.8 copy-done.11
  51.0 0.7 collective-permute-start.7
  51.8 1.3 %collective-permute-start.8 = (f32[2,32,2048]{2,1,0:T(8,128)S(1)}, f32[2,32,2048]{2,1,0:T(8,128)S(1)}, u32[]{:S(2)}, u32[]{:S(2)}) collective-permute-start(f32[2,32,2048]{2,1,0:T(8,128)S(1)} %get-tuple-element.122), channel_id=1, source_target_pairs={{8,12},{9,13},{10,14},{11,15},{24,28},{25,29},{26,30},{27,31}} | collective-permute-start | bytes 1572872 | tf_op jit(solution)/shard_map/ppermute | solution.py:562
  53.1 19.7 %collective-permute-done.8 = f32[2,32,2048]{2,1,0:T(8,128)S(1)} collective-permute-done((f32[2,32,2048]{2,1,0:T(8,128)S(1)}, f32[2,32,2048]{2,1,0:T(8,128)S(1)}, u32[]{:S(2)}, u32[]{:S(2)}) %collective-permute-start.8) | collective-permute-done | bytes 524320 | tf_op jit(solution)/shard_map/ppermute | solution.py:562
  72.7 7.6 %conditional.5 = (f32[4,3,8,2048]{3,2,1,0:T(8,128)S(1)}) conditional(s32[]{:T(128)} %convert_element_type.18, f32[4,3,8,2048]{3,2,1,0:T(8,128)S(1)} %get-tuple-element.124, (s32[]{:T(128)}, f32[72]{0:T(128)S(1)}, f32[2,32,2048]{2,1,0:T(8,128)S(1)}, s32[3,32,2048]{2,1,0:T(8,128)S(1)}, f32[3,2,16,128]{3,2,1,0:T(8,128)S(1)}, ...), branch_computations={%region_4.5_spmd, %region_5.6_spmd} | conditional | flops 1286602752 | bytes 4718600 | solution.py:560
  72.7 7.6 %branch_1_fun.5 = (f32[2,32,2048]{2,1,0:T(8,128)}, f32[4,3,8,2048]{3,2,1,0:T(8,128)S(1)}) custom-call(f32[72]{0:T(128)S(1)} %get-tuple-element.97.refs_0_, f32[2,32,2048]{2,1,0:T(8,128)S(1)} %get-tuple-element.98.refs_1_, s32[3,32,2048]{2,1,0:T(8,128)S(1)} %get-tuple-element.99.refs_2_, f32[3,2,16,128]{3,2,1,0:T(8,128)S(1)} %get-tuple-element.100.refs_3_, ...), custom_call_target="tpu_custom_call" | custom-call | flops 1286602752 | bytes 4718592 | tf_op jit(solution)/shard_map/cond/branch_1_fun/pallas_call | solution.py:395
  80.4 1.9 %collective-permute-start.12 = (f32[3,8,2048]{2,1,0:T(8,128)S(1)}, f32[3,8,2048]{2,1,0:T(8,128)S(1)}, u32[]{:S(2)}, u32[]{:S(2)}) collective-permute-start(f32[3,8,2048]{2,1,0:T(8,128)S(1)} %get-tuple-element.129), channel_id=1, source_target_pairs={{12,13},{13,14},{14,15},{15,12},{28,29},{29,30},{30,31},{31,28}} | collective-permute-start | bytes 589832 | tf_op jit(solution)/shard_map/ppermute | solution.py:550
  82.4 3.3 %collective-permute-start.13 = (f32[3,8,2048]{2,1,0:T(8,128)S(1)}, f32[3,8,2048]{2,1,0:T(8,128)S(1)}, u32[]{:S(2)}, u32[]{:S(2)}) collective-permute-start(f32[3,8,2048]{2,1,0:T(8,128)S(1)} %get-tuple-element.131), channel_id=1, source_target_pairs={{12,14},{13,15},{14,12},{15,13},{28,30},{29,31},{30,28},{31,29}} | collective-permute-start | bytes 589832 | tf_op jit(solution)/shard_map/ppermute | solution.py:550
  85.7 3.4 %collective-permute-start.14 = (f32[3,8,2048]{2,1,0:T(8,128)S(1)}, f32[3,8,2048]{2,1,0:T(8,128)S(1)}, u32[]{:S(2)}, u32[]{:S(2)}) collective-permute-start(f32[3,8,2048]{2,1,0:T(8,128)S(1)} %get-tuple-element.130), channel_id=1, source_target_pairs={{12,15},{13,12},{14,13},{15,14},{28,31},{29,28},{30,29},{31,30}} | collective-permute-start | bytes 589832 | tf_op jit(solution)/shard_map/ppermute | solution.py:550
  89.0 0.7 collective-permute-start.10
  89.7 0.7 collective-permute-start.11
  90.4 0.7 collective-permute-start.9
  91.1 4.4 %collective-permute-done.13 = f32[3,8,2048]{2,1,0:T(8,128)S(1)} collective-permute-done((f32[3,8,2048]{2,1,0:T(8,128)S(1)}, f32[3,8,2048]{2,1,0:T(8,128)S(1)}, u32[]{:S(2)}, u32[]{:S(2)}) %collective-permute-start.13) | collective-permute-done | bytes 196640 | tf_op jit(solution)/shard_map/ppermute | solution.py:550
  96.1 0.8 fusion.5
  (67 shorter events, 7.4 us)
Async XLA Ops:
  3.0 17.8 %collective-permute-start = (f32[5,8,2048]{2,1,0:T(8,128)}, f32[5,8,2048]{2,1,0:T(8,128)S(1)}, u32[]{:S(2)}, u32[]{:S(2)}) collective-permute-start(f32[5,8,2048]{2,1,0:T(8,128)} %get-tuple-element.137), channel_id=1, source_target_pairs={{0,1},{1,2},{2,3},{3,0},{8,9},{9,10},{10,11},{11,8},{12,13},{13,14... | collective-permute-start | bytes 983048 | tf_op jit(solution)/shard_map/ppermute | solution.py:524
  6.2 27.7 %collective-permute-start.1 = (f32[5,8,2048]{2,1,0:T(8,128)}, f32[5,8,2048]{2,1,0:T(8,128)S(1)}, u32[]{:S(2)}, u32[]{:S(2)}) collective-permute-start(f32[5,8,2048]{2,1,0:T(8,128)} %get-tuple-element.136), channel_id=1, source_target_pairs={{0,2},{1,3},{2,0},{3,1},{8,10},{9,11},{10,8},{11,9},{12,14},{13,15... | collective-permute-start | bytes 983048 | tf_op jit(solution)/shard_map/ppermute | solution.py:524
  9.1 27.5 %collective-permute-start.2 = (f32[5,8,2048]{2,1,0:T(8,128)S(1)}, f32[5,8,2048]{2,1,0:T(8,128)S(1)}, u32[]{:S(2)}, u32[]{:S(2)}) collective-permute-start(f32[5,8,2048]{2,1,0:T(8,128)S(1)} %get-tuple-element.135), channel_id=1, source_target_pairs={{0,3},{1,0},{2,1},{3,2},{8,11},{9,8},{10,9},{11,10},{12,15},{13,12... | collective-permute-start | bytes 983048 | tf_op jit(solution)/shard_map/ppermute | solution.py:524
  12.5 0.7 copy-start.3
  13.2 0.7 copy-start.4
  13.9 0.7 copy-start.5
  16.5 0.7 copy-start.6
  18.0 0.9 copy-start
  18.9 0.7 copy-start.7
  36.6 0.7 copy-start.2
  37.4 1.9 %copy-start.14 = (f32[2,16,128]{2,1,0:T(8,128)S(1)}, f32[2,16,128]{2,1,0:T(8,128)}, u32[]{:S(2)}) copy-start(f32[2,16,128]{2,1,0:T(8,128)} %constant.97.clone.refs_4_) | copy-start | bytes 49156
  37.5 1.9 %copy-start.10 = (bf16[256,256]{1,0:T(8,128)(2,1)S(1)}, bf16[256,256]{1,0:T(8,128)(2,1)}, u32[]{:S(2)}) copy-start(bf16[256,256]{1,0:T(8,128)(2,1)} %constant.98.clone.refs_5_) | copy-start | bytes 393220
  37.5 1.9 %copy-start.12 = (bf16[256,256]{1,0:T(8,128)(2,1)S(1)}, bf16[256,256]{1,0:T(8,128)(2,1)}, u32[]{:S(2)}) copy-start(bf16[256,256]{1,0:T(8,128)(2,1)} %constant.99.clone.refs_6_) | copy-start | bytes 393220
  37.5 1.9 %copy-start.8 = (bf16[256,256]{1,0:T(8,128)(2,1)S(1)}, bf16[256,256]{1,0:T(8,128)(2,1)}, u32[]{:S(2)}) copy-start(bf16[256,256]{1,0:T(8,128)(2,1)} %constant.100.clone.refs_7_) | copy-start | bytes 393220
  37.5 1.9 %copy-start.9 = (bf16[256,256]{1,0:T(8,128)(2,1)S(1)}, bf16[256,256]{1,0:T(8,128)(2,1)}, u32[]{:S(2)}) copy-start(bf16[256,256]{1,0:T(8,128)(2,1)} %constant.101.clone.refs_8_) | copy-start | bytes 393220
  38.6 0.8 copy-start.1
  47.2 2.8 %collective-permute-start.4 = (f32[3,8,2048]{2,1,0:T(8,128)S(1)}, f32[3,8,2048]{2,1,0:T(8,128)S(1)}, u32[]{:S(2)}, u32[]{:S(2)}) collective-permute-start(f32[3,8,2048]{2,1,0:T(8,128)S(1)} %convert_element_type.21), channel_id=1, source_target_pairs={{4,5},{5,6},{6,7},{7,4},{20,21},{21,22},{22,23},{23,20}} | collective-permute-start | bytes 589832 | tf_op jit(solution)/shard_map/ppermute | solution.py:486
  47.9 2.2 %collective-permute-start.5 = (f32[3,8,2048]{2,1,0:T(8,128)S(1)}, f32[3,8,2048]{2,1,0:T(8,128)S(1)}, u32[]{:S(2)}, u32[]{:S(2)}) collective-permute-start(f32[3,8,2048]{2,1,0:T(8,128)S(1)} %convert_element_type.21), channel_id=1, source_target_pairs={{4,6},{5,7},{6,4},{7,5},{20,22},{21,23},{22,20},{23,21}} | collective-permute-start | bytes 589832 | tf_op jit(solution)/shard_map/ppermute | solution.py:486
  48.5 1.6 %collective-permute-start.6 = (f32[3,8,2048]{2,1,0:T(8,128)S(1)}, f32[3,8,2048]{2,1,0:T(8,128)S(1)}, u32[]{:S(2)}, u32[]{:S(2)}) collective-permute-start(f32[3,8,2048]{2,1,0:T(8,128)S(1)} %convert_element_type.21), channel_id=1, source_target_pairs={{4,7},{5,4},{6,5},{7,6},{20,23},{21,20},{22,21},{23,22}} | collective-permute-start | bytes 589832 | tf_op jit(solution)/shard_map/ppermute | solution.py:486
  49.2 1.0 %collective-permute-start.3 = (f32[2,32,2048]{2,1,0:T(8,128)}, f32[2,32,2048]{2,1,0:T(8,128)S(1)}, u32[]{:S(2)}, u32[]{:S(2)}) collective-permute-start(f32[2,32,2048]{2,1,0:T(8,128)} %get-tuple-element.117), channel_id=1, source_target_pairs={{0,4},{1,5},{2,6},{3,7},{16,20},{17,21},{18,22},{19,23}} | collective-permute-start | bytes 1572872 | tf_op jit(solution)/shard_map/ppermute | solution.py:562
  50.1 0.9 copy-start.11
  51.0 0.7 collective-permute-start.7
  51.8 21.0 %collective-permute-start.8 = (f32[2,32,2048]{2,1,0:T(8,128)S(1)}, f32[2,32,2048]{2,1,0:T(8,128)S(1)}, u32[]{:S(2)}, u32[]{:S(2)}) collective-permute-start(f32[2,32,2048]{2,1,0:T(8,128)S(1)} %get-tuple-element.122), channel_id=1, source_target_pairs={{8,12},{9,13},{10,14},{11,15},{24,28},{25,29},{26,30},{27,31}} | collective-permute-start | bytes 1572872 | tf_op jit(solution)/shard_map/ppermute | solution.py:562
  80.4 10.0 %collective-permute-start.12 = (f32[3,8,2048]{2,1,0:T(8,128)S(1)}, f32[3,8,2048]{2,1,0:T(8,128)S(1)}, u32[]{:S(2)}, u32[]{:S(2)}) collective-permute-start(f32[3,8,2048]{2,1,0:T(8,128)S(1)} %get-tuple-element.129), channel_id=1, source_target_pairs={{12,13},{13,14},{14,15},{15,12},{28,29},{29,30},{30,31},{31,28}} | collective-permute-start | bytes 589832 | tf_op jit(solution)/shard_map/ppermute | solution.py:550
  82.4 13.1 %collective-permute-start.13 = (f32[3,8,2048]{2,1,0:T(8,128)S(1)}, f32[3,8,2048]{2,1,0:T(8,128)S(1)}, u32[]{:S(2)}, u32[]{:S(2)}) collective-permute-start(f32[3,8,2048]{2,1,0:T(8,128)S(1)} %get-tuple-element.131), channel_id=1, source_target_pairs={{12,14},{13,15},{14,12},{15,13},{28,30},{29,31},{30,28},{31,29}} | collective-permute-start | bytes 589832 | tf_op jit(solution)/shard_map/ppermute | solution.py:550
  85.7 10.4 %collective-permute-start.14 = (f32[3,8,2048]{2,1,0:T(8,128)S(1)}, f32[3,8,2048]{2,1,0:T(8,128)S(1)}, u32[]{:S(2)}, u32[]{:S(2)}) collective-permute-start(f32[3,8,2048]{2,1,0:T(8,128)S(1)} %get-tuple-element.130), channel_id=1, source_target_pairs={{12,15},{13,12},{14,13},{15,14},{28,31},{29,28},{30,29},{31,30}} | collective-permute-start | bytes 589832 | tf_op jit(solution)/shard_map/ppermute | solution.py:550
  89.0 7.1 %collective-permute-start.10 = (f32[3,8,2048]{2,1,0:T(8,128)S(1)}, f32[3,8,2048]{2,1,0:T(8,128)S(1)}, u32[]{:S(2)}, u32[]{:S(2)}) collective-permute-start(f32[3,8,2048]{2,1,0:T(8,128)S(1)} %get-tuple-element.128), channel_id=1, source_target_pairs={{0,2},{1,3},{2,0},{3,1},{4,6},{5,7},{6,4},{7,5},{8,10},{9,11},{10,... | collective-permute-start | bytes 589832 | tf_op jit(solution)/shard_map/ppermute | solution.py:550
  89.7 6.4 %collective-permute-start.11 = (f32[3,8,2048]{2,1,0:T(8,128)S(1)}, f32[3,8,2048]{2,1,0:T(8,128)S(1)}, u32[]{:S(2)}, u32[]{:S(2)}) collective-permute-start(f32[3,8,2048]{2,1,0:T(8,128)S(1)} %get-tuple-element.127), channel_id=1, source_target_pairs={{0,3},{1,0},{2,1},{3,2},{4,7},{5,4},{6,5},{7,6},{8,11},{9,8},{10,9... | collective-permute-start | bytes 589832 | tf_op jit(solution)/shard_map/ppermute | solution.py:550
  90.4 5.7 %collective-permute-start.9 = (f32[3,8,2048]{2,1,0:T(8,128)S(1)}, f32[3,8,2048]{2,1,0:T(8,128)S(1)}, u32[]{:S(2)}, u32[]{:S(2)}) collective-permute-start(f32[3,8,2048]{2,1,0:T(8,128)S(1)} %get-tuple-element.126), channel_id=1, source_target_pairs={{0,1},{1,2},{2,3},{3,0},{4,5},{5,6},{6,7},{7,4},{8,9},{9,10},{10,1... | collective-permute-start | bytes 589832 | tf_op jit(solution)/shard_map/ppermute | solution.py:550

commit v17 on v15

--- a/solution.py
+++ b/solution.py
@@ -543,6 +543,9 @@
         regions = regions_b if tick_no == 1 else regions_a
         if tick_no == 0:
             wave, image = sweep(regions)(wave, image)
+        elif tick_no == 1:
+            wave, fresh = sweep(regions)(wave, image)
+            image = jnp.where(segment_no == tick_no, fresh, image)
         else:
             wave, image = lax.cond(segment_no == tick_no, sweep(regions), idle, wave, image)
         if tick_no + 1 < segment_count:

time: 94.8 us -> 107 us (1.13)
  Pallas kernels: 15.5 us -> 23.5 us
  waiting for transfers between devices: 43.6 us -> 46.1 us
  starting transfers between devices: 24.8 us -> 26.3 us
    pallas_call x2 -> x3, Pallas kernels: 15.5 us -> 23.5 us  [run_section(): pl.pallas_call(lambda *refs: section_kernel(*refs, table_len=table_len),...]
    ppermute x3, waiting for transfers between devices: 19.5 us -> 21.1 us  [shards(): wave = lax.ppermute(wave, 'depth', [(tick_no, tick_no + 1)])]
    ppermute x3, starting transfers between devices: 2.68 us -> 4.22 us  [shards(): wave = lax.ppermute(wave, 'depth', [(tick_no, tick_no + 1)])]
where the time goes in v17:
time: 107 us; the launch traced here: 106 us
  waiting for transfers between devices  46.1 us (43%)
  starting transfers between devices  26.3 us (25%)
  Pallas kernels  23.5 us (22%)
  other arithmetic  5.24 us (5%)
  local copies, waits for them, and re-layouts  4.05 us (4%)
    pallas_call x3, Pallas kernels, run_section(): pl.pallas_call(lambda *refs: section_kernel(*refs, table_len=table_len),...  23.5 us
    ppermute x3, waiting for transfers between devices, shards(): wave = lax.ppermute(wave, 'depth', [(tick_no, tick_no + 1)])  21.1 us
    ppermute x6, waiting for transfers between devices, gather_strips(): lax.ppermute(piece_of(target), ('depth', 'strip'), strip_pairs(depths, st...  20.1 us
    ppermute x6, starting transfers between devices, gather_strips(): lax.ppermute(piece_of(target), ('depth', 'strip'), strip_pairs(depths, st...  11.5 us
    ppermute x6, starting transfers between devices, freq_sum(): lax.ppermute(piece, ('depth', 'strip'), strip_pairs(depths, strip_count,...  10.6 us
    ppermute x6, waiting for transfers between devices, freq_sum(): lax.ppermute(piece, ('depth', 'strip'), strip_pairs(depths, strip_count,...  4.96 us
    ppermute x3, starting transfers between devices, shards(): wave = lax.ppermute(wave, 'depth', [(tick_no, tick_no + 1)])  4.22 us
  transfers between devices with their start and end apart: 15, of which 5 were waited for; matrix products, arithmetic and copies ran while one was open for 5% of the time, Pallas kernels for 0%

profile of v17, /device:TPU:11, one launch (start us, length us, event | category | flops | bytes accessed | tf_op | source)
XLA Modules:
  0.0 105.8 jit_solution(9191513224398422947)
XLA Ops:
  0.0 0.9 convert_element_type.17
  1.0 1.1 %dynamic-slice_bitcast_fusion = (f32[2,8,2048]{2,1,0:T(8,128)S(1)}, f32[2,8,2048]{2,1,0:T(8,128)S(1)}, f32[2,8,2048]{2,1,0:T(8,128)S(1)}, f32[2,8,2048]{2,1,0:T(8,128)S(1)}) fusion(f32[2,4,8,2048]{3,2,1,0:T(8,128)} %param.16, s32[]{:T(128)S(6)} %select_n.89, s32[]{:T(128)S(6)} %select_n.81, s32[]{:T(128)S(6)} %select_n.77, s32[]{:T(128)S(6)} %select_n.85), kind=kLoop, calls=%fused_computation.21 | loop fusion | bytes 1048592 | tf_op jit(solution)/shard_map/jit(dynamic_index_in_dim)/squeeze | solution.py:510
  2.4 3.2 %collective-permute-start = (f32[5,8,2048]{2,1,0:T(8,128)S(1)}, f32[5,8,2048]{2,1,0:T(8,128)S(1)}, u32[]{:S(2)}, u32[]{:S(2)}) collective-permute-start(f32[5,8,2048]{2,1,0:T(8,128)S(1)} %get-tuple-element.117), channel_id=1, source_target_pairs={{0,1},{1,2},{2,3},{3,0},{8,9},{9,10},{10,11},{11,8},{12,13},{13,14... | collective-permute-start | bytes 983048 | tf_op jit(solution)/shard_map/ppermute | solution.py:486
  5.6 2.9 %collective-permute-start.1 = (f32[5,8,2048]{2,1,0:T(8,128)S(1)}, f32[5,8,2048]{2,1,0:T(8,128)S(1)}, u32[]{:S(2)}, u32[]{:S(2)}) collective-permute-start(f32[5,8,2048]{2,1,0:T(8,128)S(1)} %get-tuple-element.118), channel_id=1, source_target_pairs={{0,2},{1,3},{2,0},{3,1},{8,10},{9,11},{10,8},{11,9},{12,14},{13,15... | collective-permute-start | bytes 983048 | tf_op jit(solution)/shard_map/ppermute | solution.py:486
  8.6 3.4 %collective-permute-start.2 = (f32[5,8,2048]{2,1,0:T(8,128)S(1)}, f32[5,8,2048]{2,1,0:T(8,128)S(1)}, u32[]{:S(2)}, u32[]{:S(2)}) collective-permute-start(f32[5,8,2048]{2,1,0:T(8,128)S(1)} %get-tuple-element.116), channel_id=1, source_target_pairs={{0,3},{1,0},{2,1},{3,2},{8,11},{9,8},{10,9},{11,10},{12,15},{13,12... | collective-permute-start | bytes 983048 | tf_op jit(solution)/shard_map/ppermute | solution.py:486
  12.6 0.6 gather_fusion
  13.3 0.8 fusion.17
  14.1 0.7 multiply_multiply_fusion
  14.7 0.7 broadcast_divide_fusion
  15.8 17.3 %collective-permute-done.1 = f32[5,8,2048]{2,1,0:T(8,128)S(1)} collective-permute-done((f32[5,8,2048]{2,1,0:T(8,128)S(1)}, f32[5,8,2048]{2,1,0:T(8,128)S(1)}, u32[]{:S(2)}, u32[]{:S(2)}) %collective-permute-start.1) | collective-permute-done | bytes 327712 | tf_op jit(solution)/shard_map/ppermute | solution.py:486
  33.1 2.8 %collective-permute-done.2 = f32[5,8,2048]{2,1,0:T(8,128)S(1)} collective-permute-done((f32[5,8,2048]{2,1,0:T(8,128)S(1)}, f32[5,8,2048]{2,1,0:T(8,128)S(1)}, u32[]{:S(2)}, u32[]{:S(2)}) %collective-permute-start.2) | collective-permute-done | bytes 327712 | tf_op jit(solution)/shard_map/ppermute | solution.py:486
  36.0 0.8 slice.38.refs_1_
  37.2 7.8 %shard_map.118 = (f32[2,32,2048]{2,1,0:T(8,128)}, f32[4,3,8,2048]{3,2,1,0:T(8,128)S(1)}) custom-call(f32[72]{0:T(128)S(1)} %reshape.135.refs_0_, f32[2,32,2048]{2,1,0:T(8,128)} %slice.38.refs_1_, s32[3,32,2048]{2,1,0:T(8,128)S(1)} %slice_convert_fusion.refs_2_, f32[3,2,16,128]{3,2,1,0:T(8,128)S(1)} %pad_maximum_fusion.4.refs_3_, ...), custom_call_target="tpu_custom_call" | custom-call | flops 1286602752 | bytes 4718592 | tf_op jit(solution)/shard_map/pallas_call | solution.py:395
  44.9 0.7 collective-permute-start.4
  45.6 0.7 collective-permute-start.5
  46.3 0.7 collective-permute-start.6
  47.0 1.5 %collective-permute-start.3 = (f32[2,32,2048]{2,1,0:T(8,128)}, f32[2,32,2048]{2,1,0:T(8,128)}, u32[]{:S(2)}, u32[]{:S(2)}) collective-permute-start(f32[2,32,2048]{2,1,0:T(8,128)} %get-tuple-element.97), channel_id=1, source_target_pairs={{0,4},{1,5},{2,6},{3,7},{16,20},{17,21},{18,22},{19,23}} | collective-permute-start | bytes 1572872 | tf_op jit(solution)/shard_map/ppermute | solution.py:552
  48.7 1.0 convert_element_type.19.refs_2_
  49.6 8.1 %shard_map.119 = (f32[2,32,2048]{2,1,0:T(8,128)}, f32[4,3,8,2048]{3,2,1,0:T(8,128)S(1)}) custom-call(f32[72]{0:T(128)S(1)} %reshape.135.refs_0_, f32[2,32,2048]{2,1,0:T(8,128)} %collective-permute-done.3.refs_1_, s32[3,32,2048]{2,1,0:T(8,128)} %convert_element_type.19.refs_2_, f32[3,2,16,128]{3,2,1,0:T(8,128)S(1)} %pad_maximum_fusion.4.refs_3_, ...), custom_call_target="tpu_custom_call" | custom-call | flops 1286602752 | bytes 4718592 | tf_op jit(solution)/shard_map/pallas_call | solution.py:395
  57.7 1.4 %collective-permute-start.7 = (f32[2,32,2048]{2,1,0:T(8,128)}, f32[2,32,2048]{2,1,0:T(8,128)}, u32[]{:S(2)}, u32[]{:S(2)}) collective-permute-start(f32[2,32,2048]{2,1,0:T(8,128)} %get-tuple-element.101), channel_id=1, source_target_pairs={{4,8},{5,9},{6,10},{7,11},{20,24},{21,25},{22,26},{23,27}} | collective-permute-start | bytes 1572872 | tf_op jit(solution)/shard_map/ppermute | solution.py:552
  59.2 1.3 %collective-permute-start.8 = (f32[2,32,2048]{2,1,0:T(8,128)}, f32[2,32,2048]{2,1,0:T(8,128)S(1)}, u32[]{:S(2)}, u32[]{:S(2)}) collective-permute-start(f32[2,32,2048]{2,1,0:T(8,128)} %get-tuple-element.102), channel_id=1, source_target_pairs={{8,12},{9,13},{10,14},{11,15},{24,28},{25,29},{26,30},{27,31}} | collective-permute-start | bytes 1572872 | tf_op jit(solution)/shard_map/ppermute | solution.py:552
  60.5 21.1 %collective-permute-done.8 = f32[2,32,2048]{2,1,0:T(8,128)S(1)} collective-permute-done((f32[2,32,2048]{2,1,0:T(8,128)}, f32[2,32,2048]{2,1,0:T(8,128)S(1)}, u32[]{:S(2)}, u32[]{:S(2)}) %collective-permute-start.8) | collective-permute-done | bytes 524320 | tf_op jit(solution)/shard_map/ppermute | solution.py:552
  81.6 7.7 %conditional.3 = (f32[4,3,8,2048]{3,2,1,0:T(8,128)S(1)}) conditional(s32[]{:T(128)} %convert_element_type.15, f32[4,3,8,2048]{3,2,1,0:T(8,128)S(1)} %get-tuple-element.104, (s32[]{:T(128)}, f32[72]{0:T(128)S(1)}, f32[2,32,2048]{2,1,0:T(8,128)S(1)}, s32[3,32,2048]{2,1,0:T(8,128)S(1)}, f32[3,2,16,128]{3,2,1,0:T(8,128)S(1)}, ...), branch_computations={%region_2.3_spmd, %region_3.4_spmd} | conditional | flops 1286602752 | bytes 4718600 | solution.py:550
  81.6 7.7 %branch_1_fun.3 = (f32[2,32,2048]{2,1,0:T(8,128)}, f32[4,3,8,2048]{3,2,1,0:T(8,128)S(1)}) custom-call(f32[72]{0:T(128)S(1)} %get-tuple-element.77.refs_0_, f32[2,32,2048]{2,1,0:T(8,128)S(1)} %get-tuple-element.78.refs_1_, s32[3,32,2048]{2,1,0:T(8,128)S(1)} %get-tuple-element.79.refs_2_, f32[3,2,16,128]{3,2,1,0:T(8,128)S(1)} %get-tuple-element.80.refs_3_, ...), custom_call_target="tpu_custom_call" | custom-call | flops 1286602752 | bytes 4718592 | tf_op jit(solution)/shard_map/cond/branch_1_fun/pallas_call | solution.py:395
  89.3 1.9 %collective-permute-start.12 = (f32[3,8,2048]{2,1,0:T(8,128)S(1)}, f32[3,8,2048]{2,1,0:T(8,128)S(1)}, u32[]{:S(2)}, u32[]{:S(2)}) collective-permute-start(f32[3,8,2048]{2,1,0:T(8,128)S(1)} %get-tuple-element.109), channel_id=1, source_target_pairs={{12,13},{13,14},{14,15},{15,12},{28,29},{29,30},{30,31},{31,28}} | collective-permute-start | bytes 589832 | tf_op jit(solution)/shard_map/ppermute | solution.py:537
  91.3 3.3 %collective-permute-start.13 = (f32[3,8,2048]{2,1,0:T(8,128)S(1)}, f32[3,8,2048]{2,1,0:T(8,128)S(1)}, u32[]{:S(2)}, u32[]{:S(2)}) collective-permute-start(f32[3,8,2048]{2,1,0:T(8,128)S(1)} %get-tuple-element.111), channel_id=1, source_target_pairs={{12,14},{13,15},{14,12},{15,13},{28,30},{29,31},{30,28},{31,29}} | collective-permute-start | bytes 589832 | tf_op jit(solution)/shard_map/ppermute | solution.py:537
  94.6 3.4 %collective-permute-start.14 = (f32[3,8,2048]{2,1,0:T(8,128)S(1)}, f32[3,8,2048]{2,1,0:T(8,128)S(1)}, u32[]{:S(2)}, u32[]{:S(2)}) collective-permute-start(f32[3,8,2048]{2,1,0:T(8,128)S(1)} %get-tuple-element.110), channel_id=1, source_target_pairs={{12,15},{13,12},{14,13},{15,14},{28,31},{29,28},{30,29},{31,30}} | collective-permute-start | bytes 589832 | tf_op jit(solution)/shard_map/ppermute | solution.py:537
  98.0 0.7 collective-permute-start.10
  98.7 0.7 collective-permute-start.11
  99.4 0.7 collective-permute-start.9
  100.0 4.3 %collective-permute-done.13 = f32[3,8,2048]{2,1,0:T(8,128)S(1)} collective-permute-done((f32[3,8,2048]{2,1,0:T(8,128)S(1)}, f32[3,8,2048]{2,1,0:T(8,128)S(1)}, u32[]{:S(2)}, u32[]{:S(2)}) %collective-permute-start.13) | collective-permute-done | bytes 196640 | tf_op jit(solution)/shard_map/ppermute | solution.py:537
  105.0 0.8 fusion.6
  (55 shorter events, 2.7 us)
Async XLA Ops:
  2.2 9.8 %copy-start = (f32[4]{0:T(128)S(1)}, f32[4]{0:T(128)}, u32[]{:S(2)}) copy-start(f32[4]{0:T(128)} %param.17) | copy-start | bytes 52
  2.3 10.4 %copy-start.1 = (f32[8]{0:T(128)S(1)}, f32[8]{0:T(128)}, u32[]{:S(2)}) copy-start(f32[8]{0:T(128)} %param.18) | copy-start | bytes 100
  2.3 10.4 %copy-start.2 = (s32[3]{0:T(128)S(1)}, s32[3]{0:T(128)}, u32[]{:S(2)}) copy-start(s32[3]{0:T(128)} %param.21) | copy-start | bytes 40
  2.3 12.4 %copy-start.3 = (f32[8]{0:T(128)S(1)}, f32[8]{0:T(128)}, u32[]{:S(2)}) copy-start(f32[8]{0:T(128)} %param.19) | copy-start | bytes 100
  2.3 13.2 %copy-start.4 = (f32[16,128]{1,0:T(8,128)S(1)}, f32[16,128]{1,0:T(8,128)}, u32[]{:S(2)}) copy-start(f32[16,128]{1,0:T(8,128)} %constant.106) | copy-start | bytes 24580
  2.4 13.3 %collective-permute-start = (f32[5,8,2048]{2,1,0:T(8,128)S(1)}, f32[5,8,2048]{2,1,0:T(8,128)S(1)}, u32[]{:S(2)}, u32[]{:S(2)}) collective-permute-start(f32[5,8,2048]{2,1,0:T(8,128)S(1)} %get-tuple-element.117), channel_id=1, source_target_pairs={{0,1},{1,2},{2,3},{3,0},{8,9},{9,10},{10,11},{11,8},{12,13},{13,14... | collective-permute-start | bytes 983048 | tf_op jit(solution)/shard_map/ppermute | solution.py:486
  5.6 27.4 %collective-permute-start.1 = (f32[5,8,2048]{2,1,0:T(8,128)S(1)}, f32[5,8,2048]{2,1,0:T(8,128)S(1)}, u32[]{:S(2)}, u32[]{:S(2)}) collective-permute-start(f32[5,8,2048]{2,1,0:T(8,128)S(1)} %get-tuple-element.118), channel_id=1, source_target_pairs={{0,2},{1,3},{2,0},{3,1},{8,10},{9,11},{10,8},{11,9},{12,14},{13,15... | collective-permute-start | bytes 983048 | tf_op jit(solution)/shard_map/ppermute | solution.py:486
  8.6 27.3 %collective-permute-start.2 = (f32[5,8,2048]{2,1,0:T(8,128)S(1)}, f32[5,8,2048]{2,1,0:T(8,128)S(1)}, u32[]{:S(2)}, u32[]{:S(2)}) collective-permute-start(f32[5,8,2048]{2,1,0:T(8,128)S(1)} %get-tuple-element.116), channel_id=1, source_target_pairs={{0,3},{1,0},{2,1},{3,2},{8,11},{9,8},{10,9},{11,10},{12,15},{13,12... | collective-permute-start | bytes 983048 | tf_op jit(solution)/shard_map/ppermute | solution.py:486
  35.9 1.0 copy-start.5
  35.9 1.0 copy-start.6
  35.9 1.0 copy-start.7
  35.9 1.2 %copy-start.8 = (bf16[256,256]{1,0:T(8,128)(2,1)S(1)}, bf16[256,256]{1,0:T(8,128)(2,1)}, u32[]{:S(2)}) copy-start(bf16[256,256]{1,0:T(8,128)(2,1)} %constant.99.clone.refs_5_) | copy-start | bytes 393220
  36.0 1.2 %copy-start.9 = (f32[2,16,128]{2,1,0:T(8,128)S(1)}, f32[2,16,128]{2,1,0:T(8,128)}, u32[]{:S(2)}) copy-start(f32[2,16,128]{2,1,0:T(8,128)} %constant.98.clone.refs_4_) | copy-start | bytes 49156
  44.9 3.6 %collective-permute-start.4 = (f32[3,8,2048]{2,1,0:T(8,128)S(1)}, f32[3,8,2048]{2,1,0:T(8,128)S(1)}, u32[]{:S(2)}, u32[]{:S(2)}) collective-permute-start(f32[3,8,2048]{2,1,0:T(8,128)S(1)} %convert_element_type.17), channel_id=1, source_target_pairs={{4,5},{5,6},{6,7},{7,4},{20,21},{21,22},{22,23},{23,20}} | collective-permute-start | bytes 589832 | tf_op jit(solution)/shard_map/ppermute | solution.py:486
  45.6 3.0 %collective-permute-start.5 = (f32[3,8,2048]{2,1,0:T(8,128)S(1)}, f32[3,8,2048]{2,1,0:T(8,128)S(1)}, u32[]{:S(2)}, u32[]{:S(2)}) collective-permute-start(f32[3,8,2048]{2,1,0:T(8,128)S(1)} %convert_element_type.17), channel_id=1, source_target_pairs={{4,6},{5,7},{6,4},{7,5},{20,22},{21,23},{22,20},{23,21}} | collective-permute-start | bytes 589832 | tf_op jit(solution)/shard_map/ppermute | solution.py:486
  46.3 2.3 %collective-permute-start.6 = (f32[3,8,2048]{2,1,0:T(8,128)S(1)}, f32[3,8,2048]{2,1,0:T(8,128)S(1)}, u32[]{:S(2)}, u32[]{:S(2)}) collective-permute-start(f32[3,8,2048]{2,1,0:T(8,128)S(1)} %convert_element_type.17), channel_id=1, source_target_pairs={{4,7},{5,4},{6,5},{7,6},{20,23},{21,20},{22,21},{23,22}} | collective-permute-start | bytes 589832 | tf_op jit(solution)/shard_map/ppermute | solution.py:486
  47.0 2.7 %collective-permute-start.3 = (f32[2,32,2048]{2,1,0:T(8,128)}, f32[2,32,2048]{2,1,0:T(8,128)}, u32[]{:S(2)}, u32[]{:S(2)}) collective-permute-start(f32[2,32,2048]{2,1,0:T(8,128)} %get-tuple-element.97), channel_id=1, source_target_pairs={{0,4},{1,5},{2,6},{3,7},{16,20},{17,21},{18,22},{19,23}} | collective-permute-start | bytes 1572872 | tf_op jit(solution)/shard_map/ppermute | solution.py:552
  57.7 1.5 %collective-permute-start.7 = (f32[2,32,2048]{2,1,0:T(8,128)}, f32[2,32,2048]{2,1,0:T(8,128)}, u32[]{:S(2)}, u32[]{:S(2)}) collective-permute-start(f32[2,32,2048]{2,1,0:T(8,128)} %get-tuple-element.101), channel_id=1, source_target_pairs={{4,8},{5,9},{6,10},{7,11},{20,24},{21,25},{22,26},{23,27}} | collective-permute-start | bytes 1572872 | tf_op jit(solution)/shard_map/ppermute | solution.py:552
  59.2 22.4 %collective-permute-start.8 = (f32[2,32,2048]{2,1,0:T(8,128)}, f32[2,32,2048]{2,1,0:T(8,128)S(1)}, u32[]{:S(2)}, u32[]{:S(2)}) collective-permute-start(f32[2,32,2048]{2,1,0:T(8,128)} %get-tuple-element.102), channel_id=1, source_target_pairs={{8,12},{9,13},{10,14},{11,15},{24,28},{25,29},{26,30},{27,31}} | collective-permute-start | bytes 1572872 | tf_op jit(solution)/shard_map/ppermute | solution.py:552
  89.3 10.0 %collective-permute-start.12 = (f32[3,8,2048]{2,1,0:T(8,128)S(1)}, f32[3,8,2048]{2,1,0:T(8,128)S(1)}, u32[]{:S(2)}, u32[]{:S(2)}) collective-permute-start(f32[3,8,2048]{2,1,0:T(8,128)S(1)} %get-tuple-element.109), channel_id=1, source_target_pairs={{12,13},{13,14},{14,15},{15,12},{28,29},{29,30},{30,31},{31,28}} | collective-permute-start | bytes 589832 | tf_op jit(solution)/shard_map/ppermute | solution.py:537
  91.3 13.1 %collective-permute-start.13 = (f32[3,8,2048]{2,1,0:T(8,128)S(1)}, f32[3,8,2048]{2,1,0:T(8,128)S(1)}, u32[]{:S(2)}, u32[]{:S(2)}) collective-permute-start(f32[3,8,2048]{2,1,0:T(8,128)S(1)} %get-tuple-element.111), channel_id=1, source_target_pairs={{12,14},{13,15},{14,12},{15,13},{28,30},{29,31},{30,28},{31,29}} | collective-permute-start | bytes 589832 | tf_op jit(solution)/shard_map/ppermute | solution.py:537
  94.6 10.4 %collective-permute-start.14 = (f32[3,8,2048]{2,1,0:T(8,128)S(1)}, f32[3,8,2048]{2,1,0:T(8,128)S(1)}, u32[]{:S(2)}, u32[]{:S(2)}) collective-permute-start(f32[3,8,2048]{2,1,0:T(8,128)S(1)} %get-tuple-element.110), channel_id=1, source_target_pairs={{12,15},{13,12},{14,13},{15,14},{28,31},{29,28},{30,29},{31,30}} | collective-permute-start | bytes 589832 | tf_op jit(solution)/shard_map/ppermute | solution.py:537
  98.0 7.0 %collective-permute-start.10 = (f32[3,8,2048]{2,1,0:T(8,128)S(1)}, f32[3,8,2048]{2,1,0:T(8,128)S(1)}, u32[]{:S(2)}, u32[]{:S(2)}) collective-permute-start(f32[3,8,2048]{2,1,0:T(8,128)S(1)} %get-tuple-element.108), channel_id=1, source_target_pairs={{0,2},{1,3},{2,0},{3,1},{4,6},{5,7},{6,4},{7,5},{8,10},{9,11},{10,... | collective-permute-start | bytes 589832 | tf_op jit(solution)/shard_map/ppermute | solution.py:537
  98.7 6.3 %collective-permute-start.11 = (f32[3,8,2048]{2,1,0:T(8,128)S(1)}, f32[3,8,2048]{2,1,0:T(8,128)S(1)}, u32[]{:S(2)}, u32[]{:S(2)}) collective-permute-start(f32[3,8,2048]{2,1,0:T(8,128)S(1)} %get-tuple-element.107), channel_id=1, source_target_pairs={{0,3},{1,0},{2,1},{3,2},{4,7},{5,4},{6,5},{7,6},{8,11},{9,8},{10,9... | collective-permute-start | bytes 589832 | tf_op jit(solution)/shard_map/ppermute | solution.py:537
  99.4 5.6 %collective-permute-start.9 = (f32[3,8,2048]{2,1,0:T(8,128)S(1)}, f32[3,8,2048]{2,1,0:T(8,128)S(1)}, u32[]{:S(2)}, u32[]{:S(2)}) collective-permute-start(f32[3,8,2048]{2,1,0:T(8,128)S(1)} %get-tuple-element.106), channel_id=1, source_target_pairs={{0,1},{1,2},{2,3},{3,0},{4,5},{5,6},{6,7},{7,4},{8,9},{9,10},{10,1... | collective-permute-start | bytes 589832 | tf_op jit(solution)/shard_map/ppermute | solution.py:537

commit v18 on v15

--- a/solution.py
+++ b/solution.py
@@ -287,7 +287,7 @@
                 a_ref[pl.ds(cc * rows + y0, ROW_CHUNK), LANE:2 * LANE] = xi * tc - xr * ts
             return c
 
-        lax.fori_loop(0, chunks, forward_chunk, 0)
+        lax.fori_loop(0, chunks, forward_chunk, 0, unroll=True)
         spectrum = split_dot(a_ref[...], fhi_ref, flo_ref)
         for a in range(FFT_BLOCKS):
             regions = rid_ref[k, :, blk(a)]
@@ -325,7 +325,7 @@
                 v_ref[1, pl.ds(y0, ROW_CHUNK), blk(a)] = ur * sn + ui * cs
             return c
 
-        lax.fori_loop(0, chunks, inverse_chunk, 0)
+        lax.fori_loop(0, chunks, inverse_chunk, 0, unroll=True)
         row_id = lax.broadcasted_iota(jnp.int32, (rows, LANE), 0)
         lane_id = lax.broadcasted_iota(jnp.int32, (rows, LANE), 1)
         cache = {}

time: 94.8 us -> 93.6 us (0.987)
  Pallas kernels: 15.5 us -> 14.4 us
    pallas_call x2, Pallas kernels: 15.5 us -> 14.4 us  [run_section(): pl.pallas_call(lambda *refs: section_kernel(*refs, table_len=table_len),...]
where the time goes in v18:
time: 93.6 us; the launch traced here: 92.6 us
  waiting for transfers between devices  43.5 us (46%)
  starting transfers between devices  24.8 us (26%)
  Pallas kernels  14.4 us (15%)
  local copies, waits for them, and re-layouts  5.02 us (5%)
  other arithmetic  4.26 us (5%)
    ppermute x6, waiting for transfers between devices, gather_strips(): lax.ppermute(piece_of(target), ('depth', 'strip'), strip_pairs(depths, st...  19.1 us
    ppermute x3, waiting for transfers between devices, shards(): wave = lax.ppermute(wave, 'depth', [(tick_no, tick_no + 1)])  19 us
    pallas_call x2, Pallas kernels, run_section(): pl.pallas_call(lambda *refs: section_kernel(*refs, table_len=table_len),...  14.4 us
    ppermute x6, starting transfers between devices, gather_strips(): lax.ppermute(piece_of(target), ('depth', 'strip'), strip_pairs(depths, st...  11.5 us
    ppermute x6, starting transfers between devices, freq_sum(): lax.ppermute(piece, ('depth', 'strip'), strip_pairs(depths, strip_count,...  10.6 us
    ppermute x6, waiting for transfers between devices, freq_sum(): lax.ppermute(piece, ('depth', 'strip'), strip_pairs(depths, strip_count,...  5.42 us
    ppermute x3, starting transfers between devices, shards(): wave = lax.ppermute(wave, 'depth', [(tick_no, tick_no + 1)])  2.68 us
  transfers between devices with their start and end apart: 15, of which 5 were waited for; matrix products, arithmetic and copies ran while one was open for 5% of the time, Pallas kernels for 0%

profile of v18, /device:TPU:11, one launch (start us, length us, event | category | flops | bytes accessed | tf_op | source)
XLA Modules:
  0.0 92.6 jit_solution(11448681833860352288)
XLA Ops:
  0.0 0.9 %convert_element_type.21 = f32[3,8,2048]{2,1,0:T(8,128)S(1)} convert(s32[3,8,2048]{2,1,0:T(8,128)} %param.22) | non-fusion elementwise | flops 49152 | bytes 393216 | tf_op jit(solution)/shard_map/convert_element_type | solution.py:505
  1.0 1.1 %dynamic-slice_bitcast_fusion = (f32[2,8,2048]{2,1,0:T(8,128)S(1)}, f32[2,8,2048]{2,1,0:T(8,128)S(1)}, f32[2,8,2048]{2,1,0:T(8,128)S(1)}, f32[2,8,2048]{2,1,0:T(8,128)S(1)}) fusion(f32[2,4,8,2048]{3,2,1,0:T(8,128)} %param.18, s32[]{:T(128)S(6)} %select_n.79, s32[]{:T(128)S(6)} %select_n.71, s32[]{:T(128)S(6)} %select_n.67, s32[]{:T(128)S(6)} %select_n.75), kind=kLoop, calls=%fused_computation.20 | loop fusion | bytes 1048592 | tf_op jit(solution)/shard_map/jit(dynamic_index_in_dim)/squeeze | solution.py:510
  2.4 3.2 %collective-permute-start = (f32[5,8,2048]{2,1,0:T(8,128)S(1)}, f32[5,8,2048]{2,1,0:T(8,128)}, u32[]{:S(2)}, u32[]{:S(2)}) collective-permute-start(f32[5,8,2048]{2,1,0:T(8,128)S(1)} %get-tuple-element.137), channel_id=1, source_target_pairs={{0,1},{1,2},{2,3},{3,0},{8,9},{9,10},{10,11},{11,8},{12,13},{13,14... | collective-permute-start | bytes 983048 | tf_op jit(solution)/shard_map/ppermute | solution.py:486
  5.6 2.9 %collective-permute-start.1 = (f32[5,8,2048]{2,1,0:T(8,128)S(1)}, f32[5,8,2048]{2,1,0:T(8,128)S(1)}, u32[]{:S(2)}, u32[]{:S(2)}) collective-permute-start(f32[5,8,2048]{2,1,0:T(8,128)S(1)} %get-tuple-element.138), channel_id=1, source_target_pairs={{0,2},{1,3},{2,0},{3,1},{8,10},{9,11},{10,8},{11,9},{12,14},{13,15... | collective-permute-start | bytes 983048 | tf_op jit(solution)/shard_map/ppermute | solution.py:486
  8.6 3.4 %collective-permute-start.2 = (f32[5,8,2048]{2,1,0:T(8,128)S(1)}, f32[5,8,2048]{2,1,0:T(8,128)S(1)}, u32[]{:S(2)}, u32[]{:S(2)}) collective-permute-start(f32[5,8,2048]{2,1,0:T(8,128)S(1)} %get-tuple-element.136), channel_id=1, source_target_pairs={{0,3},{1,0},{2,1},{3,2},{8,11},{9,8},{10,9},{11,10},{12,15},{13,12... | collective-permute-start | bytes 983048 | tf_op jit(solution)/shard_map/ppermute | solution.py:486
  12.7 0.6 gather_fusion
  13.3 0.8 fusion.17
  14.1 0.7 multiply_multiply_fusion
  14.7 0.7 broadcast_divide_fusion
  15.7 1.0 %constant_dynamic-update-slice_fusion.6 = f32[5,32,2048]{2,1,0:T(8,128)S(1)} fusion(f32[5,32,2048]{2,1,0:T(8,128)S(1)} %get-tuple-element.139, f32[5,8,2048]{2,1,0:T(8,128)} %collective-permute-done, s32[]{:T(128)S(6)} %select_n.73), kind=kLoop, calls=%fused_computation.44 | loop fusion | bytes 655364 | tf_op jit(solution)/shard_map/dynamic_update_slice | solution.py:490
  16.7 16.3 %collective-permute-done.1 = f32[5,8,2048]{2,1,0:T(8,128)S(1)} collective-permute-done((f32[5,8,2048]{2,1,0:T(8,128)S(1)}, f32[5,8,2048]{2,1,0:T(8,128)S(1)}, u32[]{:S(2)}, u32[]{:S(2)}) %collective-permute-start.1) | collective-permute-done | bytes 327712 | tf_op jit(solution)/shard_map/ppermute | solution.py:486
  33.1 2.8 %collective-permute-done.2 = f32[5,8,2048]{2,1,0:T(8,128)S(1)} collective-permute-done((f32[5,8,2048]{2,1,0:T(8,128)S(1)}, f32[5,8,2048]{2,1,0:T(8,128)S(1)}, u32[]{:S(2)}, u32[]{:S(2)}) %collective-permute-start.2) | collective-permute-done | bytes 327712 | tf_op jit(solution)/shard_map/ppermute | solution.py:486
  36.1 0.8 slice.38.refs_1_
  37.2 7.3 %shard_map.118 = (f32[2,32,2048]{2,1,0:T(8,128)}, f32[4,3,8,2048]{3,2,1,0:T(8,128)S(1)}) custom-call(f32[72]{0:T(128)S(1)} %reshape.137.refs_0_, f32[2,32,2048]{2,1,0:T(8,128)} %slice.38.refs_1_, s32[3,32,2048]{2,1,0:T(8,128)S(1)} %slice_convert_fusion.refs_2_, f32[3,2,16,128]{3,2,1,0:T(8,128)S(1)} %pad_maximum_fusion.4.refs_3_, ...), custom_call_target="tpu_custom_call" | custom-call | flops 1286602752 | bytes 4718592 | tf_op jit(solution)/shard_map/pallas_call | solution.py:395
  44.4 0.7 collective-permute-start.4
  45.1 0.7 collective-permute-start.5
  45.8 0.7 collective-permute-start.6
  46.5 0.7 collective-permute-start.3
  47.5 0.7 collective-permute-start.7
  48.2 1.3 %collective-permute-start.8 = (f32[2,32,2048]{2,1,0:T(8,128)S(1)}, f32[2,32,2048]{2,1,0:T(8,128)S(1)}, u32[]{:S(2)}, u32[]{:S(2)}) collective-permute-start(f32[2,32,2048]{2,1,0:T(8,128)S(1)} %get-tuple-element.122), channel_id=1, source_target_pairs={{8,12},{9,13},{10,14},{11,15},{24,28},{25,29},{26,30},{27,31}} | collective-permute-start | bytes 1572872 | tf_op jit(solution)/shard_map/ppermute | solution.py:549
  49.5 19.0 %collective-permute-done.8 = f32[2,32,2048]{2,1,0:T(8,128)S(1)} collective-permute-done((f32[2,32,2048]{2,1,0:T(8,128)S(1)}, f32[2,32,2048]{2,1,0:T(8,128)S(1)}, u32[]{:S(2)}, u32[]{:S(2)}) %collective-permute-start.8) | collective-permute-done | bytes 524320 | tf_op jit(solution)/shard_map/ppermute | solution.py:549
  68.5 7.2 %conditional.5 = (f32[4,3,8,2048]{3,2,1,0:T(8,128)S(1)}) conditional(s32[]{:T(128)} %convert_element_type.18, f32[4,3,8,2048]{3,2,1,0:T(8,128)S(1)} %get-tuple-element.124, (s32[]{:T(128)}, f32[72]{0:T(128)S(1)}, f32[2,32,2048]{2,1,0:T(8,128)S(1)}, s32[3,32,2048]{2,1,0:T(8,128)S(1)}, f32[3,2,16,128]{3,2,1,0:T(8,128)S(1)}, ...), branch_computations={%region_4.5_spmd, %region_5.6_spmd} | conditional | flops 1286602752 | bytes 4718600 | solution.py:547
  68.5 7.2 %branch_1_fun.5 = (f32[2,32,2048]{2,1,0:T(8,128)}, f32[4,3,8,2048]{3,2,1,0:T(8,128)S(1)}) custom-call(f32[72]{0:T(128)S(1)} %get-tuple-element.97.refs_0_, f32[2,32,2048]{2,1,0:T(8,128)S(1)} %get-tuple-element.98.refs_1_, s32[3,32,2048]{2,1,0:T(8,128)S(1)} %get-tuple-element.99.refs_2_, f32[3,2,16,128]{3,2,1,0:T(8,128)S(1)} %get-tuple-element.100.refs_3_, ...), custom_call_target="tpu_custom_call" | custom-call | flops 1286602752 | bytes 4718592 | tf_op jit(solution)/shard_map/cond/branch_1_fun/pallas_call | solution.py:395
  75.7 1.9 %collective-permute-start.12 = (f32[3,8,2048]{2,1,0:T(8,128)S(1)}, f32[3,8,2048]{2,1,0:T(8,128)S(1)}, u32[]{:S(2)}, u32[]{:S(2)}) collective-permute-start(f32[3,8,2048]{2,1,0:T(8,128)S(1)} %get-tuple-element.129), channel_id=1, source_target_pairs={{12,13},{13,14},{14,15},{15,12},{28,29},{29,30},{30,31},{31,28}} | collective-permute-start | bytes 589832 | tf_op jit(solution)/shard_map/ppermute | solution.py:537
  77.7 3.3 %collective-permute-start.13 = (f32[3,8,2048]{2,1,0:T(8,128)S(1)}, f32[3,8,2048]{2,1,0:T(8,128)S(1)}, u32[]{:S(2)}, u32[]{:S(2)}) collective-permute-start(f32[3,8,2048]{2,1,0:T(8,128)S(1)} %get-tuple-element.131), channel_id=1, source_target_pairs={{12,14},{13,15},{14,12},{15,13},{28,30},{29,31},{30,28},{31,29}} | collective-permute-start | bytes 589832 | tf_op jit(solution)/shard_map/ppermute | solution.py:537
  81.0 3.4 %collective-permute-start.14 = (f32[3,8,2048]{2,1,0:T(8,128)S(1)}, f32[3,8,2048]{2,1,0:T(8,128)S(1)}, u32[]{:S(2)}, u32[]{:S(2)}) collective-permute-start(f32[3,8,2048]{2,1,0:T(8,128)S(1)} %get-tuple-element.130), channel_id=1, source_target_pairs={{12,15},{13,12},{14,13},{15,14},{28,31},{29,28},{30,29},{31,30}} | collective-permute-start | bytes 589832 | tf_op jit(solution)/shard_map/ppermute | solution.py:537
  84.4 0.7 collective-permute-start.10
  85.1 0.7 collective-permute-start.11
  85.8 0.7 collective-permute-start.9
  86.4 4.4 %collective-permute-done.13 = f32[3,8,2048]{2,1,0:T(8,128)S(1)} collective-permute-done((f32[3,8,2048]{2,1,0:T(8,128)S(1)}, f32[3,8,2048]{2,1,0:T(8,128)S(1)}, u32[]{:S(2)}, u32[]{:S(2)}) %collective-permute-start.13) | collective-permute-done | bytes 196640 | tf_op jit(solution)/shard_map/ppermute | solution.py:537
  90.8 1.0 %collective-permute-done.14 = f32[3,8,2048]{2,1,0:T(8,128)S(1)} collective-permute-done((f32[3,8,2048]{2,1,0:T(8,128)S(1)}, f32[3,8,2048]{2,1,0:T(8,128)S(1)}, u32[]{:S(2)}, u32[]{:S(2)}) %collective-permute-start.14) | collective-permute-done | bytes 196640 | tf_op jit(solution)/shard_map/ppermute | solution.py:537
  91.9 0.8 fusion.6
  (54 shorter events, 1.9 us)
Async XLA Ops:
  2.2 9.8 %copy-start = (f32[4]{0:T(128)S(1)}, f32[4]{0:T(128)}, u32[]{:S(2)}) copy-start(f32[4]{0:T(128)} %param.19) | copy-start | bytes 52
  2.3 10.4 %copy-start.1 = (f32[8]{0:T(128)S(1)}, f32[8]{0:T(128)}, u32[]{:S(2)}) copy-start(f32[8]{0:T(128)} %param.20) | copy-start | bytes 100
  2.3 10.4 %copy-start.2 = (s32[3]{0:T(128)S(1)}, s32[3]{0:T(128)}, u32[]{:S(2)}) copy-start(s32[3]{0:T(128)} %param.23) | copy-start | bytes 40
  2.3 12.5 %copy-start.3 = (f32[8]{0:T(128)S(1)}, f32[8]{0:T(128)}, u32[]{:S(2)}) copy-start(f32[8]{0:T(128)} %param.21) | copy-start | bytes 100
  2.3 13.2 %copy-start.4 = (f32[16,128]{1,0:T(8,128)S(1)}, f32[16,128]{1,0:T(8,128)}, u32[]{:S(2)}) copy-start(f32[16,128]{1,0:T(8,128)} %constant.105) | copy-start | bytes 24580
  2.4 13.3 %collective-permute-start = (f32[5,8,2048]{2,1,0:T(8,128)S(1)}, f32[5,8,2048]{2,1,0:T(8,128)}, u32[]{:S(2)}, u32[]{:S(2)}) collective-permute-start(f32[5,8,2048]{2,1,0:T(8,128)S(1)} %get-tuple-element.137), channel_id=1, source_target_pairs={{0,1},{1,2},{2,3},{3,0},{8,9},{9,10},{10,11},{11,8},{12,13},{13,14... | collective-permute-start | bytes 983048 | tf_op jit(solution)/shard_map/ppermute | solution.py:486
  5.6 27.4 %collective-permute-start.1 = (f32[5,8,2048]{2,1,0:T(8,128)S(1)}, f32[5,8,2048]{2,1,0:T(8,128)S(1)}, u32[]{:S(2)}, u32[]{:S(2)}) collective-permute-start(f32[5,8,2048]{2,1,0:T(8,128)S(1)} %get-tuple-element.138), channel_id=1, source_target_pairs={{0,2},{1,3},{2,0},{3,1},{8,10},{9,11},{10,8},{11,9},{12,14},{13,15... | collective-permute-start | bytes 983048 | tf_op jit(solution)/shard_map/ppermute | solution.py:486
  8.6 27.3 %collective-permute-start.2 = (f32[5,8,2048]{2,1,0:T(8,128)S(1)}, f32[5,8,2048]{2,1,0:T(8,128)S(1)}, u32[]{:S(2)}, u32[]{:S(2)}) collective-permute-start(f32[5,8,2048]{2,1,0:T(8,128)S(1)} %get-tuple-element.136), channel_id=1, source_target_pairs={{0,3},{1,0},{2,1},{3,2},{8,11},{9,8},{10,9},{11,10},{12,15},{13,12... | collective-permute-start | bytes 983048 | tf_op jit(solution)/shard_map/ppermute | solution.py:486
  35.9 1.0 %copy-start.5 = (bf16[256,256]{1,0:T(8,128)(2,1)S(1)}, bf16[256,256]{1,0:T(8,128)(2,1)}, u32[]{:S(2)}) copy-start(bf16[256,256]{1,0:T(8,128)(2,1)} %constant.100.clone.refs_7_) | copy-start | bytes 393220
  35.9 1.0 %copy-start.6 = (bf16[256,256]{1,0:T(8,128)(2,1)S(1)}, bf16[256,256]{1,0:T(8,128)(2,1)}, u32[]{:S(2)}) copy-start(bf16[256,256]{1,0:T(8,128)(2,1)} %constant.101.clone.refs_8_) | copy-start | bytes 393220
  35.9 1.0 %copy-start.7 = (bf16[256,256]{1,0:T(8,128)(2,1)S(1)}, bf16[256,256]{1,0:T(8,128)(2,1)}, u32[]{:S(2)}) copy-start(bf16[256,256]{1,0:T(8,128)(2,1)} %constant.98.clone.refs_5_) | copy-start | bytes 393220
  35.9 1.2 %copy-start.8 = (bf16[256,256]{1,0:T(8,128)(2,1)S(1)}, bf16[256,256]{1,0:T(8,128)(2,1)}, u32[]{:S(2)}) copy-start(bf16[256,256]{1,0:T(8,128)(2,1)} %constant.99.clone.refs_6_) | copy-start | bytes 393220
  36.0 1.2 %copy-start.9 = (f32[2,16,128]{2,1,0:T(8,128)S(1)}, f32[2,16,128]{2,1,0:T(8,128)}, u32[]{:S(2)}) copy-start(f32[2,16,128]{2,1,0:T(8,128)} %constant.97.clone.refs_4_) | copy-start | bytes 49156
  44.4 2.8 %collective-permute-start.4 = (f32[3,8,2048]{2,1,0:T(8,128)S(1)}, f32[3,8,2048]{2,1,0:T(8,128)S(1)}, u32[]{:S(2)}, u32[]{:S(2)}) collective-permute-start(f32[3,8,2048]{2,1,0:T(8,128)S(1)} %convert_element_type.21), channel_id=1, source_target_pairs={{4,5},{5,6},{6,7},{7,4},{20,21},{21,22},{22,23},{23,20}} | collective-permute-start | bytes 589832 | tf_op jit(solution)/shard_map/ppermute | solution.py:486
  45.1 2.2 %collective-permute-start.5 = (f32[3,8,2048]{2,1,0:T(8,128)S(1)}, f32[3,8,2048]{2,1,0:T(8,128)S(1)}, u32[]{:S(2)}, u32[]{:S(2)}) collective-permute-start(f32[3,8,2048]{2,1,0:T(8,128)S(1)} %convert_element_type.21), channel_id=1, source_target_pairs={{4,6},{5,7},{6,4},{7,5},{20,22},{21,23},{22,20},{23,21}} | collective-permute-start | bytes 589832 | tf_op jit(solution)/shard_map/ppermute | solution.py:486
  45.8 1.6 %collective-permute-start.6 = (f32[3,8,2048]{2,1,0:T(8,128)S(1)}, f32[3,8,2048]{2,1,0:T(8,128)S(1)}, u32[]{:S(2)}, u32[]{:S(2)}) collective-permute-start(f32[3,8,2048]{2,1,0:T(8,128)S(1)} %convert_element_type.21), channel_id=1, source_target_pairs={{4,7},{5,4},{6,5},{7,6},{20,23},{21,20},{22,21},{23,22}} | collective-permute-start | bytes 589832 | tf_op jit(solution)/shard_map/ppermute | solution.py:486
  46.5 1.0 %collective-permute-start.3 = (f32[2,32,2048]{2,1,0:T(8,128)}, f32[2,32,2048]{2,1,0:T(8,128)S(1)}, u32[]{:S(2)}, u32[]{:S(2)}) collective-permute-start(f32[2,32,2048]{2,1,0:T(8,128)} %get-tuple-element.117), channel_id=1, source_target_pairs={{0,4},{1,5},{2,6},{3,7},{16,20},{17,21},{18,22},{19,23}} | collective-permute-start | bytes 1572872 | tf_op jit(solution)/shard_map/ppermute | solution.py:549
  47.5 0.7 collective-permute-start.7
  48.2 20.3 %collective-permute-start.8 = (f32[2,32,2048]{2,1,0:T(8,128)S(1)}, f32[2,32,2048]{2,1,0:T(8,128)S(1)}, u32[]{:S(2)}, u32[]{:S(2)}) collective-permute-start(f32[2,32,2048]{2,1,0:T(8,128)S(1)} %get-tuple-element.122), channel_id=1, source_target_pairs={{8,12},{9,13},{10,14},{11,15},{24,28},{25,29},{26,30},{27,31}} | collective-permute-start | bytes 1572872 | tf_op jit(solution)/shard_map/ppermute | solution.py:549
  75.7 10.0 %collective-permute-start.12 = (f32[3,8,2048]{2,1,0:T(8,128)S(1)}, f32[3,8,2048]{2,1,0:T(8,128)S(1)}, u32[]{:S(2)}, u32[]{:S(2)}) collective-permute-start(f32[3,8,2048]{2,1,0:T(8,128)S(1)} %get-tuple-element.129), channel_id=1, source_target_pairs={{12,13},{13,14},{14,15},{15,12},{28,29},{29,30},{30,31},{31,28}} | collective-permute-start | bytes 589832 | tf_op jit(solution)/shard_map/ppermute | solution.py:537
  77.7 13.1 %collective-permute-start.13 = (f32[3,8,2048]{2,1,0:T(8,128)S(1)}, f32[3,8,2048]{2,1,0:T(8,128)S(1)}, u32[]{:S(2)}, u32[]{:S(2)}) collective-permute-start(f32[3,8,2048]{2,1,0:T(8,128)S(1)} %get-tuple-element.131), channel_id=1, source_target_pairs={{12,14},{13,15},{14,12},{15,13},{28,30},{29,31},{30,28},{31,29}} | collective-permute-start | bytes 589832 | tf_op jit(solution)/shard_map/ppermute | solution.py:537
  81.0 10.8 %collective-permute-start.14 = (f32[3,8,2048]{2,1,0:T(8,128)S(1)}, f32[3,8,2048]{2,1,0:T(8,128)S(1)}, u32[]{:S(2)}, u32[]{:S(2)}) collective-permute-start(f32[3,8,2048]{2,1,0:T(8,128)S(1)} %get-tuple-element.130), channel_id=1, source_target_pairs={{12,15},{13,12},{14,13},{15,14},{28,31},{29,28},{30,29},{31,30}} | collective-permute-start | bytes 589832 | tf_op jit(solution)/shard_map/ppermute | solution.py:537
  84.4 7.5 %collective-permute-start.10 = (f32[3,8,2048]{2,1,0:T(8,128)S(1)}, f32[3,8,2048]{2,1,0:T(8,128)S(1)}, u32[]{:S(2)}, u32[]{:S(2)}) collective-permute-start(f32[3,8,2048]{2,1,0:T(8,128)S(1)} %get-tuple-element.128), channel_id=1, source_target_pairs={{0,2},{1,3},{2,0},{3,1},{4,6},{5,7},{6,4},{7,5},{8,10},{9,11},{10,... | collective-permute-start | bytes 589832 | tf_op jit(solution)/shard_map/ppermute | solution.py:537
  85.1 6.8 %collective-permute-start.11 = (f32[3,8,2048]{2,1,0:T(8,128)S(1)}, f32[3,8,2048]{2,1,0:T(8,128)S(1)}, u32[]{:S(2)}, u32[]{:S(2)}) collective-permute-start(f32[3,8,2048]{2,1,0:T(8,128)S(1)} %get-tuple-element.127), channel_id=1, source_target_pairs={{0,3},{1,0},{2,1},{3,2},{4,7},{5,4},{6,5},{7,6},{8,11},{9,8},{10,9... | collective-permute-start | bytes 589832 | tf_op jit(solution)/shard_map/ppermute | solution.py:537
  85.8 6.1 %collective-permute-start.9 = (f32[3,8,2048]{2,1,0:T(8,128)S(1)}, f32[3,8,2048]{2,1,0:T(8,128)S(1)}, u32[]{:S(2)}, u32[]{:S(2)}) collective-permute-start(f32[3,8,2048]{2,1,0:T(8,128)S(1)} %get-tuple-element.126), channel_id=1, source_target_pairs={{0,1},{1,2},{2,3},{3,0},{4,5},{5,6},{6,7},{7,4},{8,9},{9,10},{10,1... | collective-permute-start | bytes 589832 | tf_op jit(solution)/shard_map/ppermute | solution.py:537

commit v19 on v18

--- a/solution.py
+++ b/solution.py
@@ -360,7 +360,7 @@
                 img_ref[slot, k, :, blk(a)] = new_re[j * rows_here:(j + 1) * rows_here]
         return carry
 
-    lax.fori_loop(0, steps, one_step, 0)
+    lax.fori_loop(0, steps, one_step, 0, unroll=True)
 
 
 def fast_constants(line_len):

time: 93.6 us -> 93.5 us (level)
  no operation moved by 1% of the time
where the time goes in v19:
time: 93.5 us; the launch traced here: 92.5 us
  waiting for transfers between devices  43.3 us (46%)
  starting transfers between devices  24.8 us (27%)
  Pallas kernels  14.3 us (15%)
  local copies, waits for them, and re-layouts  5.02 us (5%)
  other arithmetic  4.26 us (5%)
    ppermute x6, waiting for transfers between devices, gather_strips(): lax.ppermute(piece_of(target), ('depth', 'strip'), strip_pairs(depths, st...  19.1 us
    ppermute x3, waiting for transfers between devices, shards(): wave = lax.ppermute(wave, 'depth', [(tick_no, tick_no + 1)])  18.8 us
    pallas_call x2, Pallas kernels, run_section(): pl.pallas_call(lambda *refs: section_kernel(*refs, table_len=table_len),...  14.3 us
    ppermute x6, starting transfers between devices, gather_strips(): lax.ppermute(piece_of(target), ('depth', 'strip'), strip_pairs(depths, st...  11.5 us
    ppermute x6, starting transfers between devices, freq_sum(): lax.ppermute(piece, ('depth', 'strip'), strip_pairs(depths, strip_count,...  10.6 us
    ppermute x6, waiting for transfers between devices, freq_sum(): lax.ppermute(piece, ('depth', 'strip'), strip_pairs(depths, strip_count,...  5.46 us
    ppermute x3, starting transfers between devices, shards(): wave = lax.ppermute(wave, 'depth', [(tick_no, tick_no + 1)])  2.68 us
  transfers between devices with their start and end apart: 15, of which 5 were waited for; matrix products, arithmetic and copies ran while one was open for 5% of the time, Pallas kernels for 0%

profile of v19, /device:TPU:11, one launch (start us, length us, event | category | flops | bytes accessed | tf_op | source)
XLA Modules:
  0.0 92.5 jit_solution(13243710269088727142)
XLA Ops:
  0.0 0.9 %convert_element_type.21 = f32[3,8,2048]{2,1,0:T(8,128)S(1)} convert(s32[3,8,2048]{2,1,0:T(8,128)} %param.22) | non-fusion elementwise | flops 49152 | bytes 393216 | tf_op jit(solution)/shard_map/convert_element_type | solution.py:505
  1.0 1.1 %dynamic-slice_bitcast_fusion = (f32[2,8,2048]{2,1,0:T(8,128)S(1)}, f32[2,8,2048]{2,1,0:T(8,128)S(1)}, f32[2,8,2048]{2,1,0:T(8,128)S(1)}, f32[2,8,2048]{2,1,0:T(8,128)S(1)}) fusion(f32[2,4,8,2048]{3,2,1,0:T(8,128)} %param.18, s32[]{:T(128)S(6)} %select_n.79, s32[]{:T(128)S(6)} %select_n.71, s32[]{:T(128)S(6)} %select_n.67, s32[]{:T(128)S(6)} %select_n.75), kind=kLoop, calls=%fused_computation.20 | loop fusion | bytes 1048592 | tf_op jit(solution)/shard_map/jit(dynamic_index_in_dim)/squeeze | solution.py:510
  2.4 3.2 %collective-permute-start = (f32[5,8,2048]{2,1,0:T(8,128)S(1)}, f32[5,8,2048]{2,1,0:T(8,128)}, u32[]{:S(2)}, u32[]{:S(2)}) collective-permute-start(f32[5,8,2048]{2,1,0:T(8,128)S(1)} %get-tuple-element.137), channel_id=1, source_target_pairs={{0,1},{1,2},{2,3},{3,0},{8,9},{9,10},{10,11},{11,8},{12,13},{13,14... | collective-permute-start | bytes 983048 | tf_op jit(solution)/shard_map/ppermute | solution.py:486
  5.6 2.9 %collective-permute-start.1 = (f32[5,8,2048]{2,1,0:T(8,128)S(1)}, f32[5,8,2048]{2,1,0:T(8,128)S(1)}, u32[]{:S(2)}, u32[]{:S(2)}) collective-permute-start(f32[5,8,2048]{2,1,0:T(8,128)S(1)} %get-tuple-element.138), channel_id=1, source_target_pairs={{0,2},{1,3},{2,0},{3,1},{8,10},{9,11},{10,8},{11,9},{12,14},{13,15... | collective-permute-start | bytes 983048 | tf_op jit(solution)/shard_map/ppermute | solution.py:486
  8.6 3.4 %collective-permute-start.2 = (f32[5,8,2048]{2,1,0:T(8,128)S(1)}, f32[5,8,2048]{2,1,0:T(8,128)S(1)}, u32[]{:S(2)}, u32[]{:S(2)}) collective-permute-start(f32[5,8,2048]{2,1,0:T(8,128)S(1)} %get-tuple-element.136), channel_id=1, source_target_pairs={{0,3},{1,0},{2,1},{3,2},{8,11},{9,8},{10,9},{11,10},{12,15},{13,12... | collective-permute-start | bytes 983048 | tf_op jit(solution)/shard_map/ppermute | solution.py:486
  12.7 0.6 gather_fusion
  13.3 0.8 fusion.17
  14.1 0.7 multiply_multiply_fusion
  14.7 0.7 broadcast_divide_fusion
  15.7 1.0 %constant_dynamic-update-slice_fusion.6 = f32[5,32,2048]{2,1,0:T(8,128)S(1)} fusion(f32[5,32,2048]{2,1,0:T(8,128)S(1)} %get-tuple-element.139, f32[5,8,2048]{2,1,0:T(8,128)} %collective-permute-done, s32[]{:T(128)S(6)} %select_n.73), kind=kLoop, calls=%fused_computation.44 | loop fusion | bytes 655364 | tf_op jit(solution)/shard_map/dynamic_update_slice | solution.py:490
  16.7 16.3 %collective-permute-done.1 = f32[5,8,2048]{2,1,0:T(8,128)S(1)} collective-permute-done((f32[5,8,2048]{2,1,0:T(8,128)S(1)}, f32[5,8,2048]{2,1,0:T(8,128)S(1)}, u32[]{:S(2)}, u32[]{:S(2)}) %collective-permute-start.1) | collective-permute-done | bytes 327712 | tf_op jit(solution)/shard_map/ppermute | solution.py:486
  33.1 2.8 %collective-permute-done.2 = f32[5,8,2048]{2,1,0:T(8,128)S(1)} collective-permute-done((f32[5,8,2048]{2,1,0:T(8,128)S(1)}, f32[5,8,2048]{2,1,0:T(8,128)S(1)}, u32[]{:S(2)}, u32[]{:S(2)}) %collective-permute-start.2) | collective-permute-done | bytes 327712 | tf_op jit(solution)/shard_map/ppermute | solution.py:486
  36.1 0.8 slice.38.refs_1_
  37.2 7.2 %shard_map.118 = (f32[2,32,2048]{2,1,0:T(8,128)}, f32[4,3,8,2048]{3,2,1,0:T(8,128)S(1)}) custom-call(f32[72]{0:T(128)S(1)} %reshape.137.refs_0_, f32[2,32,2048]{2,1,0:T(8,128)} %slice.38.refs_1_, s32[3,32,2048]{2,1,0:T(8,128)S(1)} %slice_convert_fusion.refs_2_, f32[3,2,16,128]{3,2,1,0:T(8,128)S(1)} %pad_maximum_fusion.4.refs_3_, ...), custom_call_target="tpu_custom_call" | custom-call | flops 1286602752 | bytes 4718592 | tf_op jit(solution)/shard_map/pallas_call | solution.py:395
  44.4 0.7 collective-permute-start.4
  45.0 0.7 collective-permute-start.5
  45.7 0.7 collective-permute-start.6
  46.4 0.7 collective-permute-start.3
  47.4 0.7 collective-permute-start.7
  48.3 1.3 %collective-permute-start.8 = (f32[2,32,2048]{2,1,0:T(8,128)S(1)}, f32[2,32,2048]{2,1,0:T(8,128)S(1)}, u32[]{:S(2)}, u32[]{:S(2)}) collective-permute-start(f32[2,32,2048]{2,1,0:T(8,128)S(1)} %get-tuple-element.122), channel_id=1, source_target_pairs={{8,12},{9,13},{10,14},{11,15},{24,28},{25,29},{26,30},{27,31}} | collective-permute-start | bytes 1572872 | tf_op jit(solution)/shard_map/ppermute | solution.py:549
  49.6 18.8 %collective-permute-done.8 = f32[2,32,2048]{2,1,0:T(8,128)S(1)} collective-permute-done((f32[2,32,2048]{2,1,0:T(8,128)S(1)}, f32[2,32,2048]{2,1,0:T(8,128)S(1)}, u32[]{:S(2)}, u32[]{:S(2)}) %collective-permute-start.8) | collective-permute-done | bytes 524320 | tf_op jit(solution)/shard_map/ppermute | solution.py:549
  68.4 7.1 %conditional.5 = (f32[4,3,8,2048]{3,2,1,0:T(8,128)S(1)}) conditional(s32[]{:T(128)} %convert_element_type.18, f32[4,3,8,2048]{3,2,1,0:T(8,128)S(1)} %get-tuple-element.124, (s32[]{:T(128)}, f32[72]{0:T(128)S(1)}, f32[2,32,2048]{2,1,0:T(8,128)S(1)}, s32[3,32,2048]{2,1,0:T(8,128)S(1)}, f32[3,2,16,128]{3,2,1,0:T(8,128)S(1)}, ...), branch_computations={%region_4.5_spmd, %region_5.6_spmd} | conditional | flops 1286602752 | bytes 4718600 | solution.py:547
  68.4 7.1 %branch_1_fun.5 = (f32[2,32,2048]{2,1,0:T(8,128)}, f32[4,3,8,2048]{3,2,1,0:T(8,128)S(1)}) custom-call(f32[72]{0:T(128)S(1)} %get-tuple-element.97.refs_0_, f32[2,32,2048]{2,1,0:T(8,128)S(1)} %get-tuple-element.98.refs_1_, s32[3,32,2048]{2,1,0:T(8,128)S(1)} %get-tuple-element.99.refs_2_, f32[3,2,16,128]{3,2,1,0:T(8,128)S(1)} %get-tuple-element.100.refs_3_, ...), custom_call_target="tpu_custom_call" | custom-call | flops 1286602752 | bytes 4718592 | tf_op jit(solution)/shard_map/cond/branch_1_fun/pallas_call | solution.py:395
  75.6 1.9 %collective-permute-start.12 = (f32[3,8,2048]{2,1,0:T(8,128)S(1)}, f32[3,8,2048]{2,1,0:T(8,128)S(1)}, u32[]{:S(2)}, u32[]{:S(2)}) collective-permute-start(f32[3,8,2048]{2,1,0:T(8,128)S(1)} %get-tuple-element.129), channel_id=1, source_target_pairs={{12,13},{13,14},{14,15},{15,12},{28,29},{29,30},{30,31},{31,28}} | collective-permute-start | bytes 589832 | tf_op jit(solution)/shard_map/ppermute | solution.py:537
  77.6 3.3 %collective-permute-start.13 = (f32[3,8,2048]{2,1,0:T(8,128)S(1)}, f32[3,8,2048]{2,1,0:T(8,128)S(1)}, u32[]{:S(2)}, u32[]{:S(2)}) collective-permute-start(f32[3,8,2048]{2,1,0:T(8,128)S(1)} %get-tuple-element.131), channel_id=1, source_target_pairs={{12,14},{13,15},{14,12},{15,13},{28,30},{29,31},{30,28},{31,29}} | collective-permute-start | bytes 589832 | tf_op jit(solution)/shard_map/ppermute | solution.py:537
  80.9 3.4 %collective-permute-start.14 = (f32[3,8,2048]{2,1,0:T(8,128)S(1)}, f32[3,8,2048]{2,1,0:T(8,128)S(1)}, u32[]{:S(2)}, u32[]{:S(2)}) collective-permute-start(f32[3,8,2048]{2,1,0:T(8,128)S(1)} %get-tuple-element.130), channel_id=1, source_target_pairs={{12,15},{13,12},{14,13},{15,14},{28,31},{29,28},{30,29},{31,30}} | collective-permute-start | bytes 589832 | tf_op jit(solution)/shard_map/ppermute | solution.py:537
  84.2 0.7 collective-permute-start.10
  84.9 0.7 collective-permute-start.11
  85.6 0.7 collective-permute-start.9
  86.3 4.4 %collective-permute-done.13 = f32[3,8,2048]{2,1,0:T(8,128)S(1)} collective-permute-done((f32[3,8,2048]{2,1,0:T(8,128)S(1)}, f32[3,8,2048]{2,1,0:T(8,128)S(1)}, u32[]{:S(2)}, u32[]{:S(2)}) %collective-permute-start.13) | collective-permute-done | bytes 196640 | tf_op jit(solution)/shard_map/ppermute | solution.py:537
  90.7 1.0 %collective-permute-done.14 = f32[3,8,2048]{2,1,0:T(8,128)S(1)} collective-permute-done((f32[3,8,2048]{2,1,0:T(8,128)S(1)}, f32[3,8,2048]{2,1,0:T(8,128)S(1)}, u32[]{:S(2)}, u32[]{:S(2)}) %collective-permute-start.14) | collective-permute-done | bytes 196640 | tf_op jit(solution)/shard_map/ppermute | solution.py:537
  91.8 0.8 fusion.6
  (54 shorter events, 2.1 us)
Async XLA Ops:
  2.2 9.8 %copy-start = (f32[4]{0:T(128)S(1)}, f32[4]{0:T(128)}, u32[]{:S(2)}) copy-start(f32[4]{0:T(128)} %param.19) | copy-start | bytes 52
  2.3 10.4 %copy-start.1 = (f32[8]{0:T(128)S(1)}, f32[8]{0:T(128)}, u32[]{:S(2)}) copy-start(f32[8]{0:T(128)} %param.20) | copy-start | bytes 100
  2.3 10.4 %copy-start.2 = (s32[3]{0:T(128)S(1)}, s32[3]{0:T(128)}, u32[]{:S(2)}) copy-start(s32[3]{0:T(128)} %param.23) | copy-start | bytes 40
  2.3 12.5 %copy-start.3 = (f32[8]{0:T(128)S(1)}, f32[8]{0:T(128)}, u32[]{:S(2)}) copy-start(f32[8]{0:T(128)} %param.21) | copy-start | bytes 100
  2.3 13.2 %copy-start.4 = (f32[16,128]{1,0:T(8,128)S(1)}, f32[16,128]{1,0:T(8,128)}, u32[]{:S(2)}) copy-start(f32[16,128]{1,0:T(8,128)} %constant.105) | copy-start | bytes 24580
  2.4 13.3 %collective-permute-start = (f32[5,8,2048]{2,1,0:T(8,128)S(1)}, f32[5,8,2048]{2,1,0:T(8,128)}, u32[]{:S(2)}, u32[]{:S(2)}) collective-permute-start(f32[5,8,2048]{2,1,0:T(8,128)S(1)} %get-tuple-element.137), channel_id=1, source_target_pairs={{0,1},{1,2},{2,3},{3,0},{8,9},{9,10},{10,11},{11,8},{12,13},{13,14... | collective-permute-start | bytes 983048 | tf_op jit(solution)/shard_map/ppermute | solution.py:486
  5.6 27.4 %collective-permute-start.1 = (f32[5,8,2048]{2,1,0:T(8,128)S(1)}, f32[5,8,2048]{2,1,0:T(8,128)S(1)}, u32[]{:S(2)}, u32[]{:S(2)}) collective-permute-start(f32[5,8,2048]{2,1,0:T(8,128)S(1)} %get-tuple-element.138), channel_id=1, source_target_pairs={{0,2},{1,3},{2,0},{3,1},{8,10},{9,11},{10,8},{11,9},{12,14},{13,15... | collective-permute-start | bytes 983048 | tf_op jit(solution)/shard_map/ppermute | solution.py:486
  8.6 27.3 %collective-permute-start.2 = (f32[5,8,2048]{2,1,0:T(8,128)S(1)}, f32[5,8,2048]{2,1,0:T(8,128)S(1)}, u32[]{:S(2)}, u32[]{:S(2)}) collective-permute-start(f32[5,8,2048]{2,1,0:T(8,128)S(1)} %get-tuple-element.136), channel_id=1, source_target_pairs={{0,3},{1,0},{2,1},{3,2},{8,11},{9,8},{10,9},{11,10},{12,15},{13,12... | collective-permute-start | bytes 983048 | tf_op jit(solution)/shard_map/ppermute | solution.py:486
  35.9 1.0 %copy-start.5 = (bf16[256,256]{1,0:T(8,128)(2,1)S(1)}, bf16[256,256]{1,0:T(8,128)(2,1)}, u32[]{:S(2)}) copy-start(bf16[256,256]{1,0:T(8,128)(2,1)} %constant.100.clone.refs_7_) | copy-start | bytes 393220
  35.9 1.0 %copy-start.6 = (bf16[256,256]{1,0:T(8,128)(2,1)S(1)}, bf16[256,256]{1,0:T(8,128)(2,1)}, u32[]{:S(2)}) copy-start(bf16[256,256]{1,0:T(8,128)(2,1)} %constant.101.clone.refs_8_) | copy-start | bytes 393220
  35.9 1.0 %copy-start.7 = (bf16[256,256]{1,0:T(8,128)(2,1)S(1)}, bf16[256,256]{1,0:T(8,128)(2,1)}, u32[]{:S(2)}) copy-start(bf16[256,256]{1,0:T(8,128)(2,1)} %constant.98.clone.refs_5_) | copy-start | bytes 393220
  35.9 1.2 %copy-start.8 = (bf16[256,256]{1,0:T(8,128)(2,1)S(1)}, bf16[256,256]{1,0:T(8,128)(2,1)}, u32[]{:S(2)}) copy-start(bf16[256,256]{1,0:T(8,128)(2,1)} %constant.99.clone.refs_6_) | copy-start | bytes 393220
  36.0 1.2 %copy-start.9 = (f32[2,16,128]{2,1,0:T(8,128)S(1)}, f32[2,16,128]{2,1,0:T(8,128)}, u32[]{:S(2)}) copy-start(f32[2,16,128]{2,1,0:T(8,128)} %constant.97.clone.refs_4_) | copy-start | bytes 49156
  44.4 2.8 %collective-permute-start.4 = (f32[3,8,2048]{2,1,0:T(8,128)S(1)}, f32[3,8,2048]{2,1,0:T(8,128)S(1)}, u32[]{:S(2)}, u32[]{:S(2)}) collective-permute-start(f32[3,8,2048]{2,1,0:T(8,128)S(1)} %convert_element_type.21), channel_id=1, source_target_pairs={{4,5},{5,6},{6,7},{7,4},{20,21},{21,22},{22,23},{23,20}} | collective-permute-start | bytes 589832 | tf_op jit(solution)/shard_map/ppermute | solution.py:486
  45.0 2.2 %collective-permute-start.5 = (f32[3,8,2048]{2,1,0:T(8,128)S(1)}, f32[3,8,2048]{2,1,0:T(8,128)S(1)}, u32[]{:S(2)}, u32[]{:S(2)}) collective-permute-start(f32[3,8,2048]{2,1,0:T(8,128)S(1)} %convert_element_type.21), channel_id=1, source_target_pairs={{4,6},{5,7},{6,4},{7,5},{20,22},{21,23},{22,20},{23,21}} | collective-permute-start | bytes 589832 | tf_op jit(solution)/shard_map/ppermute | solution.py:486
  45.7 1.6 %collective-permute-start.6 = (f32[3,8,2048]{2,1,0:T(8,128)S(1)}, f32[3,8,2048]{2,1,0:T(8,128)S(1)}, u32[]{:S(2)}, u32[]{:S(2)}) collective-permute-start(f32[3,8,2048]{2,1,0:T(8,128)S(1)} %convert_element_type.21), channel_id=1, source_target_pairs={{4,7},{5,4},{6,5},{7,6},{20,23},{21,20},{22,21},{23,22}} | collective-permute-start | bytes 589832 | tf_op jit(solution)/shard_map/ppermute | solution.py:486
  46.4 1.0 %collective-permute-start.3 = (f32[2,32,2048]{2,1,0:T(8,128)}, f32[2,32,2048]{2,1,0:T(8,128)S(1)}, u32[]{:S(2)}, u32[]{:S(2)}) collective-permute-start(f32[2,32,2048]{2,1,0:T(8,128)} %get-tuple-element.117), channel_id=1, source_target_pairs={{0,4},{1,5},{2,6},{3,7},{16,20},{17,21},{18,22},{19,23}} | collective-permute-start | bytes 1572872 | tf_op jit(solution)/shard_map/ppermute | solution.py:549
  47.4 0.7 collective-permute-start.7
  48.3 20.1 %collective-permute-start.8 = (f32[2,32,2048]{2,1,0:T(8,128)S(1)}, f32[2,32,2048]{2,1,0:T(8,128)S(1)}, u32[]{:S(2)}, u32[]{:S(2)}) collective-permute-start(f32[2,32,2048]{2,1,0:T(8,128)S(1)} %get-tuple-element.122), channel_id=1, source_target_pairs={{8,12},{9,13},{10,14},{11,15},{24,28},{25,29},{26,30},{27,31}} | collective-permute-start | bytes 1572872 | tf_op jit(solution)/shard_map/ppermute | solution.py:549
  75.6 10.0 %collective-permute-start.12 = (f32[3,8,2048]{2,1,0:T(8,128)S(1)}, f32[3,8,2048]{2,1,0:T(8,128)S(1)}, u32[]{:S(2)}, u32[]{:S(2)}) collective-permute-start(f32[3,8,2048]{2,1,0:T(8,128)S(1)} %get-tuple-element.129), channel_id=1, source_target_pairs={{12,13},{13,14},{14,15},{15,12},{28,29},{29,30},{30,31},{31,28}} | collective-permute-start | bytes 589832 | tf_op jit(solution)/shard_map/ppermute | solution.py:537
  77.6 13.2 %collective-permute-start.13 = (f32[3,8,2048]{2,1,0:T(8,128)S(1)}, f32[3,8,2048]{2,1,0:T(8,128)S(1)}, u32[]{:S(2)}, u32[]{:S(2)}) collective-permute-start(f32[3,8,2048]{2,1,0:T(8,128)S(1)} %get-tuple-element.131), channel_id=1, source_target_pairs={{12,14},{13,15},{14,12},{15,13},{28,30},{29,31},{30,28},{31,29}} | collective-permute-start | bytes 589832 | tf_op jit(solution)/shard_map/ppermute | solution.py:537
  80.9 10.9 %collective-permute-start.14 = (f32[3,8,2048]{2,1,0:T(8,128)S(1)}, f32[3,8,2048]{2,1,0:T(8,128)S(1)}, u32[]{:S(2)}, u32[]{:S(2)}) collective-permute-start(f32[3,8,2048]{2,1,0:T(8,128)S(1)} %get-tuple-element.130), channel_id=1, source_target_pairs={{12,15},{13,12},{14,13},{15,14},{28,31},{29,28},{30,29},{31,30}} | collective-permute-start | bytes 589832 | tf_op jit(solution)/shard_map/ppermute | solution.py:537
  84.2 7.5 %collective-permute-start.10 = (f32[3,8,2048]{2,1,0:T(8,128)S(1)}, f32[3,8,2048]{2,1,0:T(8,128)S(1)}, u32[]{:S(2)}, u32[]{:S(2)}) collective-permute-start(f32[3,8,2048]{2,1,0:T(8,128)S(1)} %get-tuple-element.128), channel_id=1, source_target_pairs={{0,2},{1,3},{2,0},{3,1},{4,6},{5,7},{6,4},{7,5},{8,10},{9,11},{10,... | collective-permute-start | bytes 589832 | tf_op jit(solution)/shard_map/ppermute | solution.py:537
  84.9 6.8 %collective-permute-start.11 = (f32[3,8,2048]{2,1,0:T(8,128)S(1)}, f32[3,8,2048]{2,1,0:T(8,128)S(1)}, u32[]{:S(2)}, u32[]{:S(2)}) collective-permute-start(f32[3,8,2048]{2,1,0:T(8,128)S(1)} %get-tuple-element.127), channel_id=1, source_target_pairs={{0,3},{1,0},{2,1},{3,2},{4,7},{5,4},{6,5},{7,6},{8,11},{9,8},{10,9... | collective-permute-start | bytes 589832 | tf_op jit(solution)/shard_map/ppermute | solution.py:537
  85.6 6.1 %collective-permute-start.9 = (f32[3,8,2048]{2,1,0:T(8,128)S(1)}, f32[3,8,2048]{2,1,0:T(8,128)S(1)}, u32[]{:S(2)}, u32[]{:S(2)}) collective-permute-start(f32[3,8,2048]{2,1,0:T(8,128)S(1)} %get-tuple-element.126), channel_id=1, source_target_pairs={{0,1},{1,2},{2,3},{3,0},{4,5},{5,6},{6,7},{7,4},{8,9},{9,10},{10,1... | collective-permute-start | bytes 589832 | tf_op jit(solution)/shard_map/ppermute | solution.py:537

commit v20 on v18

--- a/solution.py
+++ b/solution.py
@@ -253,7 +253,7 @@
 
 def section_kernel(
     tab_ref, w_ref, rid_ref, mult_ref, tw_ref, fhi_ref, flo_ref, ghi_ref, glo_ref, pos_ref,
-    wout_ref, img_ref, a_ref, y_ref, v_ref, cs_ref, sn_ref, gn_ref, *, table_len
+    wout_ref, img_ref, a_ref, y_ref, v_ref, cs_ref, sn_ref, gn_ref, ahi_ref, alo_ref, *, table_len
 ):
     rows = w_ref.shape[1]
     line_len = w_ref.shape[2]
@@ -302,9 +302,16 @@
             yi = y_ref[band, LANE:2 * LANE]
             mr = mult_ref[k, 0, cc:cc + 1, :]
             mi = mult_ref[k, 1, cc:cc + 1, :]
-            a_ref[band, 0:LANE] = yr * mr - yi * mi
-            a_ref[band, LANE:2 * LANE] = yr * mi + yi * mr
-        y_ref[...] = split_dot(a_ref[...], ghi_ref, glo_ref)
+            for lanes, val in ((slice(0, LANE), yr * mr - yi * mi), (slice(LANE, 2 * LANE), yr * mi + yi * mr)):
+                high = val.astype(jnp.bfloat16)
+                ahi_ref[band, lanes] = high
+                alo_ref[band, lanes] = (val - high.astype(jnp.float32)).astype(jnp.bfloat16)
+        high = ahi_ref[...]
+        main = jnp.dot(high, ghi_ref[...], preferred_element_type=jnp.float32)
+        fix = jnp.dot(high, glo_ref[...], preferred_element_type=jnp.float32) + jnp.dot(
+            alo_ref[...], ghi_ref[:, :], preferred_element_type=jnp.float32
+        )
+        y_ref[...] = main + fix
 
         def inverse_chunk(i, c):
             y0 = pl.multiple_of(i * ROW_CHUNK, ROW_CHUNK)
@@ -408,6 +415,8 @@
             pltpu.VMEM((rows, line_len), jnp.float32),
             pltpu.VMEM((rows, line_len), jnp.float32),
             pltpu.VMEM((rows, line_len), jnp.float32),
+            pltpu.VMEM((FFT_BLOCKS * rows, 2 * LANE), jnp.bfloat16),
+            pltpu.VMEM((FFT_BLOCKS * rows, 2 * LANE), jnp.bfloat16),
         ],
         cost_estimate=pl.CostEstimate(
             flops=flops, transcendentals=0, bytes_accessed=4 * rows * line_len * 6 * steps

time: 93.6 us -> 94 us (level)
  no operation moved by 1% of the time
where the time goes in v20:
time: 94 us; the launch traced here: 92.9 us
  waiting for transfers between devices  43.5 us (46%)
  starting transfers between devices  24.8 us (26%)
  Pallas kernels  14.8 us (16%)
  local copies, waits for them, and re-layouts  5.02 us (5%)
  other arithmetic  4.26 us (5%)
    ppermute x3, waiting for transfers between devices, shards(): wave = lax.ppermute(wave, 'depth', [(tick_no, tick_no + 1)])  19.2 us
    ppermute x6, waiting for transfers between devices, gather_strips(): lax.ppermute(piece_of(target), ('depth', 'strip'), strip_pairs(depths, st...  19.1 us
    pallas_call x2, Pallas kernels, run_section(): pl.pallas_call(lambda *refs: section_kernel(*refs, table_len=table_len),...  14.8 us
    ppermute x6, starting transfers between devices, gather_strips(): lax.ppermute(piece_of(target), ('depth', 'strip'), strip_pairs(depths, st...  11.5 us
    ppermute x6, starting transfers between devices, freq_sum(): lax.ppermute(piece, ('depth', 'strip'), strip_pairs(depths, strip_count,...  10.6 us
    ppermute x6, waiting for transfers between devices, freq_sum(): lax.ppermute(piece, ('depth', 'strip'), strip_pairs(depths, strip_count,...  5.25 us
    ppermute x3, starting transfers between devices, shards(): wave = lax.ppermute(wave, 'depth', [(tick_no, tick_no + 1)])  2.68 us
  transfers between devices with their start and end apart: 15, of which 5 were waited for; matrix products, arithmetic and copies ran while one was open for 5% of the time, Pallas kernels for 0%

profile of v20, /device:TPU:11, one launch (start us, length us, event | category | flops | bytes accessed | tf_op | source)
XLA Modules:
  0.0 92.9 jit_solution(15771054487736928969)
XLA Ops:
  0.0 0.9 %convert_element_type.21 = f32[3,8,2048]{2,1,0:T(8,128)S(1)} convert(s32[3,8,2048]{2,1,0:T(8,128)} %param.22) | non-fusion elementwise | flops 49152 | bytes 393216 | tf_op jit(solution)/shard_map/convert_element_type | solution.py:514
  1.0 1.1 %dynamic-slice_bitcast_fusion = (f32[2,8,2048]{2,1,0:T(8,128)S(1)}, f32[2,8,2048]{2,1,0:T(8,128)S(1)}, f32[2,8,2048]{2,1,0:T(8,128)S(1)}, f32[2,8,2048]{2,1,0:T(8,128)S(1)}) fusion(f32[2,4,8,2048]{3,2,1,0:T(8,128)} %param.18, s32[]{:T(128)S(6)} %select_n.79, s32[]{:T(128)S(6)} %select_n.71, s32[]{:T(128)S(6)} %select_n.67, s32[]{:T(128)S(6)} %select_n.75), kind=kLoop, calls=%fused_computation.20 | loop fusion | bytes 1048592 | tf_op jit(solution)/shard_map/jit(dynamic_index_in_dim)/squeeze | solution.py:519
  2.4 3.2 %collective-permute-start = (f32[5,8,2048]{2,1,0:T(8,128)S(1)}, f32[5,8,2048]{2,1,0:T(8,128)}, u32[]{:S(2)}, u32[]{:S(2)}) collective-permute-start(f32[5,8,2048]{2,1,0:T(8,128)S(1)} %get-tuple-element.137), channel_id=1, source_target_pairs={{0,1},{1,2},{2,3},{3,0},{8,9},{9,10},{10,11},{11,8},{12,13},{13,14... | collective-permute-start | bytes 983048 | tf_op jit(solution)/shard_map/ppermute | solution.py:495
  5.6 2.9 %collective-permute-start.1 = (f32[5,8,2048]{2,1,0:T(8,128)S(1)}, f32[5,8,2048]{2,1,0:T(8,128)S(1)}, u32[]{:S(2)}, u32[]{:S(2)}) collective-permute-start(f32[5,8,2048]{2,1,0:T(8,128)S(1)} %get-tuple-element.138), channel_id=1, source_target_pairs={{0,2},{1,3},{2,0},{3,1},{8,10},{9,11},{10,8},{11,9},{12,14},{13,15... | collective-permute-start | bytes 983048 | tf_op jit(solution)/shard_map/ppermute | solution.py:495
  8.6 3.4 %collective-permute-start.2 = (f32[5,8,2048]{2,1,0:T(8,128)S(1)}, f32[5,8,2048]{2,1,0:T(8,128)S(1)}, u32[]{:S(2)}, u32[]{:S(2)}) collective-permute-start(f32[5,8,2048]{2,1,0:T(8,128)S(1)} %get-tuple-element.136), channel_id=1, source_target_pairs={{0,3},{1,0},{2,1},{3,2},{8,11},{9,8},{10,9},{11,10},{12,15},{13,12... | collective-permute-start | bytes 983048 | tf_op jit(solution)/shard_map/ppermute | solution.py:495
  12.7 0.6 gather_fusion
  13.3 0.8 fusion.17
  14.1 0.7 multiply_multiply_fusion
  14.7 0.7 broadcast_divide_fusion
  15.7 1.0 %constant_dynamic-update-slice_fusion.6 = f32[5,32,2048]{2,1,0:T(8,128)S(1)} fusion(f32[5,32,2048]{2,1,0:T(8,128)S(1)} %get-tuple-element.139, f32[5,8,2048]{2,1,0:T(8,128)} %collective-permute-done, s32[]{:T(128)S(6)} %select_n.73), kind=kLoop, calls=%fused_computation.44 | loop fusion | bytes 655364 | tf_op jit(solution)/shard_map/dynamic_update_slice | solution.py:499
  16.7 16.3 %collective-permute-done.1 = f32[5,8,2048]{2,1,0:T(8,128)S(1)} collective-permute-done((f32[5,8,2048]{2,1,0:T(8,128)S(1)}, f32[5,8,2048]{2,1,0:T(8,128)S(1)}, u32[]{:S(2)}, u32[]{:S(2)}) %collective-permute-start.1) | collective-permute-done | bytes 327712 | tf_op jit(solution)/shard_map/ppermute | solution.py:495
  33.1 2.8 %collective-permute-done.2 = f32[5,8,2048]{2,1,0:T(8,128)S(1)} collective-permute-done((f32[5,8,2048]{2,1,0:T(8,128)S(1)}, f32[5,8,2048]{2,1,0:T(8,128)S(1)}, u32[]{:S(2)}, u32[]{:S(2)}) %collective-permute-start.2) | collective-permute-done | bytes 327712 | tf_op jit(solution)/shard_map/ppermute | solution.py:495
  36.1 0.8 slice.38.refs_1_
  37.2 7.4 %shard_map.118 = (f32[2,32,2048]{2,1,0:T(8,128)}, f32[4,3,8,2048]{3,2,1,0:T(8,128)S(1)}) custom-call(f32[72]{0:T(128)S(1)} %reshape.137.refs_0_, f32[2,32,2048]{2,1,0:T(8,128)} %slice.38.refs_1_, s32[3,32,2048]{2,1,0:T(8,128)S(1)} %slice_convert_fusion.refs_2_, f32[3,2,16,128]{3,2,1,0:T(8,128)S(1)} %pad_maximum_fusion.4.refs_3_, ...), custom_call_target="tpu_custom_call" | custom-call | flops 1286602752 | bytes 4718592 | tf_op jit(solution)/shard_map/pallas_call | solution.py:402
  44.6 0.7 collective-permute-start.4
  45.3 0.7 collective-permute-start.5
  45.9 0.7 collective-permute-start.6
  46.6 0.7 collective-permute-start.3
  47.6 0.7 collective-permute-start.7
  48.4 1.3 %collective-permute-start.8 = (f32[2,32,2048]{2,1,0:T(8,128)S(1)}, f32[2,32,2048]{2,1,0:T(8,128)S(1)}, u32[]{:S(2)}, u32[]{:S(2)}) collective-permute-start(f32[2,32,2048]{2,1,0:T(8,128)S(1)} %get-tuple-element.122), channel_id=1, source_target_pairs={{8,12},{9,13},{10,14},{11,15},{24,28},{25,29},{26,30},{27,31}} | collective-permute-start | bytes 1572872 | tf_op jit(solution)/shard_map/ppermute | solution.py:558
  49.7 19.1 %collective-permute-done.8 = f32[2,32,2048]{2,1,0:T(8,128)S(1)} collective-permute-done((f32[2,32,2048]{2,1,0:T(8,128)S(1)}, f32[2,32,2048]{2,1,0:T(8,128)S(1)}, u32[]{:S(2)}, u32[]{:S(2)}) %collective-permute-start.8) | collective-permute-done | bytes 524320 | tf_op jit(solution)/shard_map/ppermute | solution.py:558
  68.8 7.3 %conditional.5 = (f32[4,3,8,2048]{3,2,1,0:T(8,128)S(1)}) conditional(s32[]{:T(128)} %convert_element_type.18, f32[4,3,8,2048]{3,2,1,0:T(8,128)S(1)} %get-tuple-element.124, (s32[]{:T(128)}, f32[72]{0:T(128)S(1)}, f32[2,32,2048]{2,1,0:T(8,128)S(1)}, s32[3,32,2048]{2,1,0:T(8,128)S(1)}, f32[3,2,16,128]{3,2,1,0:T(8,128)S(1)}, ...), branch_computations={%region_4.5_spmd, %region_5.6_spmd} | conditional | flops 1286602752 | bytes 4718600 | solution.py:556
  68.8 7.3 %branch_1_fun.5 = (f32[2,32,2048]{2,1,0:T(8,128)}, f32[4,3,8,2048]{3,2,1,0:T(8,128)S(1)}) custom-call(f32[72]{0:T(128)S(1)} %get-tuple-element.97.refs_0_, f32[2,32,2048]{2,1,0:T(8,128)S(1)} %get-tuple-element.98.refs_1_, s32[3,32,2048]{2,1,0:T(8,128)S(1)} %get-tuple-element.99.refs_2_, f32[3,2,16,128]{3,2,1,0:T(8,128)S(1)} %get-tuple-element.100.refs_3_, ...), custom_call_target="tpu_custom_call" | custom-call | flops 1286602752 | bytes 4718592 | tf_op jit(solution)/shard_map/cond/branch_1_fun/pallas_call | solution.py:402
  76.2 1.9 %collective-permute-start.12 = (f32[3,8,2048]{2,1,0:T(8,128)S(1)}, f32[3,8,2048]{2,1,0:T(8,128)S(1)}, u32[]{:S(2)}, u32[]{:S(2)}) collective-permute-start(f32[3,8,2048]{2,1,0:T(8,128)S(1)} %get-tuple-element.129), channel_id=1, source_target_pairs={{12,13},{13,14},{14,15},{15,12},{28,29},{29,30},{30,31},{31,28}} | collective-permute-start | bytes 589832 | tf_op jit(solution)/shard_map/ppermute | solution.py:546
  78.2 3.3 %collective-permute-start.13 = (f32[3,8,2048]{2,1,0:T(8,128)S(1)}, f32[3,8,2048]{2,1,0:T(8,128)S(1)}, u32[]{:S(2)}, u32[]{:S(2)}) collective-permute-start(f32[3,8,2048]{2,1,0:T(8,128)S(1)} %get-tuple-element.131), channel_id=1, source_target_pairs={{12,14},{13,15},{14,12},{15,13},{28,30},{29,31},{30,28},{31,29}} | collective-permute-start | bytes 589832 | tf_op jit(solution)/shard_map/ppermute | solution.py:546
  81.5 3.4 %collective-permute-start.14 = (f32[3,8,2048]{2,1,0:T(8,128)S(1)}, f32[3,8,2048]{2,1,0:T(8,128)S(1)}, u32[]{:S(2)}, u32[]{:S(2)}) collective-permute-start(f32[3,8,2048]{2,1,0:T(8,128)S(1)} %get-tuple-element.130), channel_id=1, source_target_pairs={{12,15},{13,12},{14,13},{15,14},{28,31},{29,28},{30,29},{31,30}} | collective-permute-start | bytes 589832 | tf_op jit(solution)/shard_map/ppermute | solution.py:546
  84.9 0.7 collective-permute-start.10
  85.5 0.7 collective-permute-start.11
  86.2 0.7 collective-permute-start.9
  86.9 4.3 %collective-permute-done.13 = f32[3,8,2048]{2,1,0:T(8,128)S(1)} collective-permute-done((f32[3,8,2048]{2,1,0:T(8,128)S(1)}, f32[3,8,2048]{2,1,0:T(8,128)S(1)}, u32[]{:S(2)}, u32[]{:S(2)}) %collective-permute-start.13) | collective-permute-done | bytes 196640 | tf_op jit(solution)/shard_map/ppermute | solution.py:546
  91.3 0.9 collective-permute-done.14
  92.2 0.8 fusion.6
  (54 shorter events, 1.9 us)
Async XLA Ops:
  2.2 9.8 %copy-start = (f32[4]{0:T(128)S(1)}, f32[4]{0:T(128)}, u32[]{:S(2)}) copy-start(f32[4]{0:T(128)} %param.19) | copy-start | bytes 52
  2.3 10.4 %copy-start.1 = (f32[8]{0:T(128)S(1)}, f32[8]{0:T(128)}, u32[]{:S(2)}) copy-start(f32[8]{0:T(128)} %param.20) | copy-start | bytes 100
  2.3 10.4 %copy-start.2 = (s32[3]{0:T(128)S(1)}, s32[3]{0:T(128)}, u32[]{:S(2)}) copy-start(s32[3]{0:T(128)} %param.23) | copy-start | bytes 40
  2.3 12.5 %copy-start.3 = (f32[8]{0:T(128)S(1)}, f32[8]{0:T(128)}, u32[]{:S(2)}) copy-start(f32[8]{0:T(128)} %param.21) | copy-start | bytes 100
  2.3 13.2 %copy-start.4 = (f32[16,128]{1,0:T(8,128)S(1)}, f32[16,128]{1,0:T(8,128)}, u32[]{:S(2)}) copy-start(f32[16,128]{1,0:T(8,128)} %constant.105) | copy-start | bytes 24580
  2.4 13.3 %collective-permute-start = (f32[5,8,2048]{2,1,0:T(8,128)S(1)}, f32[5,8,2048]{2,1,0:T(8,128)}, u32[]{:S(2)}, u32[]{:S(2)}) collective-permute-start(f32[5,8,2048]{2,1,0:T(8,128)S(1)} %get-tuple-element.137), channel_id=1, source_target_pairs={{0,1},{1,2},{2,3},{3,0},{8,9},{9,10},{10,11},{11,8},{12,13},{13,14... | collective-permute-start | bytes 983048 | tf_op jit(solution)/shard_map/ppermute | solution.py:495
  5.6 27.4 %collective-permute-start.1 = (f32[5,8,2048]{2,1,0:T(8,128)S(1)}, f32[5,8,2048]{2,1,0:T(8,128)S(1)}, u32[]{:S(2)}, u32[]{:S(2)}) collective-permute-start(f32[5,8,2048]{2,1,0:T(8,128)S(1)} %get-tuple-element.138), channel_id=1, source_target_pairs={{0,2},{1,3},{2,0},{3,1},{8,10},{9,11},{10,8},{11,9},{12,14},{13,15... | collective-permute-start | bytes 983048 | tf_op jit(solution)/shard_map/ppermute | solution.py:495
  8.6 27.3 %collective-permute-start.2 = (f32[5,8,2048]{2,1,0:T(8,128)S(1)}, f32[5,8,2048]{2,1,0:T(8,128)S(1)}, u32[]{:S(2)}, u32[]{:S(2)}) collective-permute-start(f32[5,8,2048]{2,1,0:T(8,128)S(1)} %get-tuple-element.136), channel_id=1, source_target_pairs={{0,3},{1,0},{2,1},{3,2},{8,11},{9,8},{10,9},{11,10},{12,15},{13,12... | collective-permute-start | bytes 983048 | tf_op jit(solution)/shard_map/ppermute | solution.py:495
  35.9 1.0 %copy-start.5 = (bf16[256,256]{1,0:T(8,128)(2,1)S(1)}, bf16[256,256]{1,0:T(8,128)(2,1)}, u32[]{:S(2)}) copy-start(bf16[256,256]{1,0:T(8,128)(2,1)} %constant.100.clone.refs_7_) | copy-start | bytes 393220
  35.9 1.0 %copy-start.6 = (bf16[256,256]{1,0:T(8,128)(2,1)S(1)}, bf16[256,256]{1,0:T(8,128)(2,1)}, u32[]{:S(2)}) copy-start(bf16[256,256]{1,0:T(8,128)(2,1)} %constant.101.clone.refs_8_) | copy-start | bytes 393220
  35.9 1.0 %copy-start.7 = (bf16[256,256]{1,0:T(8,128)(2,1)S(1)}, bf16[256,256]{1,0:T(8,128)(2,1)}, u32[]{:S(2)}) copy-start(bf16[256,256]{1,0:T(8,128)(2,1)} %constant.98.clone.refs_5_) | copy-start | bytes 393220
  35.9 1.2 %copy-start.8 = (bf16[256,256]{1,0:T(8,128)(2,1)S(1)}, bf16[256,256]{1,0:T(8,128)(2,1)}, u32[]{:S(2)}) copy-start(bf16[256,256]{1,0:T(8,128)(2,1)} %constant.99.clone.refs_6_) | copy-start | bytes 393220
  36.0 1.2 %copy-start.9 = (f32[2,16,128]{2,1,0:T(8,128)S(1)}, f32[2,16,128]{2,1,0:T(8,128)}, u32[]{:S(2)}) copy-start(f32[2,16,128]{2,1,0:T(8,128)} %constant.97.clone.refs_4_) | copy-start | bytes 49156
  44.6 2.8 %collective-permute-start.4 = (f32[3,8,2048]{2,1,0:T(8,128)S(1)}, f32[3,8,2048]{2,1,0:T(8,128)S(1)}, u32[]{:S(2)}, u32[]{:S(2)}) collective-permute-start(f32[3,8,2048]{2,1,0:T(8,128)S(1)} %convert_element_type.21), channel_id=1, source_target_pairs={{4,5},{5,6},{6,7},{7,4},{20,21},{21,22},{22,23},{23,20}} | collective-permute-start | bytes 589832 | tf_op jit(solution)/shard_map/ppermute | solution.py:495
  45.3 2.2 %collective-permute-start.5 = (f32[3,8,2048]{2,1,0:T(8,128)S(1)}, f32[3,8,2048]{2,1,0:T(8,128)S(1)}, u32[]{:S(2)}, u32[]{:S(2)}) collective-permute-start(f32[3,8,2048]{2,1,0:T(8,128)S(1)} %convert_element_type.21), channel_id=1, source_target_pairs={{4,6},{5,7},{6,4},{7,5},{20,22},{21,23},{22,20},{23,21}} | collective-permute-start | bytes 589832 | tf_op jit(solution)/shard_map/ppermute | solution.py:495
  45.9 1.6 %collective-permute-start.6 = (f32[3,8,2048]{2,1,0:T(8,128)S(1)}, f32[3,8,2048]{2,1,0:T(8,128)S(1)}, u32[]{:S(2)}, u32[]{:S(2)}) collective-permute-start(f32[3,8,2048]{2,1,0:T(8,128)S(1)} %convert_element_type.21), channel_id=1, source_target_pairs={{4,7},{5,4},{6,5},{7,6},{20,23},{21,20},{22,21},{23,22}} | collective-permute-start | bytes 589832 | tf_op jit(solution)/shard_map/ppermute | solution.py:495
  46.6 1.0 %collective-permute-start.3 = (f32[2,32,2048]{2,1,0:T(8,128)}, f32[2,32,2048]{2,1,0:T(8,128)S(1)}, u32[]{:S(2)}, u32[]{:S(2)}) collective-permute-start(f32[2,32,2048]{2,1,0:T(8,128)} %get-tuple-element.117), channel_id=1, source_target_pairs={{0,4},{1,5},{2,6},{3,7},{16,20},{17,21},{18,22},{19,23}} | collective-permute-start | bytes 1572872 | tf_op jit(solution)/shard_map/ppermute | solution.py:558
  47.6 0.7 collective-permute-start.7
  48.4 20.5 %collective-permute-start.8 = (f32[2,32,2048]{2,1,0:T(8,128)S(1)}, f32[2,32,2048]{2,1,0:T(8,128)S(1)}, u32[]{:S(2)}, u32[]{:S(2)}) collective-permute-start(f32[2,32,2048]{2,1,0:T(8,128)S(1)} %get-tuple-element.122), channel_id=1, source_target_pairs={{8,12},{9,13},{10,14},{11,15},{24,28},{25,29},{26,30},{27,31}} | collective-permute-start | bytes 1572872 | tf_op jit(solution)/shard_map/ppermute | solution.py:558
  76.2 10.0 %collective-permute-start.12 = (f32[3,8,2048]{2,1,0:T(8,128)S(1)}, f32[3,8,2048]{2,1,0:T(8,128)S(1)}, u32[]{:S(2)}, u32[]{:S(2)}) collective-permute-start(f32[3,8,2048]{2,1,0:T(8,128)S(1)} %get-tuple-element.129), channel_id=1, source_target_pairs={{12,13},{13,14},{14,15},{15,12},{28,29},{29,30},{30,31},{31,28}} | collective-permute-start | bytes 589832 | tf_op jit(solution)/shard_map/ppermute | solution.py:546
  78.2 13.1 %collective-permute-start.13 = (f32[3,8,2048]{2,1,0:T(8,128)S(1)}, f32[3,8,2048]{2,1,0:T(8,128)S(1)}, u32[]{:S(2)}, u32[]{:S(2)}) collective-permute-start(f32[3,8,2048]{2,1,0:T(8,128)S(1)} %get-tuple-element.131), channel_id=1, source_target_pairs={{12,14},{13,15},{14,12},{15,13},{28,30},{29,31},{30,28},{31,29}} | collective-permute-start | bytes 589832 | tf_op jit(solution)/shard_map/ppermute | solution.py:546
  81.5 10.7 %collective-permute-start.14 = (f32[3,8,2048]{2,1,0:T(8,128)S(1)}, f32[3,8,2048]{2,1,0:T(8,128)S(1)}, u32[]{:S(2)}, u32[]{:S(2)}) collective-permute-start(f32[3,8,2048]{2,1,0:T(8,128)S(1)} %get-tuple-element.130), channel_id=1, source_target_pairs={{12,15},{13,12},{14,13},{15,14},{28,31},{29,28},{30,29},{31,30}} | collective-permute-start | bytes 589832 | tf_op jit(solution)/shard_map/ppermute | solution.py:546
  84.9 7.3 %collective-permute-start.10 = (f32[3,8,2048]{2,1,0:T(8,128)S(1)}, f32[3,8,2048]{2,1,0:T(8,128)S(1)}, u32[]{:S(2)}, u32[]{:S(2)}) collective-permute-start(f32[3,8,2048]{2,1,0:T(8,128)S(1)} %get-tuple-element.128), channel_id=1, source_target_pairs={{0,2},{1,3},{2,0},{3,1},{4,6},{5,7},{6,4},{7,5},{8,10},{9,11},{10,... | collective-permute-start | bytes 589832 | tf_op jit(solution)/shard_map/ppermute | solution.py:546
  85.5 6.6 %collective-permute-start.11 = (f32[3,8,2048]{2,1,0:T(8,128)S(1)}, f32[3,8,2048]{2,1,0:T(8,128)S(1)}, u32[]{:S(2)}, u32[]{:S(2)}) collective-permute-start(f32[3,8,2048]{2,1,0:T(8,128)S(1)} %get-tuple-element.127), channel_id=1, source_target_pairs={{0,3},{1,0},{2,1},{3,2},{4,7},{5,4},{6,5},{7,6},{8,11},{9,8},{10,9... | collective-permute-start | bytes 589832 | tf_op jit(solution)/shard_map/ppermute | solution.py:546
  86.2 5.9 %collective-permute-start.9 = (f32[3,8,2048]{2,1,0:T(8,128)S(1)}, f32[3,8,2048]{2,1,0:T(8,128)S(1)}, u32[]{:S(2)}, u32[]{:S(2)}) collective-permute-start(f32[3,8,2048]{2,1,0:T(8,128)S(1)} %get-tuple-element.126), channel_id=1, source_target_pairs={{0,1},{1,2},{2,3},{3,0},{4,5},{5,6},{6,7},{7,4},{8,9},{9,10},{10,1... | collective-permute-start | bytes 589832 | tf_op jit(solution)/shard_map/ppermute | solution.py:546

commit v21 on v18

--- a/solution.py
+++ b/solution.py
@@ -182,6 +182,7 @@
 LANE = 128
 FFT_BLOCKS = 16
 ROW_CHUNK = 8
+FFT_ROWS = 16
 
 
 def fft4(x0, x1, x2, x3, sign):
@@ -259,7 +260,7 @@
     line_len = w_ref.shape[2]
     steps = rid_ref.shape[0]
     strip_count, rows_here = img_ref.shape[0], img_ref.shape[2]
-    chunks = rows // ROW_CHUNK
+    chunks = rows // FFT_ROWS
     inv_len = 1.0 / line_len
     wout_ref[...] = w_ref[...]
 
@@ -273,9 +274,9 @@
         gain_t = [tab_ref[base + 2 * table_len + g] for g in range(table_len)]
 
         def forward_chunk(i, c):
-            y0 = pl.multiple_of(i * ROW_CHUNK, ROW_CHUNK)
+            y0 = pl.multiple_of(i * FFT_ROWS, FFT_ROWS)
             parts = [
-                (wout_ref[0, pl.ds(y0, ROW_CHUNK), blk(a)], wout_ref[1, pl.ds(y0, ROW_CHUNK), blk(a)])
+                (wout_ref[0, pl.ds(y0, FFT_ROWS), blk(a)], wout_ref[1, pl.ds(y0, FFT_ROWS), blk(a)])
                 for a in range(FFT_BLOCKS)
             ]
             spec = fft16(parts, -1)
@@ -283,8 +284,8 @@
                 tc = tw_ref[0, cc:cc + 1, :]
                 ts = tw_ref[1, cc:cc + 1, :]
                 xr, xi = spec[cc]
-                a_ref[pl.ds(cc * rows + y0, ROW_CHUNK), 0:LANE] = xr * tc + xi * ts
-                a_ref[pl.ds(cc * rows + y0, ROW_CHUNK), LANE:2 * LANE] = xi * tc - xr * ts
+                a_ref[pl.ds(cc * rows + y0, FFT_ROWS), 0:LANE] = xr * tc + xi * ts
+                a_ref[pl.ds(cc * rows + y0, FFT_ROWS), LANE:2 * LANE] = xi * tc - xr * ts
             return c
 
         lax.fori_loop(0, chunks, forward_chunk, 0, unroll=True)
@@ -307,11 +308,11 @@
         y_ref[...] = split_dot(a_ref[...], ghi_ref, glo_ref)
 
         def inverse_chunk(i, c):
-            y0 = pl.multiple_of(i * ROW_CHUNK, ROW_CHUNK)
+            y0 = pl.multiple_of(i * FFT_ROWS, FFT_ROWS)
             parts = []
             for cc in range(FFT_BLOCKS):
-                zr = y_ref[pl.ds(cc * rows + y0, ROW_CHUNK), 0:LANE]
-                zi = y_ref[pl.ds(cc * rows + y0, ROW_CHUNK), LANE:2 * LANE]
+                zr = y_ref[pl.ds(cc * rows + y0, FFT_ROWS), 0:LANE]
+                zi = y_ref[pl.ds(cc * rows + y0, FFT_ROWS), LANE:2 * LANE]
                 tc = tw_ref[0, cc:cc + 1, :]
                 ts = tw_ref[1, cc:cc + 1, :]
                 parts.append((zr * tc - zi * ts, zr * ts + zi * tc))
@@ -319,10 +320,10 @@
             for a in range(FFT_BLOCKS):
                 ur = back[a][0] * inv_len
                 ui = back[a][1] * inv_len
-                cs = cs_ref[pl.ds(y0, ROW_CHUNK), blk(a)]
-                sn = sn_ref[pl.ds(y0, ROW_CHUNK), blk(a)]
-                v_ref[0, pl.ds(y0, ROW_CHUNK), blk(a)] = ur * cs - ui * sn
-                v_ref[1, pl.ds(y0, ROW_CHUNK), blk(a)] = ur * sn + ui * cs
+                cs = cs_ref[pl.ds(y0, FFT_ROWS), blk(a)]
+                sn = sn_ref[pl.ds(y0, FFT_ROWS), blk(a)]
+                v_ref[0, pl.ds(y0, FFT_ROWS), blk(a)] = ur * cs - ui * sn
+                v_ref[1, pl.ds(y0, FFT_ROWS), blk(a)] = ur * sn + ui * cs
             return c
 
         lax.fori_loop(0, chunks, inverse_chunk, 0, unroll=True)
@@ -444,7 +445,7 @@
     return (
         freq_count == lax.axis_size("strip")
         and line_len == FFT_BLOCKS * LANE
-        and rows % ROW_CHUNK == 0
+        and rows % FFT_ROWS == 0
         and surface.shape[2] % ROW_CHUNK == 0
         and rows <= 64
         and region_speed.shape[0] <= 16

time: 93.6 us -> 93.6 us (level)
  no operation moved by 1% of the time
where the time goes in v21:
time: 93.6 us; the launch traced here: 92.6 us
  waiting for transfers between devices  43.5 us (46%)
  starting transfers between devices  24.8 us (26%)
  Pallas kernels  14.4 us (15%)
  local copies, waits for them, and re-layouts  5.02 us (5%)
  other arithmetic  4.26 us (5%)
    ppermute x6, waiting for transfers between devices, gather_strips(): lax.ppermute(piece_of(target), ('depth', 'strip'), strip_pairs(depths, st...  19.1 us
    ppermute x3, waiting for transfers between devices, shards(): wave = lax.ppermute(wave, 'depth', [(tick_no, tick_no + 1)])  19 us
    pallas_call x2, Pallas kernels, run_section(): pl.pallas_call(lambda *refs: section_kernel(*refs, table_len=table_len),...  14.4 us
    ppermute x6, starting transfers between devices, gather_strips(): lax.ppermute(piece_of(target), ('depth', 'strip'), strip_pairs(depths, st...  11.5 us
    ppermute x6, starting transfers between devices, freq_sum(): lax.ppermute(piece, ('depth', 'strip'), strip_pairs(depths, strip_count,...  10.6 us
    ppermute x6, waiting for transfers between devices, freq_sum(): lax.ppermute(piece, ('depth', 'strip'), strip_pairs(depths, strip_count,...  5.41 us
    ppermute x3, starting transfers between devices, shards(): wave = lax.ppermute(wave, 'depth', [(tick_no, tick_no + 1)])  2.68 us
  transfers between devices with their start and end apart: 15, of which 5 were waited for; matrix products, arithmetic and copies ran while one was open for 5% of the time, Pallas kernels for 0%

profile of v21, /device:TPU:11, one launch (start us, length us, event | category | flops | bytes accessed | tf_op | source)
XLA Modules:
  0.0 92.6 jit_solution(10757310591645831357)
XLA Ops:
  0.0 0.9 %convert_element_type.21 = f32[3,8,2048]{2,1,0:T(8,128)S(1)} convert(s32[3,8,2048]{2,1,0:T(8,128)} %param.22) | non-fusion elementwise | flops 49152 | bytes 393216 | tf_op jit(solution)/shard_map/convert_element_type | solution.py:506
  1.0 1.1 %dynamic-slice_bitcast_fusion = (f32[2,8,2048]{2,1,0:T(8,128)S(1)}, f32[2,8,2048]{2,1,0:T(8,128)S(1)}, f32[2,8,2048]{2,1,0:T(8,128)S(1)}, f32[2,8,2048]{2,1,0:T(8,128)S(1)}) fusion(f32[2,4,8,2048]{3,2,1,0:T(8,128)} %param.18, s32[]{:T(128)S(6)} %select_n.79, s32[]{:T(128)S(6)} %select_n.71, s32[]{:T(128)S(6)} %select_n.67, s32[]{:T(128)S(6)} %select_n.75), kind=kLoop, calls=%fused_computation.20 | loop fusion | bytes 1048592 | tf_op jit(solution)/shard_map/jit(dynamic_index_in_dim)/squeeze | solution.py:511
  2.4 3.2 %collective-permute-start = (f32[5,8,2048]{2,1,0:T(8,128)S(1)}, f32[5,8,2048]{2,1,0:T(8,128)}, u32[]{:S(2)}, u32[]{:S(2)}) collective-permute-start(f32[5,8,2048]{2,1,0:T(8,128)S(1)} %get-tuple-element.137), channel_id=1, source_target_pairs={{0,1},{1,2},{2,3},{3,0},{8,9},{9,10},{10,11},{11,8},{12,13},{13,14... | collective-permute-start | bytes 983048 | tf_op jit(solution)/shard_map/ppermute | solution.py:487
  5.6 2.9 %collective-permute-start.1 = (f32[5,8,2048]{2,1,0:T(8,128)S(1)}, f32[5,8,2048]{2,1,0:T(8,128)S(1)}, u32[]{:S(2)}, u32[]{:S(2)}) collective-permute-start(f32[5,8,2048]{2,1,0:T(8,128)S(1)} %get-tuple-element.138), channel_id=1, source_target_pairs={{0,2},{1,3},{2,0},{3,1},{8,10},{9,11},{10,8},{11,9},{12,14},{13,15... | collective-permute-start | bytes 983048 | tf_op jit(solution)/shard_map/ppermute | solution.py:487
  8.6 3.4 %collective-permute-start.2 = (f32[5,8,2048]{2,1,0:T(8,128)S(1)}, f32[5,8,2048]{2,1,0:T(8,128)S(1)}, u32[]{:S(2)}, u32[]{:S(2)}) collective-permute-start(f32[5,8,2048]{2,1,0:T(8,128)S(1)} %get-tuple-element.136), channel_id=1, source_target_pairs={{0,3},{1,0},{2,1},{3,2},{8,11},{9,8},{10,9},{11,10},{12,15},{13,12... | collective-permute-start | bytes 983048 | tf_op jit(solution)/shard_map/ppermute | solution.py:487
  12.7 0.6 gather_fusion
  13.3 0.8 fusion.17
  14.1 0.7 multiply_multiply_fusion
  14.7 0.7 broadcast_divide_fusion
  15.7 1.0 %constant_dynamic-update-slice_fusion.6 = f32[5,32,2048]{2,1,0:T(8,128)S(1)} fusion(f32[5,32,2048]{2,1,0:T(8,128)S(1)} %get-tuple-element.139, f32[5,8,2048]{2,1,0:T(8,128)} %collective-permute-done, s32[]{:T(128)S(6)} %select_n.73), kind=kLoop, calls=%fused_computation.44 | loop fusion | bytes 655364 | tf_op jit(solution)/shard_map/dynamic_update_slice | solution.py:491
  16.7 16.3 %collective-permute-done.1 = f32[5,8,2048]{2,1,0:T(8,128)S(1)} collective-permute-done((f32[5,8,2048]{2,1,0:T(8,128)S(1)}, f32[5,8,2048]{2,1,0:T(8,128)S(1)}, u32[]{:S(2)}, u32[]{:S(2)}) %collective-permute-start.1) | collective-permute-done | bytes 327712 | tf_op jit(solution)/shard_map/ppermute | solution.py:487
  33.1 2.8 %collective-permute-done.2 = f32[5,8,2048]{2,1,0:T(8,128)S(1)} collective-permute-done((f32[5,8,2048]{2,1,0:T(8,128)S(1)}, f32[5,8,2048]{2,1,0:T(8,128)S(1)}, u32[]{:S(2)}, u32[]{:S(2)}) %collective-permute-start.2) | collective-permute-done | bytes 327712 | tf_op jit(solution)/shard_map/ppermute | solution.py:487
  36.1 0.8 slice.38.refs_1_
  37.2 7.3 %shard_map.118 = (f32[2,32,2048]{2,1,0:T(8,128)}, f32[4,3,8,2048]{3,2,1,0:T(8,128)S(1)}) custom-call(f32[72]{0:T(128)S(1)} %reshape.137.refs_0_, f32[2,32,2048]{2,1,0:T(8,128)} %slice.38.refs_1_, s32[3,32,2048]{2,1,0:T(8,128)S(1)} %slice_convert_fusion.refs_2_, f32[3,2,16,128]{3,2,1,0:T(8,128)S(1)} %pad_maximum_fusion.4.refs_3_, ...), custom_call_target="tpu_custom_call" | custom-call | flops 1286602752 | bytes 4718592 | tf_op jit(solution)/shard_map/pallas_call | solution.py:396
  44.4 0.7 collective-permute-start.4
  45.1 0.7 collective-permute-start.5
  45.8 0.7 collective-permute-start.6
  46.5 0.7 collective-permute-start.3
  47.5 0.7 collective-permute-start.7
  48.2 1.3 %collective-permute-start.8 = (f32[2,32,2048]{2,1,0:T(8,128)S(1)}, f32[2,32,2048]{2,1,0:T(8,128)S(1)}, u32[]{:S(2)}, u32[]{:S(2)}) collective-permute-start(f32[2,32,2048]{2,1,0:T(8,128)S(1)} %get-tuple-element.122), channel_id=1, source_target_pairs={{8,12},{9,13},{10,14},{11,15},{24,28},{25,29},{26,30},{27,31}} | collective-permute-start | bytes 1572872 | tf_op jit(solution)/shard_map/ppermute | solution.py:550
  49.5 19.0 %collective-permute-done.8 = f32[2,32,2048]{2,1,0:T(8,128)S(1)} collective-permute-done((f32[2,32,2048]{2,1,0:T(8,128)S(1)}, f32[2,32,2048]{2,1,0:T(8,128)S(1)}, u32[]{:S(2)}, u32[]{:S(2)}) %collective-permute-start.8) | collective-permute-done | bytes 524320 | tf_op jit(solution)/shard_map/ppermute | solution.py:550
  68.5 7.2 %conditional.5 = (f32[4,3,8,2048]{3,2,1,0:T(8,128)S(1)}) conditional(s32[]{:T(128)} %convert_element_type.18, f32[4,3,8,2048]{3,2,1,0:T(8,128)S(1)} %get-tuple-element.124, (s32[]{:T(128)}, f32[72]{0:T(128)S(1)}, f32[2,32,2048]{2,1,0:T(8,128)S(1)}, s32[3,32,2048]{2,1,0:T(8,128)S(1)}, f32[3,2,16,128]{3,2,1,0:T(8,128)S(1)}, ...), branch_computations={%region_4.5_spmd, %region_5.6_spmd} | conditional | flops 1286602752 | bytes 4718600 | solution.py:548
  68.5 7.2 %branch_1_fun.5 = (f32[2,32,2048]{2,1,0:T(8,128)}, f32[4,3,8,2048]{3,2,1,0:T(8,128)S(1)}) custom-call(f32[72]{0:T(128)S(1)} %get-tuple-element.97.refs_0_, f32[2,32,2048]{2,1,0:T(8,128)S(1)} %get-tuple-element.98.refs_1_, s32[3,32,2048]{2,1,0:T(8,128)S(1)} %get-tuple-element.99.refs_2_, f32[3,2,16,128]{3,2,1,0:T(8,128)S(1)} %get-tuple-element.100.refs_3_, ...), custom_call_target="tpu_custom_call" | custom-call | flops 1286602752 | bytes 4718592 | tf_op jit(solution)/shard_map/cond/branch_1_fun/pallas_call | solution.py:396
  75.7 1.9 %collective-permute-start.12 = (f32[3,8,2048]{2,1,0:T(8,128)S(1)}, f32[3,8,2048]{2,1,0:T(8,128)S(1)}, u32[]{:S(2)}, u32[]{:S(2)}) collective-permute-start(f32[3,8,2048]{2,1,0:T(8,128)S(1)} %get-tuple-element.129), channel_id=1, source_target_pairs={{12,13},{13,14},{14,15},{15,12},{28,29},{29,30},{30,31},{31,28}} | collective-permute-start | bytes 589832 | tf_op jit(solution)/shard_map/ppermute | solution.py:538
  77.7 3.3 %collective-permute-start.13 = (f32[3,8,2048]{2,1,0:T(8,128)S(1)}, f32[3,8,2048]{2,1,0:T(8,128)S(1)}, u32[]{:S(2)}, u32[]{:S(2)}) collective-permute-start(f32[3,8,2048]{2,1,0:T(8,128)S(1)} %get-tuple-element.131), channel_id=1, source_target_pairs={{12,14},{13,15},{14,12},{15,13},{28,30},{29,31},{30,28},{31,29}} | collective-permute-start | bytes 589832 | tf_op jit(solution)/shard_map/ppermute | solution.py:538
  81.0 3.4 %collective-permute-start.14 = (f32[3,8,2048]{2,1,0:T(8,128)S(1)}, f32[3,8,2048]{2,1,0:T(8,128)S(1)}, u32[]{:S(2)}, u32[]{:S(2)}) collective-permute-start(f32[3,8,2048]{2,1,0:T(8,128)S(1)} %get-tuple-element.130), channel_id=1, source_target_pairs={{12,15},{13,12},{14,13},{15,14},{28,31},{29,28},{30,29},{31,30}} | collective-permute-start | bytes 589832 | tf_op jit(solution)/shard_map/ppermute | solution.py:538
  84.4 0.7 collective-permute-start.10
  85.1 0.7 collective-permute-start.11
  85.8 0.7 collective-permute-start.9
  86.4 4.3 %collective-permute-done.13 = f32[3,8,2048]{2,1,0:T(8,128)S(1)} collective-permute-done((f32[3,8,2048]{2,1,0:T(8,128)S(1)}, f32[3,8,2048]{2,1,0:T(8,128)S(1)}, u32[]{:S(2)}, u32[]{:S(2)}) %collective-permute-start.13) | collective-permute-done | bytes 196640 | tf_op jit(solution)/shard_map/ppermute | solution.py:538
  90.8 1.1 %collective-permute-done.14 = f32[3,8,2048]{2,1,0:T(8,128)S(1)} collective-permute-done((f32[3,8,2048]{2,1,0:T(8,128)S(1)}, f32[3,8,2048]{2,1,0:T(8,128)S(1)}, u32[]{:S(2)}, u32[]{:S(2)}) %collective-permute-start.14) | collective-permute-done | bytes 196640 | tf_op jit(solution)/shard_map/ppermute | solution.py:538
  91.9 0.8 fusion.6
  (54 shorter events, 1.9 us)
Async XLA Ops:
  2.2 9.8 %copy-start = (f32[4]{0:T(128)S(1)}, f32[4]{0:T(128)}, u32[]{:S(2)}) copy-start(f32[4]{0:T(128)} %param.19) | copy-start | bytes 52
  2.3 10.4 %copy-start.1 = (f32[8]{0:T(128)S(1)}, f32[8]{0:T(128)}, u32[]{:S(2)}) copy-start(f32[8]{0:T(128)} %param.20) | copy-start | bytes 100
  2.3 10.4 %copy-start.2 = (s32[3]{0:T(128)S(1)}, s32[3]{0:T(128)}, u32[]{:S(2)}) copy-start(s32[3]{0:T(128)} %param.23) | copy-start | bytes 40
  2.3 12.5 %copy-start.3 = (f32[8]{0:T(128)S(1)}, f32[8]{0:T(128)}, u32[]{:S(2)}) copy-start(f32[8]{0:T(128)} %param.21) | copy-start | bytes 100
  2.3 13.2 %copy-start.4 = (f32[16,128]{1,0:T(8,128)S(1)}, f32[16,128]{1,0:T(8,128)}, u32[]{:S(2)}) copy-start(f32[16,128]{1,0:T(8,128)} %constant.105) | copy-start | bytes 24580
  2.4 13.3 %collective-permute-start = (f32[5,8,2048]{2,1,0:T(8,128)S(1)}, f32[5,8,2048]{2,1,0:T(8,128)}, u32[]{:S(2)}, u32[]{:S(2)}) collective-permute-start(f32[5,8,2048]{2,1,0:T(8,128)S(1)} %get-tuple-element.137), channel_id=1, source_target_pairs={{0,1},{1,2},{2,3},{3,0},{8,9},{9,10},{10,11},{11,8},{12,13},{13,14... | collective-permute-start | bytes 983048 | tf_op jit(solution)/shard_map/ppermute | solution.py:487
  5.6 27.4 %collective-permute-start.1 = (f32[5,8,2048]{2,1,0:T(8,128)S(1)}, f32[5,8,2048]{2,1,0:T(8,128)S(1)}, u32[]{:S(2)}, u32[]{:S(2)}) collective-permute-start(f32[5,8,2048]{2,1,0:T(8,128)S(1)} %get-tuple-element.138), channel_id=1, source_target_pairs={{0,2},{1,3},{2,0},{3,1},{8,10},{9,11},{10,8},{11,9},{12,14},{13,15... | collective-permute-start | bytes 983048 | tf_op jit(solution)/shard_map/ppermute | solution.py:487
  8.6 27.3 %collective-permute-start.2 = (f32[5,8,2048]{2,1,0:T(8,128)S(1)}, f32[5,8,2048]{2,1,0:T(8,128)S(1)}, u32[]{:S(2)}, u32[]{:S(2)}) collective-permute-start(f32[5,8,2048]{2,1,0:T(8,128)S(1)} %get-tuple-element.136), channel_id=1, source_target_pairs={{0,3},{1,0},{2,1},{3,2},{8,11},{9,8},{10,9},{11,10},{12,15},{13,12... | collective-permute-start | bytes 983048 | tf_op jit(solution)/shard_map/ppermute | solution.py:487
  35.9 1.0 %copy-start.5 = (bf16[256,256]{1,0:T(8,128)(2,1)S(1)}, bf16[256,256]{1,0:T(8,128)(2,1)}, u32[]{:S(2)}) copy-start(bf16[256,256]{1,0:T(8,128)(2,1)} %constant.100.clone.refs_7_) | copy-start | bytes 393220
  35.9 1.0 %copy-start.6 = (bf16[256,256]{1,0:T(8,128)(2,1)S(1)}, bf16[256,256]{1,0:T(8,128)(2,1)}, u32[]{:S(2)}) copy-start(bf16[256,256]{1,0:T(8,128)(2,1)} %constant.101.clone.refs_8_) | copy-start | bytes 393220
  35.9 1.0 %copy-start.7 = (bf16[256,256]{1,0:T(8,128)(2,1)S(1)}, bf16[256,256]{1,0:T(8,128)(2,1)}, u32[]{:S(2)}) copy-start(bf16[256,256]{1,0:T(8,128)(2,1)} %constant.98.clone.refs_5_) | copy-start | bytes 393220
  35.9 1.2 %copy-start.8 = (bf16[256,256]{1,0:T(8,128)(2,1)S(1)}, bf16[256,256]{1,0:T(8,128)(2,1)}, u32[]{:S(2)}) copy-start(bf16[256,256]{1,0:T(8,128)(2,1)} %constant.99.clone.refs_6_) | copy-start | bytes 393220
  36.0 1.2 %copy-start.9 = (f32[2,16,128]{2,1,0:T(8,128)S(1)}, f32[2,16,128]{2,1,0:T(8,128)}, u32[]{:S(2)}) copy-start(f32[2,16,128]{2,1,0:T(8,128)} %constant.97.clone.refs_4_) | copy-start | bytes 49156
  44.4 2.8 %collective-permute-start.4 = (f32[3,8,2048]{2,1,0:T(8,128)S(1)}, f32[3,8,2048]{2,1,0:T(8,128)S(1)}, u32[]{:S(2)}, u32[]{:S(2)}) collective-permute-start(f32[3,8,2048]{2,1,0:T(8,128)S(1)} %convert_element_type.21), channel_id=1, source_target_pairs={{4,5},{5,6},{6,7},{7,4},{20,21},{21,22},{22,23},{23,20}} | collective-permute-start | bytes 589832 | tf_op jit(solution)/shard_map/ppermute | solution.py:487
  45.1 2.2 %collective-permute-start.5 = (f32[3,8,2048]{2,1,0:T(8,128)S(1)}, f32[3,8,2048]{2,1,0:T(8,128)S(1)}, u32[]{:S(2)}, u32[]{:S(2)}) collective-permute-start(f32[3,8,2048]{2,1,0:T(8,128)S(1)} %convert_element_type.21), channel_id=1, source_target_pairs={{4,6},{5,7},{6,4},{7,5},{20,22},{21,23},{22,20},{23,21}} | collective-permute-start | bytes 589832 | tf_op jit(solution)/shard_map/ppermute | solution.py:487
  45.8 1.6 %collective-permute-start.6 = (f32[3,8,2048]{2,1,0:T(8,128)S(1)}, f32[3,8,2048]{2,1,0:T(8,128)S(1)}, u32[]{:S(2)}, u32[]{:S(2)}) collective-permute-start(f32[3,8,2048]{2,1,0:T(8,128)S(1)} %convert_element_type.21), channel_id=1, source_target_pairs={{4,7},{5,4},{6,5},{7,6},{20,23},{21,20},{22,21},{23,22}} | collective-permute-start | bytes 589832 | tf_op jit(solution)/shard_map/ppermute | solution.py:487
  46.5 1.0 %collective-permute-start.3 = (f32[2,32,2048]{2,1,0:T(8,128)}, f32[2,32,2048]{2,1,0:T(8,128)S(1)}, u32[]{:S(2)}, u32[]{:S(2)}) collective-permute-start(f32[2,32,2048]{2,1,0:T(8,128)} %get-tuple-element.117), channel_id=1, source_target_pairs={{0,4},{1,5},{2,6},{3,7},{16,20},{17,21},{18,22},{19,23}} | collective-permute-start | bytes 1572872 | tf_op jit(solution)/shard_map/ppermute | solution.py:550
  47.5 0.7 collective-permute-start.7
  48.2 20.3 %collective-permute-start.8 = (f32[2,32,2048]{2,1,0:T(8,128)S(1)}, f32[2,32,2048]{2,1,0:T(8,128)S(1)}, u32[]{:S(2)}, u32[]{:S(2)}) collective-permute-start(f32[2,32,2048]{2,1,0:T(8,128)S(1)} %get-tuple-element.122), channel_id=1, source_target_pairs={{8,12},{9,13},{10,14},{11,15},{24,28},{25,29},{26,30},{27,31}} | collective-permute-start | bytes 1572872 | tf_op jit(solution)/shard_map/ppermute | solution.py:550
  75.7 10.0 %collective-permute-start.12 = (f32[3,8,2048]{2,1,0:T(8,128)S(1)}, f32[3,8,2048]{2,1,0:T(8,128)S(1)}, u32[]{:S(2)}, u32[]{:S(2)}) collective-permute-start(f32[3,8,2048]{2,1,0:T(8,128)S(1)} %get-tuple-element.129), channel_id=1, source_target_pairs={{12,13},{13,14},{14,15},{15,12},{28,29},{29,30},{30,31},{31,28}} | collective-permute-start | bytes 589832 | tf_op jit(solution)/shard_map/ppermute | solution.py:538
  77.7 13.1 %collective-permute-start.13 = (f32[3,8,2048]{2,1,0:T(8,128)S(1)}, f32[3,8,2048]{2,1,0:T(8,128)S(1)}, u32[]{:S(2)}, u32[]{:S(2)}) collective-permute-start(f32[3,8,2048]{2,1,0:T(8,128)S(1)} %get-tuple-element.131), channel_id=1, source_target_pairs={{12,14},{13,15},{14,12},{15,13},{28,30},{29,31},{30,28},{31,29}} | collective-permute-start | bytes 589832 | tf_op jit(solution)/shard_map/ppermute | solution.py:538
  81.0 10.8 %collective-permute-start.14 = (f32[3,8,2048]{2,1,0:T(8,128)S(1)}, f32[3,8,2048]{2,1,0:T(8,128)S(1)}, u32[]{:S(2)}, u32[]{:S(2)}) collective-permute-start(f32[3,8,2048]{2,1,0:T(8,128)S(1)} %get-tuple-element.130), channel_id=1, source_target_pairs={{12,15},{13,12},{14,13},{15,14},{28,31},{29,28},{30,29},{31,30}} | collective-permute-start | bytes 589832 | tf_op jit(solution)/shard_map/ppermute | solution.py:538
  84.4 7.5 %collective-permute-start.10 = (f32[3,8,2048]{2,1,0:T(8,128)S(1)}, f32[3,8,2048]{2,1,0:T(8,128)S(1)}, u32[]{:S(2)}, u32[]{:S(2)}) collective-permute-start(f32[3,8,2048]{2,1,0:T(8,128)S(1)} %get-tuple-element.128), channel_id=1, source_target_pairs={{0,2},{1,3},{2,0},{3,1},{4,6},{5,7},{6,4},{7,5},{8,10},{9,11},{10,... | collective-permute-start | bytes 589832 | tf_op jit(solution)/shard_map/ppermute | solution.py:538
  85.1 6.8 %collective-permute-start.11 = (f32[3,8,2048]{2,1,0:T(8,128)S(1)}, f32[3,8,2048]{2,1,0:T(8,128)S(1)}, u32[]{:S(2)}, u32[]{:S(2)}) collective-permute-start(f32[3,8,2048]{2,1,0:T(8,128)S(1)} %get-tuple-element.127), channel_id=1, source_target_pairs={{0,3},{1,0},{2,1},{3,2},{4,7},{5,4},{6,5},{7,6},{8,11},{9,8},{10,9... | collective-permute-start | bytes 589832 | tf_op jit(solution)/shard_map/ppermute | solution.py:538
  85.8 6.1 %collective-permute-start.9 = (f32[3,8,2048]{2,1,0:T(8,128)S(1)}, f32[3,8,2048]{2,1,0:T(8,128)S(1)}, u32[]{:S(2)}, u32[]{:S(2)}) collective-permute-start(f32[3,8,2048]{2,1,0:T(8,128)S(1)} %get-tuple-element.126), channel_id=1, source_target_pairs={{0,1},{1,2},{2,3},{3,0},{4,5},{5,6},{6,7},{7,4},{8,9},{9,10},{10,1... | collective-permute-start | bytes 589832 | tf_op jit(solution)/shard_map/ppermute | solution.py:538
